TPU v7x, 32 devices: a whole 2x2x4 slice. The times are simulated.
32 devices in a mesh: blk: 16 (over z, y, core), rel: 2 (over x).
Axes of the slice: x: 2, y: 2, z: 4, core: 2. Of those that a mesh axis runs over, the one named last changes fastest.
Arguments:
- words: bfloat16 [4096, 800], P('blk'), may hold values from -1.5 to 1.5
- contexts: bfloat16 [4096, 800], P('blk'), may hold values from -1.5 to 1.5
- relations: bfloat16 [1024, 800], P(('blk', 'rel')), may hold values from -6 to 6
- word_index: int32 [8192], P(('blk', 'rel')), may hold values from 0 to 255
- context_index: int32 [8192], P(('blk', 'rel')), may hold values from 0 to 255
- rel_slot: int32 [8192], P(('blk', 'rel')), may hold values from 0 to 63, as said below
- neg_index: int32 [32, 1024], P(('blk', 'rel')), may hold values from 0 to 255
- requests: int32 [16, 2, 16, 2, 2], P('blk', 'rel'), may hold values from 0 to 31, as said below
- counts: int32 [16, 2, 16, 2], P('blk', 'rel'), may hold values from 0 to 2, as said below
Outputs:
- word_grad: bfloat16 [4096, 800], P('blk')
- context_grad: bfloat16 [4096, 800], P('blk')
- relation_grad: float32 [1024, 800], P(('blk', 'rel'))
Inputs may be any that keep to these rules, and one draw needn't show every extreme that they name: counts[b, r, b2, r2] is how many entries of the list of device (b, r) to owner (b2, r2) are live; each device's list to itself is full, and so are all lists to one owner. requests[b, r, b2, r2, k] is a row among the 32 relation rows of owner (b2, r2); the live entries of one list are distinct and come first, the others are 0. rel_slot of a triple of device (b, r) is a live slot s = (b2 * 2 + r2) * 2 + k of that device, with k < counts[b, r, b2, r2].
All inputs are finite; a program needn't handle non-finite values.
Results may differ from a plain program's by a relative error of at most 0.013.
Values may be sent and summed in bfloat16 or wider, within the bound.
No kernel may reach another device: no remote copies, remote signals or barrier semaphores. Data moves between devices by JAX's collectives and lax.ppermute only.
A program may use at most 64 MiB of HBM per device.

v0:
```python
import jax
import jax.numpy as jnp
from jax import lax
from jax.sharding import PartitionSpec as P


def passed_along(shard, axis, by):
    length = lax.axis_size(axis)
    return lax.ppermute(shard, axis, [(i, (i + by) % length) for i in range(length)])


def complex_product(left_vec, right_vec, half_width):
    left_re, left_im = (left_vec[:, :half_width], left_vec[:, half_width:])
    right_re, right_im = (right_vec[:, :half_width], right_vec[:, half_width:])
    return jnp.concatenate(
        [left_re * right_re - left_im * right_im, left_re * right_im + left_im * right_re], axis=1
    )


def conj_product(grad_vec, other_vec, half_width):
    grad_re, grad_im = (grad_vec[:, :half_width], grad_vec[:, half_width:])
    other_re, other_im = (other_vec[:, :half_width], other_vec[:, half_width:])
    return jnp.concatenate(
        [grad_re * other_re + grad_im * other_im, grad_im * other_re - grad_re * other_im], axis=1
    )


def one_hot_rows(index_ids, row_total):
    return (jnp.arange(row_total)[:, None] == index_ids[None, :]).astype(jnp.bfloat16)


def spread_rows(selector, terms):
    upper = terms.astype(jnp.bfloat16)
    lower = (terms - upper.astype(jnp.float32)).astype(jnp.bfloat16)
    return jnp.dot(selector, upper, preferred_element_type=jnp.float32) + jnp.dot(
        selector, lower, preferred_element_type=jnp.float32
    )


def shards(
    words, contexts, relations, word_index, context_index, rel_slot, neg_index, requests, counts
):
    row_width = words.shape[1]
    half_width = row_width // 2
    part_count = lax.axis_size("blk")
    split_count = lax.axis_size("rel")
    slot_count = requests.shape[-1]
    owned_rows = relations.shape[0]
    block_count = neg_index.shape[0]
    block_size = word_index.shape[0] // block_count
    part_rows = contexts.shape[0]
    neg_scale = float(neg_index.shape[1]) ** (-0.5)
    held_rows = passed_along(contexts, "blk", 1)
    wanted = requests[0, 0]
    incoming = lax.all_to_all(
        lax.all_to_all(wanted, "blk", split_axis=0, concat_axis=0, tiled=True),
        "rel",
        split_axis=1,
        concat_axis=1,
        tiled=True,
    )
    picked = relations[incoming.reshape(-1)].reshape(part_count, split_count, slot_count, row_width)
    fetched = lax.all_to_all(
        lax.all_to_all(picked, "blk", split_axis=0, concat_axis=0, tiled=True),
        "rel",
        split_axis=1,
        concat_axis=1,
        tiled=True,
    )
    slot_table = fetched.reshape(-1, row_width)
    slot_total = slot_table.shape[0]
    live_mask = (
        (jnp.arange(slot_count)[None, None, :] < counts[0, 0][:, :, None])
        .reshape(-1)
        .astype(jnp.float32)
    )
    word_used = words[word_index]
    ctx_used = held_rows[context_index]
    rel_used = slot_table[rel_slot]
    query = complex_product(
        word_used.astype(jnp.float32), rel_used.astype(jnp.float32), half_width
    ).astype(jnp.bfloat16)
    positive = jnp.einsum("td,td->t", query, ctx_used, preferred_element_type=jnp.float32)
    pos_grad = -jax.nn.sigmoid(-positive)
    ctx_start = spread_rows(
        one_hot_rows(context_index, part_rows), pos_grad[:, None] * query.astype(jnp.float32)
    )

    def block_step(ctx_total, inputs_one):
        query_block, ctx_block, neg_block, pos_block = inputs_one
        selector = one_hot_rows(neg_block, part_rows)
        neg_rows = lax.dot_general(
            selector, held_rows, (((0,), (0,)), ((), ())), preferred_element_type=jnp.float32
        ).astype(jnp.bfloat16)
        scores = lax.dot_general(
            query_block, neg_rows, (((1,), (1,)), ((), ())), preferred_element_type=jnp.float32
        )
        neg_grad = (jax.nn.sigmoid(scores) * neg_scale).astype(jnp.bfloat16)
        query_grad = pos_block[:, None] * ctx_block.astype(jnp.float32) + jnp.dot(
            neg_grad, neg_rows, preferred_element_type=jnp.float32
        )
        back_rows = lax.dot_general(
            neg_grad, query_block, (((0,), (0,)), ((), ())), preferred_element_type=jnp.float32
        )
        return (ctx_total + spread_rows(selector, back_rows), query_grad)

    ctx_part, query_grads = lax.scan(
        block_step,
        ctx_start,
        (
            query.reshape(block_count, block_size, row_width),
            ctx_used.reshape(block_count, block_size, row_width),
            neg_index,
            pos_grad.reshape(block_count, block_size),
        ),
    )
    query_grads = query_grads.reshape(-1, row_width)
    word_part = spread_rows(
        one_hot_rows(word_index, words.shape[0]),
        conj_product(query_grads, rel_used.astype(jnp.float32), half_width),
    )
    slot_grad = spread_rows(
        one_hot_rows(rel_slot, slot_total),
        conj_product(query_grads, word_used.astype(jnp.float32), half_width),
    )
    slot_grad = slot_grad + 0.02 * live_mask[:, None] * slot_table.astype(jnp.float32)
    word_sum, ctx_sum = (
        lax.psum(word_part.astype(jnp.bfloat16), "rel").astype(jnp.float32),
        lax.psum(ctx_part.astype(jnp.bfloat16), "rel").astype(jnp.float32),
    )
    outgoing = slot_grad.reshape(part_count, split_count, slot_count, row_width)
    returned = lax.all_to_all(
        lax.all_to_all(
            outgoing.astype(jnp.bfloat16), "blk", split_axis=0, concat_axis=0, tiled=True
        ),
        "rel",
        split_axis=1,
        concat_axis=1,
        tiled=True,
    ).astype(outgoing.dtype)
    owner_map = (incoming.reshape(-1)[None, :] == jnp.arange(owned_rows)[:, None]).astype(
        jnp.float32
    )
    relation_grad = jnp.dot(
        owner_map,
        returned.reshape(-1, row_width),
        precision=lax.Precision.HIGHEST,
        preferred_element_type=jnp.float32,
    )
    return (word_sum.astype(jnp.bfloat16), ctx_sum.astype(jnp.bfloat16), relation_grad)


def solution(mesh):
    return jax.shard_map(
        shards,
        mesh=mesh,
        in_specs=(
            P("blk", None),
            P("blk", None),
            P(("blk", "rel"), None),
            P(("blk", "rel")),
            P(("blk", "rel")),
            P(("blk", "rel")),
            P(("blk", "rel"), None),
            P("blk", "rel", None, None, None),
            P("blk", "rel", None, None),
        ),
        out_specs=(P("blk", None), P("blk", None), P(("blk", "rel"), None)),
        check_vma=False,
    )
```

profile of v0, /device:TPU:0, one launch (start us, length us, event | category | flops | bytes accessed | tf_op | source)
XLA Modules:
  0.0 111.6 jit_solution(12965899353701402154)
XLA Ops:
  7.2 1.4 %copy.51 = s32[16,2,2]{2,1,0:T(2,128)} copy(s32[16,2,2]{0,2,1:T(2,128)} %bitcast.14) | data formatting | bytes 512 | tf_op jit(solution)/shard_map/squeeze | solution.py:54
  8.6 7.4 %all-to-all-start = ((s32[16,2,2]{2,1,0:T(2,128)}), s32[16,2,2]{2,1,0:T(2,128)S(1)}, u32[]{:S(2)}, u32[]{:S(2)}) async-start(s32[16,2,2]{2,1,0:T(2,128)} %copy.51), calls=%async_computation | async-start | bytes 32768 | tf_op jit(solution)/shard_map/all_to_all | solution.py:56
  16.0 2.0 %copy.57 = bf16[256,800]{1,0:T(8,128)(2,1)} copy(bf16[256,800]{0,1:T(8,128)(2,1)} %param.10) | data formatting | bytes 819200 | tf_op args[1]
  19.8 0.8 copy.60
  20.6 1.9 %all-to-all-done = s32[16,2,2]{2,1,0:T(2,128)S(1)} async-done(((s32[16,2,2]{2,1,0:T(2,128)}), s32[16,2,2]{2,1,0:T(2,128)S(1)}, u32[]{:S(2)}, u32[]{:S(2)}) %all-to-all-start) | async-done | bytes 288 | tf_op jit(solution)/shard_map/all_to_all | solution.py:56
  23.2 3.2 %all-to-all-start.1 = ((s32[16,2,2]{0,2,1:T(2,128)}), s32[16,2,2]{0,2,1:T(2,128)S(1)}, u32[]{:S(2)}, u32[]{:S(2)}) async-start(s32[16,2,2]{0,2,1:T(2,128)} %copy.52), calls=%async_computation.1 | async-start | bytes 4096 | tf_op jit(solution)/shard_map/all_to_all | solution.py:55
  26.4 3.7 %all-to-all-done.1 = s32[16,2,2]{0,2,1:T(2,128)S(1)} async-done(((s32[16,2,2]{0,2,1:T(2,128)}), s32[16,2,2]{0,2,1:T(2,128)S(1)}, u32[]{:S(2)}, u32[]{:S(2)}) %all-to-all-start.1) | async-done | bytes 288 | tf_op jit(solution)/shard_map/all_to_all | solution.py:55
  31.8 3.9 %all-to-all-start.2 = ((bf16[16,2,2,800]{3,2,1,0:T(2,128)(2,1)}), bf16[16,2,2,800]{3,2,1,0:T(2,128)(2,1)S(1)}, u32[]{:S(2)}, u32[]{:S(2)}) async-start(bf16[16,2,2,800]{3,2,1,0:T(2,128)(2,1)} %reshape.86), calls=%async_computation.2 | async-start | bytes 229376 | tf_op jit(solution)/shard_map/all_to_all | solution.py:64
  35.7 7.7 %all-to-all-done.2 = bf16[16,2,2,800]{3,2,1,0:T(2,128)(2,1)S(1)} async-done(((bf16[16,2,2,800]{3,2,1,0:T(2,128)(2,1)}), bf16[16,2,2,800]{3,2,1,0:T(2,128)(2,1)S(1)}, u32[]{:S(2)}, u32[]{:S(2)}) %all-to-all-start.2) | async-done | bytes 102432 | tf_op jit(solution)/shard_map/all_to_all | solution.py:64
  43.4 0.7 copy.54
  44.1 3.4 %all-to-all-start.3 = ((bf16[16,2,2,800]{3,2,0,1:T(2,128)(2,1)}), bf16[16,2,2,800]{3,2,0,1:T(2,128)(2,1)S(1)}, u32[]{:S(2)}, u32[]{:S(2)}) async-start(bf16[16,2,2,800]{3,2,0,1:T(2,128)(2,1)} %copy.54), calls=%async_computation.3 | async-start | bytes 229376 | tf_op jit(solution)/shard_map/all_to_all | solution.py:63
  47.8 1.2 %gather_fusion = bf16[256,800]{1,0:T(8,128)(2,1)S(1)} fusion(bf16[256,800]{1,0:T(8,128)(2,1)S(1)} %copy.49, s32[1024]{0:T(1024)S(1)} %pad_clamp_fusion.3), kind=kCustom, calls=%fused_computation | custom fusion | bytes 820224 | tf_op jit(solution)/shard_map/gather | solution.py:77
  49.4 2.5 %all-to-all-done.3 = bf16[16,2,2,800]{3,2,0,1:T(2,128)(2,1)S(1)} async-done(((bf16[16,2,2,800]{3,2,0,1:T(2,128)(2,1)}), bf16[16,2,2,800]{3,2,0,1:T(2,128)(2,1)S(1)}, u32[]{:S(2)}, u32[]{:S(2)}) %all-to-all-start.3) | async-done | bytes 102432 | tf_op jit(solution)/shard_map/all_to_all | solution.py:63
  52.0 1.2 %gather_fusion.2 = bf16[256,800]{1,0:T(8,128)(2,1)S(1)} fusion(bf16[64,800]{1,0:T(8,128)(2,1)S(1)} %reshape.87, s32[1024]{0:T(1024)S(1)} %pad_clamp_fusion.1), kind=kCustom, calls=%fused_computation.2 | custom fusion | bytes 820224 | tf_op jit(solution)/shard_map/gather | solution.py:79
  53.7 1.2 %copy.66 = f32[256,800]{1,0:T(8,128)} copy(f32[256,800]{0,1:T(8,128)S(1)} %fusion.41) | data formatting | bytes 1638400
  55.6 0.9 fusion.6
  56.5 1.5 %fusion.42 = f32[256,800]{0,1:T(8,128)} fusion(bf16[256,1024]{1,0:T(8,128)(2,1)S(1)} %fusion.6, bf16[1024,800]{0,1:T(8,128)(2,1)S(1)} %convolution_convert_fusion), kind=kOutput, calls=%fused_computation.81 | convolution fusion | flops 419430400 | bytes 2981888 | tf_op jit(solution)/shard_map/while/body/eval_jaxpr/dot_general | solution.py:99
  58.0 2.3 %fusion.40 = f32[1024,800]{0,1:T(8,128)} fusion(bf16[256,1024]{1,0:T(8,128)(2,1)S(1)} %fusion.6, bf16[256,400]{0,1:T(8,128)(2,1)S(1)} %get-tuple-element.34, bf16[256,400]{0,1:T(8,128)(2,1)S(1)} %get-tuple-element.33), kind=kOutput, calls=%fused_computation.79 | convolution fusion | flops 420249600 | bytes 4210688 | tf_op jit(solution)/shard_map/while/body/eval_jaxpr/dot_general | solution.py:102
  60.3 1.2 %gather_fusion.3 = bf16[256,800]{1,0:T(8,128)(2,1)S(1)} fusion(bf16[256,800]{1,0:T(8,128)(2,1)S(1)} %collective-permute-done, s32[1024]{0:T(1024)S(1)} %pad_clamp_fusion), kind=kCustom, calls=%fused_computation.3 | custom fusion | bytes 820224 | tf_op jit(solution)/shard_map/gather | solution.py:78
  61.7 1.4 %multiply_reduce_fusion = f32[256]{0:T(256)S(1)} fusion(f32[256,800]{1,0:T(8,128)} %copy.66, bf16[256,800]{1,0:T(8,128)(2,1)S(1)} %gather_fusion.3), kind=kLoop, calls=%fused_computation.23 | loop fusion | flops 614144 | bytes 1229824 | tf_op jit(solution)/shard_map/td,td->t/dot_general | solution.py:83
  63.6 1.0 multiply_add_fusion.1
  64.9 0.8 copy-done.1
  66.6 1.1 fusion.7
  67.7 1.4 %fusion.8 = bf16[256,800]{0,1:T(8,128)(2,1)} fusion(f32[256,800]{0,1:T(8,128)S(1)} %convolution_add_fusion.1, f32[256,800]{0,1:T(8,128)S(1)} %fusion, f32[1024,800]{0,1:T(8,128)S(1)} %copy-done.1, s32[1024]{0:T(1024)S(1)} %bitcast.13), kind=kOutput, calls=%fused_computation.18 | convolution fusion | flops 421126144 | bytes 5328896 | tf_op jit(solution)/shard_map/while/body/eval_jaxpr/dot_general | solution.py:35
  69.8 10.3 %all_to_all.30 = bf16[16,2,2,800]{3,2,1,0:T(2,128)(2,1)S(1)} all-to-all(bf16[16,2,2,800]{3,2,1,0:T(2,128)(2,1)S(1)} %convert_element_type.113), channel_id=1, replica_groups=mesh['blk'=16,'rel'=2] {'blk'}, dimensions={0} | all-to-all | bytes 204800 | tf_op jit(solution)/shard_map/all_to_all | solution.py:133
  80.1 0.7 copy.61
  80.8 3.4 %all-to-all-start.5 = ((bf16[16,2,2,800]{3,2,0,1:T(2,128)(2,1)}), bf16[16,2,2,800]{3,2,0,1:T(2,128)(2,1)S(1)}, u32[]{:S(2)}, u32[]{:S(2)}) async-start(bf16[16,2,2,800]{3,2,0,1:T(2,128)(2,1)} %copy.61), calls=%async_computation.5 | async-start | bytes 229376 | tf_op jit(solution)/shard_map/all_to_all | solution.py:132
  84.3 4.3 %all-to-all-done.5 = bf16[16,2,2,800]{3,2,0,1:T(2,128)(2,1)S(1)} async-done(((bf16[16,2,2,800]{3,2,0,1:T(2,128)(2,1)}), bf16[16,2,2,800]{3,2,0,1:T(2,128)(2,1)S(1)}, u32[]{:S(2)}, u32[]{:S(2)}) %all-to-all-start.5) | async-done | bytes 102432 | tf_op jit(solution)/shard_map/all_to_all | solution.py:132
  88.7 0.8 fusion.33
  89.5 11.7 %all-reduce.3.cloned.1.call-done = (bf16[256,800]{0,1:T(8,128)(2,1)}, bf16[256,800]{0,1:T(8,128)(2,1)}) async-done(((bf16[256,800]{0,1:T(8,128)(2,1)}, bf16[256,800]{0,1:T(8,128)(2,1)}), (bf16[256,800]{0,1:T(8,128)(2,1)}, bf16[256,800]{0,1:T(8,128)(2,1)})) %all-reduce.3.cloned.1.call-update) | async-done | bytes 819216 | tf_op jit(solution)/shard_map/psum | solution.py:128
  101.2 1.8 %copy.69 = bf16[256,800]{0,1:T(8,128)(2,1)} copy(bf16[256,800]{0,1:T(8,128)(2,1)} %get-tuple-element.37) | data formatting | bytes 819200
  103.0 1.8 %copy.70 = bf16[256,800]{0,1:T(8,128)(2,1)} copy(bf16[256,800]{0,1:T(8,128)(2,1)} %get-tuple-element.38) | data formatting | bytes 819200
  (59 shorter events, 8.9 us)
Async XLA Ops:
  7.2 23.2 %copy-start = (bf16[32,800]{1,0:T(8,128)(2,1)S(1)}, bf16[32,800]{1,0:T(8,128)(2,1)}, u32[]{:S(2)}) copy-start(bf16[32,800]{1,0:T(8,128)(2,1)} %param.11) | copy-start | bytes 153604
  7.2 28.5 %copy-start.7 = (s32[256]{0:T(256)S(1)}, s32[256]{0:T(256)}, u32[]{:S(2)}) copy-start(s32[256]{0:T(256)} %param.13) | copy-start | bytes 3076
  7.2 40.3 %copy-start.4 = (bf16[256,800]{0,1:T(8,128)(2,1)S(1)}, bf16[256,800]{0,1:T(8,128)(2,1)}, u32[]{:S(2)}) copy-start(bf16[256,800]{0,1:T(8,128)(2,1)} %param.9) | copy-start | bytes 1228804
  8.6 13.9 %all-to-all-start = ((s32[16,2,2]{2,1,0:T(2,128)}), s32[16,2,2]{2,1,0:T(2,128)S(1)}, u32[]{:S(2)}, u32[]{:S(2)}) async-start(s32[16,2,2]{2,1,0:T(2,128)} %copy.51), calls=%async_computation | async-start | bytes 32768 | tf_op jit(solution)/shard_map/all_to_all | solution.py:56
  18.0 36.9 %collective-permute-start = (bf16[256,800]{1,0:T(8,128)(2,1)}, bf16[256,800]{1,0:T(8,128)(2,1)S(1)}, u32[]{:S(2)}, u32[]{:S(2)}) collective-permute-start(bf16[256,800]{1,0:T(8,128)(2,1)} %copy.57), channel_id=1, source_target_pairs={{0,2},{2,4},{4,6},{6,8},{8,10},{10,12},{12,14},{14,16},{16,18},{18... | collective-permute-start | bytes 1228808 | tf_op jit(solution)/shard_map/ppermute | solution.py:9
  23.2 7.0 %all-to-all-start.1 = ((s32[16,2,2]{0,2,1:T(2,128)}), s32[16,2,2]{0,2,1:T(2,128)S(1)}, u32[]{:S(2)}, u32[]{:S(2)}) async-start(s32[16,2,2]{0,2,1:T(2,128)} %copy.52), calls=%async_computation.1 | async-start | bytes 4096 | tf_op jit(solution)/shard_map/all_to_all | solution.py:55
  31.8 11.6 %all-to-all-start.2 = ((bf16[16,2,2,800]{3,2,1,0:T(2,128)(2,1)}), bf16[16,2,2,800]{3,2,1,0:T(2,128)(2,1)S(1)}, u32[]{:S(2)}, u32[]{:S(2)}) async-start(bf16[16,2,2,800]{3,2,1,0:T(2,128)(2,1)} %reshape.86), calls=%async_computation.2 | async-start | bytes 229376 | tf_op jit(solution)/shard_map/all_to_all | solution.py:64
  44.1 7.7 %all-to-all-start.3 = ((bf16[16,2,2,800]{3,2,0,1:T(2,128)(2,1)}), bf16[16,2,2,800]{3,2,0,1:T(2,128)(2,1)S(1)}, u32[]{:S(2)}, u32[]{:S(2)}) async-start(bf16[16,2,2,800]{3,2,0,1:T(2,128)(2,1)} %copy.54), calls=%async_computation.3 | async-start | bytes 229376 | tf_op jit(solution)/shard_map/all_to_all | solution.py:63
  47.5 53.8 %all-reduce.3.cloned.1.call-start = ((), (), s32[]{:S(2)}) async-start(), calls=%async_computation.6 | async-start | bytes 1638400 | tf_op jit(solution)/shard_map/psum | solution.py:128
  53.6 1.3 %copy-start.5 = (s32[1,1024]{1,0:T(1,128)S(1)}, s32[1,1024]{1,0:T(1,128)}, u32[]{:S(2)}) copy-start(s32[1,1024]{1,0:T(1,128)} %param.15) | copy-start | bytes 12292
  61.7 1.8 %copy-start.3 = (f32[256,800]{0,1:T(8,128)S(1)}, f32[256,800]{0,1:T(8,128)}, u32[]{:S(2)}) copy-start(f32[256,800]{0,1:T(8,128)} %fusion.42) | copy-start | bytes 2457604
  63.6 2.1 %copy-start.1 = (f32[1024,800]{0,1:T(8,128)S(1)}, f32[1024,800]{0,1:T(8,128)}, u32[]{:S(2)}) copy-start(f32[1024,800]{0,1:T(8,128)} %fusion.40) | copy-start | bytes 9830404
  65.7 0.7 copy-start.6
  67.7 1.5 %copy-start.2 = (f32[256,400]{0,1:T(8,128)S(1)}, f32[256,400]{0,1:T(8,128)}, u32[]{:S(2)}) copy-start(f32[256,400]{0,1:T(8,128)} %get-tuple-element.22) | copy-start | bytes 1228804
  67.7 1.5 %copy-start.8 = (s32[256]{0:T(256)S(1)}, s32[256]{0:T(256)}, u32[]{:S(2)}) copy-start(s32[256]{0:T(256)} %param.14) | copy-start | bytes 3076
  80.8 7.7 %all-to-all-start.5 = ((bf16[16,2,2,800]{3,2,0,1:T(2,128)(2,1)}), bf16[16,2,2,800]{3,2,0,1:T(2,128)(2,1)S(1)}, u32[]{:S(2)}, u32[]{:S(2)}) async-start(bf16[16,2,2,800]{3,2,0,1:T(2,128)(2,1)} %copy.61), calls=%async_computation.5 | async-start | bytes 229376 | tf_op jit(solution)/shard_map/all_to_all | solution.py:132
Sparse Core Ops, SparseCore 0:
  69.3 31.8 all-reduce.2
where the time goes:
time: 112 us
  waiting for transfers between devices  31.8 us (28%)
  starting transfers between devices  21.6 us (19%)
  local copies, waits for them, and re-layouts  18.5 us (17%)
  between operations  14.4 us (13%)
  matrix products  10.8 us (10%)
  blocking collectives  10.3 us (9%)
  other arithmetic  4.32 us (4%)
    psum x1, waiting for transfers between devices, shards(): lax.psum(word_part.astype(jnp.bfloat16), 'rel').astype(jnp.float32)  11.7 us
    all_to_all x1, blocking collectives, shards(): lax.all_to_all(outgoing.astype(jnp.bfloat16), 'blk', split_axis=0, concat...  10.3 us
    unnamed x23, local copies, waits for them, and re-layouts  7.83 us
    all_to_all x1, waiting for transfers between devices, shards(): lax.all_to_all(picked, 'blk', split_axis=0, concat_axis=0, tiled=True)  7.65 us
    all_to_all x1, starting transfers between devices, shards(): lax.all_to_all(wanted, 'blk', split_axis=0, concat_axis=0, tiled=True)  7.39 us
    all_to_all x1, waiting for transfers between devices, shards(): lax.all_to_all(lax.all_to_all(outgoing.astype(jnp.bfloat16), 'blk', split...  4.26 us
    all_to_all x1, starting transfers between devices, shards(): lax.all_to_all(picked, 'blk', split_axis=0, concat_axis=0, tiled=True)  3.87 us
    all_to_all x1, waiting for transfers between devices, shards(): lax.all_to_all(lax.all_to_all(wanted, 'blk', split_axis=0, concat_axis=0,...  3.75 us
  transfers between devices with their start and end apart: 7, of which 6 were waited for; matrix products, arithmetic and copies ran while one was open for 13% of the time, Pallas kernels for 0%

commit v1 on v0

--- a/solution.py
+++ b/solution.py
@@ -51,22 +51,11 @@
     part_rows = contexts.shape[0]
     neg_scale = float(neg_index.shape[1]) ** (-0.5)
     held_rows = passed_along(contexts, "blk", 1)
-    wanted = requests[0, 0]
-    incoming = lax.all_to_all(
-        lax.all_to_all(wanted, "blk", split_axis=0, concat_axis=0, tiled=True),
-        "rel",
-        split_axis=1,
-        concat_axis=1,
-        tiled=True,
-    )
-    picked = relations[incoming.reshape(-1)].reshape(part_count, split_count, slot_count, row_width)
-    fetched = lax.all_to_all(
-        lax.all_to_all(picked, "blk", split_axis=0, concat_axis=0, tiled=True),
-        "rel",
-        split_axis=1,
-        concat_axis=1,
-        tiled=True,
-    )
+    wanted = requests[0, 0].reshape(part_count * split_count, slot_count)
+    both = ("blk", "rel")
+    incoming = lax.all_to_all(wanted, both, split_axis=0, concat_axis=0, tiled=True)
+    picked = relations[incoming.reshape(-1)].reshape(part_count * split_count, slot_count, row_width)
+    fetched = lax.all_to_all(picked, both, split_axis=0, concat_axis=0, tiled=True)
     slot_table = fetched.reshape(-1, row_width)
     slot_total = slot_table.shape[0]
     live_mask = (
@@ -124,19 +113,13 @@
         conj_product(query_grads, word_used.astype(jnp.float32), half_width),
     )
     slot_grad = slot_grad + 0.02 * live_mask[:, None] * slot_table.astype(jnp.float32)
-    word_sum, ctx_sum = (
-        lax.psum(word_part.astype(jnp.bfloat16), "rel").astype(jnp.float32),
-        lax.psum(ctx_part.astype(jnp.bfloat16), "rel").astype(jnp.float32),
-    )
-    outgoing = slot_grad.reshape(part_count, split_count, slot_count, row_width)
+    word_half = word_part.astype(jnp.bfloat16)
+    ctx_half = ctx_part.astype(jnp.bfloat16)
+    word_sum = word_half.astype(jnp.float32) + passed_along(word_half, "rel", 1).astype(jnp.float32)
+    ctx_sum = ctx_half.astype(jnp.float32) + passed_along(ctx_half, "rel", 1).astype(jnp.float32)
+    outgoing = slot_grad.reshape(part_count * split_count, slot_count, row_width)
     returned = lax.all_to_all(
-        lax.all_to_all(
-            outgoing.astype(jnp.bfloat16), "blk", split_axis=0, concat_axis=0, tiled=True
-        ),
-        "rel",
-        split_axis=1,
-        concat_axis=1,
-        tiled=True,
+        outgoing.astype(jnp.bfloat16), both, split_axis=0, concat_axis=0, tiled=True
     ).astype(outgoing.dtype)
     owner_map = (incoming.reshape(-1)[None, :] == jnp.arange(owned_rows)[:, None]).astype(
         jnp.float32

time: 112 us -> 78.5 us (0.70)
  between operations: 14.4 us -> 0.97 us
  blocking collectives: 10.3 us -> 0 us
  waiting for transfers between devices: 31.8 us -> 23.2 us
  starting transfers between devices: 21.6 us -> 16.2 us
  other arithmetic: 4.32 us -> 9.45 us
  local copies, waits for them, and re-layouts: 18.5 us -> 15.3 us
  matrix products: 10.8 us -> 12.9 us
    ppermute x1 -> x3, waiting for transfers between devices: 0.01 us -> 12.3 us  [passed_along(): lax.ppermute(shard, axis, [(i, (i + by) % length) for i in range(length)])]
    psum x1 -> x0, waiting for transfers between devices: 11.7 us -> none  [shards(): lax.psum(word_part.astype(jnp.bfloat16), 'rel').astype(jnp.float32)]
    all_to_all x1 -> x0, blocking collectives: 10.3 us -> none  [shards(): lax.all_to_all(outgoing.astype(jnp.bfloat16), 'blk', split_axis=0, concat...]
    all_to_all x5 -> x3, waiting for transfers between devices: 20 us -> 10.9 us  [the longest x1 6.4 us: shards(): lax.all_to_all(picked, both, split_axis=0, concat_axis=0, tiled=True)]
    all_to_all x5 -> x3, starting transfers between devices: 21.2 us -> 13.8 us  [the longest x1 7.3 us: shards(): lax.all_to_all(wanted, both, split_axis=0, concat_axis=0, tiled=True)]
    unnamed x23 -> x27, local copies, waits for them, and re-layouts: 7.83 us -> 3.95 us
    convert_element_type x0 -> x2, other arithmetic: none -> 2.74 us  [the longest x1 1.87 us: shards(): ctx_sum.astype(jnp.bfloat16)]
    ppermute x1 -> x3, starting transfers between devices: 0.41 us -> 2.39 us  [passed_along(): lax.ppermute(shard, axis, [(i, (i + by) % length) for i in range(length)])]
  transfers between devices with their start and end apart: 7 -> 6, of which waited for: 6 -> 5; matrix products, arithmetic and copies ran while one was open for 13% -> 28% of each run, Pallas kernels for 0% -> 0%
where the time goes in v1:
time: 78.5 us; the launch traced here: 78 us
  waiting for transfers between devices  23.2 us (30%)
  starting transfers between devices  16.2 us (21%)
  local copies, waits for them, and re-layouts  15.3 us (19%)
  matrix products  12.9 us (16%)
  other arithmetic  9.45 us (12%)
  between operations  0.97 us (1%)
    ppermute x3, waiting for transfers between devices, passed_along(): lax.ppermute(shard, axis, [(i, (i + by) % length) for i in range(length)])  12.3 us
    all_to_all x1, starting transfers between devices, shards(): lax.all_to_all(wanted, both, split_axis=0, concat_axis=0, tiled=True)  7.3 us
    all_to_all x1, waiting for transfers between devices, shards(): lax.all_to_all(picked, both, split_axis=0, concat_axis=0, tiled=True)  6.4 us
    unnamed x27, local copies, waits for them, and re-layouts  3.95 us
    dot_general x4, matrix products, spread_rows(): jnp.dot(selector, lower, preferred_element_type=jnp.float32)  3.57 us
    all_to_all x1, starting transfers between devices, shards(): lax.all_to_all(outgoing.astype(jnp.bfloat16), both, split_axis=0, concat_...  3.26 us
    dot_general x4, matrix products, spread_rows(): jnp.dot(selector, upper, preferred_element_type=jnp.float32)  3.22 us
    all_to_all x1, starting transfers between devices, shards(): lax.all_to_all(picked, both, split_axis=0, concat_axis=0, tiled=True)  3.2 us
  transfers between devices with their start and end apart: 6, of which 5 were waited for; matrix products, arithmetic and copies ran while one was open for 28% of the time, Pallas kernels for 0%

profile of v1, /device:TPU:0, one launch (start us, length us, event | category | flops | bytes accessed | tf_op | source)
XLA Modules:
  0.0 78.0 jit_solution(962579652216225234)
XLA Ops:
  0.7 1.4 %copy.42 = s32[1,1,16,2,2]{4,3,2,1,0:T(2,128)} copy(s32[1,1,16,2,2]{2,4,3,1,0:T(2,128)} %param.16) | data formatting | bytes 512 | tf_op jit(solution)/shard_map/all_to_all | solution.py:56
  2.1 7.3 %all-to-all-start = ((s32[32,1,2]{2,1,0:T(1,128)}), s32[32,1,2]{2,1,0:T(1,128)S(1)}, u32[]{:S(2)}, u32[]{:S(2)}) async-start(s32[32,1,2]{2,1,0:T(1,128)} %bitcast), calls=%async_computation | async-start | bytes 32768 | tf_op jit(solution)/shard_map/all_to_all | solution.py:56
  9.4 1.2 %copy.35 = bf16[256,800]{1,0:T(8,128)(2,1)S(1)} copy(bf16[256,800]{0,1:T(8,128)(2,1)} %param.10) | data formatting | bytes 819200 | tf_op args[1]
  13.0 0.8 copy.37
  13.8 2.7 %all-to-all-done = s32[32,1,2]{2,1,0:T(1,128)S(1)} async-done(((s32[32,1,2]{2,1,0:T(1,128)}), s32[32,1,2]{2,1,0:T(1,128)S(1)}, u32[]{:S(2)}, u32[]{:S(2)}) %all-to-all-start) | async-done | bytes 288 | tf_op jit(solution)/shard_map/all_to_all | solution.py:56
  17.9 0.7 gather_fusion.1
  19.3 3.2 %all-to-all-start.1 = ((bf16[32,2,800]{2,1,0:T(2,128)(2,1)}), bf16[32,2,800]{2,1,0:T(2,128)(2,1)S(1)}, u32[]{:S(2)}, u32[]{:S(2)}) async-start(bf16[32,2,800]{2,1,0:T(2,128)(2,1)} %reshape.91), calls=%async_computation.1 | async-start | bytes 229376 | tf_op jit(solution)/shard_map/all_to_all | solution.py:58
  22.8 1.2 %gather_fusion = bf16[256,800]{1,0:T(8,128)(2,1)S(1)} fusion(bf16[256,800]{1,0:T(8,128)(2,1)S(1)} %copy.30, s32[1024]{0:T(1024)S(1)} %pad_clamp_fusion.3), kind=kCustom, calls=%fused_computation | custom fusion | bytes 820224 | tf_op jit(solution)/shard_map/gather | solution.py:66
  24.5 6.4 %all-to-all-done.1 = bf16[32,2,800]{2,1,0:T(2,128)(2,1)S(1)} async-done(((bf16[32,2,800]{2,1,0:T(2,128)(2,1)}), bf16[32,2,800]{2,1,0:T(2,128)(2,1)S(1)}, u32[]{:S(2)}, u32[]{:S(2)}) %all-to-all-start.1) | async-done | bytes 102432 | tf_op jit(solution)/shard_map/all_to_all | solution.py:58
  30.9 1.2 %gather_fusion.2 = bf16[256,800]{1,0:T(8,128)(2,1)S(1)} fusion(bf16[64,800]{1,0:T(8,128)(2,1)S(1)} %reshape.92, s32[1024]{0:T(1024)S(1)} %pad_clamp_fusion.1), kind=kCustom, calls=%fused_computation.2 | custom fusion | bytes 820224 | tf_op jit(solution)/shard_map/gather | solution.py:68
  32.6 1.0 %fusion.41 = f32[256,800]{0,1:T(8,128)} fusion(bf16[256,400]{0,1:T(8,128)(2,1)S(1)} %get-tuple-element.32, bf16[256,400]{0,1:T(8,128)(2,1)S(1)} %get-tuple-element.23), kind=kLoop, calls=%fused_computation.82 | loop fusion | flops 819200 | bytes 1228800
  33.6 2.4 %copy.41 = f32[256,800]{1,0:T(8,128)} copy(f32[256,800]{0,1:T(8,128)} %fusion.41) | data formatting | bytes 1638400
  36.7 0.9 %fusion.6 = bf16[256,1024]{1,0:T(8,128)(2,1)S(1)} fusion(bf16[1024,800]{0,1:T(8,128)(2,1)S(1)} %convolution_convert_fusion, bf16[256,400]{0,1:T(8,128)(2,1)S(1)} %get-tuple-element.32, bf16[256,400]{0,1:T(8,128)(2,1)S(1)} %get-tuple-element.23), kind=kOutput, calls=%fused_computation.16 | convolution fusion | flops 421560320 | bytes 2572288 | tf_op jit(solution)/shard_map/while/body/eval_jaxpr/dot_general | solution.py:84
  37.6 1.5 %fusion.42 = f32[256,800]{0,1:T(8,128)} fusion(bf16[256,1024]{1,0:T(8,128)(2,1)S(1)} %fusion.6, bf16[1024,800]{0,1:T(8,128)(2,1)S(1)} %convolution_convert_fusion), kind=kOutput, calls=%fused_computation.83 | convolution fusion | flops 419430400 | bytes 2981888 | tf_op jit(solution)/shard_map/while/body/eval_jaxpr/dot_general | solution.py:88
  39.1 2.3 %fusion.40 = f32[1024,800]{0,1:T(8,128)} fusion(bf16[256,1024]{1,0:T(8,128)(2,1)S(1)} %fusion.6, bf16[256,400]{0,1:T(8,128)(2,1)S(1)} %get-tuple-element.32, bf16[256,400]{0,1:T(8,128)(2,1)S(1)} %get-tuple-element.23), kind=kOutput, calls=%fused_computation.81 | convolution fusion | flops 420249600 | bytes 4210688 | tf_op jit(solution)/shard_map/while/body/eval_jaxpr/dot_general | solution.py:91
  41.4 1.2 %gather_fusion.3 = bf16[256,800]{1,0:T(8,128)(2,1)S(1)} fusion(bf16[256,800]{1,0:T(8,128)(2,1)S(1)} %collective-permute-done, s32[1024]{0:T(1024)S(1)} %pad_clamp_fusion), kind=kCustom, calls=%fused_computation.3 | custom fusion | bytes 820224 | tf_op jit(solution)/shard_map/gather | solution.py:67
  42.8 1.4 %multiply_reduce_fusion = f32[256]{0:T(256)S(1)} fusion(f32[256,800]{1,0:T(8,128)} %copy.41, bf16[256,800]{1,0:T(8,128)(2,1)S(1)} %gather_fusion.3), kind=kLoop, calls=%fused_computation.23 | loop fusion | flops 614144 | bytes 1229824 | tf_op jit(solution)/shard_map/td,td->t/dot_general | solution.py:72
  44.3 1.2 %fusion.15 = f32[256,800]{0,1:T(8,128)} fusion(f32[256]{0:T(256)S(1)} %divide_negate_fusion, s32[256]{0:T(256)S(1)} %copy-done.10, bf16[256,400]{0,1:T(8,128)(2,1)S(1)} %get-tuple-element.32, bf16[256,400]{0,1:T(8,128)(2,1)S(1)} %get-tuple-element.23), kind=kOutput, calls=%fused_computation.37 | convolution fusion | flops 106151936 | bytes 1230848 | tf_op jit(solution)/shard_map/dot_general | solution.py:35
  45.6 1.1 %multiply_add_fusion.1 = (f32[256,400]{0,1:T(8,128)S(1)}, f32[256,400]{0,1:T(8,128)S(1)}, f32[256,400]{0,1:T(8,128)}, f32[256,400]{0,1:T(8,128)}) fusion(f32[256,800]{0,1:T(8,128)S(1)} %multiply_add_fusion, f32[256,800]{0,1:T(8,128)S(1)} %convert_element_type.105, f32[256,800]{0,1:T(8,128)S(1)} %convert_element_type.106), kind=kLoop, calls=%fused_computation.47 | loop fusion | flops 1228800 | bytes 4096000 | tf_op jit(solution)/shard_map/add | solution.py:24
  46.9 0.9 %fusion.10 = bf16[64,800]{1,0:T(8,128)(2,1)} fusion(f32[64,800]{1,0:T(8,128)S(1)} %fusion.21, f32[256,400]{0,1:T(8,128)S(1)} %get-tuple-element.20, f32[256,400]{0,1:T(8,128)S(1)} %get-tuple-element.19, bf16[64,800]{1,0:T(8,128)(2,1)S(1)} %reshape.92, f32[64]{0:T(128)S(1)} %mul.94, s32[256]{0:T(256)S(1)} %copy-done.11), kind=kOutput, calls=%fused_computation.21 | convolution fusion | flops 27510784 | bytes 1230080 | tf_op jit(solution)/shard_map/dot_general | solution.py:35
  47.9 1.7 %convert_element_type.133 = bf16[32,2,800]{2,1,0:T(2,128)(2,1)} reshape(bf16[64,800]{1,0:T(8,128)(2,1)} %fusion.10) | data formatting | bytes 204800 | tf_op jit(solution)/shard_map/convert_element_type | solution.py:122
  49.5 3.3 %all-to-all-start.2 = ((bf16[32,2,800]{2,1,0:T(2,128)(2,1)}), bf16[32,2,800]{2,1,0:T(2,128)(2,1)}, u32[]{:S(2)}, u32[]{:S(2)}) async-start(bf16[32,2,800]{2,1,0:T(2,128)(2,1)} %convert_element_type.133), calls=%async_computation.2 | async-start | bytes 229376 | tf_op jit(solution)/shard_map/all_to_all | solution.py:121
  52.8 1.7 %convolution_add_fusion.1 = f32[256,800]{0,1:T(8,128)S(1)} fusion(f32[256,800]{0,1:T(8,128)} %fusion.15, f32[256]{0:T(256)S(1)} %divide_negate_fusion, s32[256]{0:T(256)S(1)} %copy-done.10, bf16[256,400]{0,1:T(8,128)(2,1)} %copy-done.3, bf16[256,400]{0,1:T(8,128)(2,1)} %copy-done.2), kind=kOutput, calls=%fused_computation.14 | convolution fusion | flops 106971136 | bytes 2050048 | tf_op jit(solution)/shard_map/dot_general | solution.py:35
  55.2 1.4 %fusion.8 = bf16[256,800]{0,1:T(8,128)(2,1)} fusion(f32[256,800]{0,1:T(8,128)S(1)} %convolution_add_fusion.1, f32[256,800]{0,1:T(8,128)S(1)} %fusion, f32[1024,800]{0,1:T(8,128)S(1)} %copy-done.1, s32[1024]{0:T(1024)S(1)} %bitcast.15), kind=kOutput, calls=%fused_computation.18 | convolution fusion | flops 421126144 | bytes 5328896 | tf_op jit(solution)/shard_map/while/body/eval_jaxpr/dot_general | solution.py:35
  56.6 1.6 %collective-permute-start.2 = (bf16[256,800]{0,1:T(8,128)(2,1)}, bf16[256,800]{0,1:T(8,128)(2,1)S(1)}, u32[]{:S(2)}, u32[]{:S(2)}) collective-permute-start(bf16[256,800]{0,1:T(8,128)(2,1)} %fusion.8), channel_id=1, source_target_pairs={{0,1},{1,0},{2,3},{3,2},{4,5},{5,4},{6,7},{7,6},{8,9},{9,8},{10,11... | collective-permute-start | bytes 1228808 | tf_op jit(solution)/shard_map/ppermute | solution.py:9
  59.3 1.8 %all-to-all-done.2 = bf16[32,2,800]{2,1,0:T(2,128)(2,1)} async-done(((bf16[32,2,800]{2,1,0:T(2,128)(2,1)}), bf16[32,2,800]{2,1,0:T(2,128)(2,1)}, u32[]{:S(2)}, u32[]{:S(2)}) %all-to-all-start.2) | async-done | bytes 102432 | tf_op jit(solution)/shard_map/all_to_all | solution.py:121
  61.2 1.0 %reshape.93 = bf16[64,800]{1,0:T(8,128)(2,1)S(1)} reshape(bf16[32,2,800]{2,1,0:T(2,128)(2,1)} %all-to-all-done.2) | data formatting | bytes 204800 | tf_op jit(solution)/shard_map/reshape | solution.py:129
  62.2 0.8 %fusion.33 = f32[32,800]{1,0:T(8,128)} fusion(bf16[64,800]{1,0:T(8,128)(2,1)S(1)} %reshape.93, s32[64]{0:T(128)S(1)} %eq.86), kind=kOutput, calls=%fused_computation.65 | convolution fusion | flops 3278848 | bytes 205056 | tf_op jit(solution)/shard_map/dot_general | solution.py:127
  63.0 6.2 %collective-permute-done.2 = bf16[256,800]{0,1:T(8,128)(2,1)S(1)} collective-permute-done((bf16[256,800]{0,1:T(8,128)(2,1)}, bf16[256,800]{0,1:T(8,128)(2,1)S(1)}, u32[]{:S(2)}, u32[]{:S(2)}) %collective-permute-start.2) | collective-permute-done | bytes 409632 | tf_op jit(solution)/shard_map/ppermute | solution.py:9
  69.2 1.9 %add_convert_fusion = bf16[256,800]{0,1:T(8,128)(2,1)} fusion(bf16[256,800]{0,1:T(8,128)(2,1)S(1)} %collective-permute-done.2, bf16[256,800]{0,1:T(8,128)(2,1)} %fusion.8), kind=kLoop, calls=%fused_computation.27 | loop fusion | flops 819200 | bytes 1228800 | tf_op jit(solution)/shard_map/convert_element_type | solution.py:133
  71.0 6.1 %collective-permute-done.1 = bf16[256,800]{0,1:T(8,128)(2,1)S(1)} collective-permute-done((bf16[256,800]{0,1:T(8,128)(2,1)S(1)}, bf16[256,800]{0,1:T(8,128)(2,1)S(1)}, u32[]{:S(2)}, u32[]{:S(2)}) %collective-permute-start.1) | collective-permute-done | bytes 409632 | tf_op jit(solution)/shard_map/ppermute | solution.py:9
  77.1 0.9 %add_convert_fusion.1 = bf16[256,800]{0,1:T(8,128)(2,1)} fusion(bf16[256,800]{0,1:T(8,128)(2,1)S(1)} %collective-permute-done.1, bf16[256,800]{0,1:T(8,128)(2,1)S(1)} %fusion.7), kind=kLoop, calls=%fused_computation.31 | loop fusion | flops 819200 | bytes 1228800 | tf_op jit(solution)/shard_map/convert_element_type | solution.py:133
  (57 shorter events, 8.7 us)
Async XLA Ops:
  0.6 17.2 %copy-start = (bf16[32,800]{1,0:T(8,128)(2,1)S(1)}, bf16[32,800]{1,0:T(8,128)(2,1)}, u32[]{:S(2)}) copy-start(bf16[32,800]{1,0:T(8,128)(2,1)} %param.11) | copy-start | bytes 153604
  0.6 21.9 %copy-start.7 = (bf16[256,800]{0,1:T(8,128)(2,1)S(1)}, bf16[256,800]{0,1:T(8,128)(2,1)}, u32[]{:S(2)}) copy-start(bf16[256,800]{0,1:T(8,128)(2,1)} %param.9) | copy-start | bytes 1228804
  2.1 14.4 %all-to-all-start = ((s32[32,1,2]{2,1,0:T(1,128)}), s32[32,1,2]{2,1,0:T(1,128)S(1)}, u32[]{:S(2)}, u32[]{:S(2)}) async-start(s32[32,1,2]{2,1,0:T(1,128)} %bitcast), calls=%async_computation | async-start | bytes 32768 | tf_op jit(solution)/shard_map/all_to_all | solution.py:56
  10.6 25.4 %collective-permute-start = (bf16[256,800]{1,0:T(8,128)(2,1)S(1)}, bf16[256,800]{1,0:T(8,128)(2,1)S(1)}, u32[]{:S(2)}, u32[]{:S(2)}) collective-permute-start(bf16[256,800]{1,0:T(8,128)(2,1)S(1)} %copy.35), channel_id=1, source_target_pairs={{0,2},{2,4},{4,6},{6,8},{8,10},{10,12},{12,14},{14,16},{16,18},{18... | collective-permute-start | bytes 1228808 | tf_op jit(solution)/shard_map/ppermute | solution.py:9
  19.3 11.6 %all-to-all-start.1 = ((bf16[32,2,800]{2,1,0:T(2,128)(2,1)}), bf16[32,2,800]{2,1,0:T(2,128)(2,1)S(1)}, u32[]{:S(2)}, u32[]{:S(2)}) async-start(bf16[32,2,800]{2,1,0:T(2,128)(2,1)} %reshape.91), calls=%async_computation.1 | async-start | bytes 229376 | tf_op jit(solution)/shard_map/all_to_all | solution.py:58
  32.6 11.7 %copy-start.2 = (bf16[256,400]{0,1:T(8,128)(2,1)}, bf16[256,400]{0,1:T(8,128)(2,1)S(1)}, u32[]{:S(2)}) copy-start(bf16[256,400]{0,1:T(8,128)(2,1)S(1)} %get-tuple-element.23) | copy-start | bytes 614404
  32.6 11.7 %copy-start.3 = (bf16[256,400]{0,1:T(8,128)(2,1)}, bf16[256,400]{0,1:T(8,128)(2,1)S(1)}, u32[]{:S(2)}) copy-start(bf16[256,400]{0,1:T(8,128)(2,1)S(1)} %get-tuple-element.32) | copy-start | bytes 614404
  32.6 3.4 %copy-start.8 = (s32[1,1024]{1,0:T(1,128)S(1)}, s32[1,1024]{1,0:T(1,128)}, u32[]{:S(2)}) copy-start(s32[1,1024]{1,0:T(1,128)} %param.15) | copy-start | bytes 12292
  42.6 1.7 %copy-start.10 = (s32[256]{0:T(256)S(1)}, s32[256]{0:T(256)}, u32[]{:S(2)}) copy-start(s32[256]{0:T(256)} %param.13) | copy-start | bytes 3076
  42.8 2.7 %copy-start.6 = (f32[256,800]{0,1:T(8,128)S(1)}, f32[256,800]{0,1:T(8,128)}, u32[]{:S(2)}) copy-start(f32[256,800]{0,1:T(8,128)} %fusion.42) | copy-start | bytes 2457604
  45.6 1.1 %copy-start.11 = (s32[256]{0:T(256)S(1)}, s32[256]{0:T(256)}, u32[]{:S(2)}) copy-start(s32[256]{0:T(256)} %param.14) | copy-start | bytes 3076
  46.9 7.6 %copy-start.1 = (f32[1024,800]{0,1:T(8,128)S(1)}, f32[1024,800]{0,1:T(8,128)}, u32[]{:S(2)}) copy-start(f32[1024,800]{0,1:T(8,128)} %fusion.40) | copy-start | bytes 9830404
  49.5 11.6 %all-to-all-start.2 = ((bf16[32,2,800]{2,1,0:T(2,128)(2,1)}), bf16[32,2,800]{2,1,0:T(2,128)(2,1)}, u32[]{:S(2)}, u32[]{:S(2)}) async-start(bf16[32,2,800]{2,1,0:T(2,128)(2,1)} %convert_element_type.133), calls=%async_computation.2 | async-start | bytes 229376 | tf_op jit(solution)/shard_map/all_to_all | solution.py:121
  55.2 3.0 %copy-start.4 = (f32[256,400]{0,1:T(8,128)S(1)}, f32[256,400]{0,1:T(8,128)}, u32[]{:S(2)}) copy-start(f32[256,400]{0,1:T(8,128)} %get-tuple-element.33) | copy-start | bytes 1228804
  55.2 3.0 %copy-start.5 = (f32[256,400]{0,1:T(8,128)S(1)}, f32[256,400]{0,1:T(8,128)}, u32[]{:S(2)}) copy-start(f32[256,400]{0,1:T(8,128)} %get-tuple-element.34) | copy-start | bytes 1228804
  55.2 3.0 %copy-start.9 = (s32[256]{0:T(256)S(1)}, s32[256]{0:T(256)}, u32[]{:S(2)}) copy-start(s32[256]{0:T(256)} %param.12) | copy-start | bytes 3076
  56.6 12.5 %collective-permute-start.2 = (bf16[256,800]{0,1:T(8,128)(2,1)}, bf16[256,800]{0,1:T(8,128)(2,1)S(1)}, u32[]{:S(2)}, u32[]{:S(2)}) collective-permute-start(bf16[256,800]{0,1:T(8,128)(2,1)} %fusion.8), channel_id=1, source_target_pairs={{0,1},{1,0},{2,3},{3,2},{4,5},{5,4},{6,7},{7,6},{8,9},{9,8},{10,11... | collective-permute-start | bytes 1228808 | tf_op jit(solution)/shard_map/ppermute | solution.py:9
  58.8 18.3 %collective-permute-start.1 = (bf16[256,800]{0,1:T(8,128)(2,1)S(1)}, bf16[256,800]{0,1:T(8,128)(2,1)S(1)}, u32[]{:S(2)}, u32[]{:S(2)}) collective-permute-start(bf16[256,800]{0,1:T(8,128)(2,1)S(1)} %fusion.7), channel_id=1, source_target_pairs={{0,1},{1,0},{2,3},{3,2},{4,5},{5,4},{6,7},{7,6},{8,9},{9,8},{10,11... | collective-permute-start | bytes 1228808 | tf_op jit(solution)/shard_map/ppermute | solution.py:9

commit v2 on v1

v2 whole, which is shorter than its diff:
```python
import jax
import jax.numpy as jnp
from jax import lax
from jax.sharding import PartitionSpec as P


def passed_along(shard, axis, by):
    length = lax.axis_size(axis)
    return lax.ppermute(shard, axis, [(i, (i + by) % length) for i in range(length)])


def complex_product(left_vec, right_vec, half_width):
    left_re, left_im = (left_vec[..., :half_width], left_vec[..., half_width:])
    right_re, right_im = (right_vec[..., :half_width], right_vec[..., half_width:])
    return jnp.concatenate(
        [left_re * right_re - left_im * right_im, left_re * right_im + left_im * right_re], axis=-1
    )


def conj_product(grad_vec, other_vec, half_width):
    grad_re, grad_im = (grad_vec[..., :half_width], grad_vec[..., half_width:])
    other_re, other_im = (other_vec[..., :half_width], other_vec[..., half_width:])
    return jnp.concatenate(
        [grad_re * other_re + grad_im * other_im, grad_im * other_re - grad_re * other_im], axis=-1
    )


def one_hot(index_ids, row_total):
    return (index_ids[..., None] == jnp.arange(row_total)).astype(jnp.bfloat16)


def pick_rows(selector, rows):
    return jnp.dot(selector, rows, preferred_element_type=jnp.float32)


def split_bf16(values):
    upper = values.astype(jnp.bfloat16)
    lower = (values - upper.astype(jnp.float32)).astype(jnp.bfloat16)
    return upper, lower


def spread_rows(selector, terms):
    upper, lower = split_bf16(terms)
    dims = (((0,), (0,)), ((), ()))
    return lax.dot_general(
        selector, upper, dims, preferred_element_type=jnp.float32
    ) + lax.dot_general(selector, lower, dims, preferred_element_type=jnp.float32)


def shards(
    words, contexts, relations, word_index, context_index, rel_slot, neg_index, requests, counts
):
    row_width = words.shape[1]
    half_width = row_width // 2
    part_count = lax.axis_size("blk")
    split_count = lax.axis_size("rel")
    owner_count = part_count * split_count
    slot_count = requests.shape[-1]
    slot_total = owner_count * slot_count
    owned_rows = relations.shape[0]
    part_rows = contexts.shape[0]
    trips = word_index.shape[0]
    block_count = neg_index.shape[0]
    neg_count = neg_index.shape[1]
    block_size = trips // block_count
    neg_scale = float(neg_count) ** (-0.5)
    both = ("blk", "rel")

    held_rows = passed_along(contexts, "blk", 1)

    own_ints = jnp.concatenate([word_index, context_index, rel_slot, neg_index.reshape(-1)])
    bucket_ints = jnp.stack(
        [own_ints] + [passed_along(own_ints, "rel", -j) for j in range(1, split_count)]
    )
    word_ids = bucket_ints[:, :trips].reshape(-1)
    ctx_ids = bucket_ints[:, trips : 2 * trips].reshape(-1)
    slot_ids = (
        bucket_ints[:, 2 * trips : 3 * trips] + (jnp.arange(split_count) * slot_total)[:, None]
    ).reshape(-1)
    neg_ids = bucket_ints[:, 3 * trips :].reshape(split_count * block_count, neg_count)

    wanted = requests[0, 0].reshape(owner_count, slot_count)
    incoming = lax.all_to_all(wanted, both, split_axis=0, concat_axis=0, tiled=True)
    requester = jnp.arange(owner_count)
    bucket_of = (requester // split_count) * split_count
    served = jnp.stack(
        [incoming[bucket_of + (requester + j) % split_count] for j in range(split_count)], axis=1
    )
    picked = relations[served.reshape(-1)].reshape(
        owner_count, split_count * slot_count, row_width
    )
    fetched = lax.all_to_all(picked, both, split_axis=0, concat_axis=0, tiled=True)
    slot_table = (
        fetched.reshape(owner_count, split_count, slot_count, row_width)
        .transpose(1, 0, 2, 3)
        .reshape(split_count * slot_total, row_width)
    )
    own_table = slot_table[:slot_total]
    live_mask = (
        (jnp.arange(slot_count)[None, :] < counts[0, 0].reshape(owner_count)[:, None])
        .reshape(-1)
        .astype(jnp.float32)
    )

    word_sel = one_hot(word_ids, part_rows)
    ctx_sel = one_hot(ctx_ids, part_rows)
    word_used = pick_rows(word_sel, words)
    ctx_used = pick_rows(ctx_sel, held_rows)
    rel_used = pick_rows(one_hot(slot_ids, split_count * slot_total), slot_table)
    query = complex_product(word_used, rel_used, half_width).astype(jnp.bfloat16)
    positive = jnp.sum(query.astype(jnp.float32) * ctx_used, axis=1)
    pos_grad = -jax.nn.sigmoid(-positive)

    group_count = split_count * block_count
    query_blocks = query.reshape(group_count, block_size, row_width)
    neg_sel = one_hot(neg_ids, part_rows)
    neg_rows = jnp.einsum(
        "gjp,pd->gjd", neg_sel, held_rows, preferred_element_type=jnp.float32
    ).astype(jnp.bfloat16)
    scores = jnp.einsum(
        "gtd,gjd->gtj", query_blocks, neg_rows, preferred_element_type=jnp.float32
    )
    neg_grad = (jax.nn.sigmoid(scores) * neg_scale).astype(jnp.bfloat16)
    pos_blocks = pos_grad.reshape(group_count, block_size)
    query_grads = pos_blocks[:, :, None] * ctx_used.reshape(
        group_count, block_size, row_width
    ) + jnp.einsum("gtj,gjd->gtd", neg_grad, neg_rows, preferred_element_type=jnp.float32)

    neg_weight = jnp.einsum("gtj,gjp->gpt", neg_grad, neg_sel, preferred_element_type=jnp.float32)
    pos_weight = jnp.where(
        ctx_ids.reshape(group_count, 1, block_size)
        == jnp.arange(part_rows)[None, :, None],
        pos_blocks[:, None, :],
        0.0,
    )
    weight_hi, weight_lo = split_bf16(neg_weight + pos_weight)
    ctx_sum = jnp.einsum(
        "gpt,gtd->pd", weight_hi, query_blocks, preferred_element_type=jnp.float32
    ) + jnp.einsum("gpt,gtd->pd", weight_lo, query_blocks, preferred_element_type=jnp.float32)

    query_grads = query_grads.reshape(-1, row_width)
    word_sum = spread_rows(word_sel, conj_product(query_grads, rel_used, half_width))
    slot_grad = spread_rows(
        one_hot(slot_ids[:trips], slot_total),
        conj_product(query_grads[:trips], word_used[:trips], half_width),
    )
    slot_grad = slot_grad + 0.02 * live_mask[:, None] * own_table.astype(jnp.float32)
    outgoing = slot_grad.reshape(owner_count, slot_count, row_width)
    returned = lax.all_to_all(
        outgoing.astype(jnp.bfloat16), both, split_axis=0, concat_axis=0, tiled=True
    ).astype(outgoing.dtype)
    owner_map = (incoming.reshape(-1)[None, :] == jnp.arange(owned_rows)[:, None]).astype(
        jnp.float32
    )
    relation_grad = jnp.dot(
        owner_map,
        returned.reshape(-1, row_width),
        precision=lax.Precision.HIGHEST,
        preferred_element_type=jnp.float32,
    )
    return (word_sum.astype(jnp.bfloat16), ctx_sum.astype(jnp.bfloat16), relation_grad)


def solution(mesh):
    return jax.shard_map(
        shards,
        mesh=mesh,
        in_specs=(
            P("blk", None),
            P("blk", None),
            P(("blk", "rel"), None),
            P(("blk", "rel")),
            P(("blk", "rel")),
            P(("blk", "rel")),
            P(("blk", "rel"), None),
            P("blk", "rel", None, None, None),
            P("blk", "rel", None, None),
        ),
        out_specs=(P("blk", None), P("blk", None), P(("blk", "rel"), None)),
        check_vma=False,
    )
```

time: 78.5 us -> 60.1 us (0.77)
  waiting for transfers between devices: 23.2 us -> 16.4 us
  other arithmetic: 9.45 us -> 4.02 us
  local copies, waits for them, and re-layouts: 15.3 us -> 11.1 us
  starting transfers between devices: 16.2 us -> 14.3 us
    ppermute x3 -> x2, waiting for transfers between devices: 12.3 us -> 0.01 us  [passed_along(): lax.ppermute(shard, axis, [(i, (i + by) % length) for i in range(length)])]
    convert_element_type x4 -> x1, other arithmetic: 2.85 us -> 0.02 us  [shards(): own_table.astype(jnp.float32)]
    gather x7 -> x5, local copies, waits for them, and re-layouts: 4.88 us -> 2.19 us  [the longest x4 1.31 us: shards(): incoming[bucket_of + (requester + j) % split_count]]
    all_to_all x1, waiting for transfers between devices: 1.84 us -> 4.53 us  [shards(): lax.all_to_all(outgoing.astype(jnp.bfloat16), both, split_axis=0, concat_...]
    select_n x4 -> x3, other arithmetic: 2.05 us -> 0.03 us  [the longest x2 0.02 us: shards(): incoming[bucket_of + (requester + j) % split_count]]
    all_to_all x1, waiting for transfers between devices: 6.4 us -> 8.35 us  [shards(): lax.all_to_all(picked, both, split_axis=0, concat_axis=0, tiled=True)]
    reshape x3 -> x4, local copies, waits for them, and re-layouts: 0.89 us -> 2.74 us  [the longest x1 1.66 us: shards(): query_grads = query_grads.reshape(-1, row_width)]
    unnamed x27 -> x15, local copies, waits for them, and re-layouts: 3.95 us -> 2.16 us
  transfers between devices with their start and end apart: 6 -> 5, of which waited for: 5 -> 3; matrix products, arithmetic and copies ran while one was open for 28% -> 25% of each run, Pallas kernels for 0% -> 0%
where the time goes in v2:
time: 60.1 us; the launch traced here: 59.6 us
  waiting for transfers between devices  16.4 us (27%)
  starting transfers between devices  14.3 us (24%)
  matrix products  12.9 us (21%)
  local copies, waits for them, and re-layouts  11.1 us (18%)
  other arithmetic  4.02 us (7%)
  between operations  0.97 us (2%)
    all_to_all x1, waiting for transfers between devices, shards(): lax.all_to_all(picked, both, split_axis=0, concat_axis=0, tiled=True)  8.35 us
    all_to_all x1, starting transfers between devices, shards(): lax.all_to_all(wanted, both, split_axis=0, concat_axis=0, tiled=True)  7.3 us
    all_to_all x1, waiting for transfers between devices, shards(): lax.all_to_all(outgoing.astype(jnp.bfloat16), both, split_axis=0, concat_...  4.53 us
    dot_general x3, matrix products, pick_rows(): return jnp.dot(selector, rows, preferred_element_type=jnp.float32)  3.82 us
    all_to_all x1, waiting for transfers between devices, shards(): lax.all_to_all(wanted, both, split_axis=0, concat_axis=0, tiled=True)  3.47 us
    all_to_all x1, starting transfers between devices, shards(): lax.all_to_all(picked, both, split_axis=0, concat_axis=0, tiled=True)  2.58 us
    all_to_all x1, starting transfers between devices, shards(): lax.all_to_all(outgoing.astype(jnp.bfloat16), both, split_axis=0, concat_...  2.57 us
    unnamed x15, local copies, waits for them, and re-layouts  2.16 us
  transfers between devices with their start and end apart: 5, of which 3 were waited for; matrix products, arithmetic and copies ran while one was open for 25% of the time, Pallas kernels for 0%

profile of v2, /device:TPU:0, one launch (start us, length us, event | category | flops | bytes accessed | tf_op | source)
XLA Modules:
  0.0 59.6 jit_solution(10734934669924396948)
XLA Ops:
  0.7 1.4 %copy.57 = s32[1,1,16,2,2]{4,3,2,1,0:T(2,128)} copy(s32[1,1,16,2,2]{2,4,3,1,0:T(2,128)} %param.16) | data formatting | bytes 512 | tf_op jit(solution)/shard_map/all_to_all | solution.py:83
  2.1 7.3 %all-to-all-start = ((s32[32,1,2]{2,1,0:T(1,128)}), s32[32,1,2]{2,1,0:T(1,128)S(1)}, u32[]{:S(2)}, u32[]{:S(2)}) async-start(s32[32,1,2]{2,1,0:T(1,128)} %bitcast.1), calls=%async_computation | async-start | bytes 32768 | tf_op jit(solution)/shard_map/all_to_all | solution.py:83
  9.4 0.7 %pad_add_fusion.1 = s32[1792]{0:T(1024)S(1)} fusion(s32[1024]{0:T(1024)} %bitcast.80, s32[256]{0:T(256)} %param.14, s32[256]{0:T(256)} %param.13, s32[256]{0:T(256)} %param.12), kind=kLoop, calls=%fused_computation.65 | loop fusion | flops 5376 | bytes 14336 | tf_op jit(solution)/shard_map/concatenate | solution.py:71
  10.1 1.8 %collective-permute-start = (s32[1792]{0:T(1024)S(1)}, s32[1792]{0:T(1024)S(1)}, u32[]{:S(2)}, u32[]{:S(2)}) collective-permute-start(s32[1792]{0:T(1024)S(1)} %pad_add_fusion.1), channel_id=1, source_target_pairs={{0,1},{1,0},{2,3},{3,2},{4,5},{5,4},{6,7},{7,6},{8,9},{9,8},{10,11... | collective-permute-start | bytes 21512 | tf_op jit(solution)/shard_map/ppermute | solution.py:9
  12.0 0.8 %copy.54 = s32[1,1,16,2]{3,2,1,0:T(8,128)S(1)} copy(s32[1,1,16,2]{2,3,1,0:T(2,128)} %param.17) | data formatting | bytes 256 | tf_op args[8]
  13.1 3.5 %all-to-all-done = s32[32,1,2]{2,1,0:T(1,128)S(1)} async-done(((s32[32,1,2]{2,1,0:T(1,128)}), s32[32,1,2]{2,1,0:T(1,128)S(1)}, u32[]{:S(2)}, u32[]{:S(2)}) %all-to-all-start) | async-done | bytes 288 | tf_op jit(solution)/shard_map/all_to_all | solution.py:83
  16.7 0.6 gather_fusion.1
  17.3 0.6 gather_fusion
  18.3 0.5 broadcast.280
  18.8 0.7 %reduce.3 = s32[32,2]{1,0:T(8,128)S(1)} reduce(s32[32,1,2]{2,1,0:T(1,128)S(1)} %all-to-all-done, s32[]{:T(128)} %broadcast.280), dimensions={1}, to_apply=%all_to_all.15.reduce_sub_computation.3 | reduce | bytes 516 | tf_op jit(solution)/shard_map/all_to_all | solution.py:83
  19.6 0.9 %gather_fusion.2 = bf16[128,800]{1,0:T(8,128)(2,1)S(1)} fusion(bf16[32,800]{1,0:T(8,128)(2,1)S(1)} %copy-done.1, s32[1024]{0:T(1024)S(1)} %pad_clamp_fusion), kind=kCustom, calls=%fused_computation.2 | custom fusion | bytes 410112 | tf_op jit(solution)/shard_map/gather | solution.py:89
  20.5 0.8 %reshape.246 = bf16[32,4,800]{2,1,0:T(4,128)(2,1)} reshape(bf16[128,800]{1,0:T(8,128)(2,1)S(1)} %gather_fusion.2) | data formatting | bytes 409600 | tf_op jit(solution)/shard_map/reshape | solution.py:89
  21.3 2.6 %all-to-all-start.1 = ((bf16[32,4,800]{2,1,0:T(4,128)(2,1)}), bf16[32,4,800]{2,1,0:T(4,128)(2,1)S(1)}, u32[]{:S(2)}, u32[]{:S(2)}) async-start(bf16[32,4,800]{2,1,0:T(4,128)(2,1)} %reshape.246), calls=%async_computation.1 | async-start | bytes 458752 | tf_op jit(solution)/shard_map/all_to_all | solution.py:92
  24.0 1.7 %fusion.14 = f32[512,800]{0,1:T(8,128)} fusion(bf16[256,800]{0,1:T(8,128)(2,1)S(1)} %copy-done, s32[512]{0:T(512)S(1)} %bitcast.68), kind=kOutput, calls=%fused_computation.38 | convolution fusion | flops 209846272 | bytes 2050048 | tf_op jit(solution)/shard_map/dot_general | solution.py:33
  25.7 8.4 %all-to-all-done.1 = bf16[32,4,800]{2,1,0:T(4,128)(2,1)S(1)} async-done(((bf16[32,4,800]{2,1,0:T(4,128)(2,1)}), bf16[32,4,800]{2,1,0:T(4,128)(2,1)S(1)}, u32[]{:S(2)}, u32[]{:S(2)}) %all-to-all-start.1) | async-done | bytes 204832 | tf_op jit(solution)/shard_map/all_to_all | solution.py:92
  34.8 0.5 fusion.23
  35.3 1.8 %add_convert_fusion = (bf16[512,400]{0,1:T(8,128)(2,1)S(1)}, bf16[512,400]{0,1:T(8,128)(2,1)S(1)}) fusion(f32[512,800]{0,1:T(8,128)} %fusion.14, f32[512,800]{0,1:T(8,128)S(1)} %fusion.23), kind=kLoop, calls=%fused_computation.31 | loop fusion | flops 1638400 | bytes 4096000 | tf_op jit(solution)/shard_map/convert.6
  37.2 1.6 %multiply_reduce_fusion = (f32[512]{0:T(512)S(1)}, f32[512,800]{0,1:T(8,128)}) fusion(bf16[512,400]{0,1:T(8,128)(2,1)S(1)} %get-tuple-element.5, bf16[512,400]{0,1:T(8,128)(2,1)S(1)} %get-tuple-element.6, bf16[256,800]{0,1:T(8,128)(2,1)S(1)} %collective-permute-done.1, s32[512]{0:T(512)S(1)} %bitcast.75), kind=kOutput, calls=%fused_computation.11 | convolution fusion | flops 212303360 | bytes 2871296 | tf_op jit(solution)/shard_map/dot_general | solution.py:33
  38.9 1.1 %convolution_convert_fusion = bf16[2,1024,800]{1,2,0:T(8,128)(2,1)S(1)} fusion(s32[2,1024]{1,0:T(2,128)S(1)} %pad_add_fusion, bf16[256,800]{0,1:T(8,128)(2,1)S(1)} %collective-permute-done.1), kind=kOutput, calls=%fused_computation.3 | convolution fusion | flops 841023488 | bytes 3694592 | tf_op jit(solution)/shard_map/gjp,pd->gjd/dot_general | solution.py:117
  40.0 1.6 %multiply_convert_fusion = bf16[2,256,1024]{2,1,0:T(8,128)(2,1)S(1)} fusion(bf16[2,256,800]{1,2,0:T(8,128)(2,1)S(1)} %bitcast_dynamic-update-slice_fusion, bf16[2,1024,800]{1,2,0:T(8,128)(2,1)S(1)} %convolution_convert_fusion), kind=kOutput, calls=%fused_computation.4 | convolution fusion | flops 841482240 | bytes 5144576 | tf_op jit(solution)/shard_map/gtd,gjd->gtj/dot_general | solution.py:120
  41.6 0.6 fusion.6
  42.2 0.9 %copy-done.4 = f32[512,800]{0,1:T(8,128)S(1)} copy-done((f32[512,800]{0,1:T(8,128)S(1)}, f32[512,800]{0,1:T(8,128)}, u32[]{:S(2)}) %copy-start.4) | copy-done | bytes 1638424
  43.0 1.1 %fusion.1 = f32[2,256,800]{1,2,0:T(8,128)S(1)} fusion(f32[100,2,8,256]{3,2,1,0:T(8,128)S(1)} %bitcast.62, f32[2,256]{1,0:T(2,128)S(1)} %neg.20, bf16[2,256,1024]{2,1,0:T(8,128)(2,1)S(1)} %multiply_convert_fusion, bf16[2,1024,800]{1,2,0:T(8,128)(2,1)S(1)} %convolution_convert_fusion), kind=kOutput, calls=%fused_computation.8 | convolution fusion | flops 839680000 | bytes 7604224 | tf_op jit(solution)/shard_map/gtj,gjd->gtd/dot_general | solution.py:127
  44.5 1.2 %fusion.5 = bf16[256,800]{0,1:T(8,128)(2,1)} fusion(f32[256,800]{0,1:T(8,128)S(1)} %convolution_bitcast_fusion, bf16[2,256,800]{1,2,0:T(8,128)(2,1)S(1)} %bitcast_dynamic-update-slice_fusion, f32[2,256,256]{2,1,0:T(8,128)S(1)} %fusion.6), kind=kOutput, calls=%fused_computation.18 | convolution fusion | flops 210255872 | bytes 2572288 | tf_op jit(solution)/shard_map/gpt,gtd->pd/dot_general | solution.py:137
  45.7 0.5 copy-done.3
  47.1 0.7 %convert_element_type.82 = bf16[32,2,800]{2,1,0:T(2,128)(2,1)} reshape(bf16[64,800]{1,0:T(8,128)(2,1)S(1)} %fusion.8) | data formatting | bytes 204800 | tf_op jit(solution)/shard_map/convert_element_type | solution.py:150
  47.8 2.6 %all-to-all-start.2 = ((bf16[32,2,800]{2,1,0:T(2,128)(2,1)}), bf16[32,2,800]{2,1,0:T(2,128)(2,1)S(1)}, u32[]{:S(2)}, u32[]{:S(2)}) async-start(bf16[32,2,800]{2,1,0:T(2,128)(2,1)} %convert_element_type.82), calls=%async_computation.2 | async-start | bytes 229376 | tf_op jit(solution)/shard_map/all_to_all | solution.py:149
  50.4 1.7 %copy.62 = f32[2,100,8,256]{3,2,0,1:T(8,128)S(1)} copy(f32[2,100,8,256]{3,2,1,0:T(8,128)} %bitcast.61) | data formatting | bytes 3276800 | tf_op jit(solution)/shard_map/reshape | solution.py:141
  52.4 0.5 fusion.11
  52.9 1.3 %fusion.4 = bf16[256,800]{0,1:T(8,128)(2,1)} fusion(f32[256,800]{0,1:T(8,128)S(1)} %fusion.11, f32[512,400]{0,1:T(8,128)S(1)} %get-tuple-element.4, f32[512,400]{0,1:T(8,128)S(1)} %get-tuple-element.3, s32[512]{0:T(512)S(1)} %bitcast.70), kind=kOutput, calls=%fused_computation.17 | convolution fusion | flops 212303872 | bytes 2869248 | tf_op jit(solution)/shard_map/dot_general | solution.py:47
  54.2 4.5 %all-to-all-done.2 = bf16[32,2,800]{2,1,0:T(2,128)(2,1)S(1)} async-done(((bf16[32,2,800]{2,1,0:T(2,128)(2,1)}), bf16[32,2,800]{2,1,0:T(2,128)(2,1)S(1)}, u32[]{:S(2)}, u32[]{:S(2)}) %all-to-all-start.2) | async-done | bytes 102432 | tf_op jit(solution)/shard_map/all_to_all | solution.py:149
  58.8 0.8 %fusion.32 = f32[32,800]{1,0:T(8,128)} fusion(bf16[64,800]{1,0:T(8,128)(2,1)S(1)} %reshape.251, s32[64]{0:T(128)S(1)} %eq.122), kind=kOutput, calls=%fused_computation.62 | convolution fusion | flops 3278848 | bytes 205056 | tf_op jit(solution)/shard_map/dot_general | solution.py:155
  (53 shorter events, 3.7 us)
Async XLA Ops:
  0.6 23.3 %copy-start = (bf16[256,800]{0,1:T(8,128)(2,1)S(1)}, bf16[256,800]{0,1:T(8,128)(2,1)}, u32[]{:S(2)}) copy-start(bf16[256,800]{0,1:T(8,128)(2,1)} %param.9) | copy-start | bytes 1228804
  0.6 19.0 %copy-start.1 = (bf16[32,800]{1,0:T(8,128)(2,1)S(1)}, bf16[32,800]{1,0:T(8,128)(2,1)}, u32[]{:S(2)}) copy-start(bf16[32,800]{1,0:T(8,128)(2,1)} %param.11) | copy-start | bytes 153604
  2.1 14.4 %all-to-all-start = ((s32[32,1,2]{2,1,0:T(1,128)}), s32[32,1,2]{2,1,0:T(1,128)S(1)}, u32[]{:S(2)}, u32[]{:S(2)}) async-start(s32[32,1,2]{2,1,0:T(1,128)} %bitcast.1), calls=%async_computation | async-start | bytes 32768 | tf_op jit(solution)/shard_map/all_to_all | solution.py:83
  10.1 13.7 %collective-permute-start = (s32[1792]{0:T(1024)S(1)}, s32[1792]{0:T(1024)S(1)}, u32[]{:S(2)}, u32[]{:S(2)}) collective-permute-start(s32[1792]{0:T(1024)S(1)} %pad_add_fusion.1), channel_id=1, source_target_pairs={{0,1},{1,0},{2,3},{3,2},{4,5},{5,4},{6,7},{7,6},{8,9},{9,8},{10,11... | collective-permute-start | bytes 21512 | tf_op jit(solution)/shard_map/ppermute | solution.py:9
  12.0 25.2 %collective-permute-start.1 = (bf16[256,800]{0,1:T(8,128)(2,1)}, bf16[256,800]{0,1:T(8,128)(2,1)S(1)}, u32[]{:S(2)}, u32[]{:S(2)}) collective-permute-start(bf16[256,800]{0,1:T(8,128)(2,1)} %param.10), channel_id=1, source_target_pairs={{0,2},{2,4},{4,6},{6,8},{8,10},{10,12},{12,14},{14,16},{16,18},{18... | collective-permute-start | bytes 1228808 | tf_op jit(solution)/shard_map/ppermute | solution.py:9
  21.3 12.8 %all-to-all-start.1 = ((bf16[32,4,800]{2,1,0:T(4,128)(2,1)}), bf16[32,4,800]{2,1,0:T(4,128)(2,1)S(1)}, u32[]{:S(2)}, u32[]{:S(2)}) async-start(bf16[32,4,800]{2,1,0:T(4,128)(2,1)} %reshape.246), calls=%async_computation.1 | async-start | bytes 458752 | tf_op jit(solution)/shard_map/all_to_all | solution.py:92
  41.6 1.4 %copy-start.4 = (f32[512,800]{0,1:T(8,128)S(1)}, f32[512,800]{0,1:T(8,128)}, u32[]{:S(2)}) copy-start(f32[512,800]{0,1:T(8,128)} %get-tuple-element.13) | copy-start | bytes 4915204
  44.1 1.6 %copy-start.2 = (f32[2,256,800]{1,2,0:T(8,128)}, f32[2,256,800]{1,2,0:T(8,128)S(1)}, u32[]{:S(2)}) copy-start(f32[2,256,800]{1,2,0:T(8,128)S(1)} %fusion.1) | copy-start | bytes 4915204
  44.5 1.7 %copy-start.3 = (f32[512,800]{0,1:T(8,128)S(1)}, f32[512,800]{0,1:T(8,128)}, u32[]{:S(2)}) copy-start(f32[512,800]{0,1:T(8,128)} %fusion.14) | copy-start | bytes 4915204
  47.8 10.9 %all-to-all-start.2 = ((bf16[32,2,800]{2,1,0:T(2,128)(2,1)}), bf16[32,2,800]{2,1,0:T(2,128)(2,1)S(1)}, u32[]{:S(2)}, u32[]{:S(2)}) async-start(bf16[32,2,800]{2,1,0:T(2,128)(2,1)} %convert_element_type.82), calls=%async_computation.2 | async-start | bytes 229376 | tf_op jit(solution)/shard_map/all_to_all | solution.py:149

commit v3 on v2

--- a/solution.py
+++ b/solution.py
@@ -86,9 +86,9 @@
     served = jnp.stack(
         [incoming[bucket_of + (requester + j) % split_count] for j in range(split_count)], axis=1
     )
-    picked = relations[served.reshape(-1)].reshape(
-        owner_count, split_count * slot_count, row_width
-    )
+    picked = pick_rows(one_hot(served.reshape(-1), owned_rows), relations).astype(
+        jnp.bfloat16
+    ).reshape(owner_count, split_count * slot_count, row_width)
     fetched = lax.all_to_all(picked, both, split_axis=0, concat_axis=0, tiled=True)
     slot_table = (
         fetched.reshape(owner_count, split_count, slot_count, row_width)
@@ -102,48 +102,50 @@
         .astype(jnp.float32)
     )
 
-    word_sel = one_hot(word_ids, part_rows)
-    ctx_sel = one_hot(ctx_ids, part_rows)
-    word_used = pick_rows(word_sel, words)
-    ctx_used = pick_rows(ctx_sel, held_rows)
-    rel_used = pick_rows(one_hot(slot_ids, split_count * slot_total), slot_table)
-    query = complex_product(word_used, rel_used, half_width).astype(jnp.bfloat16)
-    positive = jnp.sum(query.astype(jnp.float32) * ctx_used, axis=1)
-    pos_grad = -jax.nn.sigmoid(-positive)
-
     group_count = split_count * block_count
-    query_blocks = query.reshape(group_count, block_size, row_width)
-    neg_sel = one_hot(neg_ids, part_rows)
-    neg_rows = jnp.einsum(
-        "gjp,pd->gjd", neg_sel, held_rows, preferred_element_type=jnp.float32
-    ).astype(jnp.bfloat16)
-    scores = jnp.einsum(
-        "gtd,gjd->gtj", query_blocks, neg_rows, preferred_element_type=jnp.float32
-    )
-    neg_grad = (jax.nn.sigmoid(scores) * neg_scale).astype(jnp.bfloat16)
-    pos_blocks = pos_grad.reshape(group_count, block_size)
-    query_grads = pos_blocks[:, :, None] * ctx_used.reshape(
-        group_count, block_size, row_width
-    ) + jnp.einsum("gtj,gjd->gtd", neg_grad, neg_rows, preferred_element_type=jnp.float32)
-
-    neg_weight = jnp.einsum("gtj,gjp->gpt", neg_grad, neg_sel, preferred_element_type=jnp.float32)
-    pos_weight = jnp.where(
-        ctx_ids.reshape(group_count, 1, block_size)
-        == jnp.arange(part_rows)[None, :, None],
-        pos_blocks[:, None, :],
-        0.0,
-    )
-    weight_hi, weight_lo = split_bf16(neg_weight + pos_weight)
-    ctx_sum = jnp.einsum(
-        "gpt,gtd->pd", weight_hi, query_blocks, preferred_element_type=jnp.float32
-    ) + jnp.einsum("gpt,gtd->pd", weight_lo, query_blocks, preferred_element_type=jnp.float32)
-
-    query_grads = query_grads.reshape(-1, row_width)
-    word_sum = spread_rows(word_sel, conj_product(query_grads, rel_used, half_width))
-    slot_grad = spread_rows(
-        one_hot(slot_ids[:trips], slot_total),
-        conj_product(query_grads[:trips], word_used[:trips], half_width),
-    )
+    slot_sel = one_hot(slot_ids, split_count * slot_total)
+    word_sum = jnp.zeros((part_rows, row_width), jnp.float32)
+    ctx_sum = jnp.zeros((part_rows, row_width), jnp.float32)
+    slot_grad = jnp.zeros((slot_total, row_width), jnp.float32)
+    for group in range(group_count):
+        rows_of = slice(group * block_size, (group + 1) * block_size)
+        word_sel = one_hot(word_ids[rows_of], part_rows)
+        ctx_ids_of = ctx_ids[rows_of]
+        word_used = pick_rows(word_sel, words)
+        ctx_used = pick_rows(one_hot(ctx_ids_of, part_rows), held_rows)
+        rel_used = pick_rows(slot_sel[rows_of], slot_table)
+        query = complex_product(word_used, rel_used, half_width).astype(jnp.bfloat16)
+        positive = jnp.sum(query.astype(jnp.float32) * ctx_used, axis=1)
+        pos_grad = -jax.nn.sigmoid(-positive)
+        neg_sel = one_hot(neg_ids[group], part_rows)
+        neg_rows = pick_rows(neg_sel, held_rows).astype(jnp.bfloat16)
+        scores = lax.dot_general(
+            query, neg_rows, (((1,), (1,)), ((), ())), preferred_element_type=jnp.float32
+        )
+        neg_grad = (jax.nn.sigmoid(scores) * neg_scale).astype(jnp.bfloat16)
+        query_grad = pos_grad[:, None] * ctx_used + jnp.dot(
+            neg_grad, neg_rows, preferred_element_type=jnp.float32
+        )
+        if group < block_count:
+            slot_grad = slot_grad + spread_rows(
+                one_hot(slot_ids[rows_of], slot_total),
+                conj_product(query_grad, word_used, half_width),
+            )
+        neg_weight = lax.dot_general(
+            neg_sel, neg_grad, (((0,), (1,)), ((), ())), preferred_element_type=jnp.float32
+        )
+        pos_weight = jnp.where(
+            ctx_ids_of[None, :] == jnp.arange(part_rows)[:, None], pos_grad[None, :], 0.0
+        )
+        weight_hi, weight_lo = split_bf16(neg_weight + pos_weight)
+        ctx_sum = (
+            ctx_sum
+            + jnp.dot(weight_hi, query, preferred_element_type=jnp.float32)
+            + jnp.dot(weight_lo, query, preferred_element_type=jnp.float32)
+        )
+        word_sum = word_sum + spread_rows(
+            word_sel, conj_product(query_grad, rel_used, half_width)
+        )
     slot_grad = slot_grad + 0.02 * live_mask[:, None] * own_table.astype(jnp.float32)
     outgoing = slot_grad.reshape(owner_count, slot_count, row_width)
     returned = lax.all_to_all(

time: 60.1 us -> 59 us (0.982)
  waiting for transfers between devices: 16.4 us -> 10.8 us
  matrix products: 12.9 us -> 16.5 us
  local copies, waits for them, and re-layouts: 11.1 us -> 12.9 us
  other arithmetic: 4.02 us -> 3.2 us
    all_to_all x1, waiting for transfers between devices: 4.53 us -> 0.01 us  [shards(): lax.all_to_all(outgoing.astype(jnp.bfloat16), both, split_axis=0, concat_...]
    all_to_all x1, starting transfers between devices: 7.3 us -> 4.92 us  [shards(): lax.all_to_all(wanted, both, split_axis=0, concat_axis=0, tiled=True)]
    dot_general x6 -> x10, matrix products: 5.88 us -> 7.84 us  [the longest x2 2.44 us: shards(): jnp.dot(weight_lo, query, preferred_element_type=jnp.float32)]
    reshape x3 -> x1, local copies, waits for them, and re-layouts: 2.57 us -> 0.76 us  [shards(): picked = pick_rows(one_hot(served.reshape(-1), owned_rows), relations).as...]
    all_to_all x1, waiting for transfers between devices: 8.35 us -> 6.54 us  [shards(): lax.all_to_all(picked, both, split_axis=0, concat_axis=0, tiled=True)]
    slice x2 -> x5, local copies, waits for them, and re-layouts: 0.06 us -> 1.7 us  [the longest x2 1.13 us: shards(): ctx_ids_of = ctx_ids[rows_of]]
    ppermute x2, starting transfers between devices: 1.82 us -> 3.29 us  [passed_along(): lax.ppermute(shard, axis, [(i, (i + by) % length) for i in range(length)])]
    dot_general x3 -> x9, matrix products: 3.82 us -> 5.02 us  [pick_rows(): return jnp.dot(selector, rows, preferred_element_type=jnp.float32)]
  transfers between devices with their start and end apart: 5 -> 5, of which waited for: 3 -> 2; matrix products, arithmetic and copies ran while one was open for 25% -> 40% of each run, Pallas kernels for 0% -> 0%
where the time goes in v3:
time: 59 us; the launch traced here: 58.5 us
  matrix products  16.5 us (28%)
  starting transfers between devices  14.1 us (24%)
  local copies, waits for them, and re-layouts  12.9 us (22%)
  waiting for transfers between devices  10.8 us (18%)
  other arithmetic  3.2 us (5%)
  between operations  1.15 us (2%)
    all_to_all x1, waiting for transfers between devices, shards(): lax.all_to_all(picked, both, split_axis=0, concat_axis=0, tiled=True)  6.54 us
    dot_general x9, matrix products, pick_rows(): return jnp.dot(selector, rows, preferred_element_type=jnp.float32)  5.02 us
    all_to_all x1, starting transfers between devices, shards(): lax.all_to_all(wanted, both, split_axis=0, concat_axis=0, tiled=True)  4.92 us
    all_to_all x1, waiting for transfers between devices, shards(): lax.all_to_all(wanted, both, split_axis=0, concat_axis=0, tiled=True)  4.21 us
    ppermute x2, starting transfers between devices, passed_along(): lax.ppermute(shard, axis, [(i, (i + by) % length) for i in range(length)])  3.29 us
    all_to_all x1, starting transfers between devices, shards(): lax.all_to_all(outgoing.astype(jnp.bfloat16), both, split_axis=0, concat_...  3.28 us
    all_to_all x1, starting transfers between devices, shards(): lax.all_to_all(picked, both, split_axis=0, concat_axis=0, tiled=True)  2.58 us
    dot_general x2, matrix products, shards(): jnp.dot(weight_lo, query, preferred_element_type=jnp.float32)  2.44 us
  transfers between devices with their start and end apart: 5, of which 2 were waited for; matrix products, arithmetic and copies ran while one was open for 40% of the time, Pallas kernels for 0%

profile of v3, /device:TPU:0, one launch (start us, length us, event | category | flops | bytes accessed | tf_op | source)
XLA Modules:
  0.0 58.5 jit_solution(6673038781824390251)
XLA Ops:
  0.7 0.8 %pad_add_fusion = s32[1792]{0:T(1024)S(1)} fusion(s32[1024]{0:T(1024)} %bitcast.64, s32[256]{0:T(256)} %param.14, s32[256]{0:T(256)} %param.13, s32[256]{0:T(256)} %param.12), kind=kLoop, calls=%fused_computation.107 | loop fusion | flops 5376 | bytes 14336 | tf_op jit(solution)/shard_map/concatenate | solution.py:71
  1.4 3.0 %collective-permute-start = (s32[1792]{0:T(1024)S(1)}, s32[1792]{0:T(1024)S(1)}, u32[]{:S(2)}, u32[]{:S(2)}) collective-permute-start(s32[1792]{0:T(1024)S(1)} %pad_add_fusion), channel_id=1, source_target_pairs={{0,1},{1,0},{2,3},{3,2},{4,5},{5,4},{6,7},{7,6},{8,9},{9,8},{10,11... | collective-permute-start | bytes 21512 | tf_op jit(solution)/shard_map/ppermute | solution.py:9
  4.4 1.4 %copy.46 = s32[1,1,16,2,2]{4,3,2,1,0:T(2,128)} copy(s32[1,1,16,2,2]{2,4,3,1,0:T(2,128)} %param.16) | data formatting | bytes 512 | tf_op jit(solution)/shard_map/all_to_all | solution.py:83
  5.8 4.9 %all-to-all-start = ((s32[32,1,2]{2,1,0:T(1,128)}), s32[32,1,2]{2,1,0:T(1,128)S(1)}, u32[]{:S(2)}, u32[]{:S(2)}) async-start(s32[32,1,2]{2,1,0:T(1,128)} %bitcast.2), calls=%async_computation | async-start | bytes 32768 | tf_op jit(solution)/shard_map/all_to_all | solution.py:83
  11.1 0.6 %fusion.76 = (s32[1,256]{1,0:T(1,128)}, s32[1,256]{1,0:T(1,128)S(1)}) fusion(s32[1,1792]{1,0:T(1,128)S(1)} %stack.18), kind=kLoop, calls=%fused_computation.140 | loop fusion | bytes 4096 | tf_op jit(solution)/shard_map/slice | solution.py:113
  11.7 0.8 %copy.44 = s32[1,1,16,2]{3,2,1,0:T(8,128)S(1)} copy(s32[1,1,16,2]{2,3,1,0:T(2,128)} %param.17) | data formatting | bytes 256 | tf_op args[8]
  13.0 0.6 %mul.162 = f32[64]{0:T(128)} reshape(f32[32,2]{1,0:T(8,128)S(1)} %fusion.60) | data formatting | bytes 512 | tf_op jit(solution)/shard_map/mul | solution.py:149
  13.7 4.2 %all-to-all-done = s32[32,1,2]{2,1,0:T(1,128)S(1)} async-done(((s32[32,1,2]{2,1,0:T(1,128)}), s32[32,1,2]{2,1,0:T(1,128)S(1)}, u32[]{:S(2)}, u32[]{:S(2)}) %all-to-all-start) | async-done | bytes 288 | tf_op jit(solution)/shard_map/all_to_all | solution.py:83
  18.0 0.6 gather_fusion
  18.7 0.6 gather_fusion.1
  20.1 0.8 %reshape.219 = bf16[32,4,800]{2,1,0:T(4,128)(2,1)} reshape(bf16[128,800]{1,0:T(8,128)(2,1)S(1)} %copy.41) | data formatting | bytes 409600 | tf_op jit(solution)/shard_map/reshape | solution.py:91
  20.9 2.6 %all-to-all-start.1 = ((bf16[32,4,800]{2,1,0:T(4,128)(2,1)}), bf16[32,4,800]{2,1,0:T(4,128)(2,1)S(1)}, u32[]{:S(2)}, u32[]{:S(2)}) async-start(bf16[32,4,800]{2,1,0:T(4,128)(2,1)} %reshape.219), calls=%async_computation.1 | async-start | bytes 458752 | tf_op jit(solution)/shard_map/all_to_all | solution.py:92
  24.0 0.7 %reduce.3 = s32[32,2]{1,0:T(8,128)S(1)} reduce(s32[32,1,2]{2,1,0:T(1,128)S(1)} %all-to-all-done, s32[]{:T(128)} %broadcast.280), dimensions={1}, to_apply=%all_to_all.15.reduce_sub_computation.3 | reduce | bytes 516 | tf_op jit(solution)/shard_map/all_to_all | solution.py:83
  24.7 0.6 %eq.217 = s32[64]{0:T(128)} reshape(s32[32,2]{1,0:T(8,128)S(1)} %reduce.3) | data formatting | bytes 512 | tf_op jit(solution)/shard_map/eq | solution.py:154
  27.1 6.5 %all-to-all-done.1 = bf16[32,4,800]{2,1,0:T(4,128)(2,1)S(1)} async-done(((bf16[32,4,800]{2,1,0:T(4,128)(2,1)}), bf16[32,4,800]{2,1,0:T(4,128)(2,1)S(1)}, u32[]{:S(2)}, u32[]{:S(2)}) %all-to-all-start.1) | async-done | bytes 204832 | tf_op jit(solution)/shard_map/all_to_all | solution.py:92
  34.3 0.8 %reshape.223 = f32[64,800]{1,0:T(8,128)} reshape(f32[1,32,2,800]{3,2,1,0:T(2,128)S(1)} %copy.45) | data formatting | bytes 409600 | tf_op jit(solution)/shard_map/convert_element_type | solution.py:149
  35.6 1.3 %fusion.45 = f32[256,800]{0,1:T(8,128)S(1)} fusion(bf16[128,800]{1,0:T(8,128)(2,1)} %copy-done.5, pred[512,128]{1,0:T(32,128)(4,1)S(1)} %iota_compare_fusion.12), kind=kOutput, calls=%fused_computation.89 | convolution fusion | flops 52428800 | bytes 1056768 | tf_op jit(solution)/shard_map/dot_general | solution.py:33
  36.9 0.9 %subtract_convert_fusion.6 = (bf16[256,400]{0,1:T(8,128)(2,1)}, bf16[256,400]{0,1:T(8,128)(2,1)}) fusion(f32[256,800]{0,1:T(8,128)S(1)} %fusion.32, f32[256,800]{0,1:T(8,128)S(1)} %fusion.45), kind=kLoop, calls=%fused_computation.61 | loop fusion | flops 819200 | bytes 2048000 | tf_op jit(solution)/shard_map/convert.1
  38.3 0.7 %convolution_convert_fusion.1 = bf16[1024,800]{0,1:T(8,128)(2,1)S(1)} fusion(bf16[256,800]{0,1:T(8,128)(2,1)S(1)} %collective-permute-done.1, s32[1024]{0:T(1024)S(1)} %bitcast.44), kind=kOutput, calls=%fused_computation.3 | convolution fusion | flops 420511744 | bytes 2052096 | tf_op jit(solution)/shard_map/dot_general | solution.py:33
  39.0 0.9 %fusion.10 = bf16[256,1024]{1,0:T(8,128)(2,1)S(1)} fusion(bf16[1024,800]{0,1:T(8,128)(2,1)S(1)} %convolution_convert_fusion.1, bf16[256,400]{0,1:T(8,128)(2,1)S(1)} %get-tuple-element.12, bf16[256,400]{0,1:T(8,128)(2,1)S(1)} %get-tuple-element.11), kind=kOutput, calls=%fused_computation.21 | convolution fusion | flops 421560320 | bytes 2572288 | tf_op jit(solution)/shard_map/dot_general | solution.py:122
  39.9 1.2 %convolution_add_fusion.6 = f32[256,256]{1,0:T(8,128)} fusion(bf16[256,1024]{1,0:T(8,128)(2,1)S(1)} %fusion.10, s32[1024]{0:T(1024)S(1)} %bitcast.45, f32[256]{0:T(256)S(1)} %divide_negate_fusion.1, s32[256]{0:T(256)S(1)} %bitcast.58), kind=kOutput, calls=%fused_computation.26 | convolution fusion | flops 134938624 | bytes 792576 | tf_op jit(solution)/shard_map/dot_general | solution.py:134
  41.1 0.6 %multiply_add_fusion.1 = f32[256,800]{0,1:T(8,128)S(1)} fusion(f32[256,800]{0,1:T(8,128)S(1)} %get-tuple-element.20, f32[256]{0:T(256)S(1)} %divide_negate_fusion.1, bf16[256,1024]{1,0:T(8,128)(2,1)S(1)} %fusion.10, bf16[1024,800]{0,1:T(8,128)(2,1)S(1)} %convolution_convert_fusion.1), kind=kOutput, calls=%fused_computation.42 | convolution fusion | flops 419840000 | bytes 3802112 | tf_op jit(solution)/shard_map/dot_general | solution.py:126
  43.2 0.7 %convert_element_type.126 = bf16[32,2,800]{2,1,0:T(2,128)(2,1)} reshape(bf16[64,800]{1,0:T(8,128)(2,1)S(1)} %fusion.14) | data formatting | bytes 204800 | tf_op jit(solution)/shard_map/convert_element_type | solution.py:152
  43.8 3.3 %all-to-all-start.2 = ((bf16[32,2,800]{2,1,0:T(2,128)(2,1)}), bf16[32,2,800]{2,1,0:T(2,128)(2,1)}, u32[]{:S(2)}, u32[]{:S(2)}) async-start(bf16[32,2,800]{2,1,0:T(2,128)(2,1)} %convert_element_type.126), calls=%async_computation.2 | async-start | bytes 229376 | tf_op jit(solution)/shard_map/all_to_all | solution.py:151
  47.5 1.4 %convolution_add_fusion.2 = f32[256,800]{0,1:T(8,128)S(1)} fusion(f32[256,800]{0,1:T(8,128)S(1)} %fusion.56, f32[256,256]{1,0:T(8,128)} %convolution_add_fusion.6, bf16[256,400]{0,1:T(8,128)(2,1)} %copy-done.1, bf16[256,400]{0,1:T(8,128)(2,1)S(1)} %get-tuple-element.11), kind=kOutput, calls=%fused_computation.16 | convolution fusion | flops 106143744 | bytes 2310144 | tf_op jit(solution)/shard_map/dot_general | solution.py:144
  49.4 0.7 %convolution_convert_fusion = bf16[1024,800]{0,1:T(8,128)(2,1)S(1)} fusion(bf16[256,800]{0,1:T(8,128)(2,1)S(1)} %collective-permute-done.1, s32[1024]{0:T(1024)S(1)} %bitcast.46), kind=kOutput, calls=%fused_computation.2 | convolution fusion | flops 420511744 | bytes 2052096 | tf_op jit(solution)/shard_map/dot_general | solution.py:33
  50.1 0.9 %fusion.9 = bf16[256,1024]{1,0:T(8,128)(2,1)S(1)} fusion(bf16[1024,800]{0,1:T(8,128)(2,1)S(1)} %convolution_convert_fusion, bf16[256,400]{0,1:T(8,128)(2,1)S(1)} %copy-done.4, bf16[256,400]{0,1:T(8,128)(2,1)S(1)} %copy-done.3), kind=kOutput, calls=%fused_computation.20 | convolution fusion | flops 421560320 | bytes 2572288 | tf_op jit(solution)/shard_map/dot_general | solution.py:122
  51.5 0.6 %multiply_add_fusion = f32[256,800]{0,1:T(8,128)S(1)} fusion(f32[256,800]{0,1:T(8,128)S(1)} %get-tuple-element.22, f32[256]{0:T(256)S(1)} %divide_negate_fusion, bf16[256,1024]{1,0:T(8,128)(2,1)S(1)} %fusion.9, bf16[1024,800]{0,1:T(8,128)(2,1)S(1)} %convolution_convert_fusion), kind=kOutput, calls=%fused_computation.39 | convolution fusion | flops 419840000 | bytes 3802112 | tf_op jit(solution)/shard_map/dot_general | solution.py:126
  54.6 1.1 %fusion.11 = bf16[256,800]{0,1:T(8,128)(2,1)} fusion(f32[256,800]{0,1:T(8,128)S(1)} %convolution_add_fusion.4, f32[256,800]{0,1:T(8,128)S(1)} %fusion.28, f32[256,400]{0,1:T(8,128)S(1)} %get-tuple-element.6, f32[256,400]{0,1:T(8,128)S(1)} %get-tuple-element.5, s32[256]{0:T(256)S(1)} %bitcast.53), kind=kOutput, calls=%fused_computation.22 | convolution fusion | flops 106561536 | bytes 2868224 | tf_op jit(solution)/shard_map/dot_general | solution.py:47
  55.7 1.1 %fusion.12 = bf16[256,800]{0,1:T(8,128)(2,1)} fusion(f32[256,800]{0,1:T(8,128)S(1)} %convolution_add_fusion.1, f32[256,256]{1,0:T(8,128)S(1)} %convolution_add_fusion.5, bf16[256,400]{0,1:T(8,128)(2,1)S(1)} %copy-done.4, bf16[256,400]{0,1:T(8,128)(2,1)S(1)} %copy-done.3), kind=kOutput, calls=%fused_computation.23 | convolution fusion | flops 106348544 | bytes 1900544 | tf_op jit(solution)/shard_map/dot_general | solution.py:144
  56.7 1.0 %reshape.222 = bf16[64,800]{1,0:T(8,128)(2,1)S(1)} reshape(bf16[32,2,800]{2,1,0:T(2,128)(2,1)} %all-to-all-done.2) | data formatting | bytes 204800 | tf_op jit(solution)/shard_map/reshape | solution.py:159
  57.7 0.8 %fusion.59 = f32[32,800]{1,0:T(8,128)} fusion(bf16[64,800]{1,0:T(8,128)(2,1)S(1)} %reshape.222, s32[64]{0:T(128)S(1)} %copy-done.16), kind=kOutput, calls=%fused_computation.105 | convolution fusion | flops 3278848 | bytes 205056 | tf_op jit(solution)/shard_map/dot_general | solution.py:157
  (90 shorter events, 10.7 us)
Async XLA Ops:
  0.6 12.0 %copy-start = (bf16[256,800]{0,1:T(8,128)(2,1)S(1)}, bf16[256,800]{0,1:T(8,128)(2,1)}, u32[]{:S(2)}) copy-start(bf16[256,800]{0,1:T(8,128)(2,1)} %param.9) | copy-start | bytes 1228804
  0.6 19.0 %copy-start.8 = (bf16[32,800]{1,0:T(8,128)(2,1)S(1)}, bf16[32,800]{1,0:T(8,128)(2,1)}, u32[]{:S(2)}) copy-start(bf16[32,800]{1,0:T(8,128)(2,1)} %param.11) | copy-start | bytes 153604
  1.4 23.9 %collective-permute-start = (s32[1792]{0:T(1024)S(1)}, s32[1792]{0:T(1024)S(1)}, u32[]{:S(2)}, u32[]{:S(2)}) collective-permute-start(s32[1792]{0:T(1024)S(1)} %pad_add_fusion), channel_id=1, source_target_pairs={{0,1},{1,0},{2,3},{3,2},{4,5},{5,4},{6,7},{7,6},{8,9},{9,8},{10,11... | collective-permute-start | bytes 21512 | tf_op jit(solution)/shard_map/ppermute | solution.py:9
  5.8 12.1 %all-to-all-start = ((s32[32,1,2]{2,1,0:T(1,128)}), s32[32,1,2]{2,1,0:T(1,128)S(1)}, u32[]{:S(2)}, u32[]{:S(2)}) async-start(s32[32,1,2]{2,1,0:T(1,128)} %bitcast.2), calls=%async_computation | async-start | bytes 32768 | tf_op jit(solution)/shard_map/all_to_all | solution.py:83
  10.7 27.1 %collective-permute-start.1 = (bf16[256,800]{0,1:T(8,128)(2,1)}, bf16[256,800]{0,1:T(8,128)(2,1)S(1)}, u32[]{:S(2)}, u32[]{:S(2)}) collective-permute-start(bf16[256,800]{0,1:T(8,128)(2,1)} %param.10), channel_id=1, source_target_pairs={{0,2},{2,4},{4,6},{6,8},{8,10},{10,12},{12,14},{14,16},{16,18},{18... | collective-permute-start | bytes 1228808 | tf_op jit(solution)/shard_map/ppermute | solution.py:9
  11.7 6.3 %copy-start.9 = (s32[1,256]{1,0:T(1,128)}, s32[1,256]{1,0:T(1,128)S(1)}, u32[]{:S(2)}) copy-start(s32[1,256]{1,0:T(1,128)S(1)} %get-tuple-element.18) | copy-start | bytes 3076
  20.9 12.8 %all-to-all-start.1 = ((bf16[32,4,800]{2,1,0:T(4,128)(2,1)}), bf16[32,4,800]{2,1,0:T(4,128)(2,1)S(1)}, u32[]{:S(2)}, u32[]{:S(2)}) async-start(bf16[32,4,800]{2,1,0:T(4,128)(2,1)} %reshape.219), calls=%async_computation.1 | async-start | bytes 458752 | tf_op jit(solution)/shard_map/all_to_all | solution.py:92
  26.7 7.5 %copy-start.11 = (s32[1,256]{1,0:T(1,128)}, s32[1,256]{1,0:T(1,128)S(1)}, u32[]{:S(2)}) copy-start(s32[1,256]{1,0:T(1,128)S(1)} %get-tuple-element.16) | copy-start | bytes 3076
  34.0 1.4 %copy-start.5 = (bf16[128,800]{1,0:T(8,128)(2,1)}, bf16[128,800]{1,0:T(8,128)(2,1)S(1)}, u32[]{:S(2)}) copy-start(bf16[128,800]{1,0:T(8,128)(2,1)S(1)} %reshape.221) | copy-start | bytes 614404
  35.6 3.4 %copy-start.1 = (bf16[256,400]{0,1:T(8,128)(2,1)}, bf16[256,400]{0,1:T(8,128)(2,1)S(1)}, u32[]{:S(2)}) copy-start(bf16[256,400]{0,1:T(8,128)(2,1)S(1)} %get-tuple-element.12) | copy-start | bytes 614404
  35.6 2.2 %copy-start.14 = (s32[1,256]{1,0:T(1,128)S(1)}, s32[1,256]{1,0:T(1,128)}, u32[]{:S(2)}) copy-start(s32[1,256]{1,0:T(1,128)} %get-tuple-element.17) | copy-start | bytes 3076
  41.8 0.7 %copy-start.13 = (s32[1,256]{1,0:T(1,128)S(1)}, s32[1,256]{1,0:T(1,128)}, u32[]{:S(2)}) copy-start(s32[1,256]{1,0:T(1,128)} %slice.145) | copy-start | bytes 3076
  41.8 1.0 %copy-start.7 = (f32[64,800]{1,0:T(8,128)S(1)}, f32[64,800]{1,0:T(8,128)}, u32[]{:S(2)}) copy-start(f32[64,800]{1,0:T(8,128)} %reshape.223) | copy-start | bytes 614404
  41.8 1.0 %copy-start.17 = (f32[64]{0:T(128)S(1)}, f32[64]{0:T(128)}, u32[]{:S(2)}) copy-start(f32[64]{0:T(128)} %mul.162) | copy-start | bytes 772
  42.0 5.2 %copy-start.2 = (bf16[256,400]{0,1:T(8,128)(2,1)S(1)}, bf16[256,400]{0,1:T(8,128)(2,1)}, u32[]{:S(2)}) copy-start(bf16[256,400]{0,1:T(8,128)(2,1)} %copy-done.1) | copy-start | bytes 614404
  42.0 5.2 %copy-start.6 = (f32[256,256]{1,0:T(8,128)S(1)}, f32[256,256]{1,0:T(8,128)}, u32[]{:S(2)}) copy-start(f32[256,256]{1,0:T(8,128)} %convolution_add_fusion.6) | copy-start | bytes 786436
  43.8 12.9 %all-to-all-start.2 = ((bf16[32,2,800]{2,1,0:T(2,128)(2,1)}), bf16[32,2,800]{2,1,0:T(2,128)(2,1)}, u32[]{:S(2)}, u32[]{:S(2)}) async-start(bf16[32,2,800]{2,1,0:T(2,128)(2,1)} %convert_element_type.126), calls=%async_computation.2 | async-start | bytes 229376 | tf_op jit(solution)/shard_map/all_to_all | solution.py:151
  47.2 1.7 %copy-start.3 = (bf16[256,400]{0,1:T(8,128)(2,1)S(1)}, bf16[256,400]{0,1:T(8,128)(2,1)}, u32[]{:S(2)}) copy-start(bf16[256,400]{0,1:T(8,128)(2,1)} %get-tuple-element.7) | copy-start | bytes 614404
  47.2 1.7 %copy-start.4 = (bf16[256,400]{0,1:T(8,128)(2,1)S(1)}, bf16[256,400]{0,1:T(8,128)(2,1)}, u32[]{:S(2)}) copy-start(bf16[256,400]{0,1:T(8,128)(2,1)} %get-tuple-element.8) | copy-start | bytes 614404
  47.2 1.7 %copy-start.15 = (s32[1,256]{1,0:T(1,128)S(1)}, s32[1,256]{1,0:T(1,128)}, u32[]{:S(2)}) copy-start(s32[1,256]{1,0:T(1,128)} %get-tuple-element.15) | copy-start | bytes 3076
  52.2 0.7 %copy-start.10 = (s32[1,256]{1,0:T(1,128)S(1)}, s32[1,256]{1,0:T(1,128)}, u32[]{:S(2)}) copy-start(s32[1,256]{1,0:T(1,128)} %copy-done.9) | copy-start | bytes 3076
  53.6 0.7 %copy-start.12 = (s32[1,256]{1,0:T(1,128)S(1)}, s32[1,256]{1,0:T(1,128)}, u32[]{:S(2)}) copy-start(s32[1,256]{1,0:T(1,128)} %copy-done.11) | copy-start | bytes 3076
  55.7 2.1 %copy-start.16 = (s32[64]{0:T(128)S(1)}, s32[64]{0:T(128)}, u32[]{:S(2)}) copy-start(s32[64]{0:T(128)} %eq.217) | copy-start | bytes 772

commit v4 on v2

--- a/solution.py
+++ b/solution.py
@@ -81,55 +81,58 @@
 
     wanted = requests[0, 0].reshape(owner_count, slot_count)
     incoming = lax.all_to_all(wanted, both, split_axis=0, concat_axis=0, tiled=True)
-    requester = jnp.arange(owner_count)
-    bucket_of = (requester // split_count) * split_count
-    served = jnp.stack(
-        [incoming[bucket_of + (requester + j) % split_count] for j in range(split_count)], axis=1
+    lists = incoming.reshape(part_count, split_count, slot_count)
+    served = jnp.stack([jnp.roll(lists, -j, axis=1) for j in range(split_count)], axis=2)
+    picked = pick_rows(one_hot(served.reshape(-1), owned_rows), relations).astype(
+        jnp.bfloat16
+    ).reshape(owner_count, split_count * slot_count, row_width)
+    fetched = lax.all_to_all(picked, both, split_axis=0, concat_axis=0, tiled=True)
+    live_mask = (
+        (jnp.arange(slot_count)[None, :] < counts[0, 0].reshape(owner_count)[:, None])
+        .reshape(-1)
+        .astype(jnp.float32)
     )
-    picked = relations[served.reshape(-1)].reshape(
-        owner_count, split_count * slot_count, row_width
+
+    group_count = split_count * block_count
+    word_sel = one_hot(word_ids, part_rows)
+    ctx_sel = one_hot(ctx_ids, part_rows)
+    neg_sel = one_hot(neg_ids, part_rows)
+    word_used = pick_rows(word_sel, words)
+    ctx_used = pick_rows(ctx_sel, held_rows)
+    neg_rows = jnp.einsum(
+        "gjp,pd->gjd", neg_sel, held_rows, preferred_element_type=jnp.float32
+    ).astype(jnp.bfloat16)
+    fetched, word_used, ctx_used, neg_rows = lax.optimization_barrier(
+        (fetched, word_used, ctx_used, neg_rows)
     )
-    fetched = lax.all_to_all(picked, both, split_axis=0, concat_axis=0, tiled=True)
     slot_table = (
         fetched.reshape(owner_count, split_count, slot_count, row_width)
         .transpose(1, 0, 2, 3)
         .reshape(split_count * slot_total, row_width)
     )
     own_table = slot_table[:slot_total]
-    live_mask = (
-        (jnp.arange(slot_count)[None, :] < counts[0, 0].reshape(owner_count)[:, None])
-        .reshape(-1)
-        .astype(jnp.float32)
-    )
-
-    word_sel = one_hot(word_ids, part_rows)
-    ctx_sel = one_hot(ctx_ids, part_rows)
-    word_used = pick_rows(word_sel, words)
-    ctx_used = pick_rows(ctx_sel, held_rows)
     rel_used = pick_rows(one_hot(slot_ids, split_count * slot_total), slot_table)
     query = complex_product(word_used, rel_used, half_width).astype(jnp.bfloat16)
     positive = jnp.sum(query.astype(jnp.float32) * ctx_used, axis=1)
     pos_grad = -jax.nn.sigmoid(-positive)
-
-    group_count = split_count * block_count
     query_blocks = query.reshape(group_count, block_size, row_width)
-    neg_sel = one_hot(neg_ids, part_rows)
-    neg_rows = jnp.einsum(
-        "gjp,pd->gjd", neg_sel, held_rows, preferred_element_type=jnp.float32
-    ).astype(jnp.bfloat16)
     scores = jnp.einsum(
         "gtd,gjd->gtj", query_blocks, neg_rows, preferred_element_type=jnp.float32
     )
     neg_grad = (jax.nn.sigmoid(scores) * neg_scale).astype(jnp.bfloat16)
     pos_blocks = pos_grad.reshape(group_count, block_size)
-    query_grads = pos_blocks[:, :, None] * ctx_used.reshape(
-        group_count, block_size, row_width
-    ) + jnp.einsum("gtj,gjd->gtd", neg_grad, neg_rows, preferred_element_type=jnp.float32)
+    query_grads = (
+        pos_blocks[:, :, None] * ctx_used.reshape(group_count, block_size, row_width)
+        + jnp.einsum("gtj,gjd->gtd", neg_grad, neg_rows, preferred_element_type=jnp.float32)
+    ).reshape(-1, row_width)
+    slot_grad = spread_rows(
+        one_hot(slot_ids[:trips], slot_total),
+        conj_product(query_grads[:trips], word_used[:trips], half_width),
+    )
 
     neg_weight = jnp.einsum("gtj,gjp->gpt", neg_grad, neg_sel, preferred_element_type=jnp.float32)
     pos_weight = jnp.where(
-        ctx_ids.reshape(group_count, 1, block_size)
-        == jnp.arange(part_rows)[None, :, None],
+        ctx_ids.reshape(group_count, 1, block_size) == jnp.arange(part_rows)[None, :, None],
         pos_blocks[:, None, :],
         0.0,
     )
@@ -137,13 +140,7 @@
     ctx_sum = jnp.einsum(
         "gpt,gtd->pd", weight_hi, query_blocks, preferred_element_type=jnp.float32
     ) + jnp.einsum("gpt,gtd->pd", weight_lo, query_blocks, preferred_element_type=jnp.float32)
-
-    query_grads = query_grads.reshape(-1, row_width)
     word_sum = spread_rows(word_sel, conj_product(query_grads, rel_used, half_width))
-    slot_grad = spread_rows(
-        one_hot(slot_ids[:trips], slot_total),
-        conj_product(query_grads[:trips], word_used[:trips], half_width),
-    )
     slot_grad = slot_grad + 0.02 * live_mask[:, None] * own_table.astype(jnp.float32)
     outgoing = slot_grad.reshape(owner_count, slot_count, row_width)
     returned = lax.all_to_all(

time: 60.1 us -> 58.8 us (0.978)
  matrix products: 12.9 us -> 16.6 us
  waiting for transfers between devices: 16.4 us -> 13.3 us
  other arithmetic: 4.02 us -> 2.98 us
  local copies, waits for them, and re-layouts: 11.1 us -> 10.1 us
    all_to_all x1, waiting for transfers between devices: 8.35 us -> 5.11 us  [shards(): lax.all_to_all(picked, both, split_axis=0, concat_axis=0, tiled=True)]
    gather x5 -> x0, local copies, waits for them, and re-layouts: 2.19 us -> none  [the longest x4 1.31 us: shards(): incoming[bucket_of + (requester + j) % split_count]]
    dot_general x1, matrix products: 1.61 us -> 3.68 us  [shards(): jnp.einsum('gtd,gjd->gtj', query_blocks, neg_rows, preferred_element_type...]
    unnamed x15 -> x21, local copies, waits for them, and re-layouts: 2.16 us -> 4.19 us
    dot_general x1, matrix products: 1.09 us -> 2.75 us  [shards(): jnp.einsum('gjp,pd->gjd', neg_sel, held_rows, preferred_element_type=jnp....]
    reshape x3 -> x2, local copies, waits for them, and re-layouts: 2.57 us -> 0.99 us  [the longest x1 0.76 us: shards(): picked = pick_rows(one_hot(served.reshape(-1), owned_rows), relations).as...]
    another operation x2 -> x3, other arithmetic: 1.83 us -> 0.47 us
    all_to_all x4 -> x2, local copies, waits for them, and re-layouts: 2.12 us -> 1.93 us  [shards(): lax.all_to_all(wanted, both, split_axis=0, concat_axis=0, tiled=True)]
  transfers between devices with their start and end apart: 5 -> 5, of which waited for: 3 -> 3; matrix products, arithmetic and copies ran while one was open for 25% -> 23% of each run, Pallas kernels for 0% -> 0%
where the time goes in v4:
time: 58.8 us; the launch traced here: 58.3 us
  matrix products  16.6 us (28%)
  starting transfers between devices  14.3 us (24%)
  waiting for transfers between devices  13.3 us (23%)
  local copies, waits for them, and re-layouts  10.1 us (17%)
  other arithmetic  2.98 us (5%)
  between operations  0.97 us (2%)
    all_to_all x1, starting transfers between devices, shards(): lax.all_to_all(wanted, both, split_axis=0, concat_axis=0, tiled=True)  7.3 us
    all_to_all x1, waiting for transfers between devices, shards(): lax.all_to_all(picked, both, split_axis=0, concat_axis=0, tiled=True)  5.11 us
    all_to_all x1, waiting for transfers between devices, shards(): lax.all_to_all(outgoing.astype(jnp.bfloat16), both, split_axis=0, concat_...  4.71 us
    unnamed x21, local copies, waits for them, and re-layouts  4.19 us
    dot_general x4, matrix products, pick_rows(): return jnp.dot(selector, rows, preferred_element_type=jnp.float32)  3.77 us
    dot_general x1, matrix products, shards(): jnp.einsum('gtd,gjd->gtj', query_blocks, neg_rows, preferred_element_type...  3.68 us
    all_to_all x1, waiting for transfers between devices, shards(): lax.all_to_all(wanted, both, split_axis=0, concat_axis=0, tiled=True)  3.52 us
    dot_general x1, matrix products, shards(): jnp.einsum('gjp,pd->gjd', neg_sel, held_rows, preferred_element_type=jnp....  2.75 us
  transfers between devices with their start and end apart: 5, of which 3 were waited for; matrix products, arithmetic and copies ran while one was open for 23% of the time, Pallas kernels for 0%

profile of v4, /device:TPU:0, one launch (start us, length us, event | category | flops | bytes accessed | tf_op | source)
XLA Modules:
  0.0 58.3 jit_solution(7163922012913178866)
XLA Ops:
  0.6 1.4 %copy.74 = s32[1,1,16,2,2]{4,3,2,1,0:T(2,128)} copy(s32[1,1,16,2,2]{2,4,3,1,0:T(2,128)} %param.16) | data formatting | bytes 512 | tf_op jit(solution)/shard_map/all_to_all | solution.py:83
  2.1 7.3 %all-to-all-start = ((s32[32,1,2]{2,1,0:T(1,128)}), s32[32,1,2]{2,1,0:T(1,128)S(1)}, u32[]{:S(2)}, u32[]{:S(2)}) async-start(s32[32,1,2]{2,1,0:T(1,128)} %bitcast.1), calls=%async_computation | async-start | bytes 32768 | tf_op jit(solution)/shard_map/all_to_all | solution.py:83
  9.4 0.7 %pad_add_fusion.1 = s32[1792]{0:T(1024)S(1)} fusion(s32[1024]{0:T(1024)} %bitcast.75, s32[256]{0:T(256)} %param.14, s32[256]{0:T(256)} %param.13, s32[256]{0:T(256)} %param.12), kind=kLoop, calls=%fused_computation.68 | loop fusion | flops 5376 | bytes 14336 | tf_op jit(solution)/shard_map/concatenate | solution.py:71
  10.1 1.8 %collective-permute-start = (s32[1792]{0:T(1024)S(1)}, s32[1792]{0:T(1024)S(1)}, u32[]{:S(2)}, u32[]{:S(2)}) collective-permute-start(s32[1792]{0:T(1024)S(1)} %pad_add_fusion.1), channel_id=1, source_target_pairs={{0,1},{1,0},{2,3},{3,2},{4,5},{5,4},{6,7},{7,6},{8,9},{9,8},{10,11... | collective-permute-start | bytes 21512 | tf_op jit(solution)/shard_map/ppermute | solution.py:9
  11.9 0.8 %copy.71 = s32[1,1,16,2]{3,2,1,0:T(8,128)S(1)} copy(s32[1,1,16,2]{2,3,1,0:T(2,128)} %param.17) | data formatting | bytes 256 | tf_op args[8]
  13.0 3.5 %all-to-all-done = s32[32,1,2]{2,1,0:T(1,128)S(1)} async-done(((s32[32,1,2]{2,1,0:T(1,128)}), s32[32,1,2]{2,1,0:T(1,128)S(1)}, u32[]{:S(2)}, u32[]{:S(2)}) %all-to-all-start) | async-done | bytes 288 | tf_op jit(solution)/shard_map/all_to_all | solution.py:83
  17.4 1.1 %convolution_convert_fusion.1 = bf16[128,800]{0,1:T(8,128)(2,1)S(1)} fusion(bf16[32,800]{1,0:T(8,128)(2,1)} %param.11, s32[128]{0:T(128)S(1)} %eq.120), kind=kOutput, calls=%fused_computation.17 | convolution fusion | flops 6660096 | bytes 256512 | tf_op jit(solution)/shard_map/dot_general | solution.py:33
  18.6 0.5 broadcast.63
  19.1 0.7 %reduce.3 = s32[32,2]{1,0:T(8,128)S(1)} reduce(s32[32,1,2]{2,1,0:T(1,128)S(1)} %all-to-all-done, s32[]{:T(128)} %broadcast.63), dimensions={1}, to_apply=%all_to_all.13.reduce_sub_computation.3 | reduce | bytes 516 | tf_op jit(solution)/shard_map/all_to_all | solution.py:83
  20.0 0.8 %reshape.106 = bf16[32,4,800]{2,1,0:T(4,128)(2,1)} reshape(bf16[128,800]{1,0:T(8,128)(2,1)S(1)} %copy.63) | data formatting | bytes 409600 | tf_op jit(solution)/shard_map/reshape | solution.py:88
  20.8 2.6 %all-to-all-start.1 = ((bf16[32,4,800]{2,1,0:T(4,128)(2,1)}), bf16[32,4,800]{2,1,0:T(4,128)(2,1)S(1)}, u32[]{:S(2)}, u32[]{:S(2)}) async-start(bf16[32,4,800]{2,1,0:T(4,128)(2,1)} %reshape.106), calls=%async_computation.1 | async-start | bytes 458752 | tf_op jit(solution)/shard_map/all_to_all | solution.py:89
  23.5 1.7 %fusion.14 = f32[512,800]{0,1:T(8,128)} fusion(bf16[256,800]{0,1:T(8,128)(2,1)S(1)} %copy-done, s32[512]{0:T(512)S(1)} %bitcast.66), kind=kOutput, calls=%fused_computation.36 | convolution fusion | flops 209846272 | bytes 2050048 | tf_op jit(solution)/shard_map/dot_general | solution.py:33
  25.2 0.5 fusion.15
  25.7 2.8 %convolution_convert_fusion = bf16[2,1024,800]{1,2,0:T(8,128)(2,1)} fusion(s32[2,1024]{1,0:T(2,128)S(1)} %fusion.35, bf16[256,800]{0,1:T(8,128)(2,1)S(1)} %collective-permute-done.1), kind=kOutput, calls=%fused_computation | convolution fusion | flops 841023488 | bytes 3694592 | tf_op jit(solution)/shard_map/gjp,pd->gjd/dot_general | solution.py:102
  28.5 5.1 %all-to-all-done.1 = bf16[32,4,800]{2,1,0:T(4,128)(2,1)S(1)} async-done(((bf16[32,4,800]{2,1,0:T(4,128)(2,1)}), bf16[32,4,800]{2,1,0:T(4,128)(2,1)S(1)}, u32[]{:S(2)}, u32[]{:S(2)}) %all-to-all-start.1) | async-done | bytes 204832 | tf_op jit(solution)/shard_map/all_to_all | solution.py:89
  34.4 0.5 fusion.23
  34.9 0.9 %copy-done.6 = f32[512,800]{0,1:T(8,128)S(1)} copy-done((f32[512,800]{0,1:T(8,128)S(1)}, f32[512,800]{0,1:T(8,128)}, u32[]{:S(2)}) %copy-start.6) | copy-done | bytes 1638424
  35.8 0.5 add_convert_fusion
  36.2 0.8 %copy-done.1 = f32[512,800]{0,1:T(8,128)} copy-done((f32[512,800]{0,1:T(8,128)}, f32[512,800]{0,1:T(8,128)S(1)}, u32[]{:S(2)}) %copy-start.1) | copy-done | bytes 1638424
  37.4 3.7 %multiply_convert_fusion = bf16[2,256,1024]{2,1,0:T(8,128)(2,1)S(1)} fusion(bf16[2,256,800]{1,2,0:T(8,128)(2,1)S(1)} %bitcast_dynamic-update-slice_fusion, bf16[2,1024,800]{1,2,0:T(8,128)(2,1)} %convolution_convert_fusion), kind=kOutput, calls=%fused_computation.1 | convolution fusion | flops 841482240 | bytes 5144576 | tf_op jit(solution)/shard_map/gtd,gjd->gtj/dot_general | solution.py:119
  41.1 0.6 fusion.6
  41.7 1.1 %fusion.1 = f32[2,256,800]{1,2,0:T(8,128)S(1)} fusion(f32[100,2,8,256]{3,2,1,0:T(8,128)S(1)} %bitcast.57, bf16[2,256,1024]{2,1,0:T(8,128)(2,1)S(1)} %multiply_convert_fusion, bf16[2,1024,800]{1,2,0:T(8,128)(2,1)S(1)} %copy-done.3, f32[2,256]{1,0:T(2,128)S(1)} %neg.20), kind=kOutput, calls=%fused_computation.5 | convolution fusion | flops 839680000 | bytes 7604224 | tf_op jit(solution)/shard_map/gtj,gjd->gtd/dot_general | solution.py:126
  43.2 1.2 %fusion.5 = bf16[256,800]{0,1:T(8,128)(2,1)} fusion(f32[256,800]{0,1:T(8,128)S(1)} %convolution_bitcast_fusion, bf16[2,256,800]{1,2,0:T(8,128)(2,1)S(1)} %bitcast_dynamic-update-slice_fusion, f32[2,256,256]{2,1,0:T(8,128)S(1)} %fusion.6), kind=kOutput, calls=%fused_computation.15 | convolution fusion | flops 210255872 | bytes 2572288 | tf_op jit(solution)/shard_map/gpt,gtd->pd/dot_general | solution.py:140
  44.4 0.5 copy-done.7
  45.8 0.7 %convert_element_type.87 = bf16[32,2,800]{2,1,0:T(2,128)(2,1)} reshape(bf16[64,800]{1,0:T(8,128)(2,1)S(1)} %fusion.8) | data formatting | bytes 204800 | tf_op jit(solution)/shard_map/convert_element_type | solution.py:147
  46.5 2.6 %all-to-all-start.2 = ((bf16[32,2,800]{2,1,0:T(2,128)(2,1)}), bf16[32,2,800]{2,1,0:T(2,128)(2,1)S(1)}, u32[]{:S(2)}, u32[]{:S(2)}) async-start(bf16[32,2,800]{2,1,0:T(2,128)(2,1)} %convert_element_type.87), calls=%async_computation.2 | async-start | bytes 229376 | tf_op jit(solution)/shard_map/all_to_all | solution.py:146
  49.3 1.2 %copy-done.2 = f32[512,800]{0,1:T(8,128)S(1)} copy-done((f32[512,800]{0,1:T(8,128)S(1)}, f32[512,800]{0,1:T(8,128)}, u32[]{:S(2)}) %copy-start.2) | copy-done | bytes 1638424
  50.5 0.4 multiply_add_fusion
  50.9 0.5 fusion.11
  51.4 1.3 %fusion.4 = bf16[256,800]{0,1:T(8,128)(2,1)} fusion(f32[256,800]{0,1:T(8,128)S(1)} %fusion.11, f32[512,400]{0,1:T(8,128)S(1)} %get-tuple-element.12, f32[512,400]{0,1:T(8,128)S(1)} %get-tuple-element.11, s32[512]{0:T(512)S(1)} %bitcast.68), kind=kOutput, calls=%fused_computation.14 | convolution fusion | flops 212303872 | bytes 2869248 | tf_op jit(solution)/shard_map/dot_general | solution.py:47
  52.7 4.7 %all-to-all-done.2 = bf16[32,2,800]{2,1,0:T(2,128)(2,1)S(1)} async-done(((bf16[32,2,800]{2,1,0:T(2,128)(2,1)}), bf16[32,2,800]{2,1,0:T(2,128)(2,1)S(1)}, u32[]{:S(2)}, u32[]{:S(2)}) %all-to-all-start.2) | async-done | bytes 102432 | tf_op jit(solution)/shard_map/all_to_all | solution.py:146
  57.5 0.8 %fusion.33 = f32[32,800]{1,0:T(8,128)} fusion(bf16[64,800]{1,0:T(8,128)(2,1)S(1)} %reshape.111, s32[64]{0:T(128)S(1)} %eq.138), kind=kOutput, calls=%fused_computation.63 | convolution fusion | flops 3278848 | bytes 205056 | tf_op jit(solution)/shard_map/dot_general | solution.py:152
  (56 shorter events, 4.4 us)
Async XLA Ops:
  0.6 22.9 %copy-start = (bf16[256,800]{0,1:T(8,128)(2,1)S(1)}, bf16[256,800]{0,1:T(8,128)(2,1)}, u32[]{:S(2)}) copy-start(bf16[256,800]{0,1:T(8,128)(2,1)} %param.9) | copy-start | bytes 1228804
  2.1 14.4 %all-to-all-start = ((s32[32,1,2]{2,1,0:T(1,128)}), s32[32,1,2]{2,1,0:T(1,128)S(1)}, u32[]{:S(2)}, u32[]{:S(2)}) async-start(s32[32,1,2]{2,1,0:T(1,128)} %bitcast.1), calls=%async_computation | async-start | bytes 32768 | tf_op jit(solution)/shard_map/all_to_all | solution.py:83
  10.1 13.3 %collective-permute-start = (s32[1792]{0:T(1024)S(1)}, s32[1792]{0:T(1024)S(1)}, u32[]{:S(2)}, u32[]{:S(2)}) collective-permute-start(s32[1792]{0:T(1024)S(1)} %pad_add_fusion.1), channel_id=1, source_target_pairs={{0,1},{1,0},{2,3},{3,2},{4,5},{5,4},{6,7},{7,6},{8,9},{9,8},{10,11... | collective-permute-start | bytes 21512 | tf_op jit(solution)/shard_map/ppermute | solution.py:9
  11.9 13.3 %collective-permute-start.1 = (bf16[256,800]{0,1:T(8,128)(2,1)}, bf16[256,800]{0,1:T(8,128)(2,1)S(1)}, u32[]{:S(2)}, u32[]{:S(2)}) collective-permute-start(bf16[256,800]{0,1:T(8,128)(2,1)} %param.10), channel_id=1, source_target_pairs={{0,2},{2,4},{4,6},{6,8},{8,10},{10,12},{12,14},{14,16},{16,18},{18... | collective-permute-start | bytes 1228808 | tf_op jit(solution)/shard_map/ppermute | solution.py:9
  20.8 12.8 %all-to-all-start.1 = ((bf16[32,4,800]{2,1,0:T(4,128)(2,1)}), bf16[32,4,800]{2,1,0:T(4,128)(2,1)S(1)}, u32[]{:S(2)}, u32[]{:S(2)}) async-start(bf16[32,4,800]{2,1,0:T(4,128)(2,1)} %reshape.106), calls=%async_computation.1 | async-start | bytes 458752 | tf_op jit(solution)/shard_map/all_to_all | solution.py:89
  34.3 1.4 %copy-start.6 = (f32[512,800]{0,1:T(8,128)S(1)}, f32[512,800]{0,1:T(8,128)}, u32[]{:S(2)}) copy-start(f32[512,800]{0,1:T(8,128)} %fusion.14) | copy-start | bytes 4915204
  35.8 1.2 %copy-start.1 = (f32[512,800]{0,1:T(8,128)}, f32[512,800]{0,1:T(8,128)S(1)}, u32[]{:S(2)}) copy-start(f32[512,800]{0,1:T(8,128)S(1)} %fusion.23) | copy-start | bytes 4915204
  37.4 4.3 %copy-start.3 = (bf16[2,1024,800]{1,2,0:T(8,128)(2,1)S(1)}, bf16[2,1024,800]{1,2,0:T(8,128)(2,1)}, u32[]{:S(2)}) copy-start(bf16[2,1024,800]{1,2,0:T(8,128)(2,1)} %convolution_convert_fusion) | copy-start | bytes 9830404
  42.8 1.6 %copy-start.4 = (f32[2,256,800]{1,2,0:T(8,128)}, f32[2,256,800]{1,2,0:T(8,128)S(1)}, u32[]{:S(2)}) copy-start(f32[2,256,800]{1,2,0:T(8,128)S(1)} %fusion.1) | copy-start | bytes 4915204
  43.2 1.7 %copy-start.7 = (f32[512,800]{0,1:T(8,128)S(1)}, f32[512,800]{0,1:T(8,128)}, u32[]{:S(2)}) copy-start(f32[512,800]{0,1:T(8,128)} %fusion.14) | copy-start | bytes 4915204
  45.1 4.0 %copy-start.5 = (f32[2,256,800]{1,2,0:T(8,128)S(1)}, f32[2,256,800]{1,2,0:T(8,128)}, u32[]{:S(2)}) copy-start(f32[2,256,800]{1,2,0:T(8,128)} %copy-done.4) | copy-start | bytes 4915204
  46.5 10.9 %all-to-all-start.2 = ((bf16[32,2,800]{2,1,0:T(2,128)(2,1)}), bf16[32,2,800]{2,1,0:T(2,128)(2,1)S(1)}, u32[]{:S(2)}, u32[]{:S(2)}) async-start(bf16[32,2,800]{2,1,0:T(2,128)(2,1)} %convert_element_type.87), calls=%async_computation.2 | async-start | bytes 229376 | tf_op jit(solution)/shard_map/all_to_all | solution.py:146
  49.1 1.4 %copy-start.2 = (f32[512,800]{0,1:T(8,128)S(1)}, f32[512,800]{0,1:T(8,128)}, u32[]{:S(2)}) copy-start(f32[512,800]{0,1:T(8,128)} %copy-done.1) | copy-start | bytes 4915204

commit v5 on v4

--- a/solution.py
+++ b/solution.py
@@ -112,23 +112,36 @@
     )
     own_table = slot_table[:slot_total]
     rel_used = pick_rows(one_hot(slot_ids, split_count * slot_total), slot_table)
-    query = complex_product(word_used, rel_used, half_width).astype(jnp.bfloat16)
-    positive = jnp.sum(query.astype(jnp.float32) * ctx_used, axis=1)
-    pos_grad = -jax.nn.sigmoid(-positive)
-    query_blocks = query.reshape(group_count, block_size, row_width)
-    scores = jnp.einsum(
-        "gtd,gjd->gtj", query_blocks, neg_rows, preferred_element_type=jnp.float32
-    )
-    neg_grad = (jax.nn.sigmoid(scores) * neg_scale).astype(jnp.bfloat16)
-    pos_blocks = pos_grad.reshape(group_count, block_size)
-    query_grads = (
-        pos_blocks[:, :, None] * ctx_used.reshape(group_count, block_size, row_width)
-        + jnp.einsum("gtj,gjd->gtd", neg_grad, neg_rows, preferred_element_type=jnp.float32)
-    ).reshape(-1, row_width)
+    word_blocks = word_used.reshape(group_count, block_size, row_width)
+    ctx_blocks = ctx_used.reshape(group_count, block_size, row_width)
+    rel_blocks = rel_used.reshape(group_count, block_size, row_width)
+
+    def block_chain(group):
+        query = complex_product(word_blocks[group], rel_blocks[group], half_width).astype(
+            jnp.bfloat16
+        )
+        positive = jnp.sum(query.astype(jnp.float32) * ctx_blocks[group], axis=1)
+        pos_grad = -jax.nn.sigmoid(-positive)
+        scores = lax.dot_general(
+            query, neg_rows[group], (((1,), (1,)), ((), ())), preferred_element_type=jnp.float32
+        )
+        neg_grad = (jax.nn.sigmoid(scores) * neg_scale).astype(jnp.bfloat16)
+        query_grad = pos_grad[:, None] * ctx_blocks[group] + jnp.dot(
+            neg_grad, neg_rows[group], preferred_element_type=jnp.float32
+        )
+        return query, pos_grad, neg_grad, query_grad
+
+    chains = [block_chain(group) for group in range(block_count)]
+    own_grads = jnp.concatenate([chain[3] for chain in chains])
     slot_grad = spread_rows(
         one_hot(slot_ids[:trips], slot_total),
-        conj_product(query_grads[:trips], word_used[:trips], half_width),
+        conj_product(own_grads, word_used[:trips], half_width),
     )
+    chains += [block_chain(group) for group in range(block_count, group_count)]
+    query_blocks = jnp.stack([chain[0] for chain in chains])
+    pos_blocks = jnp.stack([chain[1] for chain in chains])
+    neg_grad = jnp.stack([chain[2] for chain in chains])
+    query_grads = jnp.concatenate([chain[3] for chain in chains])
 
     neg_weight = jnp.einsum("gtj,gjp->gpt", neg_grad, neg_sel, preferred_element_type=jnp.float32)
     pos_weight = jnp.where(

time: 58.8 us -> 58.7 us (level)
  waiting for transfers between devices: 13.3 us -> 8.64 us
  matrix products: 16.6 us -> 19.4 us
  other arithmetic: 2.98 us -> 4.18 us
    all_to_all x1, waiting for transfers between devices: 4.71 us -> 0.94 us  [shards(): lax.all_to_all(outgoing.astype(jnp.bfloat16), both, split_axis=0, concat_...]
    all_to_all x1, waiting for transfers between devices: 5.11 us -> 2.12 us  [shards(): lax.all_to_all(picked, both, split_axis=0, concat_axis=0, tiled=True)]
    all_to_all x1, starting transfers between devices: 7.3 us -> 5.2 us  [shards(): lax.all_to_all(wanted, both, split_axis=0, concat_axis=0, tiled=True)]
    all_to_all x1, waiting for transfers between devices: 3.52 us -> 5.58 us  [shards(): lax.all_to_all(wanted, both, split_axis=0, concat_axis=0, tiled=True)]
    another operation x1 -> x2, other arithmetic: 0.46 us -> 1.79 us
    dot_general x4, matrix products: 3.77 us -> 5 us  [pick_rows(): return jnp.dot(selector, rows, preferred_element_type=jnp.float32)]
    ppermute x2, starting transfers between devices: 1.82 us -> 2.99 us  [passed_along(): lax.ppermute(shard, axis, [(i, (i + by) % length) for i in range(length)])]
    all_to_all x1, starting transfers between devices: 2.57 us -> 3.71 us  [shards(): lax.all_to_all(outgoing.astype(jnp.bfloat16), both, split_axis=0, concat_...]
  transfers between devices with their start and end apart: 5 -> 5, of which waited for: 3 -> 3; matrix products, arithmetic and copies ran while one was open for 23% -> 35% of each run, Pallas kernels for 0% -> 0%
where the time goes in v5:
time: 58.7 us; the launch traced here: 58.3 us
  matrix products  19.4 us (33%)
  starting transfers between devices  14.5 us (25%)
  local copies, waits for them, and re-layouts  10.6 us (18%)
  waiting for transfers between devices  8.64 us (15%)
  other arithmetic  4.18 us (7%)
  between operations  1.03 us (2%)
    all_to_all x1, waiting for transfers between devices, shards(): lax.all_to_all(wanted, both, split_axis=0, concat_axis=0, tiled=True)  5.58 us
    all_to_all x1, starting transfers between devices, shards(): lax.all_to_all(wanted, both, split_axis=0, concat_axis=0, tiled=True)  5.2 us
    dot_general x4, matrix products, pick_rows(): return jnp.dot(selector, rows, preferred_element_type=jnp.float32)  5 us
    unnamed x40, local copies, waits for them, and re-layouts  4.03 us
    all_to_all x1, starting transfers between devices, shards(): lax.all_to_all(outgoing.astype(jnp.bfloat16), both, split_axis=0, concat_...  3.71 us
    dot_general x2, matrix products, block_chain(): jnp.dot(neg_grad, neg_rows[group], preferred_element_type=jnp.float32)  3.15 us
    ppermute x2, starting transfers between devices, passed_along(): lax.ppermute(shard, axis, [(i, (i + by) % length) for i in range(length)])  2.99 us
    dot_general x1, matrix products, shards(): jnp.einsum('gjp,pd->gjd', neg_sel, held_rows, preferred_element_type=jnp....  2.74 us
  transfers between devices with their start and end apart: 5, of which 3 were waited for; matrix products, arithmetic and copies ran while one was open for 35% of the time, Pallas kernels for 0%

profile of v5, /device:TPU:0, one launch (start us, length us, event | category | flops | bytes accessed | tf_op | source)
XLA Modules:
  0.0 58.3 jit_solution(12353962072040944157)
XLA Ops:
  0.6 0.8 %pad_add_fusion.1 = s32[1792]{0:T(1024)S(1)} fusion(s32[1024]{0:T(1024)} %bitcast.104, s32[256]{0:T(256)} %param.14, s32[256]{0:T(256)} %param.13, s32[256]{0:T(256)} %param.12), kind=kLoop, calls=%fused_computation.101 | loop fusion | flops 5376 | bytes 14336 | tf_op jit(solution)/shard_map/concatenate | solution.py:71
  1.4 3.0 %collective-permute-start = (s32[1792]{0:T(1024)S(1)}, s32[1792]{0:T(1024)S(1)}, u32[]{:S(2)}, u32[]{:S(2)}) collective-permute-start(s32[1792]{0:T(1024)S(1)} %pad_add_fusion.1), channel_id=1, source_target_pairs={{0,1},{1,0},{2,3},{3,2},{4,5},{5,4},{6,7},{7,6},{8,9},{9,8},{10,11... | collective-permute-start | bytes 21512 | tf_op jit(solution)/shard_map/ppermute | solution.py:9
  4.4 1.4 %copy.60 = s32[1,1,16,2,2]{4,3,2,1,0:T(2,128)} copy(s32[1,1,16,2,2]{2,4,3,1,0:T(2,128)} %param.16) | data formatting | bytes 512 | tf_op jit(solution)/shard_map/all_to_all | solution.py:83
  5.8 5.2 %all-to-all-start = ((s32[32,1,2]{2,1,0:T(1,128)}), s32[32,1,2]{2,1,0:T(1,128)S(1)}, u32[]{:S(2)}, u32[]{:S(2)}) async-start(s32[32,1,2]{2,1,0:T(1,128)} %bitcast.1), calls=%async_computation | async-start | bytes 32768 | tf_op jit(solution)/shard_map/all_to_all | solution.py:83
  11.0 0.8 %copy.57 = s32[1,1,16,2]{3,2,1,0:T(8,128)S(1)} copy(s32[1,1,16,2]{2,3,1,0:T(2,128)} %param.17) | data formatting | bytes 256 | tf_op args[8]
  11.9 0.6 %mul.128 = f32[64]{0:T(128)} reshape(f32[32,2]{1,0:T(8,128)S(1)} %fusion.91) | data formatting | bytes 512 | tf_op jit(solution)/shard_map/mul | solution.py:157
  12.6 5.6 %all-to-all-done = s32[32,1,2]{2,1,0:T(1,128)S(1)} async-done(((s32[32,1,2]{2,1,0:T(1,128)}), s32[32,1,2]{2,1,0:T(1,128)S(1)}, u32[]{:S(2)}, u32[]{:S(2)}) %all-to-all-start) | async-done | bytes 288 | tf_op jit(solution)/shard_map/all_to_all | solution.py:83
  19.1 1.1 %convolution_convert_fusion.1 = bf16[128,800]{0,1:T(8,128)(2,1)S(1)} fusion(bf16[32,800]{1,0:T(8,128)(2,1)} %param.11, s32[128]{0:T(128)S(1)} %eq.120), kind=kOutput, calls=%fused_computation.41 | convolution fusion | flops 6660096 | bytes 256512 | tf_op jit(solution)/shard_map/dot_general | solution.py:33
  20.4 0.8 %reshape.206 = bf16[32,4,800]{2,1,0:T(4,128)(2,1)} reshape(bf16[128,800]{1,0:T(8,128)(2,1)S(1)} %copy.53) | data formatting | bytes 409600 | tf_op jit(solution)/shard_map/reshape | solution.py:88
  21.1 2.6 %all-to-all-start.1 = ((bf16[32,4,800]{2,1,0:T(4,128)(2,1)}), bf16[32,4,800]{2,1,0:T(4,128)(2,1)S(1)}, u32[]{:S(2)}, u32[]{:S(2)}) async-start(bf16[32,4,800]{2,1,0:T(4,128)(2,1)} %reshape.206), calls=%async_computation.1 | async-start | bytes 458752 | tf_op jit(solution)/shard_map/all_to_all | solution.py:89
  24.2 0.7 %reduce.3 = s32[32,2]{1,0:T(8,128)S(1)} reduce(s32[32,1,2]{2,1,0:T(1,128)S(1)} %all-to-all-done, s32[]{:T(128)} %broadcast.102), dimensions={1}, to_apply=%all_to_all.13.reduce_sub_computation.3 | reduce | bytes 516 | tf_op jit(solution)/shard_map/all_to_all | solution.py:83
  24.9 0.6 %eq.138 = s32[64]{0:T(128)} reshape(s32[32,2]{1,0:T(8,128)S(1)} %reduce.3) | data formatting | bytes 512 | tf_op jit(solution)/shard_map/eq | solution.py:162
  25.6 1.7 %fusion.71 = f32[512,800]{0,1:T(8,128)} fusion(bf16[256,800]{0,1:T(8,128)(2,1)S(1)} %copy-done, s32[512]{0:T(512)S(1)} %bitcast.95), kind=kOutput, calls=%fused_computation.65 | convolution fusion | flops 209846272 | bytes 2050048 | tf_op jit(solution)/shard_map/dot_general | solution.py:33
  27.4 1.7 %fusion.72 = f32[512,800]{0,1:T(8,128)} fusion(bf16[256,800]{0,1:T(8,128)(2,1)S(1)} %collective-permute-done.1, s32[512]{0:T(512)S(1)} %bitcast.101), kind=kOutput, calls=%fused_computation.66 | convolution fusion | flops 209846272 | bytes 2050048 | tf_op jit(solution)/shard_map/dot_general | solution.py:33
  29.0 2.7 %convolution_convert_fusion = bf16[2,1024,800]{1,2,0:T(8,128)(2,1)} fusion(s32[2,1024]{1,0:T(2,128)S(1)} %fusion.92, bf16[256,800]{0,1:T(8,128)(2,1)S(1)} %collective-permute-done.1), kind=kOutput, calls=%fused_computation | convolution fusion | flops 841023488 | bytes 3694592 | tf_op jit(solution)/shard_map/gjp,pd->gjd/dot_general | solution.py:102
  31.8 2.1 %all-to-all-done.1 = bf16[32,4,800]{2,1,0:T(4,128)(2,1)S(1)} async-done(((bf16[32,4,800]{2,1,0:T(4,128)(2,1)}), bf16[32,4,800]{2,1,0:T(4,128)(2,1)S(1)}, u32[]{:S(2)}, u32[]{:S(2)}) %all-to-all-start.1) | async-done | bytes 204832 | tf_op jit(solution)/shard_map/all_to_all | solution.py:89
  34.8 1.8 %subtract_convert_fusion.6 = (bf16[256,400]{0,1:T(8,128)(2,1)S(1)}, bf16[256,400]{0,1:T(8,128)(2,1)S(1)}, bf16[256,400]{0,1:T(8,128)(2,1)S(1)}, bf16[256,400]{0,1:T(8,128)(2,1)S(1)}) fusion(f32[512,800]{0,1:T(8,128)S(1)} %fusion.80, f32[512,800]{0,1:T(8,128)} %fusion.71), kind=kLoop, calls=%fused_computation.76 | loop fusion | flops 1638400 | bytes 4096000 | tf_op jit(solution)/shard_map/convert.11
  36.6 0.6 %copy-done.5 = bf16[2,1024,800]{1,2,0:T(8,128)(2,1)S(1)} copy-done((bf16[2,1024,800]{1,2,0:T(8,128)(2,1)S(1)}, bf16[2,1024,800]{1,2,0:T(8,128)(2,1)}, u32[]{:S(2)}) %copy-start.5) | copy-done | bytes 3276824
  37.2 0.9 %fusion.53 = bf16[256,1024]{1,0:T(8,128)(2,1)S(1)} fusion(bf16[2,1024,800]{1,2,0:T(8,128)(2,1)S(1)} %copy-done.5, bf16[256,400]{0,1:T(8,128)(2,1)S(1)} %get-tuple-element.18, bf16[256,400]{0,1:T(8,128)(2,1)S(1)} %get-tuple-element.15), kind=kOutput, calls=%fused_computation.36 | convolution fusion | flops 421560320 | bytes 2572288 | tf_op jit(solution)/shard_map/dot_general | solution.py:125
  38.1 1.7 %fusion.44 = bf16[256,1024]{1,0:T(8,128)(2,1)} fusion(bf16[2,1024,800]{1,2,0:T(8,128)(2,1)S(1)} %copy-done.5, bf16[256,400]{0,1:T(8,128)(2,1)S(1)} %get-tuple-element.17, bf16[256,400]{0,1:T(8,128)(2,1)S(1)} %get-tuple-element.16), kind=kOutput, calls=%fused_computation.33 | convolution fusion | flops 421560320 | bytes 2572288 | tf_op jit(solution)/shard_map/dot_general | solution.py:125
  40.6 0.6 %fusion.32 = f32[256,800]{0,1:T(8,128)S(1)} fusion(bf16[256,1024]{1,0:T(8,128)(2,1)S(1)} %fusion.53, bf16[2,1024,800]{1,2,0:T(8,128)(2,1)S(1)} %copy-done.5, f32[512,800]{0,1:T(8,128)S(1)} %copy-done.2, f32[256]{0:T(256)S(1)} %get-tuple-element.27), kind=kOutput, calls=%fused_computation.29 | convolution fusion | flops 419840000 | bytes 3802112 | tf_op jit(solution)/shard_map/dot_general | solution.py:129
  41.3 0.8 %copy-done.1 = f32[512,800]{0,1:T(8,128)S(1)} copy-done((f32[512,800]{0,1:T(8,128)S(1)}, f32[512,800]{0,1:T(8,128)}, u32[]{:S(2)}) %copy-start.1) | copy-done | bytes 1638424
  42.2 0.8 %copy-done.3 = f32[256,800]{0,1:T(8,128)} copy-done((f32[256,800]{0,1:T(8,128)}, f32[256,800]{0,1:T(8,128)S(1)}, u32[]{:S(2)}) %copy-start.3) | copy-done | bytes 819224
  43.7 0.9 %fusion.61 = bf16[64,800]{1,0:T(8,128)(2,1)S(1)} fusion(f32[64,800]{1,0:T(8,128)S(1)} %fusion.73, f32[256,400]{0,1:T(8,128)S(1)} %get-tuple-element.20, f32[256,400]{0,1:T(8,128)S(1)} %get-tuple-element.19, f32[64,800]{1,0:T(8,128)S(1)} %reshape.210, f32[64]{0:T(128)} %mul.128, s32[256]{0:T(256)S(1)} %bitcast.100), kind=kOutput, calls=%fused_computation.44 | convolution fusion | flops 27475968 | bytes 1332480 | tf_op jit(solution)/shard_map/dot_general | solution.py:47
  44.6 0.7 %convert_element_type.109 = bf16[32,2,800]{2,1,0:T(2,128)(2,1)} reshape(bf16[64,800]{1,0:T(8,128)(2,1)S(1)} %fusion.61) | data formatting | bytes 204800 | tf_op jit(solution)/shard_map/convert_element_type | solution.py:160
  45.3 3.7 %all-to-all-start.2 = ((bf16[32,2,800]{2,1,0:T(2,128)(2,1)}), bf16[32,2,800]{2,1,0:T(2,128)(2,1)S(1)}, u32[]{:S(2)}, u32[]{:S(2)}) async-start(bf16[32,2,800]{2,1,0:T(2,128)(2,1)} %convert_element_type.109), calls=%async_computation.2 | async-start | bytes 229376 | tf_op jit(solution)/shard_map/all_to_all | solution.py:159
  49.1 2.5 %fusion.35 = f32[256,800]{0,1:T(8,128)S(1)} fusion(bf16[256,1024]{1,0:T(8,128)(2,1)} %fusion.44, bf16[2,1024,800]{1,2,0:T(8,128)(2,1)} %convolution_convert_fusion, f32[512,800]{0,1:T(8,128)} %fusion.72, f32[256]{0:T(256)S(1)} %get-tuple-element.26), kind=kOutput, calls=%fused_computation.30 | convolution fusion | flops 419840000 | bytes 3802112 | tf_op jit(solution)/shard_map/dot_general | solution.py:129
  51.7 0.5 fusion.59
  53.2 1.2 %fusion.58 = bf16[256,800]{0,1:T(8,128)(2,1)} fusion(f32[256,800]{0,1:T(8,128)S(1)} %convolution_bitcast_fusion, bf16[1,256,400]{1,2,0:T(8,128)(2,1)S(1)} %bitcast.90, bf16[1,256,400]{1,2,0:T(8,128)(2,1)S(1)} %bitcast.88, bf16[1,256,400]{1,2,0:T(8,128)(2,1)S(1)} %bitcast.92, bf16[1,256,400]{1,2,0:T(8,128)(2,1)S(1)} %bitcast.86, f32[2,256,256]{2,1,0:T(8,128)S(1)} %fusion.59), kind=kOutput, calls=%fused_computation.39 | convolution fusion | flops 213532672 | bytes 2572288 | tf_op jit(solution)/shard_map/gpt,gtd->pd/dot_general | solution.py:153
  55.2 1.3 %fusion.57 = bf16[256,800]{0,1:T(8,128)(2,1)} fusion(f32[256,800]{0,1:T(8,128)S(1)} %fusion.67, f32[512,400]{0,1:T(8,128)S(1)} %get-tuple-element.14, f32[512,400]{0,1:T(8,128)S(1)} %get-tuple-element.13, s32[512]{0:T(512)S(1)} %bitcast.97), kind=kOutput, calls=%fused_computation.38 | convolution fusion | flops 212303872 | bytes 2869248 | tf_op jit(solution)/shard_map/dot_general | solution.py:47
  56.5 0.9 %all-to-all-done.2 = bf16[32,2,800]{2,1,0:T(2,128)(2,1)S(1)} async-done(((bf16[32,2,800]{2,1,0:T(2,128)(2,1)}), bf16[32,2,800]{2,1,0:T(2,128)(2,1)S(1)}, u32[]{:S(2)}, u32[]{:S(2)}) %all-to-all-start.2) | async-done | bytes 102432 | tf_op jit(solution)/shard_map/all_to_all | solution.py:159
  57.5 0.8 %fusion.90 = f32[32,800]{1,0:T(8,128)} fusion(bf16[64,800]{1,0:T(8,128)(2,1)S(1)} %reshape.209, s32[64]{0:T(128)S(1)} %copy-done.14), kind=kOutput, calls=%fused_computation.96 | convolution fusion | flops 3278848 | bytes 205056 | tf_op jit(solution)/shard_map/dot_general | solution.py:165
  (74 shorter events, 6.3 us)
Async XLA Ops:
  0.6 25.0 %copy-start = (bf16[256,800]{0,1:T(8,128)(2,1)S(1)}, bf16[256,800]{0,1:T(8,128)(2,1)}, u32[]{:S(2)}) copy-start(bf16[256,800]{0,1:T(8,128)(2,1)} %param.9) | copy-start | bytes 1228804
  1.4 24.1 %collective-permute-start = (s32[1792]{0:T(1024)S(1)}, s32[1792]{0:T(1024)S(1)}, u32[]{:S(2)}, u32[]{:S(2)}) collective-permute-start(s32[1792]{0:T(1024)S(1)} %pad_add_fusion.1), channel_id=1, source_target_pairs={{0,1},{1,0},{2,3},{3,2},{4,5},{5,4},{6,7},{7,6},{8,9},{9,8},{10,11... | collective-permute-start | bytes 21512 | tf_op jit(solution)/shard_map/ppermute | solution.py:9
  4.4 22.9 %collective-permute-start.1 = (bf16[256,800]{0,1:T(8,128)(2,1)}, bf16[256,800]{0,1:T(8,128)(2,1)S(1)}, u32[]{:S(2)}, u32[]{:S(2)}) collective-permute-start(bf16[256,800]{0,1:T(8,128)(2,1)} %param.10), channel_id=1, source_target_pairs={{0,2},{2,4},{4,6},{6,8},{8,10},{10,12},{12,14},{14,16},{16,18},{18... | collective-permute-start | bytes 1228808 | tf_op jit(solution)/shard_map/ppermute | solution.py:9
  5.8 12.3 %all-to-all-start = ((s32[32,1,2]{2,1,0:T(1,128)}), s32[32,1,2]{2,1,0:T(1,128)S(1)}, u32[]{:S(2)}, u32[]{:S(2)}) async-start(s32[32,1,2]{2,1,0:T(1,128)} %bitcast.1), calls=%async_computation | async-start | bytes 32768 | tf_op jit(solution)/shard_map/all_to_all | solution.py:83
  21.1 12.8 %all-to-all-start.1 = ((bf16[32,4,800]{2,1,0:T(4,128)(2,1)}), bf16[32,4,800]{2,1,0:T(4,128)(2,1)S(1)}, u32[]{:S(2)}, u32[]{:S(2)}) async-start(bf16[32,4,800]{2,1,0:T(4,128)(2,1)} %reshape.206), calls=%async_computation.1 | async-start | bytes 458752 | tf_op jit(solution)/shard_map/all_to_all | solution.py:89
  34.8 2.4 %copy-start.5 = (bf16[2,1024,800]{1,2,0:T(8,128)(2,1)S(1)}, bf16[2,1024,800]{1,2,0:T(8,128)(2,1)}, u32[]{:S(2)}) copy-start(bf16[2,1024,800]{1,2,0:T(8,128)(2,1)} %convolution_convert_fusion) | copy-start | bytes 9830404
  36.6 3.2 %copy-start.6 = (bf16[256,400]{0,1:T(8,128)(2,1)}, bf16[256,400]{0,1:T(8,128)(2,1)S(1)}, u32[]{:S(2)}) copy-start(bf16[256,400]{0,1:T(8,128)(2,1)S(1)} %get-tuple-element.16) | copy-start | bytes 614404
  36.6 3.2 %copy-start.8 = (bf16[256,400]{0,1:T(8,128)(2,1)}, bf16[256,400]{0,1:T(8,128)(2,1)S(1)}, u32[]{:S(2)}) copy-start(bf16[256,400]{0,1:T(8,128)(2,1)S(1)} %get-tuple-element.17) | copy-start | bytes 614404
  36.6 3.2 %copy-start.10 = (bf16[256,400]{0,1:T(8,128)(2,1)}, bf16[256,400]{0,1:T(8,128)(2,1)S(1)}, u32[]{:S(2)}) copy-start(bf16[256,400]{0,1:T(8,128)(2,1)S(1)} %get-tuple-element.18) | copy-start | bytes 614404
  38.1 2.0 %copy-start.15 = (bf16[256,1024]{1,0:T(8,128)(2,1)}, bf16[256,1024]{1,0:T(8,128)(2,1)S(1)}, u32[]{:S(2)}) copy-start(bf16[256,1024]{1,0:T(8,128)(2,1)S(1)} %fusion.53) | copy-start | bytes 1572868
  38.1 1.7 %copy-start.2 = (f32[512,800]{0,1:T(8,128)S(1)}, f32[512,800]{0,1:T(8,128)}, u32[]{:S(2)}) copy-start(f32[512,800]{0,1:T(8,128)} %fusion.72) | copy-start | bytes 4915204
  40.1 0.5 copy-start.12
  40.6 1.4 %copy-start.1 = (f32[512,800]{0,1:T(8,128)S(1)}, f32[512,800]{0,1:T(8,128)}, u32[]{:S(2)}) copy-start(f32[512,800]{0,1:T(8,128)} %fusion.71) | copy-start | bytes 4915204
  42.1 0.9 %copy-start.3 = (f32[256,800]{0,1:T(8,128)}, f32[256,800]{0,1:T(8,128)S(1)}, u32[]{:S(2)}) copy-start(f32[256,800]{0,1:T(8,128)S(1)} %fusion.32) | copy-start | bytes 2457604
  45.3 12.1 %all-to-all-start.2 = ((bf16[32,2,800]{2,1,0:T(2,128)(2,1)}), bf16[32,2,800]{2,1,0:T(2,128)(2,1)S(1)}, u32[]{:S(2)}, u32[]{:S(2)}) async-start(bf16[32,2,800]{2,1,0:T(2,128)(2,1)} %convert_element_type.109), calls=%async_computation.2 | async-start | bytes 229376 | tf_op jit(solution)/shard_map/all_to_all | solution.py:159
  49.0 2.6 %copy-start.13 = (f32[256]{0:T(256)S(1)}, f32[256]{0:T(256)}, u32[]{:S(2)}) copy-start(f32[256]{0:T(256)} %copy-done.12) | copy-start | bytes 3076
  49.0 2.6 %copy-start.16 = (bf16[256,1024]{1,0:T(8,128)(2,1)S(1)}, bf16[256,1024]{1,0:T(8,128)(2,1)}, u32[]{:S(2)}) copy-start(bf16[256,1024]{1,0:T(8,128)(2,1)} %copy-done.15) | copy-start | bytes 1572868
  49.1 2.6 %copy-start.17 = (bf16[256,1024]{1,0:T(8,128)(2,1)S(1)}, bf16[256,1024]{1,0:T(8,128)(2,1)}, u32[]{:S(2)}) copy-start(bf16[256,1024]{1,0:T(8,128)(2,1)} %fusion.44) | copy-start | bytes 1572868
  51.6 0.9 %copy-start.7 = (bf16[256,400]{0,1:T(8,128)(2,1)S(1)}, bf16[256,400]{0,1:T(8,128)(2,1)}, u32[]{:S(2)}) copy-start(bf16[256,400]{0,1:T(8,128)(2,1)} %copy-done.6) | copy-start | bytes 614404
  51.6 1.0 %copy-start.9 = (bf16[256,400]{0,1:T(8,128)(2,1)S(1)}, bf16[256,400]{0,1:T(8,128)(2,1)}, u32[]{:S(2)}) copy-start(bf16[256,400]{0,1:T(8,128)(2,1)} %copy-done.8) | copy-start | bytes 614404
  51.7 1.1 %copy-start.11 = (bf16[256,400]{0,1:T(8,128)(2,1)S(1)}, bf16[256,400]{0,1:T(8,128)(2,1)}, u32[]{:S(2)}) copy-start(bf16[256,400]{0,1:T(8,128)(2,1)} %copy-done.10) | copy-start | bytes 614404
  53.2 1.2 %copy-start.4 = (f32[256,800]{0,1:T(8,128)S(1)}, f32[256,800]{0,1:T(8,128)}, u32[]{:S(2)}) copy-start(f32[256,800]{0,1:T(8,128)} %copy-done.3) | copy-start | bytes 2457604
  55.2 2.3 %copy-start.14 = (s32[64]{0:T(128)S(1)}, s32[64]{0:T(128)}, u32[]{:S(2)}) copy-start(s32[64]{0:T(128)} %eq.138) | copy-start | bytes 772

commit v6 on v4

--- a/solution.py
+++ b/solution.py
@@ -2,6 +2,9 @@
 import jax.numpy as jnp
 from jax import lax
 from jax.sharding import PartitionSpec as P
+import functools
+from jax.experimental import pallas as pl
+from jax.experimental.pallas import tpu as pltpu
 
 
 def passed_along(shard, axis, by):
@@ -45,6 +48,122 @@
     return lax.dot_general(
         selector, upper, dims, preferred_element_type=jnp.float32
     ) + lax.dot_general(selector, lower, dims, preferred_element_type=jnp.float32)
+
+
+def _sigmoid(x):
+    return 1.0 / (1.0 + jnp.exp(-x))
+
+
+def _select(ids_col, total):
+    hit = ids_col == lax.broadcasted_iota(jnp.int32, (ids_col.shape[0], total), 1)
+    return jnp.where(hit, 1.0, 0.0).astype(jnp.bfloat16)
+
+
+def _select_t(ids_row, total):
+    hit = ids_row == lax.broadcasted_iota(jnp.int32, (total, ids_row.shape[1]), 0)
+    return jnp.where(hit, 1.0, 0.0).astype(jnp.bfloat16)
+
+
+def _mm(a, b):
+    return jnp.dot(a, b, preferred_element_type=jnp.float32)
+
+
+def _spread(sel_t, terms):
+    upper = terms.astype(jnp.bfloat16)
+    lower = (terms - upper.astype(jnp.float32)).astype(jnp.bfloat16)
+    return _mm(sel_t, upper) + _mm(sel_t, lower)
+
+
+def _chain_body(groups, own_groups, block, neg_count, scale,
+                wcol, wrow, ccol, crow, scol, srow, ncol, nrow,
+                words, held, table, word_out, ctx_out, slot_out):
+    parts = words.shape[0]
+    rows = table.shape[0]
+    slots = slot_out.shape[0]
+    half = words.shape[1] // 2
+    word_out[...] = jnp.zeros(word_out.shape, jnp.float32)
+    ctx_out[...] = jnp.zeros(ctx_out.shape, jnp.float32)
+    slot_out[...] = jnp.zeros(slot_out.shape, jnp.float32)
+    for g in range(groups):
+        t0 = g * block
+        w = _mm(_select(wcol[t0:t0 + block, :], parts), words[...])
+        c = _mm(_select(ccol[t0:t0 + block, :], parts), held[...])
+        rv = _mm(_select(scol[t0:t0 + block, :], rows), table[...])
+        w_re, w_im = w[:, :half], w[:, half:]
+        r_re, r_im = rv[:, :half], rv[:, half:]
+        q = jnp.concatenate([w_re * r_re - w_im * r_im, w_re * r_im + w_im * r_re], axis=1)
+        q = q.astype(jnp.bfloat16)
+        qf = q.astype(jnp.float32)
+        pos = jnp.sum(qf * c, axis=1, keepdims=True)
+        dpos = -1.0 / (1.0 + jnp.exp(pos))
+        n0 = g * neg_count
+        neg_sel = _select(ncol[n0:n0 + neg_count, :], parts)
+        neg = _mm(neg_sel, held[...]).astype(jnp.bfloat16)
+        scores = lax.dot_general(q, neg, (((1,), (1,)), ((), ())),
+                                 preferred_element_type=jnp.float32)
+        dneg = (_sigmoid(scores) * scale).astype(jnp.bfloat16)
+        gq = dpos * c + _mm(dneg, neg)
+        g_re, g_im = gq[:, :half], gq[:, half:]
+        if g < own_groups:
+            rterm = jnp.concatenate([g_re * w_re + g_im * w_im, g_im * w_re - g_re * w_im], axis=1)
+            slot_out[...] += _spread(_select_t(srow[:, t0:t0 + block], slots), rterm)
+        wterm = jnp.concatenate([g_re * r_re + g_im * r_im, g_im * r_re - g_re * r_im], axis=1)
+        word_out[...] += _spread(_select_t(wrow[:, t0:t0 + block], parts), wterm)
+        ctx_t = _select_t(crow[:, t0:t0 + block], parts)
+        neg_t = _select_t(nrow[g:g + 1, :], parts)
+        neg_weight = lax.dot_general(neg_t, dneg, (((1,), (1,)), ((), ())),
+                                     preferred_element_type=jnp.float32)
+        ctx_out[...] += _spread(ctx_t, dpos * qf) + _spread(neg_weight, q)
+
+
+def block_chains(word_ids, ctx_ids, slot_ids, neg_ids, own_groups, scale, words, held, table,
+                 slots):
+    trips = word_ids.shape[0]
+    groups, neg_count = neg_ids.shape
+    block = trips // groups
+    parts, width = words.shape
+    own_ids = slot_ids[: max(own_groups, 1) * block]
+    body = functools.partial(_chain_body, groups, own_groups, block, neg_count, scale)
+    return pl.pallas_call(
+        body,
+        out_shape=(
+            jax.ShapeDtypeStruct((parts, width), jnp.float32),
+            jax.ShapeDtypeStruct((parts, width), jnp.float32),
+            jax.ShapeDtypeStruct((slots, width), jnp.float32),
+        ),
+        compiler_params=pltpu.CompilerParams(vmem_limit_bytes=48 * 1024 * 1024),
+    )(
+        word_ids.reshape(-1, 1),
+        word_ids.reshape(1, -1),
+        ctx_ids.reshape(-1, 1),
+        ctx_ids.reshape(1, -1),
+        slot_ids.reshape(-1, 1),
+        own_ids.reshape(1, -1),
+        neg_ids.reshape(-1, 1),
+        neg_ids,
+        words,
+        held,
+        table,
+    )
+
+
+def lanes_of(half_width):
+    return -(-half_width // 128) * 128
+
+
+def padded_halves(rows, half_width):
+    count = rows.shape[0]
+    lanes = lanes_of(half_width)
+    return jnp.pad(
+        rows.reshape(count, 2, half_width), ((0, 0), (0, 0), (0, lanes - half_width))
+    ).reshape(count, 2 * lanes)
+
+
+def unpadded_halves(rows, half_width):
+    count = rows.shape[0]
+    return rows.reshape(count, 2, lanes_of(half_width))[:, :, :half_width].reshape(
+        count, 2 * half_width
+    )
 
 
 def shards(
@@ -94,53 +213,27 @@
     )
 
     group_count = split_count * block_count
-    word_sel = one_hot(word_ids, part_rows)
-    ctx_sel = one_hot(ctx_ids, part_rows)
-    neg_sel = one_hot(neg_ids, part_rows)
-    word_used = pick_rows(word_sel, words)
-    ctx_used = pick_rows(ctx_sel, held_rows)
-    neg_rows = jnp.einsum(
-        "gjp,pd->gjd", neg_sel, held_rows, preferred_element_type=jnp.float32
-    ).astype(jnp.bfloat16)
-    fetched, word_used, ctx_used, neg_rows = lax.optimization_barrier(
-        (fetched, word_used, ctx_used, neg_rows)
-    )
+    word_table = padded_halves(words, half_width)
+    held_table = padded_halves(held_rows, half_width)
+    fetched, word_table, held_table = lax.optimization_barrier((fetched, word_table, held_table))
     slot_table = (
         fetched.reshape(owner_count, split_count, slot_count, row_width)
         .transpose(1, 0, 2, 3)
         .reshape(split_count * slot_total, row_width)
     )
     own_table = slot_table[:slot_total]
-    rel_used = pick_rows(one_hot(slot_ids, split_count * slot_total), slot_table)
-    query = complex_product(word_used, rel_used, half_width).astype(jnp.bfloat16)
-    positive = jnp.sum(query.astype(jnp.float32) * ctx_used, axis=1)
-    pos_grad = -jax.nn.sigmoid(-positive)
-    query_blocks = query.reshape(group_count, block_size, row_width)
-    scores = jnp.einsum(
-        "gtd,gjd->gtj", query_blocks, neg_rows, preferred_element_type=jnp.float32
-    )
-    neg_grad = (jax.nn.sigmoid(scores) * neg_scale).astype(jnp.bfloat16)
-    pos_blocks = pos_grad.reshape(group_count, block_size)
-    query_grads = (
-        pos_blocks[:, :, None] * ctx_used.reshape(group_count, block_size, row_width)
-        + jnp.einsum("gtj,gjd->gtd", neg_grad, neg_rows, preferred_element_type=jnp.float32)
-    ).reshape(-1, row_width)
-    slot_grad = spread_rows(
-        one_hot(slot_ids[:trips], slot_total),
-        conj_product(query_grads[:trips], word_used[:trips], half_width),
-    )
-
-    neg_weight = jnp.einsum("gtj,gjp->gpt", neg_grad, neg_sel, preferred_element_type=jnp.float32)
-    pos_weight = jnp.where(
-        ctx_ids.reshape(group_count, 1, block_size) == jnp.arange(part_rows)[None, :, None],
-        pos_blocks[:, None, :],
-        0.0,
-    )
-    weight_hi, weight_lo = split_bf16(neg_weight + pos_weight)
-    ctx_sum = jnp.einsum(
-        "gpt,gtd->pd", weight_hi, query_blocks, preferred_element_type=jnp.float32
-    ) + jnp.einsum("gpt,gtd->pd", weight_lo, query_blocks, preferred_element_type=jnp.float32)
-    word_sum = spread_rows(word_sel, conj_product(query_grads, rel_used, half_width))
+    rel_table = padded_halves(slot_table, half_width)
+    own_word, own_ctx, own_slot = block_chains(
+        word_ids[:trips], ctx_ids[:trips], slot_ids[:trips], neg_ids[:block_count],
+        block_count, neg_scale, word_table, held_table, rel_table, slot_total,
+    )
+    rest_word, rest_ctx, _ = block_chains(
+        word_ids[trips:], ctx_ids[trips:], slot_ids[trips:], neg_ids[block_count:],
+        0, neg_scale, word_table, held_table, rel_table, 8,
+    )
+    word_sum = unpadded_halves(own_word + rest_word, half_width)
+    ctx_sum = unpadded_halves(own_ctx + rest_ctx, half_width)
+    slot_grad = unpadded_halves(own_slot, half_width)
     slot_grad = slot_grad + 0.02 * live_mask[:, None] * own_table.astype(jnp.float32)
     outgoing = slot_grad.reshape(owner_count, slot_count, row_width)
     returned = lax.all_to_all(

time: 58.8 us -> 60.4 us (1.027)
  matrix products: 16.6 us -> 1.08 us
  local copies, waits for them, and re-layouts: 10.1 us -> 23.4 us
  Pallas kernels: 0 us -> 7.86 us
  waiting for transfers between devices: 13.3 us -> 7.37 us
  starting transfers between devices: 14.3 us -> 16.8 us
  other arithmetic: 2.98 us -> 2.33 us
    dot_general x10 -> x0, matrix products: 12 us -> none  [the longest x1 3.68 us: shards(): jnp.einsum('gtd,gjd->gtj', query_blocks, neg_rows, preferred_element_type...]
    reshape x2 -> x14, local copies, waits for them, and re-layouts: 0.41 us -> 9.2 us  [the longest x4 2.99 us: unpadded_halves(): rows.reshape(count, 2, lanes_of(half_width))[:, :, :half_width]]
    pallas_call x0 -> x2, Pallas kernels: none -> 7.86 us  [block_chains(): pl.pallas_call(body, out_shape=(jax.ShapeDtypeStruct((parts, width), jnp....]
    all_to_all x1, waiting for transfers between devices: 4.71 us -> 0.93 us  [shards(): lax.all_to_all(outgoing.astype(jnp.bfloat16), both, split_axis=0, concat_...]
    dot_general x4 -> x1, matrix products: 3.77 us -> 0.29 us  [pick_rows(): return jnp.dot(selector, rows, preferred_element_type=jnp.float32)]
    all_to_all x1, waiting for transfers between devices: 3.52 us -> 0.84 us  [shards(): lax.all_to_all(wanted, both, split_axis=0, concat_axis=0, tiled=True)]
    slice x2 -> x7, local copies, waits for them, and re-layouts: 0.06 us -> 2.17 us  [the longest x2 2.14 us: unpadded_halves(): rows.reshape(count, 2, lanes_of(half_width))[:, :, :half_width]]
    all_to_all x1, starting transfers between devices: 2.58 us -> 4.08 us  [shards(): lax.all_to_all(picked, both, split_axis=0, concat_axis=0, tiled=True)]
  transfers between devices with their start and end apart: 5 -> 5, of which waited for: 3 -> 3; matrix products, arithmetic and copies ran while one was open for 23% -> 24% of each run, Pallas kernels for 0% -> 6%
where the time goes in v6:
time: 60.4 us; the launch traced here: 59.9 us
  local copies, waits for them, and re-layouts  23.4 us (39%)
  starting transfers between devices  16.8 us (28%)
  Pallas kernels  7.86 us (13%)
  waiting for transfers between devices  7.37 us (12%)
  other arithmetic  2.33 us (4%)
  matrix products  1.08 us (2%)
  between operations  1.06 us (2%)
    pallas_call x2, Pallas kernels, block_chains(): pl.pallas_call(body, out_shape=(jax.ShapeDtypeStruct((parts, width), jnp....  7.86 us
    all_to_all x1, starting transfers between devices, shards(): lax.all_to_all(wanted, both, split_axis=0, concat_axis=0, tiled=True)  7.3 us
    all_to_all x1, waiting for transfers between devices, shards(): lax.all_to_all(picked, both, split_axis=0, concat_axis=0, tiled=True)  5.59 us
    unnamed x40, local copies, waits for them, and re-layouts  4.74 us
    all_to_all x1, starting transfers between devices, shards(): lax.all_to_all(picked, both, split_axis=0, concat_axis=0, tiled=True)  4.08 us
    all_to_all x1, starting transfers between devices, shards(): lax.all_to_all(outgoing.astype(jnp.bfloat16), both, split_axis=0, concat_...  3.58 us
    reshape x4, local copies, waits for them, and re-layouts, unpadded_halves(): rows.reshape(count, 2, lanes_of(half_width))[:, :, :half_width]  2.99 us
    slice x2, local copies, waits for them, and re-layouts, unpadded_halves(): rows.reshape(count, 2, lanes_of(half_width))[:, :, :half_width]  2.14 us
  transfers between devices with their start and end apart: 5, of which 3 were waited for; matrix products, arithmetic and copies ran while one was open for 24% of the time, Pallas kernels for 6%

profile of v6, /device:TPU:0, one launch (start us, length us, event | category | flops | bytes accessed | tf_op | source)
XLA Modules:
  0.0 59.9 jit_solution(356059083501993681)
XLA Ops:
  0.6 1.4 %copy.119 = s32[1,1,16,2,2]{4,3,2,1,0:T(2,128)} copy(s32[1,1,16,2,2]{2,4,3,1,0:T(2,128)} %param.16) | data formatting | bytes 512 | tf_op jit(solution)/shard_map/all_to_all | solution.py:202
  2.0 7.3 %all-to-all-start = ((s32[32,1,2]{2,1,0:T(1,128)}), s32[32,1,2]{2,1,0:T(1,128)S(1)}, u32[]{:S(2)}, u32[]{:S(2)}) async-start(s32[32,1,2]{2,1,0:T(1,128)} %bitcast.5), calls=%async_computation | async-start | bytes 32768 | tf_op jit(solution)/shard_map/all_to_all | solution.py:202
  9.4 0.6 %copy-done.15 = s32[256]{0:T(256)S(1)} copy-done((s32[256]{0:T(256)S(1)}, s32[256]{0:T(256)}, u32[]{:S(2)}) %copy-start.15) | copy-done | bytes 1048
  10.0 1.8 %collective-permute-start = (s32[1792]{0:T(1024)S(1)}, s32[1792]{0:T(1024)S(1)}, u32[]{:S(2)}, u32[]{:S(2)}) collective-permute-start(s32[1792]{0:T(1024)S(1)} %pad_add_fusion.1), channel_id=1, source_target_pairs={{0,1},{1,0},{2,3},{3,2},{4,5},{5,4},{6,7},{7,6},{8,9},{9,8},{10,11... | collective-permute-start | bytes 21512 | tf_op jit(solution)/shard_map/ppermute | solution.py:12
  11.9 0.7 %copy-done.14 = s32[1,1,16,2]{2,3,1,0:T(2,128)S(1)} copy-done((s32[1,1,16,2]{2,3,1,0:T(2,128)S(1)}, s32[1,1,16,2]{2,3,1,0:T(2,128)}, u32[]{:S(2)}) %copy-start.14) | copy-done | bytes 152
  12.8 0.8 %copy.106.wcol = s32[256,1]{1,0:T(8,128)} copy(s32[256,1]{0,1:T(1,128)S(1)} %get-tuple-element.30) | data formatting | bytes 2048 | tf_op jit(solution)/shard_map/reshape | solution.py:136
  13.6 0.8 %copy.107.ccol = s32[256,1]{1,0:T(8,128)} copy(s32[256,1]{0,1:T(1,128)S(1)} %get-tuple-element.31) | data formatting | bytes 2048 | tf_op jit(solution)/shard_map/reshape | solution.py:138
  15.6 0.8 %all-to-all-done = s32[32,1,2]{2,1,0:T(1,128)S(1)} async-done(((s32[32,1,2]{2,1,0:T(1,128)}), s32[32,1,2]{2,1,0:T(1,128)S(1)}, u32[]{:S(2)}, u32[]{:S(2)}) %all-to-all-start) | async-done | bytes 288 | tf_op jit(solution)/shard_map/all_to_all | solution.py:202
  17.7 0.5 broadcast.35
  18.2 0.7 %reduce.3 = s32[32,2]{1,0:T(8,128)S(1)} reduce(s32[32,1,2]{2,1,0:T(1,128)S(1)} %all-to-all-done, s32[]{:T(128)} %broadcast.35), dimensions={1}, to_apply=%all_to_all.13.reduce_sub_computation.3 | reduce | bytes 516 | tf_op jit(solution)/shard_map/all_to_all | solution.py:202
  19.2 0.8 %reshape.149 = bf16[32,4,800]{2,1,0:T(4,128)(2,1)} reshape(bf16[128,800]{1,0:T(8,128)(2,1)S(1)} %copy.101) | data formatting | bytes 409600 | tf_op jit(solution)/shard_map/reshape | solution.py:207
  20.0 4.1 %all-to-all-start.1 = ((bf16[32,4,800]{2,1,0:T(4,128)(2,1)}), bf16[32,4,800]{2,1,0:T(4,128)(2,1)S(1)}, u32[]{:S(2)}, u32[]{:S(2)}) async-start(bf16[32,4,800]{2,1,0:T(4,128)(2,1)} %reshape.149), calls=%async_computation.1 | async-start | bytes 458752 | tf_op jit(solution)/shard_map/all_to_all | solution.py:208
  24.2 0.8 %copy.110.wcol = s32[256,1]{1,0:T(8,128)} copy(s32[256,1]{0,1:T(1,128)S(1)} %get-tuple-element.24) | data formatting | bytes 2048 | tf_op jit(solution)/shard_map/reshape | solution.py:136
  25.0 0.8 %copy.111.ccol = s32[256,1]{1,0:T(8,128)} copy(s32[256,1]{0,1:T(1,128)S(1)} %get-tuple-element.25) | data formatting | bytes 2048 | tf_op jit(solution)/shard_map/reshape | solution.py:138
  25.8 0.8 %copy.108.scol = s32[256,1]{1,0:T(8,128)} copy(s32[256,1]{0,1:T(1,128)S(1)} %get-tuple-element.34) | data formatting | bytes 2048 | tf_op jit(solution)/shard_map/reshape | solution.py:140
  26.6 0.8 %copy.112.scol = s32[256,1]{1,0:T(8,128)} copy(s32[256,1]{0,1:T(1,128)S(1)} %get-tuple-element.35) | data formatting | bytes 2048 | tf_op jit(solution)/shard_map/reshape | solution.py:140
  28.6 5.6 %all-to-all-done.1 = bf16[32,4,800]{2,1,0:T(4,128)(2,1)S(1)} async-done(((bf16[32,4,800]{2,1,0:T(4,128)(2,1)}), bf16[32,4,800]{2,1,0:T(4,128)(2,1)S(1)}, u32[]{:S(2)}, u32[]{:S(2)}) %all-to-all-start.1) | async-done | bytes 204832 | tf_op jit(solution)/shard_map/all_to_all | solution.py:208
  35.6 0.8 %copy-done.3 = s32[256,1]{1,0:T(8,128)S(1)} copy-done((s32[256,1]{1,0:T(8,128)S(1)}, s32[256,1]{1,0:T(8,128)}, u32[]{:S(2)}) %copy-start.3) | copy-done | bytes 1048
  36.5 4.1 %shard_map.112 = (f32[256,1024]{1,0:T(8,128)S(1)}, f32[256,1024]{1,0:T(8,128)S(1)}, f32[64,1024]{1,0:T(8,128)S(1)}) custom-call(s32[256,1]{1,0:T(8,128)S(1)} %copy-done.3, s32[1,256]{1,0:T(1,128)S(1)} %get-tuple-element.32.wrow, s32[256,1]{1,0:T(8,128)S(1)} %copy-done.4, s32[1,256]{1,0:T(1,128)S(1)} %get-tuple-element.29.crow, s32[256,1]{1,0:T(8,128)S(1)} %copy-done.8, ...), custom_call_target="tpu_custom_call" | custom-call | tf_op jit(solution)/shard_map/pallas_call | solution.py:127
  40.6 1.0 %copy-done.1 = f32[256,1024]{1,0:T(8,128)} copy-done((f32[256,1024]{1,0:T(8,128)}, f32[256,1024]{1,0:T(8,128)S(1)}, u32[]{:S(2)}) %copy-start.1) | copy-done | bytes 1048600
  41.6 0.7 %copy-done.9 = f32[64,1024]{1,0:T(8,128)} copy-done((f32[64,1024]{1,0:T(8,128)}, f32[64,1024]{1,0:T(8,128)S(1)}, u32[]{:S(2)}) %copy-start.9) | copy-done | bytes 262168
  42.3 1.2 %reshape.162 = f32[64,2,512]{2,1,0:T(2,128)S(1)} reshape(f32[64,1024]{1,0:T(8,128)} %copy-done.9) | data formatting | bytes 524288 | tf_op jit(solution)/shard_map/reshape | solution.py:164
  43.5 1.1 %reshape.163 = f32[32,2,800]{2,1,0:T(2,128)} reshape(f32[64,2,400]{2,1,0:T(2,128)S(1)} %bitcast.60) | data formatting | bytes 409600 | tf_op jit(solution)/shard_map/reshape | solution.py:164
  44.6 1.0 %fusion.1 = bf16[32,2,800]{2,0,1:T(8,128)(2,1)S(1)} fusion(f32[32,2,800]{2,1,0:T(2,128)} %reshape.163, bf16[2,32,2,800]{3,1,2,0:T(8,128)(2,1)S(1)} %bitcast.58, f32[32,2]{0,1:T(2,128)S(1)} %compare_select_fusion), kind=kLoop, calls=%fused_computation.5 | loop fusion | flops 204800 | bytes 409856 | tf_op jit(solution)/shard_map/convert_element_type | solution.py:240
  45.6 0.7 %copy.118 = bf16[32,2,800]{2,1,0:T(2,128)(2,1)} copy(bf16[32,2,800]{2,0,1:T(8,128)(2,1)S(1)} %fusion.1) | data formatting | bytes 204800 | tf_op jit(solution)/shard_map/convert_element_type | solution.py:240
  46.4 3.6 %all-to-all-start.2 = ((bf16[32,2,800]{2,1,0:T(2,128)(2,1)}), bf16[32,2,800]{2,1,0:T(2,128)(2,1)}, u32[]{:S(2)}, u32[]{:S(2)}) async-start(bf16[32,2,800]{2,1,0:T(2,128)(2,1)} %copy.118), calls=%async_computation.2 | async-start | bytes 229376 | tf_op jit(solution)/shard_map/all_to_all | solution.py:239
  50.0 3.8 %shard_map.113 = (f32[256,1024]{1,0:T(8,128)S(1)}, f32[256,1024]{1,0:T(8,128)S(1)}, f32[8,1024]{1,0:T(8,128)}) custom-call(s32[256,1]{1,0:T(8,128)S(1)} %copy-done.5, s32[1,256]{1,0:T(1,128)S(1)} %get-tuple-element.26.wrow, s32[256,1]{1,0:T(8,128)S(1)} %copy-done.6, s32[1,256]{1,0:T(1,128)S(1)} %get-tuple-element.23.crow, s32[256,1]{1,0:T(8,128)S(1)} %copy-done.7, ...), custom_call_target="tpu_custom_call" | custom-call | tf_op jit(solution)/shard_map/pallas_call | solution.py:127
  54.7 1.1 %copy.115 = bf16[256,2,400]{0,2,1:T(8,128)(2,1)} copy(bf16[256,2,400]{2,1,0:T(2,128)(2,1)S(1)} %bitcast.53) | data formatting | bytes 819200 | tf_op jit(solution)/shard_map/slice | solution.py:164
  56.1 1.1 %copy.114 = bf16[256,2,400]{0,2,1:T(8,128)(2,1)} copy(bf16[256,2,400]{2,1,0:T(2,128)(2,1)S(1)} %bitcast.54) | data formatting | bytes 819200 | tf_op jit(solution)/shard_map/slice | solution.py:164
  57.2 0.9 %all-to-all-done.2 = bf16[32,2,800]{2,1,0:T(2,128)(2,1)} async-done(((bf16[32,2,800]{2,1,0:T(2,128)(2,1)}), bf16[32,2,800]{2,1,0:T(2,128)(2,1)}, u32[]{:S(2)}, u32[]{:S(2)}) %all-to-all-start.2) | async-done | bytes 102432 | tf_op jit(solution)/shard_map/all_to_all | solution.py:239
  58.1 1.0 %reshape.164 = bf16[64,800]{1,0:T(8,128)(2,1)S(1)} reshape(bf16[32,2,800]{2,1,0:T(2,128)(2,1)} %all-to-all-done.2) | data formatting | bytes 204800 | tf_op jit(solution)/shard_map/reshape | solution.py:247
  59.1 0.8 %fusion.3 = f32[32,800]{1,0:T(8,128)} fusion(bf16[64,800]{1,0:T(8,128)(2,1)S(1)} %reshape.164, s32[64]{0:T(128)S(1)} %eq.34), kind=kOutput, calls=%fused_computation.11 | convolution fusion | flops 3278848 | bytes 205056 | tf_op jit(solution)/shard_map/dot_general | solution.py:245
  (75 shorter events, 7.0 us)
Async XLA Ops:
  0.6 16.8 %copy-start = (bf16[32,800]{1,0:T(8,128)(2,1)S(1)}, bf16[32,800]{1,0:T(8,128)(2,1)}, u32[]{:S(2)}) copy-start(bf16[32,800]{1,0:T(8,128)(2,1)} %param.11) | copy-start | bytes 153604
  2.0 7.3 %copy-start.13 = (s32[1,1024]{1,0:T(1,128)S(1)}, s32[1,1024]{1,0:T(1,128)}, u32[]{:S(2)}) copy-start(s32[1,1024]{1,0:T(1,128)} %param.15) | copy-start | bytes 12292
  2.0 7.3 %copy-start.16 = (s32[256]{0:T(256)S(1)}, s32[256]{0:T(256)}, u32[]{:S(2)}) copy-start(s32[256]{0:T(256)} %param.13) | copy-start | bytes 3076
  2.0 7.3 %copy-start.17 = (s32[256]{0:T(256)S(1)}, s32[256]{0:T(256)}, u32[]{:S(2)}) copy-start(s32[256]{0:T(256)} %param.12) | copy-start | bytes 3076
  2.0 14.4 %all-to-all-start = ((s32[32,1,2]{2,1,0:T(1,128)}), s32[32,1,2]{2,1,0:T(1,128)S(1)}, u32[]{:S(2)}, u32[]{:S(2)}) async-start(s32[32,1,2]{2,1,0:T(1,128)} %bitcast.5), calls=%async_computation | async-start | bytes 32768 | tf_op jit(solution)/shard_map/all_to_all | solution.py:202
  9.3 0.7 %copy-start.15 = (s32[256]{0:T(256)S(1)}, s32[256]{0:T(256)}, u32[]{:S(2)}) copy-start(s32[256]{0:T(256)} %param.14) | copy-start | bytes 3076
  10.0 14.0 %collective-permute-start = (s32[1792]{0:T(1024)S(1)}, s32[1792]{0:T(1024)S(1)}, u32[]{:S(2)}, u32[]{:S(2)}) collective-permute-start(s32[1792]{0:T(1024)S(1)} %pad_add_fusion.1), channel_id=1, source_target_pairs={{0,1},{1,0},{2,3},{3,2},{4,5},{5,4},{6,7},{7,6},{8,9},{9,8},{10,11... | collective-permute-start | bytes 21512 | tf_op jit(solution)/shard_map/ppermute | solution.py:12
  11.9 15.7 %collective-permute-start.1 = (bf16[256,800]{0,1:T(8,128)(2,1)}, bf16[256,800]{0,1:T(8,128)(2,1)S(1)}, u32[]{:S(2)}, u32[]{:S(2)}) collective-permute-start(bf16[256,800]{0,1:T(8,128)(2,1)} %param.10), channel_id=1, source_target_pairs={{0,2},{2,4},{4,6},{6,8},{8,10},{10,12},{12,14},{14,16},{16,18},{18... | collective-permute-start | bytes 1228808 | tf_op jit(solution)/shard_map/ppermute | solution.py:12
  11.9 0.7 %copy-start.14 = (s32[1,1,16,2]{2,3,1,0:T(2,128)S(1)}, s32[1,1,16,2]{2,3,1,0:T(2,128)}, u32[]{:S(2)}) copy-start(s32[1,1,16,2]{2,3,1,0:T(2,128)} %param.17) | copy-start | bytes 388
  12.6 2.0 %copy-start.12 = (bf16[256,800]{0,1:T(8,128)(2,1)S(1)}, bf16[256,800]{0,1:T(8,128)(2,1)}, u32[]{:S(2)}) copy-start(bf16[256,800]{0,1:T(8,128)(2,1)} %param.9) | copy-start | bytes 1228804
  20.0 14.3 %all-to-all-start.1 = ((bf16[32,4,800]{2,1,0:T(4,128)(2,1)}), bf16[32,4,800]{2,1,0:T(4,128)(2,1)S(1)}, u32[]{:S(2)}, u32[]{:S(2)}) async-start(bf16[32,4,800]{2,1,0:T(4,128)(2,1)} %reshape.149), calls=%async_computation.1 | async-start | bytes 458752 | tf_op jit(solution)/shard_map/all_to_all | solution.py:208
  34.3 0.7 %copy-start.10 = (bf16[32,4,800]{2,0,1:T(8,128)(2,1)}, bf16[32,4,800]{2,0,1:T(8,128)(2,1)S(1)}, u32[]{:S(2)}) copy-start(bf16[32,4,800]{2,0,1:T(8,128)(2,1)S(1)} %copy.104) | copy-start | bytes 614404
  35.5 0.9 %copy-start.3 = (s32[256,1]{1,0:T(8,128)S(1)}, s32[256,1]{1,0:T(8,128)}, u32[]{:S(2)}) copy-start(s32[256,1]{1,0:T(8,128)} %copy.106.wcol) | copy-start | bytes 3076
  35.5 1.0 %copy-start.4 = (s32[256,1]{1,0:T(8,128)S(1)}, s32[256,1]{1,0:T(8,128)}, u32[]{:S(2)}) copy-start(s32[256,1]{1,0:T(8,128)} %copy.107.ccol) | copy-start | bytes 3076
  35.5 1.0 %copy-start.8 = (s32[256,1]{1,0:T(8,128)S(1)}, s32[256,1]{1,0:T(8,128)}, u32[]{:S(2)}) copy-start(s32[256,1]{1,0:T(8,128)} %copy.108.scol) | copy-start | bytes 3076
  40.6 1.0 %copy-start.1 = (f32[256,1024]{1,0:T(8,128)}, f32[256,1024]{1,0:T(8,128)S(1)}, u32[]{:S(2)}) copy-start(f32[256,1024]{1,0:T(8,128)S(1)} %get-tuple-element.16) | copy-start | bytes 3145732
  41.6 0.7 %copy-start.9 = (f32[64,1024]{1,0:T(8,128)}, f32[64,1024]{1,0:T(8,128)S(1)}, u32[]{:S(2)}) copy-start(f32[64,1024]{1,0:T(8,128)S(1)} %get-tuple-element.18) | copy-start | bytes 786436
  43.5 1.1 %copy-start.11 = (bf16[32,4,800]{2,0,1:T(8,128)(2,1)S(1)}, bf16[32,4,800]{2,0,1:T(8,128)(2,1)}, u32[]{:S(2)}) copy-start(bf16[32,4,800]{2,0,1:T(8,128)(2,1)} %copy-done.10) | copy-start | bytes 614404
  45.6 4.3 %copy-start.6 = (s32[256,1]{1,0:T(8,128)S(1)}, s32[256,1]{1,0:T(8,128)}, u32[]{:S(2)}) copy-start(s32[256,1]{1,0:T(8,128)} %copy.111.ccol) | copy-start | bytes 3076
  45.6 4.3 %copy-start.7 = (s32[256,1]{1,0:T(8,128)S(1)}, s32[256,1]{1,0:T(8,128)}, u32[]{:S(2)}) copy-start(s32[256,1]{1,0:T(8,128)} %copy.112.scol) | copy-start | bytes 3076
  46.4 3.6 %copy-start.5 = (s32[256,1]{1,0:T(8,128)S(1)}, s32[256,1]{1,0:T(8,128)}, u32[]{:S(2)}) copy-start(s32[256,1]{1,0:T(8,128)} %copy.110.wcol) | copy-start | bytes 3076
  46.4 11.8 %all-to-all-start.2 = ((bf16[32,2,800]{2,1,0:T(2,128)(2,1)}), bf16[32,2,800]{2,1,0:T(2,128)(2,1)}, u32[]{:S(2)}, u32[]{:S(2)}) async-start(bf16[32,2,800]{2,1,0:T(2,128)(2,1)} %copy.118), calls=%async_computation.2 | async-start | bytes 229376 | tf_op jit(solution)/shard_map/all_to_all | solution.py:239
  50.0 3.8 %copy-start.2 = (f32[256,1024]{1,0:T(8,128)S(1)}, f32[256,1024]{1,0:T(8,128)}, u32[]{:S(2)}) copy-start(f32[256,1024]{1,0:T(8,128)} %copy-done.1) | copy-start | bytes 3145732

commit v7 on v6

--- a/solution.py
+++ b/solution.py
@@ -75,7 +75,7 @@
 
 
 def _chain_body(groups, own_groups, block, neg_count, scale,
-                wcol, wrow, ccol, crow, scol, srow, ncol, nrow,
+                wcol, wrow, ccol, crow, scol, srow, ncol, nrow, ocol, live,
                 words, held, table, word_out, ctx_out, slot_out):
     parts = words.shape[0]
     rows = table.shape[0]
@@ -83,7 +83,7 @@
     half = words.shape[1] // 2
     word_out[...] = jnp.zeros(word_out.shape, jnp.float32)
     ctx_out[...] = jnp.zeros(ctx_out.shape, jnp.float32)
-    slot_out[...] = jnp.zeros(slot_out.shape, jnp.float32)
+    slot_sum = jnp.zeros(slot_out.shape, jnp.float32)
     for g in range(groups):
         t0 = g * block
         w = _mm(_select(wcol[t0:t0 + block, :], parts), words[...])
@@ -106,7 +106,7 @@
         g_re, g_im = gq[:, :half], gq[:, half:]
         if g < own_groups:
             rterm = jnp.concatenate([g_re * w_re + g_im * w_im, g_im * w_re - g_re * w_im], axis=1)
-            slot_out[...] += _spread(_select_t(srow[:, t0:t0 + block], slots), rterm)
+            slot_sum = slot_sum + _spread(_select_t(srow[:, t0:t0 + block], slots), rterm)
         wterm = jnp.concatenate([g_re * r_re + g_im * r_im, g_im * r_re - g_re * r_im], axis=1)
         word_out[...] += _spread(_select_t(wrow[:, t0:t0 + block], parts), wterm)
         ctx_t = _select_t(crow[:, t0:t0 + block], parts)
@@ -114,22 +114,25 @@
         neg_weight = lax.dot_general(neg_t, dneg, (((1,), (1,)), ((), ())),
                                      preferred_element_type=jnp.float32)
         ctx_out[...] += _spread(ctx_t, dpos * qf) + _spread(neg_weight, q)
-
-
-def block_chains(word_ids, ctx_ids, slot_ids, neg_ids, own_groups, scale, words, held, table,
-                 slots):
+    if own_groups:
+        own_rows = _mm(_select(ocol[...], rows), table[...])
+        slot_sum = slot_sum + 0.02 * live[...] * own_rows
+    slot_out[...] = slot_sum.astype(slot_out.dtype)
+
+
+def block_chains(word_ids, ctx_ids, slot_ids, own_ids, neg_ids, own_groups, scale, words, held,
+                 table, own_rows, live_mask):
     trips = word_ids.shape[0]
     groups, neg_count = neg_ids.shape
     block = trips // groups
     parts, width = words.shape
-    own_ids = slot_ids[: max(own_groups, 1) * block]
     body = functools.partial(_chain_body, groups, own_groups, block, neg_count, scale)
     return pl.pallas_call(
         body,
         out_shape=(
             jax.ShapeDtypeStruct((parts, width), jnp.float32),
             jax.ShapeDtypeStruct((parts, width), jnp.float32),
-            jax.ShapeDtypeStruct((slots, width), jnp.float32),
+            jax.ShapeDtypeStruct((own_rows.shape[0], width), jnp.bfloat16),
         ),
         compiler_params=pltpu.CompilerParams(vmem_limit_bytes=48 * 1024 * 1024),
     )(
@@ -141,6 +144,8 @@
         own_ids.reshape(1, -1),
         neg_ids.reshape(-1, 1),
         neg_ids,
+        own_rows.reshape(-1, 1),
+        live_mask.reshape(-1, 1),
         words,
         held,
         table,
@@ -193,18 +198,24 @@
     )
     word_ids = bucket_ints[:, :trips].reshape(-1)
     ctx_ids = bucket_ints[:, trips : 2 * trips].reshape(-1)
+    slot_ids = bucket_ints[:, 2 * trips : 3 * trips]
     slot_ids = (
-        bucket_ints[:, 2 * trips : 3 * trips] + (jnp.arange(split_count) * slot_total)[:, None]
+        (slot_ids // slot_count) * (split_count * slot_count)
+        + (jnp.arange(split_count) * slot_count)[:, None]
+        + slot_ids % slot_count
     ).reshape(-1)
+    own_slots = jnp.arange(slot_total)
+    own_rows = (own_slots // slot_count) * (split_count * slot_count) + own_slots % slot_count
     neg_ids = bucket_ints[:, 3 * trips :].reshape(split_count * block_count, neg_count)
 
     wanted = requests[0, 0].reshape(owner_count, slot_count)
     incoming = lax.all_to_all(wanted, both, split_axis=0, concat_axis=0, tiled=True)
     lists = incoming.reshape(part_count, split_count, slot_count)
     served = jnp.stack([jnp.roll(lists, -j, axis=1) for j in range(split_count)], axis=2)
-    picked = pick_rows(one_hot(served.reshape(-1), owned_rows), relations).astype(
-        jnp.bfloat16
-    ).reshape(owner_count, split_count * slot_count, row_width)
+    padded_width = 2 * lanes_of(half_width)
+    picked = pick_rows(
+        one_hot(served.reshape(-1), owned_rows), padded_halves(relations, half_width)
+    ).astype(jnp.bfloat16).reshape(owner_count, split_count * slot_count, padded_width)
     fetched = lax.all_to_all(picked, both, split_axis=0, concat_axis=0, tiled=True)
     live_mask = (
         (jnp.arange(slot_count)[None, :] < counts[0, 0].reshape(owner_count)[:, None])
@@ -216,38 +227,34 @@
     word_table = padded_halves(words, half_width)
     held_table = padded_halves(held_rows, half_width)
     fetched, word_table, held_table = lax.optimization_barrier((fetched, word_table, held_table))
-    slot_table = (
-        fetched.reshape(owner_count, split_count, slot_count, row_width)
-        .transpose(1, 0, 2, 3)
-        .reshape(split_count * slot_total, row_width)
-    )
-    own_table = slot_table[:slot_total]
-    rel_table = padded_halves(slot_table, half_width)
+    rel_table = fetched.reshape(split_count * slot_total, padded_width)
     own_word, own_ctx, own_slot = block_chains(
-        word_ids[:trips], ctx_ids[:trips], slot_ids[:trips], neg_ids[:block_count],
-        block_count, neg_scale, word_table, held_table, rel_table, slot_total,
+        word_ids[:trips], ctx_ids[:trips], slot_ids[:trips], rel_slot, neg_ids[:block_count],
+        block_count, neg_scale, word_table, held_table, rel_table, own_rows, live_mask,
     )
     rest_word, rest_ctx, _ = block_chains(
-        word_ids[trips:], ctx_ids[trips:], slot_ids[trips:], neg_ids[block_count:],
-        0, neg_scale, word_table, held_table, rel_table, 8,
+        word_ids[trips:], ctx_ids[trips:], slot_ids[trips:], rel_slot, neg_ids[block_count:],
+        0, neg_scale, word_table, held_table, rel_table, own_rows[:8], live_mask[:8],
     )
     word_sum = unpadded_halves(own_word + rest_word, half_width)
     ctx_sum = unpadded_halves(own_ctx + rest_ctx, half_width)
-    slot_grad = unpadded_halves(own_slot, half_width)
-    slot_grad = slot_grad + 0.02 * live_mask[:, None] * own_table.astype(jnp.float32)
-    outgoing = slot_grad.reshape(owner_count, slot_count, row_width)
     returned = lax.all_to_all(
-        outgoing.astype(jnp.bfloat16), both, split_axis=0, concat_axis=0, tiled=True
-    ).astype(outgoing.dtype)
+        own_slot.reshape(owner_count, slot_count, padded_width),
+        both,
+        split_axis=0,
+        concat_axis=0,
+        tiled=True,
+    ).astype(jnp.float32)
     owner_map = (incoming.reshape(-1)[None, :] == jnp.arange(owned_rows)[:, None]).astype(
         jnp.float32
     )
     relation_grad = jnp.dot(
         owner_map,
-        returned.reshape(-1, row_width),
+        returned.reshape(-1, padded_width),
         precision=lax.Precision.HIGHEST,
         preferred_element_type=jnp.float32,
     )
+    relation_grad = unpadded_halves(relation_grad, half_width)
     return (word_sum.astype(jnp.bfloat16), ctx_sum.astype(jnp.bfloat16), relation_grad)
 
 

time: 60.4 us -> 63.5 us (1.051)
  local copies, waits for them, and re-layouts: 23.4 us -> 29.7 us
  waiting for transfers between devices: 7.37 us -> 4.37 us
  starting transfers between devices: 16.8 us -> 17.7 us
  matrix products: 1.08 us -> 0.41 us
    unnamed x40 -> x50, local copies, waits for them, and re-layouts: 4.74 us -> 9.34 us
    reshape x2 -> x7, local copies, waits for them, and re-layouts: 1.75 us -> 3.62 us  [the longest x1 1.64 us: shards(): own_slot.reshape(owner_count, slot_count, padded_width)]
    all_to_all x1, waiting for transfers between devices: 5.59 us -> 3.79 us  [shards(): lax.all_to_all(picked, both, split_axis=0, concat_axis=0, tiled=True)]
    reshape x4 -> x3, local copies, waits for them, and re-layouts: 2.99 us -> 1.59 us  [unpadded_halves(): rows.reshape(count, 2, lanes_of(half_width))[:, :, :half_width]]
    convert_element_type x1 -> x0, other arithmetic: 1.03 us -> none  [shards(): outgoing.astype(jnp.bfloat16)]
    reshape x2 -> x3, local copies, waits for them, and re-layouts: 0.98 us -> 1.92 us  [padded_halves(): rows.reshape(count, 2, half_width)]
    all_to_all x1, waiting for transfers between devices: 0.84 us -> 0.01 us  [shards(): lax.all_to_all(wanted, both, split_axis=0, concat_axis=0, tiled=True)]
    reshape x2, local copies, waits for them, and re-layouts: 1.59 us -> 0.92 us  [block_chains(): word_ids.reshape(-1, 1)]
  transfers between devices with their start and end apart: 5 -> 5, of which waited for: 3 -> 2; matrix products, arithmetic and copies ran while one was open for 24% -> 28% of each run, Pallas kernels for 6% -> 6%
where the time goes in v7:
time: 63.5 us; the launch traced here: 62.9 us
  local copies, waits for them, and re-layouts  29.7 us (47%)
  starting transfers between devices  17.7 us (28%)
  Pallas kernels  7.8 us (12%)
  waiting for transfers between devices  4.37 us (7%)
  other arithmetic  1.91 us (3%)
  between operations  0.99 us (2%)
    unnamed x50, local copies, waits for them, and re-layouts  9.34 us
    pallas_call x2, Pallas kernels, block_chains(): pl.pallas_call(body, out_shape=(jax.ShapeDtypeStruct((parts, width), jnp....  7.8 us
    all_to_all x1, starting transfers between devices, shards(): lax.all_to_all(wanted, both, split_axis=0, concat_axis=0, tiled=True)  7.3 us
    all_to_all x1, starting transfers between devices, shards(): lax.all_to_all(picked, both, split_axis=0, concat_axis=0, tiled=True)  4.63 us
    all_to_all x1, waiting for transfers between devices, shards(): lax.all_to_all(picked, both, split_axis=0, concat_axis=0, tiled=True)  3.79 us
    all_to_all x1, starting transfers between devices, shards(): lax.all_to_all(own_slot.reshape(owner_count, slot_count, padded_width), b...  3.61 us
    slice x3, local copies, waits for them, and re-layouts, unpadded_halves(): rows.reshape(count, 2, lanes_of(half_width))[:, :, :half_width]  2.25 us
    ppermute x2, starting transfers between devices, passed_along(): lax.ppermute(shard, axis, [(i, (i + by) % length) for i in range(length)])  2.14 us
  transfers between devices with their start and end apart: 5, of which 2 were waited for; matrix products, arithmetic and copies ran while one was open for 28% of the time, Pallas kernels for 6%

profile of v7, /device:TPU:0, one launch (start us, length us, event | category | flops | bytes accessed | tf_op | source)
XLA Modules:
  0.0 62.9 jit_solution(1158379887793552631)
XLA Ops:
  0.6 1.4 %copy.100 = s32[1,1,16,2,2]{4,3,2,1,0:T(2,128)} copy(s32[1,1,16,2,2]{2,4,3,1,0:T(2,128)} %param.16) | data formatting | bytes 512 | tf_op jit(solution)/shard_map/all_to_all | solution.py:212
  2.0 7.3 %all-to-all-start = ((s32[32,1,2]{2,1,0:T(1,128)}), s32[32,1,2]{2,1,0:T(1,128)S(1)}, u32[]{:S(2)}, u32[]{:S(2)}) async-start(s32[32,1,2]{2,1,0:T(1,128)} %bitcast.6), calls=%async_computation | async-start | bytes 32768 | tf_op jit(solution)/shard_map/all_to_all | solution.py:212
  10.0 1.8 %collective-permute-start = (s32[1792]{0:T(1024)S(1)}, s32[1792]{0:T(1024)S(1)}, u32[]{:S(2)}, u32[]{:S(2)}) collective-permute-start(s32[1792]{0:T(1024)S(1)} %pad_add_fusion.1), channel_id=1, source_target_pairs={{0,1},{1,0},{2,3},{3,2},{4,5},{5,4},{6,7},{7,6},{8,9},{9,8},{10,11... | collective-permute-start | bytes 21512 | tf_op jit(solution)/shard_map/ppermute | solution.py:12
  12.4 0.6 fusion.9.ocol
  13.1 0.9 %reshape.226 = bf16[32,2,400]{2,1,0:T(2,128)(2,1)S(1)} reshape(bf16[32,800]{1,0:T(8,128)(2,1)} %param.11) | data formatting | bytes 102400 | tf_op jit(solution)/shard_map/reshape | solution.py:163
  16.1 0.8 %copy.86.ccol = s32[256,1]{1,0:T(8,128)} copy(s32[256,1]{0,1:T(1,128)S(1)} %get-tuple-element.31) | data formatting | bytes 2048 | tf_op jit(solution)/shard_map/reshape | solution.py:141
  17.2 0.7 %reshape.250.live = f32[64,1]{1,0:T(8,128)} reshape(f32[32,2]{1,0:T(8,128)S(1)} %get-tuple-element.36) | data formatting | bytes 512 | tf_op jit(solution)/shard_map/convert_element_type | solution.py:223
  19.2 0.8 %reshape.228 = bf16[32,4,1024]{2,1,0:T(4,128)(2,1)} reshape(bf16[128,1024]{1,0:T(8,128)(2,1)S(1)} %convolution_convert_fusion) | data formatting | bytes 524288 | tf_op jit(solution)/shard_map/reshape | solution.py:218
  20.1 4.6 %all-to-all-start.1 = ((bf16[32,4,1024]{2,1,0:T(4,128)(2,1)}), bf16[32,4,1024]{2,1,0:T(4,128)(2,1)S(1)}, u32[]{:S(2)}, u32[]{:S(2)}) async-start(bf16[32,4,1024]{2,1,0:T(4,128)(2,1)} %reshape.228), calls=%async_computation.1 | async-start | bytes 524288 | tf_op jit(solution)/shard_map/all_to_all | solution.py:219
  25.8 0.6 eq.38
  26.6 0.8 %copy.87.scol = s32[256,1]{1,0:T(8,128)} copy(s32[256,1]{0,1:T(1,128)S(1)} %get-tuple-element.34) | data formatting | bytes 2048 | tf_op jit(solution)/shard_map/reshape | solution.py:143
  27.4 0.8 %copy.92.scol = s32[256,1]{1,0:T(8,128)} copy(s32[256,1]{0,1:T(1,128)S(1)} %get-tuple-element.33) | data formatting | bytes 2048 | tf_op jit(solution)/shard_map/reshape | solution.py:143
  28.7 0.8 %copy.90.wcol = s32[256,1]{1,0:T(8,128)} copy(s32[256,1]{0,1:T(1,128)S(1)} %get-tuple-element.24) | data formatting | bytes 2048 | tf_op jit(solution)/shard_map/reshape | solution.py:139
  29.5 0.8 %copy.91.ccol = s32[256,1]{1,0:T(8,128)} copy(s32[256,1]{0,1:T(1,128)S(1)} %get-tuple-element.25) | data formatting | bytes 2048 | tf_op jit(solution)/shard_map/reshape | solution.py:141
  31.6 3.8 %all-to-all-done.1 = bf16[32,4,1024]{2,1,0:T(4,128)(2,1)S(1)} async-done(((bf16[32,4,1024]{2,1,0:T(4,128)(2,1)}), bf16[32,4,1024]{2,1,0:T(4,128)(2,1)S(1)}, u32[]{:S(2)}, u32[]{:S(2)}) %all-to-all-start.1) | async-done | bytes 262176 | tf_op jit(solution)/shard_map/all_to_all | solution.py:219
  35.5 0.7 %copy-done.11 = s32[256]{0:T(256)S(1)} copy-done((s32[256]{0:T(256)S(1)}, s32[256]{0:T(256)}, u32[]{:S(2)}) %copy-start.11) | copy-done | bytes 1048
  36.1 0.9 %copy-done.2 = s32[256,1]{1,0:T(8,128)S(1)} copy-done((s32[256,1]{1,0:T(8,128)S(1)}, s32[256,1]{1,0:T(8,128)}, u32[]{:S(2)}) %copy-start.2) | copy-done | bytes 1048
  37.0 0.9 %copy-done.6 = s32[256,1]{1,0:T(8,128)S(1)} copy-done((s32[256,1]{1,0:T(8,128)S(1)}, s32[256,1]{1,0:T(8,128)}, u32[]{:S(2)}) %copy-start.6) | copy-done | bytes 1048
  37.9 0.8 %copy-done.7 = s32[64,1]{1,0:T(8,128)S(1)} copy-done((s32[64,1]{1,0:T(8,128)S(1)}, s32[64,1]{1,0:T(8,128)}, u32[]{:S(2)}) %copy-start.7) | copy-done | bytes 280
  38.7 0.8 %copy-done.8 = f32[64,1]{1,0:T(8,128)S(1)} copy-done((f32[64,1]{1,0:T(8,128)S(1)}, f32[64,1]{1,0:T(8,128)}, u32[]{:S(2)}) %copy-start.8) | copy-done | bytes 280
  39.5 0.7 %copy-done.13 = s32[1,256]{1,0:T(1,128)S(1)} copy-done((s32[1,256]{1,0:T(1,128)S(1)}, s32[1,256]{1,0:T(1,128)}, u32[]{:S(2)}) %copy-start.13) | copy-done | bytes 1048
  40.1 0.6 copy-done.14
  40.7 4.0 %shard_map.112 = (f32[256,1024]{1,0:T(8,128)S(1)}, f32[256,1024]{1,0:T(8,128)S(1)}, bf16[64,1024]{1,0:T(8,128)(2,1)S(1)}) custom-call(s32[256,1]{1,0:T(8,128)S(1)} %copy.85.wcol, s32[1,256]{1,0:T(1,128)S(1)} %copy-done.14, s32[256,1]{1,0:T(8,128)S(1)} %copy-done.2, s32[1,256]{1,0:T(1,128)S(1)} %copy-done.13, s32[256,1]{1,0:T(8,128)S(1)} %copy-done.6, ...), custom_call_target="tpu_custom_call" | custom-call | tf_op jit(solution)/shard_map/pallas_call | solution.py:130
  44.8 1.0 %copy-done = f32[256,1024]{1,0:T(8,128)} copy-done((f32[256,1024]{1,0:T(8,128)}, f32[256,1024]{1,0:T(8,128)S(1)}, u32[]{:S(2)}) %copy-start) | copy-done | bytes 1048600
  45.8 0.7 %copy-done.9 = bf16[64,1024]{1,0:T(8,128)(2,1)} copy-done((bf16[64,1024]{1,0:T(8,128)(2,1)}, bf16[64,1024]{1,0:T(8,128)(2,1)S(1)}, u32[]{:S(2)}) %copy-start.9) | copy-done | bytes 131096
  46.4 1.6 %reshape.243 = bf16[32,2,1024]{2,1,0:T(2,128)(2,1)} reshape(bf16[64,1024]{1,0:T(8,128)(2,1)} %copy-done.9) | data formatting | bytes 262144 | tf_op jit(solution)/shard_map/reshape | solution.py:242
  48.1 3.6 %all-to-all-start.2 = ((bf16[32,2,1024]{2,1,0:T(2,128)(2,1)}), bf16[32,2,1024]{2,1,0:T(2,128)(2,1)}, u32[]{:S(2)}, u32[]{:S(2)}) async-start(bf16[32,2,1024]{2,1,0:T(2,128)(2,1)} %reshape.243), calls=%async_computation.2 | async-start | bytes 262144 | tf_op jit(solution)/shard_map/all_to_all | solution.py:241
  52.4 3.8 %shard_map.113 = (f32[256,1024]{1,0:T(8,128)S(1)}, f32[256,1024]{1,0:T(8,128)S(1)}, bf16[8,1024]{1,0:T(8,128)(2,1)}) custom-call(s32[256,1]{1,0:T(8,128)S(1)} %copy-done.4, s32[1,256]{1,0:T(1,128)S(1)} %copy-done.16, s32[256,1]{1,0:T(8,128)S(1)} %copy-done.5, s32[1,256]{1,0:T(1,128)S(1)} %copy-done.15, s32[256,1]{1,0:T(8,128)S(1)} %copy-done.3, ...), custom_call_target="tpu_custom_call" | custom-call | tf_op jit(solution)/shard_map/pallas_call | solution.py:130
  57.0 1.1 %copy.96 = bf16[256,2,400]{0,2,1:T(8,128)(2,1)} copy(bf16[256,2,400]{2,1,0:T(2,128)(2,1)S(1)} %bitcast.55) | data formatting | bytes 819200 | tf_op jit(solution)/shard_map/slice | solution.py:169
  58.5 1.1 %copy.97 = bf16[256,2,400]{0,2,1:T(8,128)(2,1)} copy(bf16[256,2,400]{2,1,0:T(2,128)(2,1)S(1)} %bitcast.56) | data formatting | bytes 819200 | tf_op jit(solution)/shard_map/slice | solution.py:169
  60.1 1.0 %reshape.244 = bf16[64,1024]{1,0:T(8,128)(2,1)S(1)} reshape(bf16[32,2,1024]{2,1,0:T(2,128)(2,1)} %all-to-all-done.2) | data formatting | bytes 262144 | tf_op jit(solution)/shard_map/reshape | solution.py:253
  62.0 0.8 %reshape.245 = f32[32,800]{1,0:T(8,128)} reshape(f32[32,2,400]{2,1,0:T(2,128)S(1)} %copy.99) | data formatting | bytes 204800 | tf_op jit(solution)/shard_map/reshape | solution.py:169
  (90 shorter events, 11.4 us)
Async XLA Ops:
  2.0 7.6 %copy-start.18 = (s32[1,1024]{1,0:T(1,128)S(1)}, s32[1,1024]{1,0:T(1,128)}, u32[]{:S(2)}) copy-start(s32[1,1024]{1,0:T(1,128)} %param.15) | copy-start | bytes 12292
  2.0 7.6 %copy-start.21 = (s32[256]{0:T(256)S(1)}, s32[256]{0:T(256)}, u32[]{:S(2)}) copy-start(s32[256]{0:T(256)} %param.13) | copy-start | bytes 3076
  2.0 7.6 %copy-start.22 = (s32[256]{0:T(256)S(1)}, s32[256]{0:T(256)}, u32[]{:S(2)}) copy-start(s32[256]{0:T(256)} %param.12) | copy-start | bytes 3076
  2.0 16.0 %all-to-all-start = ((s32[32,1,2]{2,1,0:T(1,128)}), s32[32,1,2]{2,1,0:T(1,128)S(1)}, u32[]{:S(2)}, u32[]{:S(2)}) async-start(s32[32,1,2]{2,1,0:T(1,128)} %bitcast.6), calls=%async_computation | async-start | bytes 32768 | tf_op jit(solution)/shard_map/all_to_all | solution.py:212
  9.3 0.7 %copy-start.10 = (s32[256]{0:T(256)S(1)}, s32[256]{0:T(256)}, u32[]{:S(2)}) copy-start(s32[256]{0:T(256)} %param.14) | copy-start | bytes 3076
  9.3 4.8 %copy-start.17 = (bf16[256,800]{0,1:T(8,128)(2,1)S(1)}, bf16[256,800]{0,1:T(8,128)(2,1)}, u32[]{:S(2)}) copy-start(bf16[256,800]{0,1:T(8,128)(2,1)} %param.9) | copy-start | bytes 1228804
  9.3 21.2 %collective-permute-start.1 = (bf16[256,800]{0,1:T(8,128)(2,1)}, bf16[256,800]{0,1:T(8,128)(2,1)S(1)}, u32[]{:S(2)}, u32[]{:S(2)}) collective-permute-start(bf16[256,800]{0,1:T(8,128)(2,1)} %param.10), channel_id=1, source_target_pairs={{0,2},{2,4},{4,6},{6,8},{8,10},{10,12},{12,14},{14,16},{16,18},{18... | collective-permute-start | bytes 1228808 | tf_op jit(solution)/shard_map/ppermute | solution.py:12
  10.0 16.5 %collective-permute-start = (s32[1792]{0:T(1024)S(1)}, s32[1792]{0:T(1024)S(1)}, u32[]{:S(2)}, u32[]{:S(2)}) collective-permute-start(s32[1792]{0:T(1024)S(1)} %pad_add_fusion.1), channel_id=1, source_target_pairs={{0,1},{1,0},{2,3},{3,2},{4,5},{5,4},{6,7},{7,6},{8,9},{9,8},{10,11... | collective-permute-start | bytes 21512 | tf_op jit(solution)/shard_map/ppermute | solution.py:12
  15.0 0.7 %copy-start.20 = (s32[1,1,16,2]{2,3,1,0:T(2,128)S(1)}, s32[1,1,16,2]{2,3,1,0:T(2,128)}, u32[]{:S(2)}) copy-start(s32[1,1,16,2]{2,3,1,0:T(2,128)} %param.17) | copy-start | bytes 388
  20.1 15.3 %all-to-all-start.1 = ((bf16[32,4,1024]{2,1,0:T(4,128)(2,1)}), bf16[32,4,1024]{2,1,0:T(4,128)(2,1)S(1)}, u32[]{:S(2)}, u32[]{:S(2)}) async-start(bf16[32,4,1024]{2,1,0:T(4,128)(2,1)} %reshape.228), calls=%async_computation.1 | async-start | bytes 524288 | tf_op jit(solution)/shard_map/all_to_all | solution.py:219
  35.4 0.7 %copy-start.11 = (s32[256]{0:T(256)S(1)}, s32[256]{0:T(256)}, u32[]{:S(2)}) copy-start(s32[256]{0:T(256)} %param.14) | copy-start | bytes 3076
  36.1 0.9 %copy-start.2 = (s32[256,1]{1,0:T(8,128)S(1)}, s32[256,1]{1,0:T(8,128)}, u32[]{:S(2)}) copy-start(s32[256,1]{1,0:T(8,128)} %copy.86.ccol) | copy-start | bytes 3076
  37.0 0.9 %copy-start.6 = (s32[256,1]{1,0:T(8,128)S(1)}, s32[256,1]{1,0:T(8,128)}, u32[]{:S(2)}) copy-start(s32[256,1]{1,0:T(8,128)} %copy.87.scol) | copy-start | bytes 3076
  37.9 0.8 %copy-start.7 = (s32[64,1]{1,0:T(8,128)S(1)}, s32[64,1]{1,0:T(8,128)}, u32[]{:S(2)}) copy-start(s32[64,1]{1,0:T(8,128)} %fusion.9.ocol) | copy-start | bytes 772
  38.7 0.8 %copy-start.8 = (f32[64,1]{1,0:T(8,128)S(1)}, f32[64,1]{1,0:T(8,128)}, u32[]{:S(2)}) copy-start(f32[64,1]{1,0:T(8,128)} %reshape.250.live) | copy-start | bytes 772
  39.5 0.7 %copy-start.13 = (s32[1,256]{1,0:T(1,128)S(1)}, s32[1,256]{1,0:T(1,128)}, u32[]{:S(2)}) copy-start(s32[1,256]{1,0:T(1,128)} %get-tuple-element.29.crow) | copy-start | bytes 3076
  40.1 0.6 copy-start.14
  44.8 1.0 %copy-start = (f32[256,1024]{1,0:T(8,128)}, f32[256,1024]{1,0:T(8,128)S(1)}, u32[]{:S(2)}) copy-start(f32[256,1024]{1,0:T(8,128)S(1)} %get-tuple-element.16) | copy-start | bytes 3145732
  45.8 0.7 %copy-start.9 = (bf16[64,1024]{1,0:T(8,128)(2,1)}, bf16[64,1024]{1,0:T(8,128)(2,1)S(1)}, u32[]{:S(2)}) copy-start(bf16[64,1024]{1,0:T(8,128)(2,1)S(1)} %get-tuple-element.18) | copy-start | bytes 393220
  46.4 5.3 %copy-start.5 = (s32[256,1]{1,0:T(8,128)S(1)}, s32[256,1]{1,0:T(8,128)}, u32[]{:S(2)}) copy-start(s32[256,1]{1,0:T(8,128)} %copy.91.ccol) | copy-start | bytes 3076
  48.1 3.7 %copy-start.3 = (s32[256,1]{1,0:T(8,128)S(1)}, s32[256,1]{1,0:T(8,128)}, u32[]{:S(2)}) copy-start(s32[256,1]{1,0:T(8,128)} %copy.92.scol) | copy-start | bytes 3076
  48.1 3.7 %copy-start.4 = (s32[256,1]{1,0:T(8,128)S(1)}, s32[256,1]{1,0:T(8,128)}, u32[]{:S(2)}) copy-start(s32[256,1]{1,0:T(8,128)} %copy.90.wcol) | copy-start | bytes 3076
  48.1 3.7 %copy-start.15 = (s32[1,256]{1,0:T(1,128)S(1)}, s32[1,256]{1,0:T(1,128)}, u32[]{:S(2)}) copy-start(s32[1,256]{1,0:T(1,128)} %get-tuple-element.23.crow) | copy-start | bytes 3076
  48.1 3.7 %copy-start.16 = (s32[1,256]{1,0:T(1,128)S(1)}, s32[1,256]{1,0:T(1,128)}, u32[]{:S(2)}) copy-start(s32[1,256]{1,0:T(1,128)} %get-tuple-element.26.wrow) | copy-start | bytes 3076
  48.1 12.0 %all-to-all-start.2 = ((bf16[32,2,1024]{2,1,0:T(2,128)(2,1)}), bf16[32,2,1024]{2,1,0:T(2,128)(2,1)}, u32[]{:S(2)}, u32[]{:S(2)}) async-start(bf16[32,2,1024]{2,1,0:T(2,128)(2,1)} %reshape.243), calls=%async_computation.2 | async-start | bytes 262144 | tf_op jit(solution)/shard_map/all_to_all | solution.py:241
  51.7 0.7 %copy-start.12 = (s32[256]{0:T(256)S(1)}, s32[256]{0:T(256)}, u32[]{:S(2)}) copy-start(s32[256]{0:T(256)} %param.14) | copy-start | bytes 3076
  52.4 3.8 %copy-start.1 = (f32[256,1024]{1,0:T(8,128)S(1)}, f32[256,1024]{1,0:T(8,128)}, u32[]{:S(2)}) copy-start(f32[256,1024]{1,0:T(8,128)} %copy-done) | copy-start | bytes 3145732
  61.1 0.6 copy-start.19

commit v8 on v7

--- a/solution.py
+++ b/solution.py
@@ -54,11 +54,6 @@
     return 1.0 / (1.0 + jnp.exp(-x))
 
 
-def _select(ids_col, total):
-    hit = ids_col == lax.broadcasted_iota(jnp.int32, (ids_col.shape[0], total), 1)
-    return jnp.where(hit, 1.0, 0.0).astype(jnp.bfloat16)
-
-
 def _select_t(ids_row, total):
     hit = ids_row == lax.broadcasted_iota(jnp.int32, (total, ids_row.shape[1]), 0)
     return jnp.where(hit, 1.0, 0.0).astype(jnp.bfloat16)
@@ -66,6 +61,11 @@
 
 def _mm(a, b):
     return jnp.dot(a, b, preferred_element_type=jnp.float32)
+
+
+def _pick(sel_t, rows):
+    return lax.dot_general(sel_t, rows, (((0,), (0,)), ((), ())),
+                           preferred_element_type=jnp.float32)
 
 
 def _spread(sel_t, terms):
@@ -75,7 +75,7 @@
 
 
 def _chain_body(groups, own_groups, block, neg_count, scale,
-                wcol, wrow, ccol, crow, scol, srow, ncol, nrow, ocol, live,
+                wrow, crow, scomb, srow, nrow, orow, live,
                 words, held, table, word_out, ctx_out, slot_out):
     parts = words.shape[0]
     rows = table.shape[0]
@@ -86,9 +86,11 @@
     slot_sum = jnp.zeros(slot_out.shape, jnp.float32)
     for g in range(groups):
         t0 = g * block
-        w = _mm(_select(wcol[t0:t0 + block, :], parts), words[...])
-        c = _mm(_select(ccol[t0:t0 + block, :], parts), held[...])
-        rv = _mm(_select(scol[t0:t0 + block, :], rows), table[...])
+        word_t = _select_t(wrow[:, t0:t0 + block], parts)
+        ctx_t = _select_t(crow[:, t0:t0 + block], parts)
+        w = _pick(word_t, words[...])
+        c = _pick(ctx_t, held[...])
+        rv = _pick(_select_t(scomb[:, t0:t0 + block], rows), table[...])
         w_re, w_im = w[:, :half], w[:, half:]
         r_re, r_im = rv[:, :half], rv[:, half:]
         q = jnp.concatenate([w_re * r_re - w_im * r_im, w_re * r_im + w_im * r_re], axis=1)
@@ -96,9 +98,8 @@
         qf = q.astype(jnp.float32)
         pos = jnp.sum(qf * c, axis=1, keepdims=True)
         dpos = -1.0 / (1.0 + jnp.exp(pos))
-        n0 = g * neg_count
-        neg_sel = _select(ncol[n0:n0 + neg_count, :], parts)
-        neg = _mm(neg_sel, held[...]).astype(jnp.bfloat16)
+        neg_t = _select_t(nrow[g:g + 1, :], parts)
+        neg = _pick(neg_t, held[...]).astype(jnp.bfloat16)
         scores = lax.dot_general(q, neg, (((1,), (1,)), ((), ())),
                                  preferred_element_type=jnp.float32)
         dneg = (_sigmoid(scores) * scale).astype(jnp.bfloat16)
@@ -108,15 +109,14 @@
             rterm = jnp.concatenate([g_re * w_re + g_im * w_im, g_im * w_re - g_re * w_im], axis=1)
             slot_sum = slot_sum + _spread(_select_t(srow[:, t0:t0 + block], slots), rterm)
         wterm = jnp.concatenate([g_re * r_re + g_im * r_im, g_im * r_re - g_re * r_im], axis=1)
-        word_out[...] += _spread(_select_t(wrow[:, t0:t0 + block], parts), wterm)
-        ctx_t = _select_t(crow[:, t0:t0 + block], parts)
-        neg_t = _select_t(nrow[g:g + 1, :], parts)
+        word_out[...] += _spread(word_t, wterm)
         neg_weight = lax.dot_general(neg_t, dneg, (((1,), (1,)), ((), ())),
                                      preferred_element_type=jnp.float32)
         ctx_out[...] += _spread(ctx_t, dpos * qf) + _spread(neg_weight, q)
     if own_groups:
-        own_rows = _mm(_select(ocol[...], rows), table[...])
-        slot_sum = slot_sum + 0.02 * live[...] * own_rows
+        hit = orow[...] == lax.broadcasted_iota(jnp.int32, (rows, orow.shape[1]), 0)
+        live_t = jnp.where(hit, live[...], 0.0).astype(jnp.bfloat16)
+        slot_sum = slot_sum + 0.02 * _pick(live_t, table[...])
     slot_out[...] = slot_sum.astype(slot_out.dtype)
 
 
@@ -136,16 +136,13 @@
         ),
         compiler_params=pltpu.CompilerParams(vmem_limit_bytes=48 * 1024 * 1024),
     )(
-        word_ids.reshape(-1, 1),
         word_ids.reshape(1, -1),
-        ctx_ids.reshape(-1, 1),
         ctx_ids.reshape(1, -1),
-        slot_ids.reshape(-1, 1),
+        slot_ids.reshape(1, -1),
         own_ids.reshape(1, -1),
-        neg_ids.reshape(-1, 1),
         neg_ids,
-        own_rows.reshape(-1, 1),
-        live_mask.reshape(-1, 1),
+        own_rows.reshape(1, -1),
+        live_mask.reshape(1, -1),
         words,
         held,
         table,

time: 63.5 us -> 58.7 us (0.924)
  local copies, waits for them, and re-layouts: 29.7 us -> 20.6 us
  waiting for transfers between devices: 4.37 us -> 9.06 us
    unnamed x50 -> x36, local copies, waits for them, and re-layouts: 9.34 us -> 4.15 us
    all_to_all x1, waiting for transfers between devices: 3.79 us -> 8.41 us  [shards(): lax.all_to_all(picked, both, split_axis=0, concat_axis=0, tiled=True)]
    reshape x12 -> x2, local copies, waits for them, and re-layouts: 4.76 us -> 1.11 us  [the longest x1 0.58 us: block_chains(): live_mask.reshape(1, -1)]
    reshape x1, local copies, waits for them, and re-layouts: 1.64 us -> 0.7 us  [shards(): own_slot.reshape(owner_count, slot_count, padded_width)]
  transfers between devices with their start and end apart: 5 -> 5, of which waited for: 2 -> 2; matrix products, arithmetic and copies ran while one was open for 28% -> 25% of each run, Pallas kernels for 6% -> 6%
where the time goes in v8:
time: 58.7 us; the launch traced here: 58.2 us
  local copies, waits for them, and re-layouts  20.6 us (35%)
  starting transfers between devices  17.6 us (30%)
  waiting for transfers between devices  9.06 us (15%)
  Pallas kernels  7.69 us (13%)
  other arithmetic  1.92 us (3%)
  between operations  0.96 us (2%)
    all_to_all x1, waiting for transfers between devices, shards(): lax.all_to_all(picked, both, split_axis=0, concat_axis=0, tiled=True)  8.41 us
    pallas_call x2, Pallas kernels, block_chains(): pl.pallas_call(body, out_shape=(jax.ShapeDtypeStruct((parts, width), jnp....  7.69 us
    all_to_all x1, starting transfers between devices, shards(): lax.all_to_all(wanted, both, split_axis=0, concat_axis=0, tiled=True)  7.3 us
    all_to_all x1, starting transfers between devices, shards(): lax.all_to_all(picked, both, split_axis=0, concat_axis=0, tiled=True)  4.91 us
    unnamed x36, local copies, waits for them, and re-layouts  4.15 us
    all_to_all x1, starting transfers between devices, shards(): lax.all_to_all(own_slot.reshape(owner_count, slot_count, padded_width), b...  3.59 us
    slice x3, local copies, waits for them, and re-layouts, unpadded_halves(): rows.reshape(count, 2, lanes_of(half_width))[:, :, :half_width]  2.25 us
    reshape x3, local copies, waits for them, and re-layouts, padded_halves(): rows.reshape(count, 2, half_width)  1.91 us
  transfers between devices with their start and end apart: 5, of which 2 were waited for; matrix products, arithmetic and copies ran while one was open for 25% of the time, Pallas kernels for 6%

profile of v8, /device:TPU:0, one launch (start us, length us, event | category | flops | bytes accessed | tf_op | source)
XLA Modules:
  0.0 58.2 jit_solution(14919639348978047901)
XLA Ops:
  0.6 1.4 %copy.64 = s32[1,1,16,2,2]{4,3,2,1,0:T(2,128)} copy(s32[1,1,16,2,2]{2,4,3,1,0:T(2,128)} %param.16) | data formatting | bytes 512 | tf_op jit(solution)/shard_map/all_to_all | solution.py:209
  2.0 7.3 %all-to-all-start = ((s32[32,1,2]{2,1,0:T(1,128)}), s32[32,1,2]{2,1,0:T(1,128)S(1)}, u32[]{:S(2)}, u32[]{:S(2)}) async-start(s32[32,1,2]{2,1,0:T(1,128)} %bitcast.2), calls=%async_computation | async-start | bytes 32768 | tf_op jit(solution)/shard_map/all_to_all | solution.py:209
  9.4 0.6 %copy-done = s32[256]{0:T(256)S(1)} copy-done((s32[256]{0:T(256)S(1)}, s32[256]{0:T(256)}, u32[]{:S(2)}) %copy-start) | copy-done | bytes 1048
  10.0 1.8 %collective-permute-start = (s32[1792]{0:T(1024)S(1)}, s32[1792]{0:T(1024)S(1)}, u32[]{:S(2)}, u32[]{:S(2)}) collective-permute-start(s32[1792]{0:T(1024)S(1)} %pad_add_fusion.1), channel_id=1, source_target_pairs={{0,1},{1,0},{2,3},{3,2},{4,5},{5,4},{6,7},{7,6},{8,9},{9,8},{10,11... | collective-permute-start | bytes 21512 | tf_op jit(solution)/shard_map/ppermute | solution.py:12
  11.9 0.6 fusion.7.orow
  12.4 0.6 fusion.14
  13.0 0.5 slice_bitcast_fusion.orow
  13.8 0.6 reshape.214.live
  14.4 0.7 %reshape.212.live = f32[1,64]{1,0:T(1,128)} reshape(f32[32,2]{1,0:T(8,128)S(1)} %get-tuple-element.28) | data formatting | bytes 512 | tf_op jit(solution)/shard_map/convert_element_type | solution.py:220
  15.1 0.9 %reshape.196 = bf16[32,2,400]{2,1,0:T(2,128)(2,1)S(1)} reshape(bf16[32,800]{1,0:T(8,128)(2,1)} %param.11) | data formatting | bytes 102400 | tf_op jit(solution)/shard_map/reshape | solution.py:160
  18.4 0.5 broadcast.114
  18.9 0.7 %reduce.3 = s32[32,2]{1,0:T(8,128)S(1)} reduce(s32[32,1,2]{2,1,0:T(1,128)S(1)} %all-to-all-done, s32[]{:T(128)} %broadcast.114), dimensions={1}, to_apply=%all_to_all.13.reduce_sub_computation.3 | reduce | bytes 516 | tf_op jit(solution)/shard_map/all_to_all | solution.py:209
  19.6 0.7 %eq.38 = s32[64]{0:T(128)} reshape(s32[32,2]{1,0:T(8,128)S(1)} %reduce.3) | data formatting | bytes 512 | tf_op jit(solution)/shard_map/eq | solution.py:245
  20.2 0.8 %reshape.198 = bf16[32,4,1024]{2,1,0:T(4,128)(2,1)} reshape(bf16[128,1024]{1,0:T(8,128)(2,1)S(1)} %convolution_convert_fusion) | data formatting | bytes 524288 | tf_op jit(solution)/shard_map/reshape | solution.py:215
  21.0 4.9 %all-to-all-start.1 = ((bf16[32,4,1024]{2,1,0:T(4,128)(2,1)}), bf16[32,4,1024]{2,1,0:T(4,128)(2,1)S(1)}, u32[]{:S(2)}, u32[]{:S(2)}) async-start(bf16[32,4,1024]{2,1,0:T(4,128)(2,1)} %reshape.198), calls=%async_computation.1 | async-start | bytes 524288 | tf_op jit(solution)/shard_map/all_to_all | solution.py:216
  26.0 0.6 %fusion.13 = (s32[1,256]{1,0:T(1,128)}, s32[1,256]{1,0:T(1,128)}) fusion(s32[1,1792]{1,0:T(1,128)S(1)} %stack.19), kind=kLoop, calls=%fused_computation.40 | loop fusion | bytes 4096 | tf_op jit(solution)/shard_map/slice | solution.py:233
  26.7 0.6 fusion.15
  28.2 8.4 %all-to-all-done.1 = bf16[32,4,1024]{2,1,0:T(4,128)(2,1)S(1)} async-done(((bf16[32,4,1024]{2,1,0:T(4,128)(2,1)}), bf16[32,4,1024]{2,1,0:T(4,128)(2,1)S(1)}, u32[]{:S(2)}, u32[]{:S(2)}) %all-to-all-start.1) | async-done | bytes 262176 | tf_op jit(solution)/shard_map/all_to_all | solution.py:216
  36.7 0.7 %copy-done.1 = s32[1,256]{1,0:T(1,128)S(1)} copy-done((s32[1,256]{1,0:T(1,128)S(1)}, s32[1,256]{1,0:T(1,128)}, u32[]{:S(2)}) %copy-start.1) | copy-done | bytes 1048
  37.4 0.7 %copy-done.5 = s32[1,256]{1,0:T(1,128)S(1)} copy-done((s32[1,256]{1,0:T(1,128)S(1)}, s32[1,256]{1,0:T(1,128)}, u32[]{:S(2)}) %copy-start.5) | copy-done | bytes 1048
  38.1 0.6 %copy-done.9 = s32[1,64]{1,0:T(1,128)S(1)} copy-done((s32[1,64]{1,0:T(1,128)S(1)}, s32[1,64]{1,0:T(1,128)}, u32[]{:S(2)}) %copy-start.9) | copy-done | bytes 280
  38.7 4.0 %shard_map.112 = (f32[256,1024]{1,0:T(8,128)S(1)}, f32[256,1024]{1,0:T(8,128)S(1)}, bf16[64,1024]{1,0:T(8,128)(2,1)S(1)}) custom-call(s32[1,256]{1,0:T(1,128)S(1)} %copy-done.1, s32[1,256]{1,0:T(1,128)S(1)} %get-tuple-element.23.crow, s32[1,256]{1,0:T(1,128)S(1)} %copy-done.5, s32[1,256]{1,0:T(1,128)S(1)} %bitcast.37, s32[1,1024]{1,0:T(1,128)S(1)} %slice.95.nrow, ...), custom_call_target="tpu_custom_call" | custom-call | tf_op jit(solution)/shard_map/pallas_call | solution.py:130
  42.7 0.7 %reshape.209 = bf16[32,2,1024]{2,1,0:T(2,128)(2,1)} reshape(bf16[64,1024]{1,0:T(8,128)(2,1)S(1)} %get-tuple-element.18) | data formatting | bytes 262144 | tf_op jit(solution)/shard_map/reshape | solution.py:239
  43.4 3.6 %all-to-all-start.2 = ((bf16[32,2,1024]{2,1,0:T(2,128)(2,1)}), bf16[32,2,1024]{2,1,0:T(2,128)(2,1)}, u32[]{:S(2)}, u32[]{:S(2)}) async-start(bf16[32,2,1024]{2,1,0:T(2,128)(2,1)} %reshape.209), calls=%async_computation.2 | async-start | bytes 262144 | tf_op jit(solution)/shard_map/all_to_all | solution.py:238
  47.1 0.6 %copy-done.2 = s32[1,256]{1,0:T(1,128)S(1)} copy-done((s32[1,256]{1,0:T(1,128)S(1)}, s32[1,256]{1,0:T(1,128)}, u32[]{:S(2)}) %copy-start.2) | copy-done | bytes 1048
  47.7 3.7 %shard_map.113 = (f32[256,1024]{1,0:T(8,128)S(1)}, f32[256,1024]{1,0:T(8,128)S(1)}, bf16[8,1024]{1,0:T(8,128)(2,1)}) custom-call(s32[1,256]{1,0:T(1,128)S(1)} %copy-done.3, s32[1,256]{1,0:T(1,128)S(1)} %copy-done.2, s32[1,256]{1,0:T(1,128)S(1)} %copy-done.4, s32[1,256]{1,0:T(1,128)S(1)} %bitcast.38, s32[1,1024]{1,0:T(1,128)S(1)} %slice.101.nrow, ...), custom_call_target="tpu_custom_call" | custom-call | tf_op jit(solution)/shard_map/pallas_call | solution.py:130
  52.3 1.1 %copy.61 = bf16[256,2,400]{0,2,1:T(8,128)(2,1)} copy(bf16[256,2,400]{2,1,0:T(2,128)(2,1)S(1)} %bitcast.39) | data formatting | bytes 819200 | tf_op jit(solution)/shard_map/slice | solution.py:166
  53.7 1.1 %copy.60 = bf16[256,2,400]{0,2,1:T(8,128)(2,1)} copy(bf16[256,2,400]{2,1,0:T(2,128)(2,1)S(1)} %bitcast.40) | data formatting | bytes 819200 | tf_op jit(solution)/shard_map/slice | solution.py:166
  54.8 0.6 %all-to-all-done.2 = bf16[32,2,1024]{2,1,0:T(2,128)(2,1)} async-done(((bf16[32,2,1024]{2,1,0:T(2,128)(2,1)}), bf16[32,2,1024]{2,1,0:T(2,128)(2,1)}, u32[]{:S(2)}, u32[]{:S(2)}) %all-to-all-start.2) | async-done | bytes 131104 | tf_op jit(solution)/shard_map/all_to_all | solution.py:238
  55.4 1.0 %reshape.210 = bf16[64,1024]{1,0:T(8,128)(2,1)S(1)} reshape(bf16[32,2,1024]{2,1,0:T(2,128)(2,1)} %all-to-all-done.2) | data formatting | bytes 262144 | tf_op jit(solution)/shard_map/reshape | solution.py:250
  56.5 0.7 %copy-done.12 = s32[64]{0:T(128)S(1)} copy-done((s32[64]{0:T(128)S(1)}, s32[64]{0:T(128)}, u32[]{:S(2)}) %copy-start.12) | copy-done | bytes 280
  57.4 0.8 %reshape.211 = f32[32,800]{1,0:T(8,128)} reshape(f32[32,2,400]{2,1,0:T(2,128)S(1)} %copy.63) | data formatting | bytes 204800 | tf_op jit(solution)/shard_map/reshape | solution.py:166
  (67 shorter events, 5.3 us)
Async XLA Ops:
  2.0 7.3 %copy-start.11 = (s32[1,1024]{1,0:T(1,128)S(1)}, s32[1,1024]{1,0:T(1,128)}, u32[]{:S(2)}) copy-start(s32[1,1024]{1,0:T(1,128)} %param.15) | copy-start | bytes 12292
  2.0 7.4 %copy-start.14 = (s32[256]{0:T(256)S(1)}, s32[256]{0:T(256)}, u32[]{:S(2)}) copy-start(s32[256]{0:T(256)} %param.13) | copy-start | bytes 3076
  2.0 7.4 %copy-start.15 = (s32[256]{0:T(256)S(1)}, s32[256]{0:T(256)}, u32[]{:S(2)}) copy-start(s32[256]{0:T(256)} %param.12) | copy-start | bytes 3076
  2.0 11.5 %copy-start.13 = (s32[1,1,16,2]{2,3,1,0:T(2,128)S(1)}, s32[1,1,16,2]{2,3,1,0:T(2,128)}, u32[]{:S(2)}) copy-start(s32[1,1,16,2]{2,3,1,0:T(2,128)} %param.17) | copy-start | bytes 388
  2.0 15.1 %all-to-all-start = ((s32[32,1,2]{2,1,0:T(1,128)}), s32[32,1,2]{2,1,0:T(1,128)S(1)}, u32[]{:S(2)}, u32[]{:S(2)}) async-start(s32[32,1,2]{2,1,0:T(1,128)} %bitcast.2), calls=%async_computation | async-start | bytes 32768 | tf_op jit(solution)/shard_map/all_to_all | solution.py:209
  9.3 0.7 %copy-start = (s32[256]{0:T(256)S(1)}, s32[256]{0:T(256)}, u32[]{:S(2)}) copy-start(s32[256]{0:T(256)} %param.14) | copy-start | bytes 3076
  9.3 6.8 %copy-start.10 = (bf16[256,800]{0,1:T(8,128)(2,1)S(1)}, bf16[256,800]{0,1:T(8,128)(2,1)}, u32[]{:S(2)}) copy-start(bf16[256,800]{0,1:T(8,128)(2,1)} %param.9) | copy-start | bytes 1228804
  10.0 16.0 %collective-permute-start = (s32[1792]{0:T(1024)S(1)}, s32[1792]{0:T(1024)S(1)}, u32[]{:S(2)}, u32[]{:S(2)}) collective-permute-start(s32[1792]{0:T(1024)S(1)} %pad_add_fusion.1), channel_id=1, source_target_pairs={{0,1},{1,0},{2,3},{3,2},{4,5},{5,4},{6,7},{7,6},{8,9},{9,8},{10,11... | collective-permute-start | bytes 21512 | tf_op jit(solution)/shard_map/ppermute | solution.py:12
  11.8 15.4 %collective-permute-start.1 = (bf16[256,800]{0,1:T(8,128)(2,1)}, bf16[256,800]{0,1:T(8,128)(2,1)S(1)}, u32[]{:S(2)}, u32[]{:S(2)}) collective-permute-start(bf16[256,800]{0,1:T(8,128)(2,1)} %param.10), channel_id=1, source_target_pairs={{0,2},{2,4},{4,6},{6,8},{8,10},{10,12},{12,14},{14,16},{16,18},{18... | collective-permute-start | bytes 1228808 | tf_op jit(solution)/shard_map/ppermute | solution.py:12
  21.0 15.6 %all-to-all-start.1 = ((bf16[32,4,1024]{2,1,0:T(4,128)(2,1)}), bf16[32,4,1024]{2,1,0:T(4,128)(2,1)S(1)}, u32[]{:S(2)}, u32[]{:S(2)}) async-start(bf16[32,4,1024]{2,1,0:T(4,128)(2,1)} %reshape.198), calls=%async_computation.1 | async-start | bytes 524288 | tf_op jit(solution)/shard_map/all_to_all | solution.py:216
  36.7 0.7 %copy-start.1 = (s32[1,256]{1,0:T(1,128)S(1)}, s32[1,256]{1,0:T(1,128)}, u32[]{:S(2)}) copy-start(s32[1,256]{1,0:T(1,128)} %get-tuple-element.24.wrow) | copy-start | bytes 3076
  36.7 0.7 %copy-start.7 = (f32[1,64]{1,0:T(1,128)S(1)}, f32[1,64]{1,0:T(1,128)}, u32[]{:S(2)}) copy-start(f32[1,64]{1,0:T(1,128)} %reshape.212.live) | copy-start | bytes 772
  37.4 0.7 %copy-start.5 = (s32[1,256]{1,0:T(1,128)S(1)}, s32[1,256]{1,0:T(1,128)}, u32[]{:S(2)}) copy-start(s32[1,256]{1,0:T(1,128)} %get-tuple-element.26.scomb) | copy-start | bytes 3076
  38.1 0.6 %copy-start.9 = (s32[1,64]{1,0:T(1,128)S(1)}, s32[1,64]{1,0:T(1,128)}, u32[]{:S(2)}) copy-start(s32[1,64]{1,0:T(1,128)} %fusion.7.orow) | copy-start | bytes 772
  43.4 3.6 %copy-start.3 = (s32[1,256]{1,0:T(1,128)S(1)}, s32[1,256]{1,0:T(1,128)}, u32[]{:S(2)}) copy-start(s32[1,256]{1,0:T(1,128)} %get-tuple-element.22.wrow) | copy-start | bytes 3076
  43.4 3.6 %copy-start.4 = (s32[1,256]{1,0:T(1,128)S(1)}, s32[1,256]{1,0:T(1,128)}, u32[]{:S(2)}) copy-start(s32[1,256]{1,0:T(1,128)} %get-tuple-element.25.scomb) | copy-start | bytes 3076
  43.4 3.6 %copy-start.8 = (s32[1,8]{1,0:T(1,128)S(1)}, s32[1,8]{1,0:T(1,128)}, u32[]{:S(2)}) copy-start(s32[1,8]{1,0:T(1,128)} %slice_bitcast_fusion.orow) | copy-start | bytes 100
  43.4 12.0 %all-to-all-start.2 = ((bf16[32,2,1024]{2,1,0:T(2,128)(2,1)}), bf16[32,2,1024]{2,1,0:T(2,128)(2,1)}, u32[]{:S(2)}, u32[]{:S(2)}) async-start(bf16[32,2,1024]{2,1,0:T(2,128)(2,1)} %reshape.209), calls=%async_computation.2 | async-start | bytes 262144 | tf_op jit(solution)/shard_map/all_to_all | solution.py:238
  47.0 0.7 %copy-start.2 = (s32[1,256]{1,0:T(1,128)S(1)}, s32[1,256]{1,0:T(1,128)}, u32[]{:S(2)}) copy-start(s32[1,256]{1,0:T(1,128)} %get-tuple-element.21.crow) | copy-start | bytes 3076
  47.0 0.7 %copy-start.6 = (f32[1,8]{1,0:T(1,128)S(1)}, f32[1,8]{1,0:T(1,128)}, u32[]{:S(2)}) copy-start(f32[1,8]{1,0:T(1,128)} %reshape.214.live) | copy-start | bytes 100
  56.5 0.7 %copy-start.12 = (s32[64]{0:T(128)S(1)}, s32[64]{0:T(128)}, u32[]{:S(2)}) copy-start(s32[64]{0:T(128)} %eq.38) | copy-start | bytes 772

commit v9 on v8

--- a/solution.py
+++ b/solution.py
@@ -210,9 +210,9 @@
     lists = incoming.reshape(part_count, split_count, slot_count)
     served = jnp.stack([jnp.roll(lists, -j, axis=1) for j in range(split_count)], axis=2)
     padded_width = 2 * lanes_of(half_width)
-    picked = pick_rows(
-        one_hot(served.reshape(-1), owned_rows), padded_halves(relations, half_width)
-    ).astype(jnp.bfloat16).reshape(owner_count, split_count * slot_count, padded_width)
+    picked = pick_rows(one_hot(served.reshape(-1), owned_rows), relations).astype(
+        jnp.bfloat16
+    ).reshape(owner_count, split_count * slot_count, row_width)
     fetched = lax.all_to_all(picked, both, split_axis=0, concat_axis=0, tiled=True)
     live_mask = (
         (jnp.arange(slot_count)[None, :] < counts[0, 0].reshape(owner_count)[:, None])
@@ -224,7 +224,7 @@
     word_table = padded_halves(words, half_width)
     held_table = padded_halves(held_rows, half_width)
     fetched, word_table, held_table = lax.optimization_barrier((fetched, word_table, held_table))
-    rel_table = fetched.reshape(split_count * slot_total, padded_width)
+    rel_table = padded_halves(fetched.reshape(split_count * slot_total, row_width), half_width)
     own_word, own_ctx, own_slot = block_chains(
         word_ids[:trips], ctx_ids[:trips], slot_ids[:trips], rel_slot, neg_ids[:block_count],
         block_count, neg_scale, word_table, held_table, rel_table, own_rows, live_mask,

time: 58.7 us -> 54.8 us (0.934)
  local copies, waits for them, and re-layouts: 20.6 us -> 16 us
  waiting for transfers between devices: 9.06 us -> 11.9 us
  starting transfers between devices: 17.6 us -> 16 us
    unnamed x36 -> x18, local copies, waits for them, and re-layouts: 4.15 us -> 2.22 us
    all_to_all x1, waiting for transfers between devices: 0.01 us -> 1.53 us  [shards(): lax.all_to_all(wanted, both, split_axis=0, concat_axis=0, tiled=True)]
    all_to_all x1, starting transfers between devices: 4.91 us -> 3.38 us  [shards(): lax.all_to_all(picked, both, split_axis=0, concat_axis=0, tiled=True)]
    reshape x1, local copies, waits for them, and re-layouts: 0.7 us -> 1.62 us  [shards(): own_slot.reshape(owner_count, slot_count, padded_width)]
    all_to_all x1, waiting for transfers between devices: 0.64 us -> 1.31 us  [shards(): lax.all_to_all(own_slot.reshape(owner_count, slot_count, padded_width), b...]
    all_to_all x1, waiting for transfers between devices: 8.41 us -> 9.03 us  [shards(): lax.all_to_all(picked, both, split_axis=0, concat_axis=0, tiled=True)]
    convert_element_type x1, local copies, waits for them, and re-layouts: 0.7 us -> 0.11 us  [shards(): live_mask = (jnp.arange(slot_count)[None, :] < counts[0, 0].reshape(owner...]
    reshape x3 -> x2, local copies, waits for them, and re-layouts: 1.91 us -> 1.81 us  [padded_halves(): rows.reshape(count, 2, half_width)]
  transfers between devices with their start and end apart: 5 -> 5, of which waited for: 2 -> 3; matrix products, arithmetic and copies ran while one was open for 25% -> 19% of each run, Pallas kernels for 6% -> 7%
where the time goes in v9:
time: 54.8 us; the launch traced here: 54.4 us
  local copies, waits for them, and re-layouts  16 us (29%)
  starting transfers between devices  16 us (29%)
  waiting for transfers between devices  11.9 us (22%)
  Pallas kernels  7.7 us (14%)
  other arithmetic  1.37 us (2%)
  between operations  0.95 us (2%)
    all_to_all x1, waiting for transfers between devices, shards(): lax.all_to_all(picked, both, split_axis=0, concat_axis=0, tiled=True)  9.03 us
    pallas_call x2, Pallas kernels, block_chains(): pl.pallas_call(body, out_shape=(jax.ShapeDtypeStruct((parts, width), jnp....  7.7 us
    all_to_all x1, starting transfers between devices, shards(): lax.all_to_all(wanted, both, split_axis=0, concat_axis=0, tiled=True)  7.3 us
    all_to_all x1, starting transfers between devices, shards(): lax.all_to_all(own_slot.reshape(owner_count, slot_count, padded_width), b...  3.47 us
    all_to_all x1, starting transfers between devices, shards(): lax.all_to_all(picked, both, split_axis=0, concat_axis=0, tiled=True)  3.38 us
    slice x3, local copies, waits for them, and re-layouts, unpadded_halves(): rows.reshape(count, 2, lanes_of(half_width))[:, :, :half_width]  2.25 us
    unnamed x18, local copies, waits for them, and re-layouts  2.22 us
    all_to_all x2, local copies, waits for them, and re-layouts, shards(): lax.all_to_all(wanted, both, split_axis=0, concat_axis=0, tiled=True)  1.9 us
  transfers between devices with their start and end apart: 5, of which 3 were waited for; matrix products, arithmetic and copies ran while one was open for 19% of the time, Pallas kernels for 7%

profile of v9, /device:TPU:0, one launch (start us, length us, event | category | flops | bytes accessed | tf_op | source)
XLA Modules:
  0.0 54.4 jit_solution(13437760794301580196)
XLA Ops:
  0.6 1.4 %copy.68 = s32[1,1,16,2,2]{4,3,2,1,0:T(2,128)} copy(s32[1,1,16,2,2]{2,4,3,1,0:T(2,128)} %param.16) | data formatting | bytes 512 | tf_op jit(solution)/shard_map/all_to_all | solution.py:209
  2.0 7.3 %all-to-all-start = ((s32[32,1,2]{2,1,0:T(1,128)}), s32[32,1,2]{2,1,0:T(1,128)S(1)}, u32[]{:S(2)}, u32[]{:S(2)}) async-start(s32[32,1,2]{2,1,0:T(1,128)} %bitcast.2), calls=%async_computation | async-start | bytes 32768 | tf_op jit(solution)/shard_map/all_to_all | solution.py:209
  9.4 0.6 %copy-done.2 = s32[256]{0:T(256)S(1)} copy-done((s32[256]{0:T(256)S(1)}, s32[256]{0:T(256)}, u32[]{:S(2)}) %copy-start.2) | copy-done | bytes 1048
  10.0 1.8 %collective-permute-start = (s32[1792]{0:T(1024)S(1)}, s32[1792]{0:T(1024)S(1)}, u32[]{:S(2)}, u32[]{:S(2)}) collective-permute-start(s32[1792]{0:T(1024)S(1)} %pad_add_fusion.1), channel_id=1, source_target_pairs={{0,1},{1,0},{2,3},{3,2},{4,5},{5,4},{6,7},{7,6},{8,9},{9,8},{10,11... | collective-permute-start | bytes 21512 | tf_op jit(solution)/shard_map/ppermute | solution.py:12
  12.0 0.7 %copy-done.4 = s32[1,1,16,2]{2,3,1,0:T(2,128)S(1)} copy-done((s32[1,1,16,2]{2,3,1,0:T(2,128)S(1)}, s32[1,1,16,2]{2,3,1,0:T(2,128)}, u32[]{:S(2)}) %copy-start.4) | copy-done | bytes 152
  13.1 1.3 %copy.62 = bf16[256,2,400]{2,1,0:T(2,128)(2,1)S(1)} copy(bf16[256,2,400]{0,2,1:T(8,128)(2,1)} %bitcast.48) | data formatting | bytes 819200 | tf_op jit(solution)/shard_map/reshape | solution.py:160
  14.4 0.4 pad.11
  14.9 1.5 %all-to-all-done = s32[32,1,2]{2,1,0:T(1,128)S(1)} async-done(((s32[32,1,2]{2,1,0:T(1,128)}), s32[32,1,2]{2,1,0:T(1,128)S(1)}, u32[]{:S(2)}, u32[]{:S(2)}) %all-to-all-start) | async-done | bytes 288 | tf_op jit(solution)/shard_map/all_to_all | solution.py:209
  17.0 0.3 copy.60
  17.4 0.3 convolution_convert_fusion
  17.7 0.5 broadcast.114
  18.2 0.7 %reduce.3 = s32[32,2]{1,0:T(8,128)S(1)} reduce(s32[32,1,2]{2,1,0:T(1,128)S(1)} %all-to-all-done, s32[]{:T(128)} %broadcast.114), dimensions={1}, to_apply=%all_to_all.13.reduce_sub_computation.3 | reduce | bytes 516 | tf_op jit(solution)/shard_map/all_to_all | solution.py:209
  19.2 0.8 %reshape.190 = bf16[32,4,800]{2,1,0:T(4,128)(2,1)} reshape(bf16[128,800]{1,0:T(8,128)(2,1)S(1)} %copy.61) | data formatting | bytes 409600 | tf_op jit(solution)/shard_map/reshape | solution.py:215
  20.0 3.4 %all-to-all-start.1 = ((bf16[32,4,800]{2,1,0:T(4,128)(2,1)}), bf16[32,4,800]{2,1,0:T(4,128)(2,1)S(1)}, u32[]{:S(2)}, u32[]{:S(2)}) async-start(bf16[32,4,800]{2,1,0:T(4,128)(2,1)} %reshape.190), calls=%async_computation.1 | async-start | bytes 458752 | tf_op jit(solution)/shard_map/all_to_all | solution.py:216
  23.5 0.5 copy.63
  24.0 0.4 pad.12
  24.5 9.0 %all-to-all-done.1 = bf16[32,4,800]{2,1,0:T(4,128)(2,1)S(1)} async-done(((bf16[32,4,800]{2,1,0:T(4,128)(2,1)}), bf16[32,4,800]{2,1,0:T(4,128)(2,1)S(1)}, u32[]{:S(2)}, u32[]{:S(2)}) %all-to-all-start.1) | async-done | bytes 204832 | tf_op jit(solution)/shard_map/all_to_all | solution.py:216
  33.5 0.2 reshape_reshape.3
  33.8 0.2 pad.13
  34.0 4.0 %shard_map.112 = (f32[256,1024]{1,0:T(8,128)S(1)}, f32[256,1024]{1,0:T(8,128)S(1)}, bf16[64,1024]{1,0:T(8,128)(2,1)S(1)}) custom-call(s32[1,256]{1,0:T(1,128)S(1)} %get-tuple-element.24.wrow, s32[1,256]{1,0:T(1,128)S(1)} %get-tuple-element.23.crow, s32[1,256]{1,0:T(1,128)S(1)} %get-tuple-element.26.scomb, s32[1,256]{1,0:T(1,128)S(1)} %bitcast.39, ...), custom_call_target="tpu_custom_call" | custom-call | tf_op jit(solution)/shard_map/pallas_call | solution.py:130
  38.1 0.6 %copy-done.1 = bf16[64,1024]{1,0:T(8,128)(2,1)} copy-done((bf16[64,1024]{1,0:T(8,128)(2,1)}, bf16[64,1024]{1,0:T(8,128)(2,1)S(1)}, u32[]{:S(2)}) %copy-start.1) | copy-done | bytes 131096
  38.7 1.6 %reshape.201 = bf16[32,2,1024]{2,1,0:T(2,128)(2,1)} reshape(bf16[64,1024]{1,0:T(8,128)(2,1)} %copy-done.1) | data formatting | bytes 262144 | tf_op jit(solution)/shard_map/reshape | solution.py:239
  40.3 3.5 %all-to-all-start.2 = ((bf16[32,2,1024]{2,1,0:T(2,128)(2,1)}), bf16[32,2,1024]{2,1,0:T(2,128)(2,1)}, u32[]{:S(2)}, u32[]{:S(2)}) async-start(bf16[32,2,1024]{2,1,0:T(2,128)(2,1)} %reshape.201), calls=%async_computation.2 | async-start | bytes 262144 | tf_op jit(solution)/shard_map/all_to_all | solution.py:238
  43.8 3.7 %shard_map.113 = (f32[256,1024]{1,0:T(8,128)S(1)}, f32[256,1024]{1,0:T(8,128)S(1)}, bf16[8,1024]{1,0:T(8,128)(2,1)}) custom-call(s32[1,256]{1,0:T(1,128)S(1)} %get-tuple-element.22.wrow, s32[1,256]{1,0:T(1,128)S(1)} %get-tuple-element.21.crow, s32[1,256]{1,0:T(1,128)S(1)} %get-tuple-element.25.scomb, s32[1,256]{1,0:T(1,128)S(1)} %bitcast.40, ...), custom_call_target="tpu_custom_call" | custom-call | tf_op jit(solution)/shard_map/pallas_call | solution.py:130
  47.5 0.5 add_convert_fusion
  48.0 0.4 reshape.200
  48.4 1.1 %copy.65 = bf16[256,2,400]{0,2,1:T(8,128)(2,1)} copy(bf16[256,2,400]{2,1,0:T(2,128)(2,1)S(1)} %bitcast.41) | data formatting | bytes 819200 | tf_op jit(solution)/shard_map/slice | solution.py:166
  49.5 0.4 reshape.199
  49.8 1.1 %copy.64 = bf16[256,2,400]{0,2,1:T(8,128)(2,1)} copy(bf16[256,2,400]{2,1,0:T(2,128)(2,1)S(1)} %bitcast.42) | data formatting | bytes 819200 | tf_op jit(solution)/shard_map/slice | solution.py:166
  50.9 1.3 %all-to-all-done.2 = bf16[32,2,1024]{2,1,0:T(2,128)(2,1)} async-done(((bf16[32,2,1024]{2,1,0:T(2,128)(2,1)}), bf16[32,2,1024]{2,1,0:T(2,128)(2,1)}, u32[]{:S(2)}, u32[]{:S(2)}) %all-to-all-start.2) | async-done | bytes 131104 | tf_op jit(solution)/shard_map/all_to_all | solution.py:238
  52.2 1.0 %reshape.202 = bf16[64,1024]{1,0:T(8,128)(2,1)S(1)} reshape(bf16[32,2,1024]{2,1,0:T(2,128)(2,1)} %all-to-all-done.2) | data formatting | bytes 262144 | tf_op jit(solution)/shard_map/reshape | solution.py:250
  53.5 0.8 %reshape.203 = f32[32,800]{1,0:T(8,128)} reshape(f32[32,2,400]{2,1,0:T(2,128)S(1)} %copy.67) | data formatting | bytes 204800 | tf_op jit(solution)/shard_map/reshape | solution.py:166
  (49 shorter events, 2.0 us)
Async XLA Ops:
  0.6 16.8 %copy-start = (bf16[32,800]{1,0:T(8,128)(2,1)S(1)}, bf16[32,800]{1,0:T(8,128)(2,1)}, u32[]{:S(2)}) copy-start(bf16[32,800]{1,0:T(8,128)(2,1)} %param.11) | copy-start | bytes 153604
  2.0 7.3 %copy-start.3 = (s32[1,1024]{1,0:T(1,128)S(1)}, s32[1,1024]{1,0:T(1,128)}, u32[]{:S(2)}) copy-start(s32[1,1024]{1,0:T(1,128)} %param.15) | copy-start | bytes 12292
  2.0 7.3 %copy-start.5 = (s32[256]{0:T(256)S(1)}, s32[256]{0:T(256)}, u32[]{:S(2)}) copy-start(s32[256]{0:T(256)} %param.13) | copy-start | bytes 3076
  2.0 7.3 %copy-start.6 = (s32[256]{0:T(256)S(1)}, s32[256]{0:T(256)}, u32[]{:S(2)}) copy-start(s32[256]{0:T(256)} %param.12) | copy-start | bytes 3076
  2.0 14.4 %all-to-all-start = ((s32[32,1,2]{2,1,0:T(1,128)}), s32[32,1,2]{2,1,0:T(1,128)S(1)}, u32[]{:S(2)}, u32[]{:S(2)}) async-start(s32[32,1,2]{2,1,0:T(1,128)} %bitcast.2), calls=%async_computation | async-start | bytes 32768 | tf_op jit(solution)/shard_map/all_to_all | solution.py:209
  9.3 0.7 %copy-start.2 = (s32[256]{0:T(256)S(1)}, s32[256]{0:T(256)}, u32[]{:S(2)}) copy-start(s32[256]{0:T(256)} %param.14) | copy-start | bytes 3076
  10.0 13.3 %collective-permute-start = (s32[1792]{0:T(1024)S(1)}, s32[1792]{0:T(1024)S(1)}, u32[]{:S(2)}, u32[]{:S(2)}) collective-permute-start(s32[1792]{0:T(1024)S(1)} %pad_add_fusion.1), channel_id=1, source_target_pairs={{0,1},{1,0},{2,3},{3,2},{4,5},{5,4},{6,7},{7,6},{8,9},{9,8},{10,11... | collective-permute-start | bytes 21512 | tf_op jit(solution)/shard_map/ppermute | solution.py:12
  11.9 11.6 %collective-permute-start.1 = (bf16[256,800]{0,1:T(8,128)(2,1)}, bf16[256,800]{0,1:T(8,128)(2,1)S(1)}, u32[]{:S(2)}, u32[]{:S(2)}) collective-permute-start(bf16[256,800]{0,1:T(8,128)(2,1)} %param.10), channel_id=1, source_target_pairs={{0,2},{2,4},{4,6},{6,8},{8,10},{10,12},{12,14},{14,16},{16,18},{18... | collective-permute-start | bytes 1228808 | tf_op jit(solution)/shard_map/ppermute | solution.py:12
  11.9 0.7 %copy-start.4 = (s32[1,1,16,2]{2,3,1,0:T(2,128)S(1)}, s32[1,1,16,2]{2,3,1,0:T(2,128)}, u32[]{:S(2)}) copy-start(s32[1,1,16,2]{2,3,1,0:T(2,128)} %param.17) | copy-start | bytes 388
  20.0 13.6 %all-to-all-start.1 = ((bf16[32,4,800]{2,1,0:T(4,128)(2,1)}), bf16[32,4,800]{2,1,0:T(4,128)(2,1)S(1)}, u32[]{:S(2)}, u32[]{:S(2)}) async-start(bf16[32,4,800]{2,1,0:T(4,128)(2,1)} %reshape.190), calls=%async_computation.1 | async-start | bytes 458752 | tf_op jit(solution)/shard_map/all_to_all | solution.py:216
  38.0 0.7 %copy-start.1 = (bf16[64,1024]{1,0:T(8,128)(2,1)}, bf16[64,1024]{1,0:T(8,128)(2,1)S(1)}, u32[]{:S(2)}) copy-start(bf16[64,1024]{1,0:T(8,128)(2,1)S(1)} %get-tuple-element.18) | copy-start | bytes 393220
  40.3 11.9 %all-to-all-start.2 = ((bf16[32,2,1024]{2,1,0:T(2,128)(2,1)}), bf16[32,2,1024]{2,1,0:T(2,128)(2,1)}, u32[]{:S(2)}, u32[]{:S(2)}) async-start(bf16[32,2,1024]{2,1,0:T(2,128)(2,1)} %reshape.201), calls=%async_computation.2 | async-start | bytes 262144 | tf_op jit(solution)/shard_map/all_to_all | solution.py:238

commit v10 on v9

--- a/solution.py
+++ b/solution.py
@@ -75,15 +75,15 @@
 
 
 def _chain_body(groups, own_groups, block, neg_count, scale,
-                wrow, crow, scomb, srow, nrow, orow, live,
+                wrow, crow, scomb, srow, nrow, live,
                 words, held, table, word_out, ctx_out, slot_out):
     parts = words.shape[0]
     rows = table.shape[0]
-    slots = slot_out.shape[0]
     half = words.shape[1] // 2
     word_out[...] = jnp.zeros(word_out.shape, jnp.float32)
     ctx_out[...] = jnp.zeros(ctx_out.shape, jnp.float32)
     slot_sum = jnp.zeros(slot_out.shape, jnp.float32)
+    rterms = []
     for g in range(groups):
         t0 = g * block
         word_t = _select_t(wrow[:, t0:t0 + block], parts)
@@ -107,21 +107,35 @@
         g_re, g_im = gq[:, :half], gq[:, half:]
         if g < own_groups:
             rterm = jnp.concatenate([g_re * w_re + g_im * w_im, g_im * w_re - g_re * w_im], axis=1)
-            slot_sum = slot_sum + _spread(_select_t(srow[:, t0:t0 + block], slots), rterm)
+            rterms.append(rterm)
         wterm = jnp.concatenate([g_re * r_re + g_im * r_im, g_im * r_re - g_re * r_im], axis=1)
         word_out[...] += _spread(word_t, wterm)
         neg_weight = lax.dot_general(neg_t, dneg, (((1,), (1,)), ((), ())),
                                      preferred_element_type=jnp.float32)
         ctx_out[...] += _spread(ctx_t, dpos * qf) + _spread(neg_weight, q)
     if own_groups:
-        hit = orow[...] == lax.broadcasted_iota(jnp.int32, (rows, orow.shape[1]), 0)
-        live_t = jnp.where(hit, live[...], 0.0).astype(jnp.bfloat16)
-        slot_sum = slot_sum + 0.02 * _pick(live_t, table[...])
+        entries = live.shape[0]
+        owners = slot_out.shape[0]
+        pieces = []
+        for entry in range(entries):
+            piece = jnp.zeros((owners, words.shape[1]), jnp.float32)
+            for g in range(own_groups):
+                t0 = g * block
+                ids = srow[:, t0:t0 + block]
+                hit = ids == lax.broadcasted_iota(jnp.int32, (owners, block), 0) * entries + entry
+                sel_t = jnp.where(hit, 1.0, 0.0).astype(jnp.bfloat16)
+                piece = piece + _spread(sel_t, rterms[g])
+            own = lax.broadcasted_iota(jnp.int32, (rows, owners), 1) * (rows // owners) + entry
+            own_hit = own == lax.broadcasted_iota(jnp.int32, (rows, owners), 0)
+            own_sel_t = jnp.where(own_hit, live[entry:entry + 1, :], 0.0).astype(jnp.bfloat16)
+            piece = piece + 0.02 * _pick(own_sel_t, table[...])
+            pieces.append(piece)
+        slot_sum = jnp.concatenate(pieces, axis=1)
     slot_out[...] = slot_sum.astype(slot_out.dtype)
 
 
 def block_chains(word_ids, ctx_ids, slot_ids, own_ids, neg_ids, own_groups, scale, words, held,
-                 table, own_rows, live_mask):
+                 table, live_mask):
     trips = word_ids.shape[0]
     groups, neg_count = neg_ids.shape
     block = trips // groups
@@ -132,7 +146,7 @@
         out_shape=(
             jax.ShapeDtypeStruct((parts, width), jnp.float32),
             jax.ShapeDtypeStruct((parts, width), jnp.float32),
-            jax.ShapeDtypeStruct((own_rows.shape[0], width), jnp.bfloat16),
+            jax.ShapeDtypeStruct((live_mask.shape[1], live_mask.shape[0] * width), jnp.bfloat16),
         ),
         compiler_params=pltpu.CompilerParams(vmem_limit_bytes=48 * 1024 * 1024),
     )(
@@ -141,8 +155,7 @@
         slot_ids.reshape(1, -1),
         own_ids.reshape(1, -1),
         neg_ids,
-        own_rows.reshape(1, -1),
-        live_mask.reshape(1, -1),
+        live_mask,
         words,
         held,
         table,
@@ -201,8 +214,6 @@
         + (jnp.arange(split_count) * slot_count)[:, None]
         + slot_ids % slot_count
     ).reshape(-1)
-    own_slots = jnp.arange(slot_total)
-    own_rows = (own_slots // slot_count) * (split_count * slot_count) + own_slots % slot_count
     neg_ids = bucket_ints[:, 3 * trips :].reshape(split_count * block_count, neg_count)
 
     wanted = requests[0, 0].reshape(owner_count, slot_count)
@@ -221,35 +232,31 @@
     )
 
     group_count = split_count * block_count
+    live_rows = live_mask.reshape(owner_count, slot_count).T
     word_table = padded_halves(words, half_width)
     held_table = padded_halves(held_rows, half_width)
     fetched, word_table, held_table = lax.optimization_barrier((fetched, word_table, held_table))
     rel_table = padded_halves(fetched.reshape(split_count * slot_total, row_width), half_width)
     own_word, own_ctx, own_slot = block_chains(
         word_ids[:trips], ctx_ids[:trips], slot_ids[:trips], rel_slot, neg_ids[:block_count],
-        block_count, neg_scale, word_table, held_table, rel_table, own_rows, live_mask,
+        block_count, neg_scale, word_table, held_table, rel_table, live_rows,
     )
     rest_word, rest_ctx, _ = block_chains(
         word_ids[trips:], ctx_ids[trips:], slot_ids[trips:], rel_slot, neg_ids[block_count:],
-        0, neg_scale, word_table, held_table, rel_table, own_rows[:8], live_mask[:8],
+        0, neg_scale, word_table, held_table, rel_table, live_rows[:, :8],
     )
     word_sum = unpadded_halves(own_word + rest_word, half_width)
     ctx_sum = unpadded_halves(own_ctx + rest_ctx, half_width)
-    returned = lax.all_to_all(
-        own_slot.reshape(owner_count, slot_count, padded_width),
-        both,
-        split_axis=0,
-        concat_axis=0,
-        tiled=True,
-    ).astype(jnp.float32)
-    owner_map = (incoming.reshape(-1)[None, :] == jnp.arange(owned_rows)[:, None]).astype(
-        jnp.float32
-    )
-    relation_grad = jnp.dot(
-        owner_map,
-        returned.reshape(-1, padded_width),
-        precision=lax.Precision.HIGHEST,
-        preferred_element_type=jnp.float32,
+    returned = lax.all_to_all(own_slot, both, split_axis=0, concat_axis=0, tiled=True)
+    requested = incoming.reshape(owner_count, slot_count)
+    relation_grad = sum(
+        jnp.dot(
+            (requested[:, entry][None, :] == jnp.arange(owned_rows)[:, None]).astype(jnp.float32),
+            returned[:, entry * padded_width : (entry + 1) * padded_width].astype(jnp.float32),
+            precision=lax.Precision.HIGHEST,
+            preferred_element_type=jnp.float32,
+        )
+        for entry in range(slot_count)
     )
     relation_grad = unpadded_halves(relation_grad, half_width)
     return (word_sum.astype(jnp.bfloat16), ctx_sum.astype(jnp.bfloat16), relation_grad)

time: 54.8 us -> 56.9 us (1.038)
  other arithmetic: 1.37 us -> 2.85 us
    unnamed x18 -> x21, local copies, waits for them, and re-layouts: 2.22 us -> 5.33 us
    reshape x4 -> x0, local copies, waits for them, and re-layouts: 2.66 us -> none  [the longest x1 1.62 us: shards(): own_slot.reshape(owner_count, slot_count, padded_width)]
    all_to_all x1, other arithmetic: 0.69 us -> 2.26 us  [shards(): lax.all_to_all(own_slot, both, split_axis=0, concat_axis=0, tiled=True)]
    reshape x3 -> x4, local copies, waits for them, and re-layouts: 1.59 us -> 1.7 us  [unpadded_halves(): rows.reshape(count, 2, lanes_of(half_width))[:, :, :half_width]]
    slice x3 -> x2, local copies, waits for them, and re-layouts: 2.25 us -> 2.14 us  [unpadded_halves(): rows.reshape(count, 2, lanes_of(half_width))[:, :, :half_width]]
  transfers between devices with their start and end apart: 5 -> 5, of which waited for: 3 -> 4; matrix products, arithmetic and copies ran while one was open for 19% -> 15% of each run, Pallas kernels for 7% -> 7%
where the time goes in v10:
time: 56.9 us; the launch traced here: 56.5 us
  local copies, waits for them, and re-layouts  16.3 us (29%)
  starting transfers between devices  15.7 us (28%)
  waiting for transfers between devices  12.2 us (21%)
  Pallas kernels  7.95 us (14%)
  other arithmetic  2.85 us (5%)
  between operations  0.94 us (2%)
  matrix products  0.59 us (1%)
    all_to_all x1, waiting for transfers between devices, shards(): lax.all_to_all(picked, both, split_axis=0, concat_axis=0, tiled=True)  8.85 us
    pallas_call x2, Pallas kernels, block_chains(): pl.pallas_call(body, out_shape=(jax.ShapeDtypeStruct((parts, width), jnp....  7.95 us
    all_to_all x1, starting transfers between devices, shards(): lax.all_to_all(wanted, both, split_axis=0, concat_axis=0, tiled=True)  7.3 us
    unnamed x21, local copies, waits for them, and re-layouts  5.33 us
    all_to_all x1, starting transfers between devices, shards(): lax.all_to_all(own_slot, both, split_axis=0, concat_axis=0, tiled=True)  3.47 us
    all_to_all x1, starting transfers between devices, shards(): lax.all_to_all(picked, both, split_axis=0, concat_axis=0, tiled=True)  3.09 us
    all_to_all x1, other arithmetic, shards(): lax.all_to_all(own_slot, both, split_axis=0, concat_axis=0, tiled=True)  2.26 us
    slice x2, local copies, waits for them, and re-layouts, unpadded_halves(): rows.reshape(count, 2, lanes_of(half_width))[:, :, :half_width]  2.14 us
  transfers between devices with their start and end apart: 5, of which 4 were waited for; matrix products, arithmetic and copies ran while one was open for 15% of the time, Pallas kernels for 7%

profile of v10, /device:TPU:0, one launch (start us, length us, event | category | flops | bytes accessed | tf_op | source)
XLA Modules:
  0.0 56.5 jit_solution(13596601405440575503)
XLA Ops:
  0.6 1.4 %copy.80 = s32[1,1,16,2,2]{4,3,2,1,0:T(2,128)} copy(s32[1,1,16,2,2]{2,4,3,1,0:T(2,128)} %param.16) | data formatting | bytes 512 | tf_op jit(solution)/shard_map/all_to_all | solution.py:220
  2.0 7.3 %all-to-all-start = ((s32[32,1,2]{2,1,0:T(1,128)}), s32[32,1,2]{2,1,0:T(1,128)S(1)}, u32[]{:S(2)}, u32[]{:S(2)}) async-start(s32[32,1,2]{2,1,0:T(1,128)} %bitcast.2), calls=%async_computation | async-start | bytes 32768 | tf_op jit(solution)/shard_map/all_to_all | solution.py:220
  9.4 0.6 %copy-done.2 = s32[256]{0:T(256)S(1)} copy-done((s32[256]{0:T(256)S(1)}, s32[256]{0:T(256)}, u32[]{:S(2)}) %copy-start.2) | copy-done | bytes 1048
  10.0 1.8 %collective-permute-start = (s32[1792]{0:T(1024)S(1)}, s32[1792]{0:T(1024)S(1)}, u32[]{:S(2)}, u32[]{:S(2)}) collective-permute-start(s32[1792]{0:T(1024)S(1)} %pad_add_fusion.1), channel_id=1, source_target_pairs={{0,1},{1,0},{2,3},{3,2},{4,5},{5,4},{6,7},{7,6},{8,9},{9,8},{10,11... | collective-permute-start | bytes 21512 | tf_op jit(solution)/shard_map/ppermute | solution.py:12
  11.9 0.7 %copy-done.4 = s32[1,1,16,2]{2,3,1,0:T(2,128)S(1)} copy-done((s32[1,1,16,2]{2,3,1,0:T(2,128)S(1)}, s32[1,1,16,2]{2,3,1,0:T(2,128)}, u32[]{:S(2)}) %copy-start.4) | copy-done | bytes 152
  12.8 1.3 %copy.74 = bf16[256,2,400]{2,1,0:T(2,128)(2,1)S(1)} copy(bf16[256,2,400]{0,2,1:T(8,128)(2,1)} %bitcast.51) | data formatting | bytes 819200 | tf_op jit(solution)/shard_map/reshape | solution.py:173
  14.1 0.4 pad.11
  14.6 1.8 %all-to-all-done = s32[32,1,2]{2,1,0:T(1,128)S(1)} async-done(((s32[32,1,2]{2,1,0:T(1,128)}), s32[32,1,2]{2,1,0:T(1,128)S(1)}, u32[]{:S(2)}, u32[]{:S(2)}) %all-to-all-start) | async-done | bytes 288 | tf_op jit(solution)/shard_map/all_to_all | solution.py:220
  17.0 0.3 copy.72
  17.4 0.3 convolution_convert_fusion
  18.0 0.8 %reshape.96 = bf16[32,4,800]{2,1,0:T(4,128)(2,1)} reshape(bf16[128,800]{1,0:T(8,128)(2,1)S(1)} %copy.73) | data formatting | bytes 409600 | tf_op jit(solution)/shard_map/reshape | solution.py:226
  18.7 3.1 %all-to-all-start.1 = ((bf16[32,4,800]{2,1,0:T(4,128)(2,1)}), bf16[32,4,800]{2,1,0:T(4,128)(2,1)S(1)}, u32[]{:S(2)}, u32[]{:S(2)}) async-start(bf16[32,4,800]{2,1,0:T(4,128)(2,1)} %reshape.96), calls=%async_computation.1 | async-start | bytes 458752 | tf_op jit(solution)/shard_map/all_to_all | solution.py:227
  22.2 0.5 copy.75
  22.6 0.4 pad.12
  23.2 8.8 %all-to-all-done.1 = bf16[32,4,800]{2,1,0:T(4,128)(2,1)S(1)} async-done(((bf16[32,4,800]{2,1,0:T(4,128)(2,1)}), bf16[32,4,800]{2,1,0:T(4,128)(2,1)S(1)}, u32[]{:S(2)}, u32[]{:S(2)}) %all-to-all-start.1) | async-done | bytes 204832 | tf_op jit(solution)/shard_map/all_to_all | solution.py:227
  32.0 0.2 reshape_reshape.3
  32.3 0.2 pad.13
  32.5 4.2 %shard_map.112 = (f32[256,1024]{1,0:T(8,128)S(1)}, f32[256,1024]{1,0:T(8,128)S(1)}, bf16[32,2048]{1,0:T(8,128)(2,1)S(1)}) custom-call(s32[1,256]{1,0:T(1,128)S(1)} %get-tuple-element.24.wrow, s32[1,256]{1,0:T(1,128)S(1)} %get-tuple-element.23.crow, s32[1,256]{1,0:T(1,128)S(1)} %get-tuple-element.26.scomb, s32[1,256]{1,0:T(1,128)S(1)} %bitcast.40, ...), custom_call_target="tpu_custom_call" | custom-call | tf_op jit(solution)/shard_map/pallas_call | solution.py:144
  36.8 0.6 %copy-done.1 = bf16[32,2048]{1,0:T(8,128)(2,1)} copy-done((bf16[32,2048]{1,0:T(8,128)(2,1)}, bf16[32,2048]{1,0:T(8,128)(2,1)S(1)}, u32[]{:S(2)}) %copy-start.1) | copy-done | bytes 131096
  37.4 0.5 broadcast.31
  37.9 2.3 %reduce = bf16[32,2048]{1,0:T(8,128)(2,1)} reduce(bf16[32,1,2048]{2,0,1:T(8,128)(2,1)} %bitcast.39, bf16[]{:T(256)} %broadcast.31), dimensions={1}, to_apply=%copy.79.reduce_sub_computation | reduce | bytes 262146 | tf_op jit(solution)/shard_map/all_to_all | solution.py:250
  40.2 1.6 %reshape.106 = bf16[32,2,1024]{2,1,0:T(2,128)(2,1)} reshape(bf16[32,2048]{1,0:T(8,128)(2,1)} %reduce) | data formatting | bytes 262144
  41.9 3.5 %all-to-all-start.2 = ((bf16[32,2,1024]{2,1,0:T(2,128)(2,1)}), bf16[32,2,1024]{2,1,0:T(2,128)(2,1)}, u32[]{:S(2)}, u32[]{:S(2)}) async-start(bf16[32,2,1024]{2,1,0:T(2,128)(2,1)} %reshape.106), calls=%async_computation.2 | async-start | bytes 262144 | tf_op jit(solution)/shard_map/all_to_all | solution.py:250
  45.3 3.7 %shard_map.113 = (f32[256,1024]{1,0:T(8,128)S(1)}, f32[256,1024]{1,0:T(8,128)S(1)}, bf16[8,2048]{1,0:T(8,128)(2,1)}) custom-call(s32[1,256]{1,0:T(1,128)S(1)} %get-tuple-element.22.wrow, s32[1,256]{1,0:T(1,128)S(1)} %get-tuple-element.21.crow, s32[1,256]{1,0:T(1,128)S(1)} %get-tuple-element.25.scomb, s32[1,256]{1,0:T(1,128)S(1)} %bitcast.41, ...), custom_call_target="tpu_custom_call" | custom-call | tf_op jit(solution)/shard_map/pallas_call | solution.py:144
  49.0 0.5 add_convert_fusion
  49.5 0.4 reshape.103
  49.9 1.1 %copy.77 = bf16[256,2,400]{0,2,1:T(8,128)(2,1)} copy(bf16[256,2,400]{2,1,0:T(2,128)(2,1)S(1)} %bitcast.43) | data formatting | bytes 819200 | tf_op jit(solution)/shard_map/slice | solution.py:179
  51.0 0.4 reshape.102
  51.4 1.1 %copy.76 = bf16[256,2,400]{0,2,1:T(8,128)(2,1)} copy(bf16[256,2,400]{2,1,0:T(2,128)(2,1)S(1)} %bitcast.44) | data formatting | bytes 819200 | tf_op jit(solution)/shard_map/slice | solution.py:179
  52.4 1.3 %all-to-all-done.2 = bf16[32,2,1024]{2,1,0:T(2,128)(2,1)} async-done(((bf16[32,2,1024]{2,1,0:T(2,128)(2,1)}), bf16[32,2,1024]{2,1,0:T(2,128)(2,1)}, u32[]{:S(2)}, u32[]{:S(2)}) %all-to-all-start.2) | async-done | bytes 131104 | tf_op jit(solution)/shard_map/all_to_all | solution.py:250
  53.7 1.4 %reshape.107 = bf16[32,1,2048]{2,1,0:T(2,128)(2,1)S(1)} reshape(bf16[32,2,1024]{2,1,0:T(2,128)(2,1)} %all-to-all-done.2) | data formatting | bytes 262144
  55.6 0.8 %reshape.105 = f32[32,800]{1,0:T(8,128)} reshape(f32[32,2,400]{2,1,0:T(2,128)S(1)} %bitcast.50) | data formatting | bytes 204800 | tf_op jit(solution)/shard_map/reshape | solution.py:179
  (45 shorter events, 2.0 us)
Async XLA Ops:
  0.6 16.8 %copy-start = (bf16[32,800]{1,0:T(8,128)(2,1)S(1)}, bf16[32,800]{1,0:T(8,128)(2,1)}, u32[]{:S(2)}) copy-start(bf16[32,800]{1,0:T(8,128)(2,1)} %param.11) | copy-start | bytes 153604
  2.0 7.3 %copy-start.3 = (s32[1,1024]{1,0:T(1,128)S(1)}, s32[1,1024]{1,0:T(1,128)}, u32[]{:S(2)}) copy-start(s32[1,1024]{1,0:T(1,128)} %param.15) | copy-start | bytes 12292
  2.0 7.3 %copy-start.5 = (s32[256]{0:T(256)S(1)}, s32[256]{0:T(256)}, u32[]{:S(2)}) copy-start(s32[256]{0:T(256)} %param.13) | copy-start | bytes 3076
  2.0 7.3 %copy-start.6 = (s32[256]{0:T(256)S(1)}, s32[256]{0:T(256)}, u32[]{:S(2)}) copy-start(s32[256]{0:T(256)} %param.12) | copy-start | bytes 3076
  2.0 14.4 %all-to-all-start = ((s32[32,1,2]{2,1,0:T(1,128)}), s32[32,1,2]{2,1,0:T(1,128)S(1)}, u32[]{:S(2)}, u32[]{:S(2)}) async-start(s32[32,1,2]{2,1,0:T(1,128)} %bitcast.2), calls=%async_computation | async-start | bytes 32768 | tf_op jit(solution)/shard_map/all_to_all | solution.py:220
  9.3 0.7 %copy-start.2 = (s32[256]{0:T(256)S(1)}, s32[256]{0:T(256)}, u32[]{:S(2)}) copy-start(s32[256]{0:T(256)} %param.14) | copy-start | bytes 3076
  10.0 11.8 %collective-permute-start = (s32[1792]{0:T(1024)S(1)}, s32[1792]{0:T(1024)S(1)}, u32[]{:S(2)}, u32[]{:S(2)}) collective-permute-start(s32[1792]{0:T(1024)S(1)} %pad_add_fusion.1), channel_id=1, source_target_pairs={{0,1},{1,0},{2,3},{3,2},{4,5},{5,4},{6,7},{7,6},{8,9},{9,8},{10,11... | collective-permute-start | bytes 21512 | tf_op jit(solution)/shard_map/ppermute | solution.py:12
  11.9 10.3 %collective-permute-start.1 = (bf16[256,800]{0,1:T(8,128)(2,1)}, bf16[256,800]{0,1:T(8,128)(2,1)S(1)}, u32[]{:S(2)}, u32[]{:S(2)}) collective-permute-start(bf16[256,800]{0,1:T(8,128)(2,1)} %param.10), channel_id=1, source_target_pairs={{0,2},{2,4},{4,6},{6,8},{8,10},{10,12},{12,14},{14,16},{16,18},{18... | collective-permute-start | bytes 1228808 | tf_op jit(solution)/shard_map/ppermute | solution.py:12
  11.9 0.7 %copy-start.4 = (s32[1,1,16,2]{2,3,1,0:T(2,128)S(1)}, s32[1,1,16,2]{2,3,1,0:T(2,128)}, u32[]{:S(2)}) copy-start(s32[1,1,16,2]{2,3,1,0:T(2,128)} %param.17) | copy-start | bytes 388
  18.7 13.3 %all-to-all-start.1 = ((bf16[32,4,800]{2,1,0:T(4,128)(2,1)}), bf16[32,4,800]{2,1,0:T(4,128)(2,1)S(1)}, u32[]{:S(2)}, u32[]{:S(2)}) async-start(bf16[32,4,800]{2,1,0:T(4,128)(2,1)} %reshape.96), calls=%async_computation.1 | async-start | bytes 458752 | tf_op jit(solution)/shard_map/all_to_all | solution.py:227
  36.8 0.7 %copy-start.1 = (bf16[32,2048]{1,0:T(8,128)(2,1)}, bf16[32,2048]{1,0:T(8,128)(2,1)S(1)}, u32[]{:S(2)}) copy-start(bf16[32,2048]{1,0:T(8,128)(2,1)S(1)} %get-tuple-element.18) | copy-start | bytes 393220
  41.9 11.9 %all-to-all-start.2 = ((bf16[32,2,1024]{2,1,0:T(2,128)(2,1)}), bf16[32,2,1024]{2,1,0:T(2,128)(2,1)}, u32[]{:S(2)}, u32[]{:S(2)}) async-start(bf16[32,2,1024]{2,1,0:T(2,128)(2,1)} %reshape.106), calls=%async_computation.2 | async-start | bytes 262144 | tf_op jit(solution)/shard_map/all_to_all | solution.py:250

commit v11 on v9

--- a/solution.py
+++ b/solution.py
@@ -83,7 +83,7 @@
     half = words.shape[1] // 2
     word_out[...] = jnp.zeros(word_out.shape, jnp.float32)
     ctx_out[...] = jnp.zeros(ctx_out.shape, jnp.float32)
-    slot_sum = jnp.zeros(slot_out.shape, jnp.float32)
+    slot_sum = jnp.zeros((slot_out.shape[0], words.shape[1]), jnp.float32)
     for g in range(groups):
         t0 = g * block
         word_t = _select_t(wrow[:, t0:t0 + block], parts)
@@ -117,11 +117,13 @@
         hit = orow[...] == lax.broadcasted_iota(jnp.int32, (rows, orow.shape[1]), 0)
         live_t = jnp.where(hit, live[...], 0.0).astype(jnp.bfloat16)
         slot_sum = slot_sum + 0.02 * _pick(live_t, table[...])
-    slot_out[...] = slot_sum.astype(slot_out.dtype)
+    kept = slot_out.shape[1] // 2
+    slot_out[:, :kept] = slot_sum[:, :kept].astype(slot_out.dtype)
+    slot_out[:, kept:] = slot_sum[:, half:half + kept].astype(slot_out.dtype)
 
 
 def block_chains(word_ids, ctx_ids, slot_ids, own_ids, neg_ids, own_groups, scale, words, held,
-                 table, own_rows, live_mask):
+                 table, own_rows, live_mask, row_width):
     trips = word_ids.shape[0]
     groups, neg_count = neg_ids.shape
     block = trips // groups
@@ -132,7 +134,7 @@
         out_shape=(
             jax.ShapeDtypeStruct((parts, width), jnp.float32),
             jax.ShapeDtypeStruct((parts, width), jnp.float32),
-            jax.ShapeDtypeStruct((own_rows.shape[0], width), jnp.bfloat16),
+            jax.ShapeDtypeStruct((own_rows.shape[0], row_width), jnp.bfloat16),
         ),
         compiler_params=pltpu.CompilerParams(vmem_limit_bytes=48 * 1024 * 1024),
     )(
@@ -228,15 +230,17 @@
     own_word, own_ctx, own_slot = block_chains(
         word_ids[:trips], ctx_ids[:trips], slot_ids[:trips], rel_slot, neg_ids[:block_count],
         block_count, neg_scale, word_table, held_table, rel_table, own_rows, live_mask,
+        row_width,
     )
     rest_word, rest_ctx, _ = block_chains(
         word_ids[trips:], ctx_ids[trips:], slot_ids[trips:], rel_slot, neg_ids[block_count:],
         0, neg_scale, word_table, held_table, rel_table, own_rows[:8], live_mask[:8],
+        row_width,
     )
     word_sum = unpadded_halves(own_word + rest_word, half_width)
     ctx_sum = unpadded_halves(own_ctx + rest_ctx, half_width)
     returned = lax.all_to_all(
-        own_slot.reshape(owner_count, slot_count, padded_width),
+        own_slot.reshape(owner_count, slot_count, row_width),
         both,
         split_axis=0,
         concat_axis=0,
@@ -247,11 +251,10 @@
     )
     relation_grad = jnp.dot(
         owner_map,
-        returned.reshape(-1, padded_width),
+        returned.reshape(-1, row_width),
         precision=lax.Precision.HIGHEST,
         preferred_element_type=jnp.float32,
     )
-    relation_grad = unpadded_halves(relation_grad, half_width)
     return (word_sum.astype(jnp.bfloat16), ctx_sum.astype(jnp.bfloat16), relation_grad)
 
 

time: 54.8 us -> 54.1 us (0.987)
  local copies, waits for them, and re-layouts: 16 us -> 15 us
  waiting for transfers between devices: 11.9 us -> 11.1 us
  matrix products: 0.44 us -> 1.08 us
    reshape x3 -> x2, local copies, waits for them, and re-layouts: 1.59 us -> 0.75 us  [unpadded_halves(): rows.reshape(count, 2, lanes_of(half_width))[:, :, :half_width]]
    all_to_all x1, waiting for transfers between devices: 1.31 us -> 0.57 us  [shards(): lax.all_to_all(own_slot.reshape(owner_count, slot_count, row_width), both...]
    dot_general x1, matrix products: 0.14 us -> 0.78 us  [shards(): jnp.dot(owner_map, returned.reshape(-1, row_width), precision=lax.Precisi...]
    slice x3 -> x2, local copies, waits for them, and re-layouts: 2.25 us -> 2.14 us  [unpadded_halves(): rows.reshape(count, 2, lanes_of(half_width))[:, :, :half_width]]
  transfers between devices with their start and end apart: 5 -> 5, of which waited for: 3 -> 3; matrix products, arithmetic and copies ran while one was open for 19% -> 19% of each run, Pallas kernels for 7% -> 8%
where the time goes in v11:
time: 54.1 us; the launch traced here: 53.7 us
  starting transfers between devices  16 us (30%)
  local copies, waits for them, and re-layouts  15 us (28%)
  waiting for transfers between devices  11.1 us (21%)
  Pallas kernels  8.22 us (15%)
  other arithmetic  1.37 us (3%)
  matrix products  1.08 us (2%)
  between operations  0.93 us (2%)
    all_to_all x1, waiting for transfers between devices, shards(): lax.all_to_all(picked, both, split_axis=0, concat_axis=0, tiled=True)  9.03 us
    pallas_call x2, Pallas kernels, block_chains(): pl.pallas_call(body, out_shape=(jax.ShapeDtypeStruct((parts, width), jnp....  8.22 us
    all_to_all x1, starting transfers between devices, shards(): lax.all_to_all(wanted, both, split_axis=0, concat_axis=0, tiled=True)  7.3 us
    all_to_all x1, starting transfers between devices, shards(): lax.all_to_all(own_slot.reshape(owner_count, slot_count, row_width), both...  3.44 us
    all_to_all x1, starting transfers between devices, shards(): lax.all_to_all(picked, both, split_axis=0, concat_axis=0, tiled=True)  3.38 us
    unnamed x18, local copies, waits for them, and re-layouts  2.21 us
    slice x2, local copies, waits for them, and re-layouts, unpadded_halves(): rows.reshape(count, 2, lanes_of(half_width))[:, :, :half_width]  2.14 us
    all_to_all x2, local copies, waits for them, and re-layouts, shards(): lax.all_to_all(wanted, both, split_axis=0, concat_axis=0, tiled=True)  1.9 us
  transfers between devices with their start and end apart: 5, of which 3 were waited for; matrix products, arithmetic and copies ran while one was open for 19% of the time, Pallas kernels for 8%

profile of v11, /device:TPU:0, one launch (start us, length us, event | category | flops | bytes accessed | tf_op | source)
XLA Modules:
  0.0 53.7 jit_solution(11899380786389476848)
XLA Ops:
  0.6 1.4 %copy.62 = s32[1,1,16,2,2]{4,3,2,1,0:T(2,128)} copy(s32[1,1,16,2,2]{2,4,3,1,0:T(2,128)} %param.16) | data formatting | bytes 512 | tf_op jit(solution)/shard_map/all_to_all | solution.py:211
  2.0 7.3 %all-to-all-start = ((s32[32,1,2]{2,1,0:T(1,128)}), s32[32,1,2]{2,1,0:T(1,128)S(1)}, u32[]{:S(2)}, u32[]{:S(2)}) async-start(s32[32,1,2]{2,1,0:T(1,128)} %bitcast.2), calls=%async_computation | async-start | bytes 32768 | tf_op jit(solution)/shard_map/all_to_all | solution.py:211
  9.4 0.6 %copy-done.2 = s32[256]{0:T(256)S(1)} copy-done((s32[256]{0:T(256)S(1)}, s32[256]{0:T(256)}, u32[]{:S(2)}) %copy-start.2) | copy-done | bytes 1048
  10.0 1.8 %collective-permute-start = (s32[1792]{0:T(1024)S(1)}, s32[1792]{0:T(1024)S(1)}, u32[]{:S(2)}, u32[]{:S(2)}) collective-permute-start(s32[1792]{0:T(1024)S(1)} %pad_add_fusion.1), channel_id=1, source_target_pairs={{0,1},{1,0},{2,3},{3,2},{4,5},{5,4},{6,7},{7,6},{8,9},{9,8},{10,11... | collective-permute-start | bytes 21512 | tf_op jit(solution)/shard_map/ppermute | solution.py:12
  12.0 0.7 %copy-done.4 = s32[1,1,16,2]{2,3,1,0:T(2,128)S(1)} copy-done((s32[1,1,16,2]{2,3,1,0:T(2,128)S(1)}, s32[1,1,16,2]{2,3,1,0:T(2,128)}, u32[]{:S(2)}) %copy-start.4) | copy-done | bytes 152
  13.1 1.3 %copy.58 = bf16[256,2,400]{2,1,0:T(2,128)(2,1)S(1)} copy(bf16[256,2,400]{0,2,1:T(8,128)(2,1)} %bitcast.38) | data formatting | bytes 819200 | tf_op jit(solution)/shard_map/reshape | solution.py:162
  14.4 0.4 pad.11
  14.9 1.5 %all-to-all-done = s32[32,1,2]{2,1,0:T(1,128)S(1)} async-done(((s32[32,1,2]{2,1,0:T(1,128)}), s32[32,1,2]{2,1,0:T(1,128)S(1)}, u32[]{:S(2)}, u32[]{:S(2)}) %all-to-all-start) | async-done | bytes 288 | tf_op jit(solution)/shard_map/all_to_all | solution.py:211
  17.0 0.3 copy.56
  17.4 0.3 convolution_convert_fusion
  17.7 0.5 broadcast.114
  18.2 0.7 %reduce.3 = s32[32,2]{1,0:T(8,128)S(1)} reduce(s32[32,1,2]{2,1,0:T(1,128)S(1)} %all-to-all-done, s32[]{:T(128)} %broadcast.114), dimensions={1}, to_apply=%all_to_all.13.reduce_sub_computation.3 | reduce | bytes 516 | tf_op jit(solution)/shard_map/all_to_all | solution.py:211
  19.2 0.8 %reshape.185 = bf16[32,4,800]{2,1,0:T(4,128)(2,1)} reshape(bf16[128,800]{1,0:T(8,128)(2,1)S(1)} %copy.57) | data formatting | bytes 409600 | tf_op jit(solution)/shard_map/reshape | solution.py:217
  20.0 3.4 %all-to-all-start.1 = ((bf16[32,4,800]{2,1,0:T(4,128)(2,1)}), bf16[32,4,800]{2,1,0:T(4,128)(2,1)S(1)}, u32[]{:S(2)}, u32[]{:S(2)}) async-start(bf16[32,4,800]{2,1,0:T(4,128)(2,1)} %reshape.185), calls=%async_computation.1 | async-start | bytes 458752 | tf_op jit(solution)/shard_map/all_to_all | solution.py:218
  23.5 0.5 copy.59
  24.0 0.4 pad.12
  24.5 9.0 %all-to-all-done.1 = bf16[32,4,800]{2,1,0:T(4,128)(2,1)S(1)} async-done(((bf16[32,4,800]{2,1,0:T(4,128)(2,1)}), bf16[32,4,800]{2,1,0:T(4,128)(2,1)S(1)}, u32[]{:S(2)}, u32[]{:S(2)}) %all-to-all-start.1) | async-done | bytes 204832 | tf_op jit(solution)/shard_map/all_to_all | solution.py:218
  33.5 0.2 reshape_reshape.3
  33.8 0.2 pad.13
  34.0 4.0 %shard_map.112 = (f32[256,1024]{1,0:T(8,128)S(1)}, f32[256,1024]{1,0:T(8,128)S(1)}, bf16[64,800]{1,0:T(8,128)(2,1)S(1)}) custom-call(s32[1,256]{1,0:T(1,128)S(1)} %get-tuple-element.24.wrow, s32[1,256]{1,0:T(1,128)S(1)} %get-tuple-element.23.crow, s32[1,256]{1,0:T(1,128)S(1)} %get-tuple-element.26.scomb, s32[1,256]{1,0:T(1,128)S(1)} %bitcast.31, ...), custom_call_target="tpu_custom_call" | custom-call | tf_op jit(solution)/shard_map/pallas_call | solution.py:132
  38.1 0.6 %copy-done.1 = bf16[64,800]{1,0:T(8,128)(2,1)} copy-done((bf16[64,800]{1,0:T(8,128)(2,1)}, bf16[64,800]{1,0:T(8,128)(2,1)S(1)}, u32[]{:S(2)}) %copy-start.1) | copy-done | bytes 102424
  38.7 1.6 %reshape.196 = bf16[32,2,800]{2,1,0:T(2,128)(2,1)} reshape(bf16[64,800]{1,0:T(8,128)(2,1)} %copy-done.1) | data formatting | bytes 204800 | tf_op jit(solution)/shard_map/reshape | solution.py:243
  40.3 3.4 %all-to-all-start.2 = ((bf16[32,2,800]{2,1,0:T(2,128)(2,1)}), bf16[32,2,800]{2,1,0:T(2,128)(2,1)}, u32[]{:S(2)}, u32[]{:S(2)}) async-start(bf16[32,2,800]{2,1,0:T(2,128)(2,1)} %reshape.196), calls=%async_computation.2 | async-start | bytes 229376 | tf_op jit(solution)/shard_map/all_to_all | solution.py:242
  43.7 4.2 %shard_map.113 = (f32[256,1024]{1,0:T(8,128)S(1)}, f32[256,1024]{1,0:T(8,128)S(1)}, bf16[8,800]{1,0:T(8,128)(2,1)}) custom-call(s32[1,256]{1,0:T(1,128)S(1)} %get-tuple-element.22.wrow, s32[1,256]{1,0:T(1,128)S(1)} %get-tuple-element.21.crow, s32[1,256]{1,0:T(1,128)S(1)} %get-tuple-element.25.scomb, s32[1,256]{1,0:T(1,128)S(1)} %bitcast.32, ...), custom_call_target="tpu_custom_call" | custom-call | tf_op jit(solution)/shard_map/pallas_call | solution.py:132
  48.0 0.5 add_convert_fusion
  48.5 0.4 reshape.195
  48.8 1.1 %copy.61 = bf16[256,2,400]{0,2,1:T(8,128)(2,1)} copy(bf16[256,2,400]{2,1,0:T(2,128)(2,1)S(1)} %bitcast.33) | data formatting | bytes 819200 | tf_op jit(solution)/shard_map/slice | solution.py:168
  49.9 0.4 reshape.194
  50.3 1.1 %copy.60 = bf16[256,2,400]{0,2,1:T(8,128)(2,1)} copy(bf16[256,2,400]{2,1,0:T(2,128)(2,1)S(1)} %bitcast.34) | data formatting | bytes 819200 | tf_op jit(solution)/shard_map/slice | solution.py:168
  51.4 0.6 %all-to-all-done.2 = bf16[32,2,800]{2,1,0:T(2,128)(2,1)} async-done(((bf16[32,2,800]{2,1,0:T(2,128)(2,1)}), bf16[32,2,800]{2,1,0:T(2,128)(2,1)}, u32[]{:S(2)}, u32[]{:S(2)}) %all-to-all-start.2) | async-done | bytes 102432 | tf_op jit(solution)/shard_map/all_to_all | solution.py:242
  51.9 1.0 %reshape.197 = bf16[64,800]{1,0:T(8,128)(2,1)S(1)} reshape(bf16[32,2,800]{2,1,0:T(2,128)(2,1)} %all-to-all-done.2) | data formatting | bytes 204800 | tf_op jit(solution)/shard_map/reshape | solution.py:254
  52.9 0.8 %fusion.1 = f32[32,800]{1,0:T(8,128)} fusion(bf16[64,800]{1,0:T(8,128)(2,1)S(1)} %reshape.197, s32[64]{0:T(128)S(1)} %eq.38), kind=kOutput, calls=%fused_computation.8 | convolution fusion | flops 3278848 | bytes 205056 | tf_op jit(solution)/shard_map/dot_general | solution.py:252
  (46 shorter events, 1.7 us)
Async XLA Ops:
  0.6 16.8 %copy-start = (bf16[32,800]{1,0:T(8,128)(2,1)S(1)}, bf16[32,800]{1,0:T(8,128)(2,1)}, u32[]{:S(2)}) copy-start(bf16[32,800]{1,0:T(8,128)(2,1)} %param.11) | copy-start | bytes 153604
  2.0 7.3 %copy-start.3 = (s32[1,1024]{1,0:T(1,128)S(1)}, s32[1,1024]{1,0:T(1,128)}, u32[]{:S(2)}) copy-start(s32[1,1024]{1,0:T(1,128)} %param.15) | copy-start | bytes 12292
  2.0 7.3 %copy-start.5 = (s32[256]{0:T(256)S(1)}, s32[256]{0:T(256)}, u32[]{:S(2)}) copy-start(s32[256]{0:T(256)} %param.13) | copy-start | bytes 3076
  2.0 7.3 %copy-start.6 = (s32[256]{0:T(256)S(1)}, s32[256]{0:T(256)}, u32[]{:S(2)}) copy-start(s32[256]{0:T(256)} %param.12) | copy-start | bytes 3076
  2.0 14.4 %all-to-all-start = ((s32[32,1,2]{2,1,0:T(1,128)}), s32[32,1,2]{2,1,0:T(1,128)S(1)}, u32[]{:S(2)}, u32[]{:S(2)}) async-start(s32[32,1,2]{2,1,0:T(1,128)} %bitcast.2), calls=%async_computation | async-start | bytes 32768 | tf_op jit(solution)/shard_map/all_to_all | solution.py:211
  9.3 0.7 %copy-start.2 = (s32[256]{0:T(256)S(1)}, s32[256]{0:T(256)}, u32[]{:S(2)}) copy-start(s32[256]{0:T(256)} %param.14) | copy-start | bytes 3076
  10.0 13.3 %collective-permute-start = (s32[1792]{0:T(1024)S(1)}, s32[1792]{0:T(1024)S(1)}, u32[]{:S(2)}, u32[]{:S(2)}) collective-permute-start(s32[1792]{0:T(1024)S(1)} %pad_add_fusion.1), channel_id=1, source_target_pairs={{0,1},{1,0},{2,3},{3,2},{4,5},{5,4},{6,7},{7,6},{8,9},{9,8},{10,11... | collective-permute-start | bytes 21512 | tf_op jit(solution)/shard_map/ppermute | solution.py:12
  11.9 11.6 %collective-permute-start.1 = (bf16[256,800]{0,1:T(8,128)(2,1)}, bf16[256,800]{0,1:T(8,128)(2,1)S(1)}, u32[]{:S(2)}, u32[]{:S(2)}) collective-permute-start(bf16[256,800]{0,1:T(8,128)(2,1)} %param.10), channel_id=1, source_target_pairs={{0,2},{2,4},{4,6},{6,8},{8,10},{10,12},{12,14},{14,16},{16,18},{18... | collective-permute-start | bytes 1228808 | tf_op jit(solution)/shard_map/ppermute | solution.py:12
  11.9 0.7 %copy-start.4 = (s32[1,1,16,2]{2,3,1,0:T(2,128)S(1)}, s32[1,1,16,2]{2,3,1,0:T(2,128)}, u32[]{:S(2)}) copy-start(s32[1,1,16,2]{2,3,1,0:T(2,128)} %param.17) | copy-start | bytes 388
  20.0 13.6 %all-to-all-start.1 = ((bf16[32,4,800]{2,1,0:T(4,128)(2,1)}), bf16[32,4,800]{2,1,0:T(4,128)(2,1)S(1)}, u32[]{:S(2)}, u32[]{:S(2)}) async-start(bf16[32,4,800]{2,1,0:T(4,128)(2,1)} %reshape.185), calls=%async_computation.1 | async-start | bytes 458752 | tf_op jit(solution)/shard_map/all_to_all | solution.py:218
  38.0 0.6 %copy-start.1 = (bf16[64,800]{1,0:T(8,128)(2,1)}, bf16[64,800]{1,0:T(8,128)(2,1)S(1)}, u32[]{:S(2)}) copy-start(bf16[64,800]{1,0:T(8,128)(2,1)S(1)} %get-tuple-element.18) | copy-start | bytes 307204
  40.3 11.6 %all-to-all-start.2 = ((bf16[32,2,800]{2,1,0:T(2,128)(2,1)}), bf16[32,2,800]{2,1,0:T(2,128)(2,1)}, u32[]{:S(2)}, u32[]{:S(2)}) async-start(bf16[32,2,800]{2,1,0:T(2,128)(2,1)} %reshape.196), calls=%async_computation.2 | async-start | bytes 229376 | tf_op jit(solution)/shard_map/all_to_all | solution.py:242

commit v12 on v11

--- a/solution.py
+++ b/solution.py
@@ -212,9 +212,12 @@
     lists = incoming.reshape(part_count, split_count, slot_count)
     served = jnp.stack([jnp.roll(lists, -j, axis=1) for j in range(split_count)], axis=2)
     padded_width = 2 * lanes_of(half_width)
-    picked = pick_rows(one_hot(served.reshape(-1), owned_rows), relations).astype(
-        jnp.bfloat16
-    ).reshape(owner_count, split_count * slot_count, row_width)
+    picked = jnp.einsum(
+        "dkr,rf->dkf",
+        one_hot(served.reshape(owner_count, split_count * slot_count), owned_rows),
+        relations,
+        preferred_element_type=jnp.float32,
+    ).astype(jnp.bfloat16)
     fetched = lax.all_to_all(picked, both, split_axis=0, concat_axis=0, tiled=True)
     live_mask = (
         (jnp.arange(slot_count)[None, :] < counts[0, 0].reshape(owner_count)[:, None])
@@ -246,6 +249,7 @@
         concat_axis=0,
         tiled=True,
     ).astype(jnp.float32)
+    incoming, returned = lax.optimization_barrier((incoming, returned))
     owner_map = (incoming.reshape(-1)[None, :] == jnp.arange(owned_rows)[:, None]).astype(
         jnp.float32
     )

time: 54.1 us -> 52.7 us (0.974)
  local copies, waits for them, and re-layouts: 15 us -> 13.3 us
    convert_element_type x0 -> x1, other arithmetic: none -> 0.98 us  [shards(): returned = lax.all_to_all(own_slot.reshape(owner_count, slot_count, row_w...]
    reshape x1, local copies, waits for them, and re-layouts: 0.99 us -> 0.16 us  [shards(): returned.reshape(-1, row_width)]
    reshape x1 -> x0, local copies, waits for them, and re-layouts: 0.76 us -> none  [shards(): picked = pick_rows(one_hot(served.reshape(-1), owned_rows), relations).as...]
    all_to_all x1 -> x0, other arithmetic: 0.69 us -> none  [shards(): lax.all_to_all(wanted, both, split_axis=0, concat_axis=0, tiled=True)]
    convert_element_type x1, local copies, waits for them, and re-layouts: 0.17 us -> 0.81 us  [shards(): picked = jnp.einsum('dkr,rf->dkf', one_hot(served.reshape(owner_count, sp...]
  transfers between devices with their start and end apart: 5 -> 5, of which waited for: 3 -> 4; matrix products, arithmetic and copies ran while one was open for 19% -> 16% of each run, Pallas kernels for 8% -> 8%
where the time goes in v12:
time: 52.7 us; the launch traced here: 52.3 us
  starting transfers between devices  16 us (30%)
  local copies, waits for them, and re-layouts  13.3 us (25%)
  waiting for transfers between devices  11.1 us (21%)
  Pallas kernels  8.23 us (16%)
  other arithmetic  1.66 us (3%)
  matrix products  1.12 us (2%)
  between operations  0.92 us (2%)
    all_to_all x1, waiting for transfers between devices, shards(): lax.all_to_all(picked, both, split_axis=0, concat_axis=0, tiled=True)  8.53 us
    pallas_call x2, Pallas kernels, block_chains(): pl.pallas_call(body, out_shape=(jax.ShapeDtypeStruct((parts, width), jnp....  8.23 us
    all_to_all x1, starting transfers between devices, shards(): lax.all_to_all(wanted, both, split_axis=0, concat_axis=0, tiled=True)  7.3 us
    all_to_all x1, starting transfers between devices, shards(): lax.all_to_all(own_slot.reshape(owner_count, slot_count, row_width), both...  3.45 us
    all_to_all x1, starting transfers between devices, shards(): lax.all_to_all(picked, both, split_axis=0, concat_axis=0, tiled=True)  3.38 us
    unnamed x18, local copies, waits for them, and re-layouts  2.21 us
    slice x2, local copies, waits for them, and re-layouts, unpadded_halves(): rows.reshape(count, 2, lanes_of(half_width))[:, :, :half_width]  2.14 us
    ppermute x2, starting transfers between devices, passed_along(): lax.ppermute(shard, axis, [(i, (i + by) % length) for i in range(length)])  1.84 us
  transfers between devices with their start and end apart: 5, of which 4 were waited for; matrix products, arithmetic and copies ran while one was open for 16% of the time, Pallas kernels for 8%

profile of v12, /device:TPU:0, one launch (start us, length us, event | category | flops | bytes accessed | tf_op | source)
XLA Modules:
  0.0 52.3 jit_solution(13257837555403333446)
XLA Ops:
  0.6 1.4 %copy.62 = s32[1,1,16,2,2]{4,3,2,1,0:T(2,128)} copy(s32[1,1,16,2,2]{2,4,3,1,0:T(2,128)} %param.16) | data formatting | bytes 512 | tf_op jit(solution)/shard_map/all_to_all | solution.py:211
  2.0 7.3 %all-to-all-start = ((s32[32,1,2]{2,1,0:T(1,128)}), s32[32,1,2]{2,1,0:T(1,128)S(1)}, u32[]{:S(2)}, u32[]{:S(2)}) async-start(s32[32,1,2]{2,1,0:T(1,128)} %bitcast.2), calls=%async_computation | async-start | bytes 32768 | tf_op jit(solution)/shard_map/all_to_all | solution.py:211
  9.4 0.6 %copy-done.2 = s32[256]{0:T(256)S(1)} copy-done((s32[256]{0:T(256)S(1)}, s32[256]{0:T(256)}, u32[]{:S(2)}) %copy-start.2) | copy-done | bytes 1048
  10.0 1.8 %collective-permute-start = (s32[1792]{0:T(1024)S(1)}, s32[1792]{0:T(1024)S(1)}, u32[]{:S(2)}, u32[]{:S(2)}) collective-permute-start(s32[1792]{0:T(1024)S(1)} %pad_add_fusion.1), channel_id=1, source_target_pairs={{0,1},{1,0},{2,3},{3,2},{4,5},{5,4},{6,7},{7,6},{8,9},{9,8},{10,11... | collective-permute-start | bytes 21512 | tf_op jit(solution)/shard_map/ppermute | solution.py:12
  12.0 0.7 %copy-done.4 = s32[1,1,16,2]{2,3,1,0:T(2,128)S(1)} copy-done((s32[1,1,16,2]{2,3,1,0:T(2,128)S(1)}, s32[1,1,16,2]{2,3,1,0:T(2,128)}, u32[]{:S(2)}) %copy-start.4) | copy-done | bytes 152
  13.1 1.3 %copy.56 = bf16[256,2,400]{2,1,0:T(2,128)(2,1)S(1)} copy(bf16[256,2,400]{0,2,1:T(8,128)(2,1)} %bitcast.45) | data formatting | bytes 819200 | tf_op jit(solution)/shard_map/reshape | solution.py:162
  14.4 0.4 pad.11
  14.9 1.5 %all-to-all-done = s32[32,1,2]{2,1,0:T(1,128)S(1)} async-done(((s32[32,1,2]{2,1,0:T(1,128)}), s32[32,1,2]{2,1,0:T(1,128)S(1)}, u32[]{:S(2)}, u32[]{:S(2)}) %all-to-all-start) | async-done | bytes 288 | tf_op jit(solution)/shard_map/all_to_all | solution.py:211
  16.5 0.2 copy.63
  17.1 0.3 convolution_convert_fusion
  17.3 0.8 %copy.55 = bf16[32,4,800]{2,1,0:T(4,128)(2,1)} copy(bf16[32,4,800]{2,0,1:T(8,128)(2,1)S(1)} %convolution_convert_fusion) | data formatting | bytes 409600 | tf_op jit(solution)/shard_map/convert_element_type | solution.py:220
  18.1 3.4 %all-to-all-start.1 = ((bf16[32,4,800]{2,1,0:T(4,128)(2,1)}), bf16[32,4,800]{2,1,0:T(4,128)(2,1)S(1)}, u32[]{:S(2)}, u32[]{:S(2)}) async-start(bf16[32,4,800]{2,1,0:T(4,128)(2,1)} %copy.55), calls=%async_computation.1 | async-start | bytes 458752 | tf_op jit(solution)/shard_map/all_to_all | solution.py:221
  21.7 0.4 collective-permute-done.1
  22.2 0.5 copy.57
  22.6 0.4 pad.12
  23.2 8.5 %all-to-all-done.1 = bf16[32,4,800]{2,1,0:T(4,128)(2,1)S(1)} async-done(((bf16[32,4,800]{2,1,0:T(4,128)(2,1)}), bf16[32,4,800]{2,1,0:T(4,128)(2,1)S(1)}, u32[]{:S(2)}, u32[]{:S(2)}) %all-to-all-start.1) | async-done | bytes 204832 | tf_op jit(solution)/shard_map/all_to_all | solution.py:221
  31.7 0.2 reshape_reshape.3
  31.9 0.2 pad.13
  32.2 4.0 %shard_map.112 = (f32[256,1024]{1,0:T(8,128)S(1)}, f32[256,1024]{1,0:T(8,128)S(1)}, bf16[64,800]{1,0:T(8,128)(2,1)S(1)}) custom-call(s32[1,256]{1,0:T(1,128)S(1)} %get-tuple-element.28.wrow, s32[1,256]{1,0:T(1,128)S(1)} %get-tuple-element.27.crow, s32[1,256]{1,0:T(1,128)S(1)} %get-tuple-element.30.scomb, s32[1,256]{1,0:T(1,128)S(1)} %bitcast.38, ...), custom_call_target="tpu_custom_call" | custom-call | tf_op jit(solution)/shard_map/pallas_call | solution.py:132
  36.2 0.6 %copy-done.1 = bf16[64,800]{1,0:T(8,128)(2,1)} copy-done((bf16[64,800]{1,0:T(8,128)(2,1)}, bf16[64,800]{1,0:T(8,128)(2,1)S(1)}, u32[]{:S(2)}) %copy-start.1) | copy-done | bytes 102424
  36.9 1.6 %reshape.191 = bf16[32,2,800]{2,1,0:T(2,128)(2,1)} reshape(bf16[64,800]{1,0:T(8,128)(2,1)} %copy-done.1) | data formatting | bytes 204800 | tf_op jit(solution)/shard_map/reshape | solution.py:246
  38.5 3.5 %all-to-all-start.2 = ((bf16[32,2,800]{2,1,0:T(2,128)(2,1)}), bf16[32,2,800]{2,1,0:T(2,128)(2,1)}, u32[]{:S(2)}, u32[]{:S(2)}) async-start(bf16[32,2,800]{2,1,0:T(2,128)(2,1)} %reshape.191), calls=%async_computation.2 | async-start | bytes 229376 | tf_op jit(solution)/shard_map/all_to_all | solution.py:245
  41.9 4.2 %shard_map.113 = (f32[256,1024]{1,0:T(8,128)S(1)}, f32[256,1024]{1,0:T(8,128)S(1)}, bf16[8,800]{1,0:T(8,128)(2,1)}) custom-call(s32[1,256]{1,0:T(1,128)S(1)} %get-tuple-element.26.wrow, s32[1,256]{1,0:T(1,128)S(1)} %get-tuple-element.25.crow, s32[1,256]{1,0:T(1,128)S(1)} %get-tuple-element.29.scomb, s32[1,256]{1,0:T(1,128)S(1)} %bitcast.39, ...), custom_call_target="tpu_custom_call" | custom-call | tf_op jit(solution)/shard_map/pallas_call | solution.py:132
  46.1 0.5 add_convert_fusion
  46.6 0.4 reshape.190
  47.0 1.1 %copy.59 = bf16[256,2,400]{0,2,1:T(8,128)(2,1)} copy(bf16[256,2,400]{2,1,0:T(2,128)(2,1)S(1)} %bitcast.40) | data formatting | bytes 819200 | tf_op jit(solution)/shard_map/slice | solution.py:168
  48.1 0.4 reshape.189
  48.5 1.1 %copy.58 = bf16[256,2,400]{0,2,1:T(8,128)(2,1)} copy(bf16[256,2,400]{2,1,0:T(2,128)(2,1)S(1)} %bitcast.41) | data formatting | bytes 819200 | tf_op jit(solution)/shard_map/slice | solution.py:168
  49.5 0.6 %all-to-all-done.2 = bf16[32,2,800]{2,1,0:T(2,128)(2,1)} async-done(((bf16[32,2,800]{2,1,0:T(2,128)(2,1)}), bf16[32,2,800]{2,1,0:T(2,128)(2,1)}, u32[]{:S(2)}, u32[]{:S(2)}) %all-to-all-start.2) | async-done | bytes 102432 | tf_op jit(solution)/shard_map/all_to_all | solution.py:245
  50.1 1.0 %convert_element_type.40 = f32[32,2,800]{2,1,0:T(2,128)S(1)} convert(bf16[32,2,800]{2,1,0:T(2,128)(2,1)} %all-to-all-done.2) | non-fusion elementwise | flops 51200 | bytes 307200 | tf_op jit(solution)/shard_map/convert_element_type | solution.py:251
  51.3 0.2 reshape.192
  51.4 0.9 %fusion.2 = f32[32,800]{1,0:T(8,128)} fusion(f32[64,800]{1,0:T(8,128)S(1)} %reshape.192, s32[64]{0:T(128)S(1)} %eq.38), kind=kOutput, calls=%fused_computation.9 | convolution fusion | flops 19662848 | bytes 307456 | tf_op jit(solution)/shard_map/dot_general | solution.py:256
  (45 shorter events, 1.4 us)
Async XLA Ops:
  0.6 16.4 %copy-start = (bf16[32,800]{1,0:T(8,128)(2,1)S(1)}, bf16[32,800]{1,0:T(8,128)(2,1)}, u32[]{:S(2)}) copy-start(bf16[32,800]{1,0:T(8,128)(2,1)} %param.11) | copy-start | bytes 153604
  2.0 7.3 %copy-start.3 = (s32[1,1024]{1,0:T(1,128)S(1)}, s32[1,1024]{1,0:T(1,128)}, u32[]{:S(2)}) copy-start(s32[1,1024]{1,0:T(1,128)} %param.15) | copy-start | bytes 12292
  2.0 7.3 %copy-start.5 = (s32[256]{0:T(256)S(1)}, s32[256]{0:T(256)}, u32[]{:S(2)}) copy-start(s32[256]{0:T(256)} %param.13) | copy-start | bytes 3076
  2.0 7.3 %copy-start.6 = (s32[256]{0:T(256)S(1)}, s32[256]{0:T(256)}, u32[]{:S(2)}) copy-start(s32[256]{0:T(256)} %param.12) | copy-start | bytes 3076
  2.0 14.4 %all-to-all-start = ((s32[32,1,2]{2,1,0:T(1,128)}), s32[32,1,2]{2,1,0:T(1,128)S(1)}, u32[]{:S(2)}, u32[]{:S(2)}) async-start(s32[32,1,2]{2,1,0:T(1,128)} %bitcast.2), calls=%async_computation | async-start | bytes 32768 | tf_op jit(solution)/shard_map/all_to_all | solution.py:211
  9.3 0.7 %copy-start.2 = (s32[256]{0:T(256)S(1)}, s32[256]{0:T(256)}, u32[]{:S(2)}) copy-start(s32[256]{0:T(256)} %param.14) | copy-start | bytes 3076
  10.0 11.6 %collective-permute-start = (s32[1792]{0:T(1024)S(1)}, s32[1792]{0:T(1024)S(1)}, u32[]{:S(2)}, u32[]{:S(2)}) collective-permute-start(s32[1792]{0:T(1024)S(1)} %pad_add_fusion.1), channel_id=1, source_target_pairs={{0,1},{1,0},{2,3},{3,2},{4,5},{5,4},{6,7},{7,6},{8,9},{9,8},{10,11... | collective-permute-start | bytes 21512 | tf_op jit(solution)/shard_map/ppermute | solution.py:12
  11.9 10.3 %collective-permute-start.1 = (bf16[256,800]{0,1:T(8,128)(2,1)}, bf16[256,800]{0,1:T(8,128)(2,1)S(1)}, u32[]{:S(2)}, u32[]{:S(2)}) collective-permute-start(bf16[256,800]{0,1:T(8,128)(2,1)} %param.10), channel_id=1, source_target_pairs={{0,2},{2,4},{4,6},{6,8},{8,10},{10,12},{12,14},{14,16},{16,18},{18... | collective-permute-start | bytes 1228808 | tf_op jit(solution)/shard_map/ppermute | solution.py:12
  11.9 0.7 %copy-start.4 = (s32[1,1,16,2]{2,3,1,0:T(2,128)S(1)}, s32[1,1,16,2]{2,3,1,0:T(2,128)}, u32[]{:S(2)}) copy-start(s32[1,1,16,2]{2,3,1,0:T(2,128)} %param.17) | copy-start | bytes 388
  18.1 13.6 %all-to-all-start.1 = ((bf16[32,4,800]{2,1,0:T(4,128)(2,1)}), bf16[32,4,800]{2,1,0:T(4,128)(2,1)S(1)}, u32[]{:S(2)}, u32[]{:S(2)}) async-start(bf16[32,4,800]{2,1,0:T(4,128)(2,1)} %copy.55), calls=%async_computation.1 | async-start | bytes 458752 | tf_op jit(solution)/shard_map/all_to_all | solution.py:221
  36.2 0.6 %copy-start.1 = (bf16[64,800]{1,0:T(8,128)(2,1)}, bf16[64,800]{1,0:T(8,128)(2,1)S(1)}, u32[]{:S(2)}) copy-start(bf16[64,800]{1,0:T(8,128)(2,1)S(1)} %get-tuple-element.20) | copy-start | bytes 307204
  38.5 11.6 %all-to-all-start.2 = ((bf16[32,2,800]{2,1,0:T(2,128)(2,1)}), bf16[32,2,800]{2,1,0:T(2,128)(2,1)}, u32[]{:S(2)}, u32[]{:S(2)}) async-start(bf16[32,2,800]{2,1,0:T(2,128)(2,1)} %reshape.191), calls=%async_computation.2 | async-start | bytes 229376 | tf_op jit(solution)/shard_map/all_to_all | solution.py:245

commit v13 on v12

--- a/solution.py
+++ b/solution.py
@@ -134,7 +134,7 @@
         out_shape=(
             jax.ShapeDtypeStruct((parts, width), jnp.float32),
             jax.ShapeDtypeStruct((parts, width), jnp.float32),
-            jax.ShapeDtypeStruct((own_rows.shape[0], row_width), jnp.bfloat16),
+            jax.ShapeDtypeStruct((own_rows.shape[0], row_width), jnp.float32),
         ),
         compiler_params=pltpu.CompilerParams(vmem_limit_bytes=48 * 1024 * 1024),
     )(
@@ -243,7 +243,7 @@
     word_sum = unpadded_halves(own_word + rest_word, half_width)
     ctx_sum = unpadded_halves(own_ctx + rest_ctx, half_width)
     returned = lax.all_to_all(
-        own_slot.reshape(owner_count, slot_count, row_width),
+        own_slot.astype(jnp.bfloat16).reshape(owner_count, slot_count, row_width),
         both,
         split_axis=0,
         concat_axis=0,

time: 52.7 us -> 52.7 us (level)
  other arithmetic: 1.66 us -> 2.32 us
  local copies, waits for them, and re-layouts: 13.3 us -> 12.7 us
    convert_element_type x1 -> x2, other arithmetic: 0.98 us -> 1.64 us  [the longest x1 0.98 us: shards(): returned = lax.all_to_all(own_slot.astype(jnp.bfloat16).reshape(owner_cou...]
    unnamed x18 -> x16, local copies, waits for them, and re-layouts: 2.21 us -> 1.57 us
where the time goes in v13:
time: 52.7 us; the launch traced here: 52.3 us
  starting transfers between devices  16 us (30%)
  local copies, waits for them, and re-layouts  12.7 us (24%)
  waiting for transfers between devices  11 us (21%)
  Pallas kernels  8.29 us (16%)
  other arithmetic  2.32 us (4%)
  matrix products  1.12 us (2%)
  between operations  0.91 us (2%)
    all_to_all x1, waiting for transfers between devices, shards(): lax.all_to_all(picked, both, split_axis=0, concat_axis=0, tiled=True)  8.53 us
    pallas_call x2, Pallas kernels, block_chains(): pl.pallas_call(body, out_shape=(jax.ShapeDtypeStruct((parts, width), jnp....  8.29 us
    all_to_all x1, starting transfers between devices, shards(): lax.all_to_all(wanted, both, split_axis=0, concat_axis=0, tiled=True)  7.3 us
    all_to_all x1, starting transfers between devices, shards(): lax.all_to_all(own_slot.astype(jnp.bfloat16).reshape(owner_count, slot_co...  3.45 us
    all_to_all x1, starting transfers between devices, shards(): lax.all_to_all(picked, both, split_axis=0, concat_axis=0, tiled=True)  3.38 us
    slice x2, local copies, waits for them, and re-layouts, unpadded_halves(): rows.reshape(count, 2, lanes_of(half_width))[:, :, :half_width]  2.14 us
    ppermute x2, starting transfers between devices, passed_along(): lax.ppermute(shard, axis, [(i, (i + by) % length) for i in range(length)])  1.84 us
    reshape x2, local copies, waits for them, and re-layouts, padded_halves(): rows.reshape(count, 2, half_width)  1.81 us
  transfers between devices with their start and end apart: 5, of which 4 were waited for; matrix products, arithmetic and copies ran while one was open for 16% of the time, Pallas kernels for 8%

profile of v13, /device:TPU:0, one launch (start us, length us, event | category | flops | bytes accessed | tf_op | source)
XLA Modules:
  0.0 52.3 jit_solution(3613412077760766098)
XLA Ops:
  0.6 1.4 %copy.62 = s32[1,1,16,2,2]{4,3,2,1,0:T(2,128)} copy(s32[1,1,16,2,2]{2,4,3,1,0:T(2,128)} %param.16) | data formatting | bytes 512 | tf_op jit(solution)/shard_map/all_to_all | solution.py:211
  2.0 7.3 %all-to-all-start = ((s32[32,1,2]{2,1,0:T(1,128)}), s32[32,1,2]{2,1,0:T(1,128)S(1)}, u32[]{:S(2)}, u32[]{:S(2)}) async-start(s32[32,1,2]{2,1,0:T(1,128)} %bitcast.2), calls=%async_computation | async-start | bytes 32768 | tf_op jit(solution)/shard_map/all_to_all | solution.py:211
  9.4 0.6 %copy-done.1 = s32[256]{0:T(256)S(1)} copy-done((s32[256]{0:T(256)S(1)}, s32[256]{0:T(256)}, u32[]{:S(2)}) %copy-start.1) | copy-done | bytes 1048
  10.0 1.8 %collective-permute-start = (s32[1792]{0:T(1024)S(1)}, s32[1792]{0:T(1024)S(1)}, u32[]{:S(2)}, u32[]{:S(2)}) collective-permute-start(s32[1792]{0:T(1024)S(1)} %pad_add_fusion.1), channel_id=1, source_target_pairs={{0,1},{1,0},{2,3},{3,2},{4,5},{5,4},{6,7},{7,6},{8,9},{9,8},{10,11... | collective-permute-start | bytes 21512 | tf_op jit(solution)/shard_map/ppermute | solution.py:12
  12.0 0.7 %copy-done.3 = s32[1,1,16,2]{2,3,1,0:T(2,128)S(1)} copy-done((s32[1,1,16,2]{2,3,1,0:T(2,128)S(1)}, s32[1,1,16,2]{2,3,1,0:T(2,128)}, u32[]{:S(2)}) %copy-start.3) | copy-done | bytes 152
  13.1 1.3 %copy.56 = bf16[256,2,400]{2,1,0:T(2,128)(2,1)S(1)} copy(bf16[256,2,400]{0,2,1:T(8,128)(2,1)} %bitcast.45) | data formatting | bytes 819200 | tf_op jit(solution)/shard_map/reshape | solution.py:162
  14.4 0.4 pad.11
  14.9 1.5 %all-to-all-done = s32[32,1,2]{2,1,0:T(1,128)S(1)} async-done(((s32[32,1,2]{2,1,0:T(1,128)}), s32[32,1,2]{2,1,0:T(1,128)S(1)}, u32[]{:S(2)}, u32[]{:S(2)}) %all-to-all-start) | async-done | bytes 288 | tf_op jit(solution)/shard_map/all_to_all | solution.py:211
  16.5 0.2 copy.63
  17.1 0.3 convolution_convert_fusion
  17.3 0.8 %copy.55 = bf16[32,4,800]{2,1,0:T(4,128)(2,1)} copy(bf16[32,4,800]{2,0,1:T(8,128)(2,1)S(1)} %convolution_convert_fusion) | data formatting | bytes 409600 | tf_op jit(solution)/shard_map/convert_element_type | solution.py:220
  18.1 3.4 %all-to-all-start.1 = ((bf16[32,4,800]{2,1,0:T(4,128)(2,1)}), bf16[32,4,800]{2,1,0:T(4,128)(2,1)S(1)}, u32[]{:S(2)}, u32[]{:S(2)}) async-start(bf16[32,4,800]{2,1,0:T(4,128)(2,1)} %copy.55), calls=%async_computation.1 | async-start | bytes 458752 | tf_op jit(solution)/shard_map/all_to_all | solution.py:221
  21.7 0.4 collective-permute-done.1
  22.2 0.5 copy.57
  22.6 0.4 pad.12
  23.2 8.5 %all-to-all-done.1 = bf16[32,4,800]{2,1,0:T(4,128)(2,1)S(1)} async-done(((bf16[32,4,800]{2,1,0:T(4,128)(2,1)}), bf16[32,4,800]{2,1,0:T(4,128)(2,1)S(1)}, u32[]{:S(2)}, u32[]{:S(2)}) %all-to-all-start.1) | async-done | bytes 204832 | tf_op jit(solution)/shard_map/all_to_all | solution.py:221
  31.7 0.2 reshape_reshape.3
  31.9 0.2 pad.13
  32.2 4.0 %shard_map.112 = (f32[256,1024]{1,0:T(8,128)S(1)}, f32[256,1024]{1,0:T(8,128)S(1)}, f32[64,800]{1,0:T(8,128)S(1)}) custom-call(s32[1,256]{1,0:T(1,128)S(1)} %get-tuple-element.28.wrow, s32[1,256]{1,0:T(1,128)S(1)} %get-tuple-element.27.crow, s32[1,256]{1,0:T(1,128)S(1)} %get-tuple-element.30.scomb, s32[1,256]{1,0:T(1,128)S(1)} %bitcast.38, ...), custom_call_target="tpu_custom_call" | custom-call | tf_op jit(solution)/shard_map/pallas_call | solution.py:132
  36.2 0.7 %convert_element_type.43 = bf16[64,800]{1,0:T(8,128)(2,1)} convert(f32[64,800]{1,0:T(8,128)S(1)} %get-tuple-element.20) | non-fusion elementwise | flops 51200 | bytes 307200 | tf_op jit(solution)/shard_map/convert_element_type | solution.py:246
  36.9 1.6 %reshape.191 = bf16[32,2,800]{2,1,0:T(2,128)(2,1)} reshape(bf16[64,800]{1,0:T(8,128)(2,1)} %convert_element_type.43) | data formatting | bytes 204800 | tf_op jit(solution)/shard_map/reshape | solution.py:246
  38.5 3.4 %all-to-all-start.2 = ((bf16[32,2,800]{2,1,0:T(2,128)(2,1)}), bf16[32,2,800]{2,1,0:T(2,128)(2,1)}, u32[]{:S(2)}, u32[]{:S(2)}) async-start(bf16[32,2,800]{2,1,0:T(2,128)(2,1)} %reshape.191), calls=%async_computation.2 | async-start | bytes 229376 | tf_op jit(solution)/shard_map/all_to_all | solution.py:245
  41.9 4.3 %shard_map.113 = (f32[256,1024]{1,0:T(8,128)S(1)}, f32[256,1024]{1,0:T(8,128)S(1)}, f32[8,800]{1,0:T(8,128)}) custom-call(s32[1,256]{1,0:T(1,128)S(1)} %get-tuple-element.26.wrow, s32[1,256]{1,0:T(1,128)S(1)} %get-tuple-element.25.crow, s32[1,256]{1,0:T(1,128)S(1)} %get-tuple-element.29.scomb, s32[1,256]{1,0:T(1,128)S(1)} %bitcast.39, ...), custom_call_target="tpu_custom_call" | custom-call | tf_op jit(solution)/shard_map/pallas_call | solution.py:132
  46.2 0.5 add_convert_fusion
  46.7 0.4 reshape.190
  47.1 1.1 %copy.59 = bf16[256,2,400]{0,2,1:T(8,128)(2,1)} copy(bf16[256,2,400]{2,1,0:T(2,128)(2,1)S(1)} %bitcast.40) | data formatting | bytes 819200 | tf_op jit(solution)/shard_map/slice | solution.py:168
  48.1 0.4 reshape.189
  48.5 1.1 %copy.58 = bf16[256,2,400]{0,2,1:T(8,128)(2,1)} copy(bf16[256,2,400]{2,1,0:T(2,128)(2,1)S(1)} %bitcast.41) | data formatting | bytes 819200 | tf_op jit(solution)/shard_map/slice | solution.py:168
  49.6 0.5 all-to-all-done.2
  50.1 1.0 %convert_element_type.44 = f32[32,2,800]{2,1,0:T(2,128)S(1)} convert(bf16[32,2,800]{2,1,0:T(2,128)(2,1)} %all-to-all-done.2) | non-fusion elementwise | flops 51200 | bytes 307200 | tf_op jit(solution)/shard_map/convert_element_type | solution.py:251
  51.3 0.2 reshape.192
  51.5 0.9 %fusion.2 = f32[32,800]{1,0:T(8,128)} fusion(f32[64,800]{1,0:T(8,128)S(1)} %reshape.192, s32[64]{0:T(128)S(1)} %eq.38), kind=kOutput, calls=%fused_computation.9 | convolution fusion | flops 19662848 | bytes 307456 | tf_op jit(solution)/shard_map/dot_general | solution.py:256
  (44 shorter events, 1.4 us)
Async XLA Ops:
  0.6 16.4 %copy-start = (bf16[32,800]{1,0:T(8,128)(2,1)S(1)}, bf16[32,800]{1,0:T(8,128)(2,1)}, u32[]{:S(2)}) copy-start(bf16[32,800]{1,0:T(8,128)(2,1)} %param.11) | copy-start | bytes 153604
  2.0 7.3 %copy-start.2 = (s32[1,1024]{1,0:T(1,128)S(1)}, s32[1,1024]{1,0:T(1,128)}, u32[]{:S(2)}) copy-start(s32[1,1024]{1,0:T(1,128)} %param.15) | copy-start | bytes 12292
  2.0 7.3 %copy-start.4 = (s32[256]{0:T(256)S(1)}, s32[256]{0:T(256)}, u32[]{:S(2)}) copy-start(s32[256]{0:T(256)} %param.13) | copy-start | bytes 3076
  2.0 7.3 %copy-start.5 = (s32[256]{0:T(256)S(1)}, s32[256]{0:T(256)}, u32[]{:S(2)}) copy-start(s32[256]{0:T(256)} %param.12) | copy-start | bytes 3076
  2.0 14.4 %all-to-all-start = ((s32[32,1,2]{2,1,0:T(1,128)}), s32[32,1,2]{2,1,0:T(1,128)S(1)}, u32[]{:S(2)}, u32[]{:S(2)}) async-start(s32[32,1,2]{2,1,0:T(1,128)} %bitcast.2), calls=%async_computation | async-start | bytes 32768 | tf_op jit(solution)/shard_map/all_to_all | solution.py:211
  9.3 0.7 %copy-start.1 = (s32[256]{0:T(256)S(1)}, s32[256]{0:T(256)}, u32[]{:S(2)}) copy-start(s32[256]{0:T(256)} %param.14) | copy-start | bytes 3076
  10.0 11.6 %collective-permute-start = (s32[1792]{0:T(1024)S(1)}, s32[1792]{0:T(1024)S(1)}, u32[]{:S(2)}, u32[]{:S(2)}) collective-permute-start(s32[1792]{0:T(1024)S(1)} %pad_add_fusion.1), channel_id=1, source_target_pairs={{0,1},{1,0},{2,3},{3,2},{4,5},{5,4},{6,7},{7,6},{8,9},{9,8},{10,11... | collective-permute-start | bytes 21512 | tf_op jit(solution)/shard_map/ppermute | solution.py:12
  11.9 10.3 %collective-permute-start.1 = (bf16[256,800]{0,1:T(8,128)(2,1)}, bf16[256,800]{0,1:T(8,128)(2,1)S(1)}, u32[]{:S(2)}, u32[]{:S(2)}) collective-permute-start(bf16[256,800]{0,1:T(8,128)(2,1)} %param.10), channel_id=1, source_target_pairs={{0,2},{2,4},{4,6},{6,8},{8,10},{10,12},{12,14},{14,16},{16,18},{18... | collective-permute-start | bytes 1228808 | tf_op jit(solution)/shard_map/ppermute | solution.py:12
  11.9 0.7 %copy-start.3 = (s32[1,1,16,2]{2,3,1,0:T(2,128)S(1)}, s32[1,1,16,2]{2,3,1,0:T(2,128)}, u32[]{:S(2)}) copy-start(s32[1,1,16,2]{2,3,1,0:T(2,128)} %param.17) | copy-start | bytes 388
  18.1 13.6 %all-to-all-start.1 = ((bf16[32,4,800]{2,1,0:T(4,128)(2,1)}), bf16[32,4,800]{2,1,0:T(4,128)(2,1)S(1)}, u32[]{:S(2)}, u32[]{:S(2)}) async-start(bf16[32,4,800]{2,1,0:T(4,128)(2,1)} %copy.55), calls=%async_computation.1 | async-start | bytes 458752 | tf_op jit(solution)/shard_map/all_to_all | solution.py:221
  38.5 11.6 %all-to-all-start.2 = ((bf16[32,2,800]{2,1,0:T(2,128)(2,1)}), bf16[32,2,800]{2,1,0:T(2,128)(2,1)}, u32[]{:S(2)}, u32[]{:S(2)}) async-start(bf16[32,2,800]{2,1,0:T(2,128)(2,1)} %reshape.191), calls=%async_computation.2 | async-start | bytes 229376 | tf_op jit(solution)/shard_map/all_to_all | solution.py:245

commit v14 on v13

--- a/solution.py
+++ b/solution.py
@@ -248,16 +248,11 @@
         split_axis=0,
         concat_axis=0,
         tiled=True,
-    ).astype(jnp.float32)
+    )
     incoming, returned = lax.optimization_barrier((incoming, returned))
-    owner_map = (incoming.reshape(-1)[None, :] == jnp.arange(owned_rows)[:, None]).astype(
-        jnp.float32
-    )
-    relation_grad = jnp.dot(
-        owner_map,
-        returned.reshape(-1, row_width),
-        precision=lax.Precision.HIGHEST,
-        preferred_element_type=jnp.float32,
+    owner_map = one_hot(incoming.reshape(owner_count, slot_count), owned_rows)
+    relation_grad = jnp.einsum(
+        "dkr,dkf->rf", owner_map, returned, preferred_element_type=jnp.float32
     )
     return (word_sum.astype(jnp.bfloat16), ctx_sum.astype(jnp.bfloat16), relation_grad)
 

time: 52.7 us -> 52 us (0.987)
  other arithmetic: 2.32 us -> 1.35 us
  matrix products: 1.12 us -> 2.01 us
  local copies, waits for them, and re-layouts: 12.7 us -> 12.1 us
    convert_element_type x1 -> x0, other arithmetic: 0.98 us -> none  [shards(): returned = lax.all_to_all(own_slot.astype(jnp.bfloat16).reshape(owner_cou...]
    dot_general x1, matrix products: 0.86 us -> 1.76 us  [shards(): jnp.einsum('dkr,dkf->rf', owner_map, returned, preferred_element_type=jnp...]
  transfers between devices with their start and end apart: 5 -> 5, of which waited for: 4 -> 3; matrix products, arithmetic and copies ran while one was open for 16% -> 16% of each run, Pallas kernels for 8% -> 8%
where the time goes in v14:
time: 52 us; the launch traced here: 51.6 us
  starting transfers between devices  16 us (31%)
  local copies, waits for them, and re-layouts  12.1 us (23%)
  waiting for transfers between devices  11.1 us (21%)
  Pallas kernels  8.26 us (16%)
  matrix products  2.01 us (4%)
  other arithmetic  1.35 us (3%)
  between operations  0.87 us (2%)
    all_to_all x1, waiting for transfers between devices, shards(): lax.all_to_all(picked, both, split_axis=0, concat_axis=0, tiled=True)  8.96 us
    pallas_call x2, Pallas kernels, block_chains(): pl.pallas_call(body, out_shape=(jax.ShapeDtypeStruct((parts, width), jnp....  8.26 us
    all_to_all x1, starting transfers between devices, shards(): lax.all_to_all(wanted, both, split_axis=0, concat_axis=0, tiled=True)  7.3 us
    all_to_all x1, starting transfers between devices, shards(): lax.all_to_all(own_slot.astype(jnp.bfloat16).reshape(owner_count, slot_co...  3.45 us
    all_to_all x1, starting transfers between devices, shards(): lax.all_to_all(picked, both, split_axis=0, concat_axis=0, tiled=True)  3.07 us
    slice x2, local copies, waits for them, and re-layouts, unpadded_halves(): rows.reshape(count, 2, lanes_of(half_width))[:, :, :half_width]  2.14 us
    ppermute x2, starting transfers between devices, passed_along(): lax.ppermute(shard, axis, [(i, (i + by) % length) for i in range(length)])  2.14 us
    reshape x2, local copies, waits for them, and re-layouts, padded_halves(): rows.reshape(count, 2, half_width)  1.81 us
  transfers between devices with their start and end apart: 5, of which 3 were waited for; matrix products, arithmetic and copies ran while one was open for 16% of the time, Pallas kernels for 8%

profile of v14, /device:TPU:0, one launch (start us, length us, event | category | flops | bytes accessed | tf_op | source)
XLA Modules:
  0.0 51.6 jit_solution(15036817359876802623)
XLA Ops:
  0.6 1.4 %copy.62 = s32[1,1,16,2,2]{4,3,2,1,0:T(2,128)} copy(s32[1,1,16,2,2]{2,4,3,1,0:T(2,128)} %param.16) | data formatting | bytes 512 | tf_op jit(solution)/shard_map/all_to_all | solution.py:211
  2.0 7.3 %all-to-all-start = ((s32[32,1,2]{2,1,0:T(1,128)}), s32[32,1,2]{2,1,0:T(1,128)S(1)}, u32[]{:S(2)}, u32[]{:S(2)}) async-start(s32[32,1,2]{2,1,0:T(1,128)} %bitcast.2), calls=%async_computation | async-start | bytes 32768 | tf_op jit(solution)/shard_map/all_to_all | solution.py:211
  9.4 0.3 collective-permute-start.1
  9.7 0.4 copy-done.1
  10.0 1.8 %collective-permute-start = (s32[1792]{0:T(1024)S(1)}, s32[1792]{0:T(1024)S(1)}, u32[]{:S(2)}, u32[]{:S(2)}) collective-permute-start(s32[1792]{0:T(1024)S(1)} %pad_add_fusion.1), channel_id=1, source_target_pairs={{0,1},{1,0},{2,3},{3,2},{4,5},{5,4},{6,7},{7,6},{8,9},{9,8},{10,11... | collective-permute-start | bytes 21512 | tf_op jit(solution)/shard_map/ppermute | solution.py:12
  11.9 0.7 %copy-done.3 = s32[1,1,16,2]{2,3,1,0:T(2,128)S(1)} copy-done((s32[1,1,16,2]{2,3,1,0:T(2,128)S(1)}, s32[1,1,16,2]{2,3,1,0:T(2,128)}, u32[]{:S(2)}) %copy-start.3) | copy-done | bytes 152
  12.9 1.3 %copy.56 = bf16[256,2,400]{2,1,0:T(2,128)(2,1)S(1)} copy(bf16[256,2,400]{0,2,1:T(8,128)(2,1)} %bitcast.46) | data formatting | bytes 819200 | tf_op jit(solution)/shard_map/reshape | solution.py:162
  14.2 0.4 pad.11
  14.7 0.1 reshape.189.live
  14.9 1.6 %all-to-all-done = s32[32,1,2]{2,1,0:T(1,128)S(1)} async-done(((s32[32,1,2]{2,1,0:T(1,128)}), s32[32,1,2]{2,1,0:T(1,128)S(1)}, u32[]{:S(2)}, u32[]{:S(2)}) %all-to-all-start) | async-done | bytes 288 | tf_op jit(solution)/shard_map/all_to_all | solution.py:211
  16.7 0.1 copy.54
  16.8 0.2 copy.63
  17.1 0.3 convolution_convert_fusion
  17.3 0.8 %copy.55 = bf16[32,4,800]{2,1,0:T(4,128)(2,1)} copy(bf16[32,4,800]{2,0,1:T(8,128)(2,1)S(1)} %convolution_convert_fusion) | data formatting | bytes 409600 | tf_op jit(solution)/shard_map/convert_element_type | solution.py:220
  18.2 3.1 %all-to-all-start.1 = ((bf16[32,4,800]{2,1,0:T(4,128)(2,1)}), bf16[32,4,800]{2,1,0:T(4,128)(2,1)S(1)}, u32[]{:S(2)}, u32[]{:S(2)}) async-start(bf16[32,4,800]{2,1,0:T(4,128)(2,1)} %copy.55), calls=%async_computation.1 | async-start | bytes 458752 | tf_op jit(solution)/shard_map/all_to_all | solution.py:221
  21.4 0.5 copy.57
  21.9 0.4 pad.12
  22.4 9.0 %all-to-all-done.1 = bf16[32,4,800]{2,1,0:T(4,128)(2,1)S(1)} async-done(((bf16[32,4,800]{2,1,0:T(4,128)(2,1)}), bf16[32,4,800]{2,1,0:T(4,128)(2,1)S(1)}, u32[]{:S(2)}, u32[]{:S(2)}) %all-to-all-start.1) | async-done | bytes 204832 | tf_op jit(solution)/shard_map/all_to_all | solution.py:221
  31.4 0.2 reshape_reshape.3
  31.6 0.2 pad.13
  31.9 4.0 %shard_map.112 = (f32[256,1024]{1,0:T(8,128)S(1)}, f32[256,1024]{1,0:T(8,128)S(1)}, f32[64,800]{1,0:T(8,128)S(1)}) custom-call(s32[1,256]{1,0:T(1,128)S(1)} %get-tuple-element.28.wrow, s32[1,256]{1,0:T(1,128)S(1)} %get-tuple-element.27.crow, s32[1,256]{1,0:T(1,128)S(1)} %get-tuple-element.30.scomb, s32[1,256]{1,0:T(1,128)S(1)} %bitcast.39, ...), custom_call_target="tpu_custom_call" | custom-call | tf_op jit(solution)/shard_map/pallas_call | solution.py:132
  35.9 0.7 %convert_element_type.40 = bf16[64,800]{1,0:T(8,128)(2,1)} convert(f32[64,800]{1,0:T(8,128)S(1)} %get-tuple-element.20) | non-fusion elementwise | flops 51200 | bytes 307200 | tf_op jit(solution)/shard_map/convert_element_type | solution.py:246
  36.6 1.6 %reshape.188 = bf16[32,2,800]{2,1,0:T(2,128)(2,1)} reshape(bf16[64,800]{1,0:T(8,128)(2,1)} %convert_element_type.40) | data formatting | bytes 204800 | tf_op jit(solution)/shard_map/reshape | solution.py:246
  38.2 3.4 %all-to-all-start.2 = ((bf16[32,2,800]{2,1,0:T(2,128)(2,1)}), bf16[32,2,800]{2,1,0:T(2,128)(2,1)}, u32[]{:S(2)}, u32[]{:S(2)}) async-start(bf16[32,2,800]{2,1,0:T(2,128)(2,1)} %reshape.188), calls=%async_computation.2 | async-start | bytes 229376 | tf_op jit(solution)/shard_map/all_to_all | solution.py:245
  41.6 4.3 %shard_map.113 = (f32[256,1024]{1,0:T(8,128)S(1)}, f32[256,1024]{1,0:T(8,128)S(1)}, f32[8,800]{1,0:T(8,128)}) custom-call(s32[1,256]{1,0:T(1,128)S(1)} %get-tuple-element.26.wrow, s32[1,256]{1,0:T(1,128)S(1)} %get-tuple-element.25.crow, s32[1,256]{1,0:T(1,128)S(1)} %get-tuple-element.29.scomb, s32[1,256]{1,0:T(1,128)S(1)} %bitcast.40, ...), custom_call_target="tpu_custom_call" | custom-call | tf_op jit(solution)/shard_map/pallas_call | solution.py:132
  45.9 0.5 add_convert_fusion
  46.4 0.4 reshape.186
  46.8 1.1 %copy.58 = bf16[256,2,400]{0,2,1:T(8,128)(2,1)} copy(bf16[256,2,400]{2,1,0:T(2,128)(2,1)S(1)} %bitcast.41) | data formatting | bytes 819200 | tf_op jit(solution)/shard_map/slice | solution.py:168
  47.8 0.4 reshape.187
  48.2 1.1 %copy.59 = bf16[256,2,400]{0,2,1:T(8,128)(2,1)} copy(bf16[256,2,400]{2,1,0:T(2,128)(2,1)S(1)} %bitcast.42) | data formatting | bytes 819200 | tf_op jit(solution)/shard_map/slice | solution.py:168
  49.3 0.5 %all-to-all-done.2 = bf16[32,2,800]{2,1,0:T(2,128)(2,1)} async-done(((bf16[32,2,800]{2,1,0:T(2,128)(2,1)}), bf16[32,2,800]{2,1,0:T(2,128)(2,1)}, u32[]{:S(2)}, u32[]{:S(2)}) %all-to-all-start.2) | async-done | bytes 102432 | tf_op jit(solution)/shard_map/all_to_all | solution.py:245
  49.8 1.8 %convolution_bitcast_fusion = f32[32,800]{1,0:T(8,128)} fusion(bf16[32,2,800]{2,1,0:T(2,128)(2,1)} %all-to-all-done.2, s32[32,2]{0,1:T(2,128)S(1)} %bitcast.52), kind=kOutput, calls=%fused_computation.1 | convolution fusion | flops 3278848 | bytes 205056 | tf_op jit(solution)/shard_map/dkr,dkf->rf/dot_general | solution.py:254
  (40 shorter events, 1.0 us)
Async XLA Ops:
  0.6 16.4 %copy-start = (bf16[32,800]{1,0:T(8,128)(2,1)S(1)}, bf16[32,800]{1,0:T(8,128)(2,1)}, u32[]{:S(2)}) copy-start(bf16[32,800]{1,0:T(8,128)(2,1)} %param.11) | copy-start | bytes 153604
  2.0 7.6 %copy-start.2 = (s32[1,1024]{1,0:T(1,128)S(1)}, s32[1,1024]{1,0:T(1,128)}, u32[]{:S(2)}) copy-start(s32[1,1024]{1,0:T(1,128)} %param.15) | copy-start | bytes 12292
  2.0 7.6 %copy-start.4 = (s32[256]{0:T(256)S(1)}, s32[256]{0:T(256)}, u32[]{:S(2)}) copy-start(s32[256]{0:T(256)} %param.13) | copy-start | bytes 3076
  2.0 7.6 %copy-start.5 = (s32[256]{0:T(256)S(1)}, s32[256]{0:T(256)}, u32[]{:S(2)}) copy-start(s32[256]{0:T(256)} %param.12) | copy-start | bytes 3076
  2.0 14.4 %all-to-all-start = ((s32[32,1,2]{2,1,0:T(1,128)}), s32[32,1,2]{2,1,0:T(1,128)S(1)}, u32[]{:S(2)}, u32[]{:S(2)}) async-start(s32[32,1,2]{2,1,0:T(1,128)} %bitcast.2), calls=%async_computation | async-start | bytes 32768 | tf_op jit(solution)/shard_map/all_to_all | solution.py:211
  9.3 0.7 %copy-start.1 = (s32[256]{0:T(256)S(1)}, s32[256]{0:T(256)}, u32[]{:S(2)}) copy-start(s32[256]{0:T(256)} %param.14) | copy-start | bytes 3076
  9.4 12.1 %collective-permute-start.1 = (bf16[256,800]{0,1:T(8,128)(2,1)}, bf16[256,800]{0,1:T(8,128)(2,1)S(1)}, u32[]{:S(2)}, u32[]{:S(2)}) collective-permute-start(bf16[256,800]{0,1:T(8,128)(2,1)} %param.10), channel_id=1, source_target_pairs={{0,2},{2,4},{4,6},{6,8},{8,10},{10,12},{12,14},{14,16},{16,18},{18... | collective-permute-start | bytes 1228808 | tf_op jit(solution)/shard_map/ppermute | solution.py:12
  10.0 11.3 %collective-permute-start = (s32[1792]{0:T(1024)S(1)}, s32[1792]{0:T(1024)S(1)}, u32[]{:S(2)}, u32[]{:S(2)}) collective-permute-start(s32[1792]{0:T(1024)S(1)} %pad_add_fusion.1), channel_id=1, source_target_pairs={{0,1},{1,0},{2,3},{3,2},{4,5},{5,4},{6,7},{7,6},{8,9},{9,8},{10,11... | collective-permute-start | bytes 21512 | tf_op jit(solution)/shard_map/ppermute | solution.py:12
  11.9 0.7 %copy-start.3 = (s32[1,1,16,2]{2,3,1,0:T(2,128)S(1)}, s32[1,1,16,2]{2,3,1,0:T(2,128)}, u32[]{:S(2)}) copy-start(s32[1,1,16,2]{2,3,1,0:T(2,128)} %param.17) | copy-start | bytes 388
  18.2 13.3 %all-to-all-start.1 = ((bf16[32,4,800]{2,1,0:T(4,128)(2,1)}), bf16[32,4,800]{2,1,0:T(4,128)(2,1)S(1)}, u32[]{:S(2)}, u32[]{:S(2)}) async-start(bf16[32,4,800]{2,1,0:T(4,128)(2,1)} %copy.55), calls=%async_computation.1 | async-start | bytes 458752 | tf_op jit(solution)/shard_map/all_to_all | solution.py:221
  38.2 11.6 %all-to-all-start.2 = ((bf16[32,2,800]{2,1,0:T(2,128)(2,1)}), bf16[32,2,800]{2,1,0:T(2,128)(2,1)}, u32[]{:S(2)}, u32[]{:S(2)}) async-start(bf16[32,2,800]{2,1,0:T(2,128)(2,1)} %reshape.188), calls=%async_computation.2 | async-start | bytes 229376 | tf_op jit(solution)/shard_map/all_to_all | solution.py:245

commit v15 on v14

--- a/solution.py
+++ b/solution.py
@@ -198,19 +198,26 @@
     word_ids = bucket_ints[:, :trips].reshape(-1)
     ctx_ids = bucket_ints[:, trips : 2 * trips].reshape(-1)
     slot_ids = bucket_ints[:, 2 * trips : 3 * trips]
+    list_of = (lax.axis_index("rel") + jnp.arange(split_count)) % split_count
     slot_ids = (
         (slot_ids // slot_count) * (split_count * slot_count)
-        + (jnp.arange(split_count) * slot_count)[:, None]
+        + (list_of * slot_count)[:, None]
         + slot_ids % slot_count
     ).reshape(-1)
     own_slots = jnp.arange(slot_total)
-    own_rows = (own_slots // slot_count) * (split_count * slot_count) + own_slots % slot_count
+    own_rows = (
+        (own_slots // slot_count) * (split_count * slot_count)
+        + list_of[0] * slot_count
+        + own_slots % slot_count
+    )
     neg_ids = bucket_ints[:, 3 * trips :].reshape(split_count * block_count, neg_count)
 
     wanted = requests[0, 0].reshape(owner_count, slot_count)
     incoming = lax.all_to_all(wanted, both, split_axis=0, concat_axis=0, tiled=True)
     lists = incoming.reshape(part_count, split_count, slot_count)
-    served = jnp.stack([jnp.roll(lists, -j, axis=1) for j in range(split_count)], axis=2)
+    served = jnp.broadcast_to(
+        lists[:, None], (part_count, split_count, split_count, slot_count)
+    )
     padded_width = 2 * lanes_of(half_width)
     picked = jnp.einsum(
         "dkr,rf->dkf",

time: 52 us -> 52 us (level)
    all_to_all x1, waiting for transfers between devices: 8.96 us -> 8.29 us  [shards(): lax.all_to_all(picked, both, split_axis=0, concat_axis=0, tiled=True)]
    ppermute x2, waiting for transfers between devices: 0.01 us -> 0.68 us  [passed_along(): lax.ppermute(shard, axis, [(i, (i + by) % length) for i in range(length)])]
  transfers between devices with their start and end apart: 5 -> 5, of which waited for: 3 -> 4; matrix products, arithmetic and copies ran while one was open for 16% -> 16% of each run, Pallas kernels for 8% -> 8%
where the time goes in v15:
time: 52 us; the launch traced here: 51.6 us
  starting transfers between devices  16 us (31%)
  local copies, waits for them, and re-layouts  12.1 us (23%)
  waiting for transfers between devices  10.9 us (21%)
  Pallas kernels  8.27 us (16%)
  matrix products  2.01 us (4%)
  other arithmetic  1.37 us (3%)
  between operations  0.94 us (2%)
    all_to_all x1, waiting for transfers between devices, shards(): lax.all_to_all(picked, both, split_axis=0, concat_axis=0, tiled=True)  8.29 us
    pallas_call x2, Pallas kernels, block_chains(): pl.pallas_call(body, out_shape=(jax.ShapeDtypeStruct((parts, width), jnp....  8.27 us
    all_to_all x1, starting transfers between devices, shards(): lax.all_to_all(wanted, both, split_axis=0, concat_axis=0, tiled=True)  7.3 us
    all_to_all x1, starting transfers between devices, shards(): lax.all_to_all(picked, both, split_axis=0, concat_axis=0, tiled=True)  3.46 us
    all_to_all x1, starting transfers between devices, shards(): lax.all_to_all(own_slot.astype(jnp.bfloat16).reshape(owner_count, slot_co...  3.44 us
    slice x2, local copies, waits for them, and re-layouts, unpadded_halves(): rows.reshape(count, 2, lanes_of(half_width))[:, :, :half_width]  2.14 us
    ppermute x2, starting transfers between devices, passed_along(): lax.ppermute(shard, axis, [(i, (i + by) % length) for i in range(length)])  1.84 us
    reshape x2, local copies, waits for them, and re-layouts, padded_halves(): rows.reshape(count, 2, half_width)  1.81 us
  transfers between devices with their start and end apart: 5, of which 4 were waited for; matrix products, arithmetic and copies ran while one was open for 16% of the time, Pallas kernels for 8%

profile of v15, /device:TPU:0, one launch (start us, length us, event | category | flops | bytes accessed | tf_op | source)
XLA Modules:
  0.0 51.6 jit_solution(9759427259120718981)
XLA Ops:
  0.6 1.4 %copy.41 = s32[1,1,16,2,2]{4,3,2,1,0:T(2,128)} copy(s32[1,1,16,2,2]{2,4,3,1,0:T(2,128)} %param.16) | data formatting | bytes 512 | tf_op jit(solution)/shard_map/all_to_all | solution.py:216
  2.0 7.3 %all-to-all-start = ((s32[32,1,2]{2,1,0:T(1,128)}), s32[32,1,2]{2,1,0:T(1,128)S(1)}, u32[]{:S(2)}, u32[]{:S(2)}) async-start(s32[32,1,2]{2,1,0:T(1,128)} %bitcast.3), calls=%async_computation | async-start | bytes 32768 | tf_op jit(solution)/shard_map/all_to_all | solution.py:216
  9.4 0.6 %copy-done.1 = s32[256]{0:T(256)S(1)} copy-done((s32[256]{0:T(256)S(1)}, s32[256]{0:T(256)}, u32[]{:S(2)}) %copy-start.1) | copy-done | bytes 1048
  10.0 1.8 %collective-permute-start = (s32[1792]{0:T(1024)S(1)}, s32[1792]{0:T(1024)S(1)}, u32[]{:S(2)}, u32[]{:S(2)}) collective-permute-start(s32[1792]{0:T(1024)S(1)} %pad_add_fusion), channel_id=1, source_target_pairs={{0,1},{1,0},{2,3},{3,2},{4,5},{5,4},{6,7},{7,6},{8,9},{9,8},{10,11... | collective-permute-start | bytes 21512 | tf_op jit(solution)/shard_map/ppermute | solution.py:12
  12.0 0.7 %copy-done.3 = s32[1,1,16,2]{2,3,1,0:T(2,128)S(1)} copy-done((s32[1,1,16,2]{2,3,1,0:T(2,128)S(1)}, s32[1,1,16,2]{2,3,1,0:T(2,128)}, u32[]{:S(2)}) %copy-start.3) | copy-done | bytes 152
  13.0 0.1 reshape.201.live
  13.1 1.3 %copy.35 = bf16[256,2,400]{2,1,0:T(2,128)(2,1)S(1)} copy(bf16[256,2,400]{0,2,1:T(8,128)(2,1)} %bitcast.45) | data formatting | bytes 819200 | tf_op jit(solution)/shard_map/reshape | solution.py:162
  14.5 0.4 pad.11
  15.0 1.5 %all-to-all-done = s32[32,1,2]{2,1,0:T(1,128)S(1)} async-done(((s32[32,1,2]{2,1,0:T(1,128)}), s32[32,1,2]{2,1,0:T(1,128)S(1)}, u32[]{:S(2)}, u32[]{:S(2)}) %all-to-all-start) | async-done | bytes 288 | tf_op jit(solution)/shard_map/all_to_all | solution.py:216
  16.5 0.1 copy.33
  16.6 0.1 eq.34
  16.7 0.3 convolution_convert_fusion
  17.0 0.8 %copy.34 = bf16[32,4,800]{2,1,0:T(4,128)(2,1)} copy(bf16[32,4,800]{2,0,1:T(8,128)(2,1)S(1)} %convolution_convert_fusion) | data formatting | bytes 409600 | tf_op jit(solution)/shard_map/convert_element_type | solution.py:227
  17.8 3.5 %all-to-all-start.1 = ((bf16[32,4,800]{2,1,0:T(4,128)(2,1)}), bf16[32,4,800]{2,1,0:T(4,128)(2,1)S(1)}, u32[]{:S(2)}, u32[]{:S(2)}) async-start(bf16[32,4,800]{2,1,0:T(4,128)(2,1)} %copy.34), calls=%async_computation.1 | async-start | bytes 458752 | tf_op jit(solution)/shard_map/all_to_all | solution.py:228
  21.5 0.7 %collective-permute-done.1 = bf16[256,800]{0,1:T(8,128)(2,1)S(1)} collective-permute-done((bf16[256,800]{0,1:T(8,128)(2,1)}, bf16[256,800]{0,1:T(8,128)(2,1)S(1)}, u32[]{:S(2)}, u32[]{:S(2)}) %collective-permute-start.1) | collective-permute-done | bytes 409632 | tf_op jit(solution)/shard_map/ppermute | solution.py:12
  22.2 0.5 copy.36
  22.6 0.4 pad.12
  23.2 8.3 %all-to-all-done.1 = bf16[32,4,800]{2,1,0:T(4,128)(2,1)S(1)} async-done(((bf16[32,4,800]{2,1,0:T(4,128)(2,1)}), bf16[32,4,800]{2,1,0:T(4,128)(2,1)S(1)}, u32[]{:S(2)}, u32[]{:S(2)}) %all-to-all-start.1) | async-done | bytes 204832 | tf_op jit(solution)/shard_map/all_to_all | solution.py:228
  31.5 0.2 reshape_reshape.3
  31.7 0.2 pad.13
  32.0 4.0 %shard_map.112 = (f32[256,1024]{1,0:T(8,128)S(1)}, f32[256,1024]{1,0:T(8,128)S(1)}, f32[64,800]{1,0:T(8,128)S(1)}) custom-call(s32[1,256]{1,0:T(1,128)S(1)} %get-tuple-element.26.wrow, s32[1,256]{1,0:T(1,128)S(1)} %get-tuple-element.25.crow, s32[1,256]{1,0:T(1,128)S(1)} %get-tuple-element.28.scomb, s32[1,256]{1,0:T(1,128)S(1)} %bitcast.38, ...), custom_call_target="tpu_custom_call" | custom-call | tf_op jit(solution)/shard_map/pallas_call | solution.py:132
  36.0 0.7 %convert_element_type.40 = bf16[64,800]{1,0:T(8,128)(2,1)} convert(f32[64,800]{1,0:T(8,128)S(1)} %get-tuple-element.20) | non-fusion elementwise | flops 51200 | bytes 307200 | tf_op jit(solution)/shard_map/convert_element_type | solution.py:253
  36.6 1.6 %reshape.200 = bf16[32,2,800]{2,1,0:T(2,128)(2,1)} reshape(bf16[64,800]{1,0:T(8,128)(2,1)} %convert_element_type.40) | data formatting | bytes 204800 | tf_op jit(solution)/shard_map/reshape | solution.py:253
  38.2 3.4 %all-to-all-start.2 = ((bf16[32,2,800]{2,1,0:T(2,128)(2,1)}), bf16[32,2,800]{2,1,0:T(2,128)(2,1)}, u32[]{:S(2)}, u32[]{:S(2)}) async-start(bf16[32,2,800]{2,1,0:T(2,128)(2,1)} %reshape.200), calls=%async_computation.2 | async-start | bytes 229376 | tf_op jit(solution)/shard_map/all_to_all | solution.py:252
  41.7 4.3 %shard_map.113 = (f32[256,1024]{1,0:T(8,128)S(1)}, f32[256,1024]{1,0:T(8,128)S(1)}, f32[8,800]{1,0:T(8,128)}) custom-call(s32[1,256]{1,0:T(1,128)S(1)} %get-tuple-element.24.wrow, s32[1,256]{1,0:T(1,128)S(1)} %get-tuple-element.23.crow, s32[1,256]{1,0:T(1,128)S(1)} %get-tuple-element.27.scomb, s32[1,256]{1,0:T(1,128)S(1)} %bitcast.39, ...), custom_call_target="tpu_custom_call" | custom-call | tf_op jit(solution)/shard_map/pallas_call | solution.py:132
  46.0 0.5 add_convert_fusion
  46.5 0.4 reshape.199
  46.8 1.1 %copy.38 = bf16[256,2,400]{0,2,1:T(8,128)(2,1)} copy(bf16[256,2,400]{2,1,0:T(2,128)(2,1)S(1)} %bitcast.40) | data formatting | bytes 819200 | tf_op jit(solution)/shard_map/slice | solution.py:168
  47.9 0.4 reshape.198
  48.3 1.1 %copy.37 = bf16[256,2,400]{0,2,1:T(8,128)(2,1)} copy(bf16[256,2,400]{2,1,0:T(2,128)(2,1)S(1)} %bitcast.41) | data formatting | bytes 819200 | tf_op jit(solution)/shard_map/slice | solution.py:168
  49.4 0.5 all-to-all-done.2
  49.9 1.8 %convolution_bitcast_fusion = f32[32,800]{1,0:T(8,128)} fusion(bf16[32,2,800]{2,1,0:T(2,128)(2,1)} %all-to-all-done.2, s32[32,2]{0,1:T(2,128)S(1)} %bitcast.50), kind=kOutput, calls=%fused_computation.1 | convolution fusion | flops 3278848 | bytes 205056 | tf_op jit(solution)/shard_map/dkr,dkf->rf/dot_general | solution.py:261
  (36 shorter events, 0.8 us)
Async XLA Ops:
  0.6 16.1 %copy-start = (bf16[32,800]{1,0:T(8,128)(2,1)S(1)}, bf16[32,800]{1,0:T(8,128)(2,1)}, u32[]{:S(2)}) copy-start(bf16[32,800]{1,0:T(8,128)(2,1)} %param.11) | copy-start | bytes 153604
  2.0 7.3 %copy-start.2 = (s32[1,1024]{1,0:T(1,128)S(1)}, s32[1,1024]{1,0:T(1,128)}, u32[]{:S(2)}) copy-start(s32[1,1024]{1,0:T(1,128)} %param.15) | copy-start | bytes 12292
  2.0 7.3 %copy-start.4 = (s32[256]{0:T(256)S(1)}, s32[256]{0:T(256)}, u32[]{:S(2)}) copy-start(s32[256]{0:T(256)} %param.13) | copy-start | bytes 3076
  2.0 7.3 %copy-start.5 = (s32[256]{0:T(256)S(1)}, s32[256]{0:T(256)}, u32[]{:S(2)}) copy-start(s32[256]{0:T(256)} %param.12) | copy-start | bytes 3076
  2.0 14.4 %all-to-all-start = ((s32[32,1,2]{2,1,0:T(1,128)}), s32[32,1,2]{2,1,0:T(1,128)S(1)}, u32[]{:S(2)}, u32[]{:S(2)}) async-start(s32[32,1,2]{2,1,0:T(1,128)} %bitcast.3), calls=%async_computation | async-start | bytes 32768 | tf_op jit(solution)/shard_map/all_to_all | solution.py:216
  9.3 0.7 %copy-start.1 = (s32[256]{0:T(256)S(1)}, s32[256]{0:T(256)}, u32[]{:S(2)}) copy-start(s32[256]{0:T(256)} %param.14) | copy-start | bytes 3076
  10.0 11.3 %collective-permute-start = (s32[1792]{0:T(1024)S(1)}, s32[1792]{0:T(1024)S(1)}, u32[]{:S(2)}, u32[]{:S(2)}) collective-permute-start(s32[1792]{0:T(1024)S(1)} %pad_add_fusion), channel_id=1, source_target_pairs={{0,1},{1,0},{2,3},{3,2},{4,5},{5,4},{6,7},{7,6},{8,9},{9,8},{10,11... | collective-permute-start | bytes 21512 | tf_op jit(solution)/shard_map/ppermute | solution.py:12
  11.9 10.3 %collective-permute-start.1 = (bf16[256,800]{0,1:T(8,128)(2,1)}, bf16[256,800]{0,1:T(8,128)(2,1)S(1)}, u32[]{:S(2)}, u32[]{:S(2)}) collective-permute-start(bf16[256,800]{0,1:T(8,128)(2,1)} %param.10), channel_id=1, source_target_pairs={{0,2},{2,4},{4,6},{6,8},{8,10},{10,12},{12,14},{14,16},{16,18},{18... | collective-permute-start | bytes 1228808 | tf_op jit(solution)/shard_map/ppermute | solution.py:12
  12.0 0.7 %copy-start.3 = (s32[1,1,16,2]{2,3,1,0:T(2,128)S(1)}, s32[1,1,16,2]{2,3,1,0:T(2,128)}, u32[]{:S(2)}) copy-start(s32[1,1,16,2]{2,3,1,0:T(2,128)} %param.17) | copy-start | bytes 388
  17.8 13.6 %all-to-all-start.1 = ((bf16[32,4,800]{2,1,0:T(4,128)(2,1)}), bf16[32,4,800]{2,1,0:T(4,128)(2,1)S(1)}, u32[]{:S(2)}, u32[]{:S(2)}) async-start(bf16[32,4,800]{2,1,0:T(4,128)(2,1)} %copy.34), calls=%async_computation.1 | async-start | bytes 458752 | tf_op jit(solution)/shard_map/all_to_all | solution.py:228
  38.2 11.6 %all-to-all-start.2 = ((bf16[32,2,800]{2,1,0:T(2,128)(2,1)}), bf16[32,2,800]{2,1,0:T(2,128)(2,1)}, u32[]{:S(2)}, u32[]{:S(2)}) async-start(bf16[32,2,800]{2,1,0:T(2,128)(2,1)} %reshape.200), calls=%async_computation.2 | async-start | bytes 229376 | tf_op jit(solution)/shard_map/all_to_all | solution.py:252

commit v16 on v15

--- a/solution.py
+++ b/solution.py
@@ -74,15 +74,16 @@
     return _mm(sel_t, upper) + _mm(sel_t, lower)
 
 
-def _chain_body(groups, own_groups, block, neg_count, scale,
-                wrow, crow, scomb, srow, nrow, orow, live,
-                words, held, table, word_out, ctx_out, slot_out):
+def _chain_body(groups, own_groups, block, neg_count, scale, accumulate, *refs):
+    wrow, crow, scomb, srow, nrow, orow, live, words, held, table = refs[:10]
+    word_out, ctx_out, slot_out = refs[-3:]
     parts = words.shape[0]
     rows = table.shape[0]
     slots = slot_out.shape[0]
     half = words.shape[1] // 2
-    word_out[...] = jnp.zeros(word_out.shape, jnp.float32)
-    ctx_out[...] = jnp.zeros(ctx_out.shape, jnp.float32)
+    if not accumulate:
+        word_out[...] = jnp.zeros(word_out.shape, jnp.float32)
+        ctx_out[...] = jnp.zeros(ctx_out.shape, jnp.float32)
     slot_sum = jnp.zeros((slot_out.shape[0], words.shape[1]), jnp.float32)
     for g in range(groups):
         t0 = g * block
@@ -123,12 +124,14 @@
 
 
 def block_chains(word_ids, ctx_ids, slot_ids, own_ids, neg_ids, own_groups, scale, words, held,
-                 table, own_rows, live_mask, row_width):
+                 table, own_rows, live_mask, row_width, totals=()):
     trips = word_ids.shape[0]
     groups, neg_count = neg_ids.shape
     block = trips // groups
     parts, width = words.shape
-    body = functools.partial(_chain_body, groups, own_groups, block, neg_count, scale)
+    body = functools.partial(
+        _chain_body, groups, own_groups, block, neg_count, scale, bool(totals)
+    )
     return pl.pallas_call(
         body,
         out_shape=(
@@ -137,6 +140,7 @@
             jax.ShapeDtypeStruct((own_rows.shape[0], row_width), jnp.float32),
         ),
         compiler_params=pltpu.CompilerParams(vmem_limit_bytes=48 * 1024 * 1024),
+        input_output_aliases={10 + i: i for i in range(len(totals))},
     )(
         word_ids.reshape(1, -1),
         ctx_ids.reshape(1, -1),
@@ -148,6 +152,7 @@
         words,
         held,
         table,
+        *totals,
     )
 
 
@@ -242,13 +247,13 @@
         block_count, neg_scale, word_table, held_table, rel_table, own_rows, live_mask,
         row_width,
     )
-    rest_word, rest_ctx, _ = block_chains(
+    all_word, all_ctx, _ = block_chains(
         word_ids[trips:], ctx_ids[trips:], slot_ids[trips:], rel_slot, neg_ids[block_count:],
         0, neg_scale, word_table, held_table, rel_table, own_rows[:8], live_mask[:8],
-        row_width,
-    )
-    word_sum = unpadded_halves(own_word + rest_word, half_width)
-    ctx_sum = unpadded_halves(own_ctx + rest_ctx, half_width)
+        row_width, totals=(own_word, own_ctx),
+    )
+    word_sum = unpadded_halves(all_word, half_width)
+    ctx_sum = unpadded_halves(all_ctx, half_width)
     returned = lax.all_to_all(
         own_slot.astype(jnp.bfloat16).reshape(owner_count, slot_count, row_width),
         both,

time: 52 us -> 52 us (level)
  transfers between devices with their start and end apart: 5 -> 5, of which waited for: 4 -> 4; matrix products, arithmetic and copies ran while one was open for 16% -> 15% of each run, Pallas kernels for 8% -> 8%
where the time goes in v16:
time: 52 us; the launch traced here: 51.6 us
  starting transfers between devices  16 us (31%)
  local copies, waits for them, and re-layouts  12 us (23%)
  waiting for transfers between devices  11.3 us (22%)
  Pallas kernels  8.3 us (16%)
  matrix products  2.01 us (4%)
  other arithmetic  1 us (2%)
  between operations  0.96 us (2%)
    pallas_call x2, Pallas kernels, block_chains(): pl.pallas_call(body, out_shape=(jax.ShapeDtypeStruct((parts, width), jnp....  8.3 us
    all_to_all x1, waiting for transfers between devices, shards(): lax.all_to_all(picked, both, split_axis=0, concat_axis=0, tiled=True)  8.28 us
    all_to_all x1, starting transfers between devices, shards(): lax.all_to_all(wanted, both, split_axis=0, concat_axis=0, tiled=True)  7.3 us
    all_to_all x1, starting transfers between devices, shards(): lax.all_to_all(own_slot.astype(jnp.bfloat16).reshape(owner_count, slot_co...  3.45 us
    all_to_all x1, starting transfers between devices, shards(): lax.all_to_all(picked, both, split_axis=0, concat_axis=0, tiled=True)  3.45 us
    slice x2, local copies, waits for them, and re-layouts, unpadded_halves(): rows.reshape(count, 2, lanes_of(half_width))[:, :, :half_width]  2.14 us
    ppermute x2, starting transfers between devices, passed_along(): lax.ppermute(shard, axis, [(i, (i + by) % length) for i in range(length)])  1.84 us
    reshape x2, local copies, waits for them, and re-layouts, padded_halves(): rows.reshape(count, 2, half_width)  1.81 us
  transfers between devices with their start and end apart: 5, of which 4 were waited for; matrix products, arithmetic and copies ran while one was open for 15% of the time, Pallas kernels for 8%

profile of v16, /device:TPU:0, one launch (start us, length us, event | category | flops | bytes accessed | tf_op | source)
XLA Modules:
  0.0 51.6 jit_solution(7009527383966110891)
XLA Ops:
  0.6 1.4 %copy.43 = s32[1,1,16,2,2]{4,3,2,1,0:T(2,128)} copy(s32[1,1,16,2,2]{2,4,3,1,0:T(2,128)} %param.16) | data formatting | bytes 512 | tf_op jit(solution)/shard_map/all_to_all | solution.py:221
  2.0 7.3 %all-to-all-start = ((s32[32,1,2]{2,1,0:T(1,128)}), s32[32,1,2]{2,1,0:T(1,128)S(1)}, u32[]{:S(2)}, u32[]{:S(2)}) async-start(s32[32,1,2]{2,1,0:T(1,128)} %bitcast.4), calls=%async_computation | async-start | bytes 32768 | tf_op jit(solution)/shard_map/all_to_all | solution.py:221
  9.4 0.6 %copy-done.1 = s32[256]{0:T(256)S(1)} copy-done((s32[256]{0:T(256)S(1)}, s32[256]{0:T(256)}, u32[]{:S(2)}) %copy-start.1) | copy-done | bytes 1048
  10.0 1.8 %collective-permute-start = (s32[1792]{0:T(1024)S(1)}, s32[1792]{0:T(1024)S(1)}, u32[]{:S(2)}, u32[]{:S(2)}) collective-permute-start(s32[1792]{0:T(1024)S(1)} %pad_add_fusion), channel_id=1, source_target_pairs={{0,1},{1,0},{2,3},{3,2},{4,5},{5,4},{6,7},{7,6},{8,9},{9,8},{10,11... | collective-permute-start | bytes 21512 | tf_op jit(solution)/shard_map/ppermute | solution.py:12
  12.0 0.7 %copy-done.3 = s32[1,1,16,2]{2,3,1,0:T(2,128)S(1)} copy-done((s32[1,1,16,2]{2,3,1,0:T(2,128)S(1)}, s32[1,1,16,2]{2,3,1,0:T(2,128)}, u32[]{:S(2)}) %copy-start.3) | copy-done | bytes 152
  12.8 0.1 lt.49
  12.9 0.1 reshape.203.refs_6_
  13.1 1.3 %copy.37 = bf16[256,2,400]{2,1,0:T(2,128)(2,1)S(1)} copy(bf16[256,2,400]{0,2,1:T(8,128)(2,1)} %bitcast.45) | data formatting | bytes 819200 | tf_op jit(solution)/shard_map/reshape | solution.py:167
  14.5 0.4 pad.11
  15.0 1.5 %all-to-all-done = s32[32,1,2]{2,1,0:T(1,128)S(1)} async-done(((s32[32,1,2]{2,1,0:T(1,128)}), s32[32,1,2]{2,1,0:T(1,128)S(1)}, u32[]{:S(2)}, u32[]{:S(2)}) %all-to-all-start) | async-done | bytes 288 | tf_op jit(solution)/shard_map/all_to_all | solution.py:221
  16.5 0.1 copy.35
  16.6 0.1 eq.34
  16.7 0.3 convolution_convert_fusion
  17.0 0.8 %copy.36 = bf16[32,4,800]{2,1,0:T(4,128)(2,1)} copy(bf16[32,4,800]{2,0,1:T(8,128)(2,1)S(1)} %convolution_convert_fusion) | data formatting | bytes 409600 | tf_op jit(solution)/shard_map/convert_element_type | solution.py:232
  17.8 3.4 %all-to-all-start.1 = ((bf16[32,4,800]{2,1,0:T(4,128)(2,1)}), bf16[32,4,800]{2,1,0:T(4,128)(2,1)S(1)}, u32[]{:S(2)}, u32[]{:S(2)}) async-start(bf16[32,4,800]{2,1,0:T(4,128)(2,1)} %copy.36), calls=%async_computation.1 | async-start | bytes 458752 | tf_op jit(solution)/shard_map/all_to_all | solution.py:233
  21.4 0.8 %collective-permute-done.1 = bf16[256,800]{0,1:T(8,128)(2,1)S(1)} collective-permute-done((bf16[256,800]{0,1:T(8,128)(2,1)}, bf16[256,800]{0,1:T(8,128)(2,1)S(1)}, u32[]{:S(2)}, u32[]{:S(2)}) %collective-permute-start.1) | collective-permute-done | bytes 409632 | tf_op jit(solution)/shard_map/ppermute | solution.py:12
  22.2 0.5 copy.38
  22.6 0.4 pad.12
  23.2 8.3 %all-to-all-done.1 = bf16[32,4,800]{2,1,0:T(4,128)(2,1)S(1)} async-done(((bf16[32,4,800]{2,1,0:T(4,128)(2,1)}), bf16[32,4,800]{2,1,0:T(4,128)(2,1)S(1)}, u32[]{:S(2)}, u32[]{:S(2)}) %all-to-all-start.1) | async-done | bytes 204832 | tf_op jit(solution)/shard_map/all_to_all | solution.py:233
  31.4 0.2 reshape_reshape.3
  31.7 0.2 pad.13
  31.9 4.0 %shard_map.112 = (f32[256,1024]{1,0:T(8,128)S(1)}, f32[256,1024]{1,0:T(8,128)S(1)}, f32[64,800]{1,0:T(8,128)S(1)}) custom-call(s32[1,256]{1,0:T(1,128)S(1)} %get-tuple-element.24.refs_0_, s32[1,256]{1,0:T(1,128)S(1)} %get-tuple-element.23.refs_1_, s32[1,256]{1,0:T(1,128)S(1)} %get-tuple-element.32.refs_2_, s32[1,256]{1,0:T(1,128)S(1)} %bitcast.38, ...), custom_call_target="tpu_custom_call" | custom-call | tf_op jit(solution)/shard_map/pallas_call | solution.py:135
  36.0 0.7 %convert_element_type.40 = bf16[64,800]{1,0:T(8,128)(2,1)} convert(f32[64,800]{1,0:T(8,128)S(1)} %get-tuple-element.20) | non-fusion elementwise | flops 51200 | bytes 307200 | tf_op jit(solution)/shard_map/convert_element_type | solution.py:258
  36.6 1.6 %reshape.200 = bf16[32,2,800]{2,1,0:T(2,128)(2,1)} reshape(bf16[64,800]{1,0:T(8,128)(2,1)} %convert_element_type.40) | data formatting | bytes 204800 | tf_op jit(solution)/shard_map/reshape | solution.py:258
  38.2 3.5 %all-to-all-start.2 = ((bf16[32,2,800]{2,1,0:T(2,128)(2,1)}), bf16[32,2,800]{2,1,0:T(2,128)(2,1)}, u32[]{:S(2)}, u32[]{:S(2)}) async-start(bf16[32,2,800]{2,1,0:T(2,128)(2,1)} %reshape.200), calls=%async_computation.2 | async-start | bytes 229376 | tf_op jit(solution)/shard_map/all_to_all | solution.py:257
  41.8 4.3 %shard_map.113 = (f32[256,1024]{1,0:T(8,128)S(1)}, f32[256,1024]{1,0:T(8,128)S(1)}, f32[8,800]{1,0:T(8,128)}) custom-call(s32[1,256]{1,0:T(1,128)S(1)} %get-tuple-element.26.refs_0_, s32[1,256]{1,0:T(1,128)S(1)} %get-tuple-element.25.refs_1_, s32[1,256]{1,0:T(1,128)S(1)} %get-tuple-element.31.refs_2_, ...), custom_call_target="tpu_custom_call", output_to_operand_aliasing={{0}: (10, {}), {1}: (11, {})} | custom-call | tf_op jit(solution)/shard_map/pallas_call | solution.py:135
  46.1 0.4 reshape.198
  46.5 1.1 %copy.39 = bf16[256,2,400]{0,2,1:T(8,128)(2,1)} copy(bf16[256,2,400]{2,1,0:T(2,128)(2,1)S(1)} %bitcast.40) | data formatting | bytes 819200 | tf_op jit(solution)/shard_map/slice | solution.py:173
  47.7 0.4 reshape.199
  48.0 1.1 %copy.40 = bf16[256,2,400]{0,2,1:T(8,128)(2,1)} copy(bf16[256,2,400]{2,1,0:T(2,128)(2,1)S(1)} %bitcast.41) | data formatting | bytes 819200 | tf_op jit(solution)/shard_map/slice | solution.py:173
  49.1 0.7 %all-to-all-done.2 = bf16[32,2,800]{2,1,0:T(2,128)(2,1)} async-done(((bf16[32,2,800]{2,1,0:T(2,128)(2,1)}), bf16[32,2,800]{2,1,0:T(2,128)(2,1)}, u32[]{:S(2)}, u32[]{:S(2)}) %all-to-all-start.2) | async-done | bytes 102432 | tf_op jit(solution)/shard_map/all_to_all | solution.py:257
  49.8 1.8 %convolution_bitcast_fusion = f32[32,800]{1,0:T(8,128)} fusion(bf16[32,2,800]{2,1,0:T(2,128)(2,1)} %all-to-all-done.2, s32[32,2]{0,1:T(2,128)S(1)} %bitcast.50), kind=kOutput, calls=%fused_computation.1 | convolution fusion | flops 3278848 | bytes 205056 | tf_op jit(solution)/shard_map/dkr,dkf->rf/dot_general | solution.py:266
  (36 shorter events, 0.9 us)
Async XLA Ops:
  0.6 16.1 %copy-start = (bf16[32,800]{1,0:T(8,128)(2,1)S(1)}, bf16[32,800]{1,0:T(8,128)(2,1)}, u32[]{:S(2)}) copy-start(bf16[32,800]{1,0:T(8,128)(2,1)} %param.11) | copy-start | bytes 153604
  2.0 7.3 %copy-start.2 = (s32[1,1024]{1,0:T(1,128)S(1)}, s32[1,1024]{1,0:T(1,128)}, u32[]{:S(2)}) copy-start(s32[1,1024]{1,0:T(1,128)} %param.15) | copy-start | bytes 12292
  2.0 7.3 %copy-start.4 = (s32[256]{0:T(256)S(1)}, s32[256]{0:T(256)}, u32[]{:S(2)}) copy-start(s32[256]{0:T(256)} %param.13) | copy-start | bytes 3076
  2.0 7.3 %copy-start.5 = (s32[256]{0:T(256)S(1)}, s32[256]{0:T(256)}, u32[]{:S(2)}) copy-start(s32[256]{0:T(256)} %param.12) | copy-start | bytes 3076
  2.0 14.4 %all-to-all-start = ((s32[32,1,2]{2,1,0:T(1,128)}), s32[32,1,2]{2,1,0:T(1,128)S(1)}, u32[]{:S(2)}, u32[]{:S(2)}) async-start(s32[32,1,2]{2,1,0:T(1,128)} %bitcast.4), calls=%async_computation | async-start | bytes 32768 | tf_op jit(solution)/shard_map/all_to_all | solution.py:221
  9.3 0.7 %copy-start.1 = (s32[256]{0:T(256)S(1)}, s32[256]{0:T(256)}, u32[]{:S(2)}) copy-start(s32[256]{0:T(256)} %param.14) | copy-start | bytes 3076
  10.0 11.2 %collective-permute-start = (s32[1792]{0:T(1024)S(1)}, s32[1792]{0:T(1024)S(1)}, u32[]{:S(2)}, u32[]{:S(2)}) collective-permute-start(s32[1792]{0:T(1024)S(1)} %pad_add_fusion), channel_id=1, source_target_pairs={{0,1},{1,0},{2,3},{3,2},{4,5},{5,4},{6,7},{7,6},{8,9},{9,8},{10,11... | collective-permute-start | bytes 21512 | tf_op jit(solution)/shard_map/ppermute | solution.py:12
  11.9 10.3 %collective-permute-start.1 = (bf16[256,800]{0,1:T(8,128)(2,1)}, bf16[256,800]{0,1:T(8,128)(2,1)S(1)}, u32[]{:S(2)}, u32[]{:S(2)}) collective-permute-start(bf16[256,800]{0,1:T(8,128)(2,1)} %param.10), channel_id=1, source_target_pairs={{0,2},{2,4},{4,6},{6,8},{8,10},{10,12},{12,14},{14,16},{16,18},{18... | collective-permute-start | bytes 1228808 | tf_op jit(solution)/shard_map/ppermute | solution.py:12
  12.0 0.7 %copy-start.3 = (s32[1,1,16,2]{2,3,1,0:T(2,128)S(1)}, s32[1,1,16,2]{2,3,1,0:T(2,128)}, u32[]{:S(2)}) copy-start(s32[1,1,16,2]{2,3,1,0:T(2,128)} %param.17) | copy-start | bytes 388
  17.8 13.6 %all-to-all-start.1 = ((bf16[32,4,800]{2,1,0:T(4,128)(2,1)}), bf16[32,4,800]{2,1,0:T(4,128)(2,1)S(1)}, u32[]{:S(2)}, u32[]{:S(2)}) async-start(bf16[32,4,800]{2,1,0:T(4,128)(2,1)} %copy.36), calls=%async_computation.1 | async-start | bytes 458752 | tf_op jit(solution)/shard_map/all_to_all | solution.py:233
  38.2 11.6 %all-to-all-start.2 = ((bf16[32,2,800]{2,1,0:T(2,128)(2,1)}), bf16[32,2,800]{2,1,0:T(2,128)(2,1)}, u32[]{:S(2)}, u32[]{:S(2)}) async-start(bf16[32,2,800]{2,1,0:T(2,128)(2,1)} %reshape.200), calls=%async_computation.2 | async-start | bytes 229376 | tf_op jit(solution)/shard_map/all_to_all | solution.py:257

commit v17 on v14

--- a/solution.py
+++ b/solution.py
@@ -189,9 +189,21 @@
     neg_scale = float(neg_count) ** (-0.5)
     both = ("blk", "rel")
 
+    wanted = requests[0, 0].reshape(owner_count, slot_count)
+    incoming = lax.all_to_all(wanted, both, split_axis=0, concat_axis=0, tiled=True)
+    lists = incoming.reshape(part_count, split_count, slot_count)
+    served = jnp.stack([jnp.roll(lists, -j, axis=1) for j in range(split_count)], axis=2)
+    padded_width = 2 * lanes_of(half_width)
+    picked = jnp.einsum(
+        "dkr,rf->dkf",
+        one_hot(served.reshape(owner_count, split_count * slot_count), owned_rows),
+        relations,
+        preferred_element_type=jnp.float32,
+    ).astype(jnp.bfloat16)
+    own_ints = jnp.concatenate([word_index, context_index, rel_slot, neg_index.reshape(-1)])
+    picked, contexts, own_ints = lax.optimization_barrier((picked, contexts, own_ints))
     held_rows = passed_along(contexts, "blk", 1)
 
-    own_ints = jnp.concatenate([word_index, context_index, rel_slot, neg_index.reshape(-1)])
     bucket_ints = jnp.stack(
         [own_ints] + [passed_along(own_ints, "rel", -j) for j in range(1, split_count)]
     )
@@ -207,17 +219,6 @@
     own_rows = (own_slots // slot_count) * (split_count * slot_count) + own_slots % slot_count
     neg_ids = bucket_ints[:, 3 * trips :].reshape(split_count * block_count, neg_count)
 
-    wanted = requests[0, 0].reshape(owner_count, slot_count)
-    incoming = lax.all_to_all(wanted, both, split_axis=0, concat_axis=0, tiled=True)
-    lists = incoming.reshape(part_count, split_count, slot_count)
-    served = jnp.stack([jnp.roll(lists, -j, axis=1) for j in range(split_count)], axis=2)
-    padded_width = 2 * lanes_of(half_width)
-    picked = jnp.einsum(
-        "dkr,rf->dkf",
-        one_hot(served.reshape(owner_count, split_count * slot_count), owned_rows),
-        relations,
-        preferred_element_type=jnp.float32,
-    ).astype(jnp.bfloat16)
     fetched = lax.all_to_all(picked, both, split_axis=0, concat_axis=0, tiled=True)
     live_mask = (
         (jnp.arange(slot_count)[None, :] < counts[0, 0].reshape(owner_count)[:, None])

time: 52 us -> 55.3 us (1.063)
  waiting for transfers between devices: 11.1 us -> 12.8 us
  starting transfers between devices: 16 us -> 17.1 us
    ppermute x2, waiting for transfers between devices: 0.01 us -> 3.38 us  [passed_along(): lax.ppermute(shard, axis, [(i, (i + by) % length) for i in range(length)])]
    all_to_all x1, waiting for transfers between devices: 8.96 us -> 5.59 us  [shards(): lax.all_to_all(picked, both, split_axis=0, concat_axis=0, tiled=True)]
    all_to_all x1, starting transfers between devices: 3.07 us -> 5.74 us  [shards(): lax.all_to_all(picked, both, split_axis=0, concat_axis=0, tiled=True)]
    all_to_all x1, waiting for transfers between devices: 1.57 us -> 3.36 us  [shards(): lax.all_to_all(wanted, both, split_axis=0, concat_axis=0, tiled=True)]
    ppermute x2, starting transfers between devices: 2.14 us -> 0.64 us  [passed_along(): lax.ppermute(shard, axis, [(i, (i + by) % length) for i in range(length)])]
    convert_element_type x1 -> x0, local copies, waits for them, and re-layouts: 0.81 us -> none  [shards(): picked = jnp.einsum('dkr,rf->dkf', one_hot(served.reshape(owner_count, sp...]
    optimization_barrier x0 -> x1, local copies, waits for them, and re-layouts: none -> 0.81 us  [shards(): lax.optimization_barrier((picked, contexts, own_ints))]
    unnamed x16 -> x18, local copies, waits for them, and re-layouts: 1.29 us -> 1.61 us
  transfers between devices with their start and end apart: 5 -> 5, of which waited for: 3 -> 4; matrix products, arithmetic and copies ran while one was open for 16% -> 14% of each run, Pallas kernels for 8% -> 8%
where the time goes in v17:
time: 55.3 us; the launch traced here: 54.9 us
  starting transfers between devices  17.1 us (31%)
  waiting for transfers between devices  12.8 us (23%)
  local copies, waits for them, and re-layouts  12.4 us (22%)
  Pallas kernels  8.27 us (15%)
  matrix products  2.02 us (4%)
  other arithmetic  1.36 us (2%)
  between operations  0.92 us (2%)
    pallas_call x2, Pallas kernels, block_chains(): pl.pallas_call(body, out_shape=(jax.ShapeDtypeStruct((parts, width), jnp....  8.27 us
    all_to_all x1, starting transfers between devices, shards(): lax.all_to_all(wanted, both, split_axis=0, concat_axis=0, tiled=True)  7.3 us
    all_to_all x1, starting transfers between devices, shards(): lax.all_to_all(picked, both, split_axis=0, concat_axis=0, tiled=True)  5.74 us
    all_to_all x1, waiting for transfers between devices, shards(): lax.all_to_all(picked, both, split_axis=0, concat_axis=0, tiled=True)  5.59 us
    all_to_all x1, starting transfers between devices, shards(): lax.all_to_all(own_slot.astype(jnp.bfloat16).reshape(owner_count, slot_co...  3.45 us
    ppermute x2, waiting for transfers between devices, passed_along(): lax.ppermute(shard, axis, [(i, (i + by) % length) for i in range(length)])  3.38 us
    all_to_all x1, waiting for transfers between devices, shards(): lax.all_to_all(wanted, both, split_axis=0, concat_axis=0, tiled=True)  3.36 us
    slice x2, local copies, waits for them, and re-layouts, unpadded_halves(): rows.reshape(count, 2, lanes_of(half_width))[:, :, :half_width]  2.14 us
  transfers between devices with their start and end apart: 5, of which 4 were waited for; matrix products, arithmetic and copies ran while one was open for 14% of the time, Pallas kernels for 8%

profile of v17, /device:TPU:0, one launch (start us, length us, event | category | flops | bytes accessed | tf_op | source)
XLA Modules:
  0.0 54.9 jit_solution(7974157055471423133)
XLA Ops:
  0.6 1.4 %copy.62 = s32[1,1,16,2,2]{4,3,2,1,0:T(2,128)} copy(s32[1,1,16,2,2]{2,4,3,1,0:T(2,128)} %param.16) | data formatting | bytes 512 | tf_op jit(solution)/shard_map/all_to_all | solution.py:193
  2.0 7.3 %all-to-all-start = ((s32[32,1,2]{2,1,0:T(1,128)}), s32[32,1,2]{2,1,0:T(1,128)S(1)}, u32[]{:S(2)}, u32[]{:S(2)}) async-start(s32[32,1,2]{2,1,0:T(1,128)} %bitcast), calls=%async_computation | async-start | bytes 32768 | tf_op jit(solution)/shard_map/all_to_all | solution.py:193
  9.4 0.7 %copy-done.3 = s32[1,1,16,2]{2,3,1,0:T(2,128)S(1)} copy-done((s32[1,1,16,2]{2,3,1,0:T(2,128)S(1)}, s32[1,1,16,2]{2,3,1,0:T(2,128)}, u32[]{:S(2)}) %copy-start.3) | copy-done | bytes 152
  10.4 0.6 %copy-done.2 = s32[1,1024]{1,0:T(1,128)S(1)} copy-done((s32[1,1024]{1,0:T(1,128)S(1)}, s32[1,1024]{1,0:T(1,128)}, u32[]{:S(2)}) %copy-start.2) | copy-done | bytes 4120
  11.0 1.3 %copy.56 = bf16[256,2,400]{2,1,0:T(2,128)(2,1)S(1)} copy(bf16[256,2,400]{0,2,1:T(8,128)(2,1)} %bitcast.46) | data formatting | bytes 819200 | tf_op jit(solution)/shard_map/reshape | solution.py:162
  12.4 0.4 pad.11
  12.9 0.1 reshape.189.live
  13.1 3.4 %all-to-all-done = s32[32,1,2]{2,1,0:T(1,128)S(1)} async-done(((s32[32,1,2]{2,1,0:T(1,128)}), s32[32,1,2]{2,1,0:T(1,128)S(1)}, u32[]{:S(2)}, u32[]{:S(2)}) %all-to-all-start) | async-done | bytes 288 | tf_op jit(solution)/shard_map/all_to_all | solution.py:193
  16.7 0.2 copy.63
  16.9 0.1 eq.32
  17.1 0.3 convolution_convert_fusion
  17.3 0.6 %collective-permute-start = (s32[1792]{0:T(1024)S(1)}, s32[1792]{0:T(1024)S(1)}, u32[]{:S(2)}, u32[]{:S(2)}) collective-permute-start(s32[1792]{0:T(1024)S(1)} %pad_add_fusion.1), channel_id=1, source_target_pairs={{0,1},{1,0},{2,3},{3,2},{4,5},{5,4},{6,7},{7,6},{8,9},{9,8},{10,11... | collective-permute-start | bytes 21512 | tf_op jit(solution)/shard_map/ppermute | solution.py:12
  18.0 0.8 %copy.55 = bf16[32,4,800]{2,1,0:T(4,128)(2,1)} copy(bf16[32,4,800]{2,0,1:T(8,128)(2,1)S(1)} %convolution_convert_fusion) | data formatting | bytes 409600 | tf_op jit(solution)/shard_map/optimization_barrier | solution.py:204
  18.8 5.7 %all-to-all-start.1 = ((bf16[32,4,800]{2,1,0:T(4,128)(2,1)}), bf16[32,4,800]{2,1,0:T(4,128)(2,1)S(1)}, u32[]{:S(2)}, u32[]{:S(2)}) async-start(bf16[32,4,800]{2,1,0:T(4,128)(2,1)} %copy.55), calls=%async_computation.1 | async-start | bytes 458752 | tf_op jit(solution)/shard_map/all_to_all | solution.py:222
  24.8 3.4 %collective-permute-done.1 = bf16[256,800]{0,1:T(8,128)(2,1)S(1)} collective-permute-done((bf16[256,800]{0,1:T(8,128)(2,1)S(1)}, bf16[256,800]{0,1:T(8,128)(2,1)S(1)}, u32[]{:S(2)}, u32[]{:S(2)}) %collective-permute-start.1) | collective-permute-done | bytes 409632 | tf_op jit(solution)/shard_map/ppermute | solution.py:12
  28.1 0.5 copy.57
  28.6 0.4 pad.12
  29.1 5.6 %all-to-all-done.1 = bf16[32,4,800]{2,1,0:T(4,128)(2,1)S(1)} async-done(((bf16[32,4,800]{2,1,0:T(4,128)(2,1)}), bf16[32,4,800]{2,1,0:T(4,128)(2,1)S(1)}, u32[]{:S(2)}, u32[]{:S(2)}) %all-to-all-start.1) | async-done | bytes 204832 | tf_op jit(solution)/shard_map/all_to_all | solution.py:222
  34.7 0.2 reshape_reshape.3
  35.0 0.2 pad.13
  35.2 4.0 %shard_map.112 = (f32[256,1024]{1,0:T(8,128)S(1)}, f32[256,1024]{1,0:T(8,128)S(1)}, f32[64,800]{1,0:T(8,128)S(1)}) custom-call(s32[1,256]{1,0:T(1,128)S(1)} %get-tuple-element.34.wrow, s32[1,256]{1,0:T(1,128)S(1)} %get-tuple-element.33.crow, s32[1,256]{1,0:T(1,128)S(1)} %get-tuple-element.36.scomb, s32[1,256]{1,0:T(1,128)S(1)} %bitcast.39, ...), custom_call_target="tpu_custom_call" | custom-call | tf_op jit(solution)/shard_map/pallas_call | solution.py:132
  39.3 0.7 %convert_element_type.40 = bf16[64,800]{1,0:T(8,128)(2,1)} convert(f32[64,800]{1,0:T(8,128)S(1)} %get-tuple-element.26) | non-fusion elementwise | flops 51200 | bytes 307200 | tf_op jit(solution)/shard_map/convert_element_type | solution.py:247
  39.9 1.6 %reshape.188 = bf16[32,2,800]{2,1,0:T(2,128)(2,1)} reshape(bf16[64,800]{1,0:T(8,128)(2,1)} %convert_element_type.40) | data formatting | bytes 204800 | tf_op jit(solution)/shard_map/reshape | solution.py:247
  41.5 3.5 %all-to-all-start.2 = ((bf16[32,2,800]{2,1,0:T(2,128)(2,1)}), bf16[32,2,800]{2,1,0:T(2,128)(2,1)}, u32[]{:S(2)}, u32[]{:S(2)}) async-start(bf16[32,2,800]{2,1,0:T(2,128)(2,1)} %reshape.188), calls=%async_computation.2 | async-start | bytes 229376 | tf_op jit(solution)/shard_map/all_to_all | solution.py:246
  45.0 4.3 %shard_map.113 = (f32[256,1024]{1,0:T(8,128)S(1)}, f32[256,1024]{1,0:T(8,128)S(1)}, f32[8,800]{1,0:T(8,128)}) custom-call(s32[1,256]{1,0:T(1,128)S(1)} %get-tuple-element.32.wrow, s32[1,256]{1,0:T(1,128)S(1)} %get-tuple-element.31.crow, s32[1,256]{1,0:T(1,128)S(1)} %get-tuple-element.35.scomb, s32[1,256]{1,0:T(1,128)S(1)} %bitcast.40, ...), custom_call_target="tpu_custom_call" | custom-call | tf_op jit(solution)/shard_map/pallas_call | solution.py:132
  49.2 0.5 add_convert_fusion
  49.7 0.4 reshape.186
  50.1 1.1 %copy.58 = bf16[256,2,400]{0,2,1:T(8,128)(2,1)} copy(bf16[256,2,400]{2,1,0:T(2,128)(2,1)S(1)} %bitcast.41) | data formatting | bytes 819200 | tf_op jit(solution)/shard_map/slice | solution.py:168
  51.2 0.4 reshape.187
  51.6 1.1 %copy.59 = bf16[256,2,400]{0,2,1:T(8,128)(2,1)} copy(bf16[256,2,400]{2,1,0:T(2,128)(2,1)S(1)} %bitcast.42) | data formatting | bytes 819200 | tf_op jit(solution)/shard_map/slice | solution.py:168
  52.6 0.5 all-to-all-done.2
  53.1 1.8 %convolution_bitcast_fusion = f32[32,800]{1,0:T(8,128)} fusion(bf16[32,2,800]{2,1,0:T(2,128)(2,1)} %all-to-all-done.2, s32[32,2]{0,1:T(2,128)S(1)} %bitcast.52), kind=kOutput, calls=%fused_computation.1 | convolution fusion | flops 3278848 | bytes 205056 | tf_op jit(solution)/shard_map/dkr,dkf->rf/dot_general | solution.py:255
  (42 shorter events, 1.1 us)
Async XLA Ops:
  0.6 16.4 %copy-start = (bf16[32,800]{1,0:T(8,128)(2,1)S(1)}, bf16[32,800]{1,0:T(8,128)(2,1)}, u32[]{:S(2)}) copy-start(bf16[32,800]{1,0:T(8,128)(2,1)} %param.11) | copy-start | bytes 153604
  2.0 14.4 %all-to-all-start = ((s32[32,1,2]{2,1,0:T(1,128)}), s32[32,1,2]{2,1,0:T(1,128)S(1)}, u32[]{:S(2)}, u32[]{:S(2)}) async-start(s32[32,1,2]{2,1,0:T(1,128)} %bitcast), calls=%async_computation | async-start | bytes 32768 | tf_op jit(solution)/shard_map/all_to_all | solution.py:193
  9.4 0.7 %copy-start.3 = (s32[1,1,16,2]{2,3,1,0:T(2,128)S(1)}, s32[1,1,16,2]{2,3,1,0:T(2,128)}, u32[]{:S(2)}) copy-start(s32[1,1,16,2]{2,3,1,0:T(2,128)} %param.17) | copy-start | bytes 388
  10.3 0.7 %copy-start.2 = (s32[1,1024]{1,0:T(1,128)S(1)}, s32[1,1024]{1,0:T(1,128)}, u32[]{:S(2)}) copy-start(s32[1,1024]{1,0:T(1,128)} %param.15) | copy-start | bytes 12292
  10.3 0.7 %copy-start.4 = (s32[256]{0:T(256)S(1)}, s32[256]{0:T(256)}, u32[]{:S(2)}) copy-start(s32[256]{0:T(256)} %param.13) | copy-start | bytes 3076
  10.3 0.7 %copy-start.5 = (s32[256]{0:T(256)S(1)}, s32[256]{0:T(256)}, u32[]{:S(2)}) copy-start(s32[256]{0:T(256)} %param.12) | copy-start | bytes 3076
  10.3 0.7 %copy-start.1 = (s32[256]{0:T(256)S(1)}, s32[256]{0:T(256)}, u32[]{:S(2)}) copy-start(s32[256]{0:T(256)} %param.14) | copy-start | bytes 3076
  12.9 5.0 %copy-start.6 = (bf16[256,800]{0,1:T(8,128)(2,1)S(1)}, bf16[256,800]{0,1:T(8,128)(2,1)}, u32[]{:S(2)}) copy-start(bf16[256,800]{0,1:T(8,128)(2,1)} %param.10) | copy-start | bytes 1228804
  17.3 7.3 %collective-permute-start = (s32[1792]{0:T(1024)S(1)}, s32[1792]{0:T(1024)S(1)}, u32[]{:S(2)}, u32[]{:S(2)}) collective-permute-start(s32[1792]{0:T(1024)S(1)} %pad_add_fusion.1), channel_id=1, source_target_pairs={{0,1},{1,0},{2,3},{3,2},{4,5},{5,4},{6,7},{7,6},{8,9},{9,8},{10,11... | collective-permute-start | bytes 21512 | tf_op jit(solution)/shard_map/ppermute | solution.py:12
  17.9 10.2 %collective-permute-start.1 = (bf16[256,800]{0,1:T(8,128)(2,1)S(1)}, bf16[256,800]{0,1:T(8,128)(2,1)S(1)}, u32[]{:S(2)}, u32[]{:S(2)}) collective-permute-start(bf16[256,800]{0,1:T(8,128)(2,1)S(1)} %copy-done.6), channel_id=1, source_target_pairs={{0,2},{2,4},{4,6},{6,8},{8,10},{10,12},{12,14},{14,16},{16,18},{18... | collective-permute-start | bytes 1228808 | tf_op jit(solution)/shard_map/ppermute | solution.py:12
  18.8 15.9 %all-to-all-start.1 = ((bf16[32,4,800]{2,1,0:T(4,128)(2,1)}), bf16[32,4,800]{2,1,0:T(4,128)(2,1)S(1)}, u32[]{:S(2)}, u32[]{:S(2)}) async-start(bf16[32,4,800]{2,1,0:T(4,128)(2,1)} %copy.55), calls=%async_computation.1 | async-start | bytes 458752 | tf_op jit(solution)/shard_map/all_to_all | solution.py:222
  41.5 11.6 %all-to-all-start.2 = ((bf16[32,2,800]{2,1,0:T(2,128)(2,1)}), bf16[32,2,800]{2,1,0:T(2,128)(2,1)}, u32[]{:S(2)}, u32[]{:S(2)}) async-start(bf16[32,2,800]{2,1,0:T(2,128)(2,1)} %reshape.188), calls=%async_computation.2 | async-start | bytes 229376 | tf_op jit(solution)/shard_map/all_to_all | solution.py:246
